TPU v7x, 128 devices: a whole 4x4x4 slice. The times are simulated.
128 devices in a mesh: row: 8 (over z, core), col: 16 (over y, x).
Axes of the slice: x: 4, y: 4, z: 4, core: 2. Of those that a mesh axis runs over, the one named last changes fastest.
Arguments:
- state: bfloat16 [13, 1024, 4096], P(None, 'row', 'col'), may hold values from -6 to 6
- tile_ids: int32 [8, 32], P('row'), may hold values from 0 to 127, as said below
- kernel_one: bfloat16 [64, 13, 3, 3], replicated, may hold values from -0.5 to 0.5
- bias_one: float32 [64], replicated, may hold values from -3 to 3
- kernel_two: bfloat16 [64, 64, 3, 3], replicated, may hold values from -0.25 to 0.25
- bias_two: float32 [64], replicated, may hold values from -3 to 3
- kernel_three: bfloat16 [64, 64, 3, 3], replicated, may hold values from -0.25 to 0.25
- bias_three: float32 [64], replicated, may hold values from -3 to 3
- kernel_flux: bfloat16 [26, 64, 3, 3], replicated, may hold values from -0.25 to 0.25
- bias_flux: float32 [26], replicated, may hold values from -3 to 3
Outputs:
- closure: bfloat16 [13, 1024, 4096], P(None, 'row', 'col')
Inputs may be any that keep to these rules, and one draw needn't show every extreme that they name: Each row of tile_ids holds 32 distinct ids in ascending order; at most 4 of them name tiles of one block, and in every row some block holds exactly that many.
All inputs are finite; a program needn't handle non-finite values.
Results may differ from a plain program's by a relative error of at most 0.012.
The roundings to bfloat16 on the way count: a program that leaves them out, or rounds other values in their place, can miss the bound.
Values may be sent and summed in bfloat16 or wider, within the bound.
No kernel may reach another device: no remote copies, remote signals or barrier semaphores. Data moves between devices by JAX's collectives and lax.ppermute only.
A program may use at most 64 MiB of HBM per device.

v0:
```python
import jax
import jax.numpy as jnp
from jax import lax
from jax.sharding import PartitionSpec as P

TILE = 64


dilations = (1, 2, 4, 8)


def with_halo(cells, sides, width):
    for axis, dim in sides:
        count = lax.axis_size(axis)
        ends = count - 1
        head = lax.slice_in_dim(cells, 0, width, axis=dim)
        tail = lax.slice_in_dim(cells, cells.shape[dim] - width, cells.shape[dim], axis=dim)
        cells = jnp.concatenate(
            [
                lax.ppermute(tail, axis, [(i, (i + 1) % count) for i in range(ends)]),
                cells,
                lax.ppermute(head, axis, [((i + 1) % count, i) for i in range(ends)]),
            ],
            axis=dim,
        )
    return cells


def evaluate(windows, anchor_y, anchor_x, layers, grid_h, grid_w):
    values = windows
    offset = sum(dilations)
    for layer_index in range(4):
        spread = dilations[layer_index]
        kernel, bias_term = layers[layer_index]
        summed = lax.conv_general_dilated(
            values,
            kernel,
            (1, 1),
            "VALID",
            rhs_dilation=(spread, spread),
            dimension_numbers=("NCHW", "OIHW", "NCHW"),
            preferred_element_type=jnp.float32,
        )
        summed = summed + bias_term[None, :, None, None]
        offset = offset - spread
        if layer_index < 3:
            indices = jnp.arange(summed.shape[2], dtype=jnp.int32)
            row_ids = anchor_y[:, None] - offset + indices[None, :]
            col_ids = anchor_x[:, None] - offset + indices[None, :]
            inside = ((row_ids >= 0) & (row_ids < grid_h))[:, None, :, None] & (
                (col_ids >= 0) & (col_ids < grid_w)
            )[:, None, None, :]
            values = jnp.where(inside, jax.nn.silu(summed), 0.0).astype(jnp.bfloat16)
        else:
            values = summed.astype(jnp.bfloat16)
    return values


def body(
    state,
    tile_ids,
    kernel_one,
    bias_one,
    kernel_two,
    bias_two,
    kernel_three,
    bias_three,
    kernel_flux,
    bias_flux,
):
    moments, block_h, block_w = state.shape
    col_count = lax.axis_size("col")
    row_count = lax.axis_size("row")
    my_row = lax.axis_index("row")
    my_col = lax.axis_index("col")
    margin = sum(dilations)
    per_row = block_h // TILE
    per_col = block_w // TILE
    per_block = per_row * per_col
    window = TILE + 2 * margin
    grid_h = block_h * row_count
    grid_w = block_w * col_count
    listed = tile_ids[0]
    list_len = listed.shape[0]
    owners = listed // per_block
    local_ids = listed % per_block
    local_y = local_ids // per_col * TILE
    local_x = local_ids % per_col * TILE
    anchor_y = my_row * block_h + local_y
    anchor_x = owners * block_w + local_x
    layers = (
        (kernel_one, bias_one),
        (kernel_two, bias_two),
        (kernel_three, bias_three),
        (kernel_flux, bias_flux),
    )
    extended = with_halo(state, (("row", 1), ("col", 2)), margin)
    first_pos = jnp.sum((owners < my_col).astype(jnp.int32))
    own_count = jnp.sum((owners == my_col).astype(jnp.int32))

    def cut_window(top_cell, left_cell):
        return lax.dynamic_slice(
            extended, (jnp.int32(0), top_cell, left_cell), (moments, window, window)
        )

    per_eval = list_len // col_count
    capacity = (2 * per_eval + col_count - 1) // col_count
    rotation = 1
    peer_ids = jnp.arange(col_count, dtype=jnp.int32)
    lag_slot = (peer_ids - rotation - first_pos) % col_count
    send_rank = lag_slot[:, None] + col_count * jnp.arange(capacity, dtype=jnp.int32)[None, :]
    filled = (send_rank < own_count).reshape(-1)
    sent_pos = jnp.minimum(first_pos + send_rank, list_len - 1).reshape(-1)
    windows_out = jax.vmap(cut_window)(local_y[sent_pos], local_x[sent_pos])
    windows_out = jnp.where(filled[:, None, None, None], windows_out, jnp.zeros((), jnp.bfloat16))
    windows_out = windows_out.reshape(col_count, capacity, moments, window, window)
    arrived = lax.all_to_all(windows_out, "col", split_axis=0, concat_axis=0, tiled=True)
    first_of = jnp.sum((owners[None, :] < peer_ids[:, None]).astype(jnp.int32), axis=1)
    held_pos = (my_col - rotation) % col_count + col_count * jnp.arange(per_eval, dtype=jnp.int32)
    sources = owners[held_pos]
    slot_ids = (held_pos - first_of[sources]) // col_count
    results = evaluate(
        arrived[sources, slot_ids], anchor_y[held_pos], anchor_x[held_pos], layers, grid_h, grid_w
    )
    outgoing = (
        jnp.zeros((col_count, capacity, 2 * moments, TILE, TILE), jnp.bfloat16)
        .at[sources, slot_ids]
        .set(results)
    )
    returned = lax.all_to_all(outgoing, "col", split_axis=0, concat_axis=0, tiled=True)
    returned = returned.reshape(col_count * capacity, 2 * moments, TILE, TILE)
    slot_match = (
        local_ids[sent_pos][None, :] == jnp.arange(per_block, dtype=jnp.int32)[:, None]
    ) & filled[None, :]
    flat_ids = jnp.arange(col_count * capacity, dtype=jnp.int32)
    slot_of = jnp.sum(jnp.where(slot_match, flat_ids[None, :], 0), axis=1)
    present = jnp.any(slot_match, axis=1)
    placed = jnp.where(present[:, None, None, None], returned[slot_of], jnp.zeros((), jnp.bfloat16))
    flux_field = (
        placed.reshape(per_row, per_col, 2 * moments, TILE, TILE)
        .transpose(2, 0, 3, 1, 4)
        .reshape(2 * moments, block_h, block_w)
    )
    rimmed = with_halo(flux_field, (("row", 1), ("col", 2)), 1)
    across = rimmed[:moments, 1:-1, :].astype(jnp.float32)
    downward = rimmed[moments:, :, 1:-1].astype(jnp.float32)
    difference = across[:, :, 2:] - across[:, :, :-2] + (downward[:, 2:, :] - downward[:, :-2, :])
    return (-0.5 * difference).astype(jnp.bfloat16)


def solution(mesh):
    return jax.shard_map(
        body,
        mesh=mesh,
        in_specs=(P(None, "row", "col"), P("row", None), P(), P(), P(), P(), P(), P(), P(), P()),
        out_specs=P(None, "row", "col"),
        check_vma=False,
    )
```

profile of v0, /device:TPU:7, one launch (start us, length us, event | category | flops | bytes accessed | tf_op | source)
XLA Modules:
  0.0 484.7 jit_solution(14288733174458986676)
XLA Ops:
  1.0 4.1 collective-permute-start
  5.1 1.9 collective-permute-start.1
  13.9 3.1 collective-permute-start.2
  17.1 2.2 collective-permute-start.3
  20.5 4.1 collective-permute-done.3
  24.6 2.9 pad_maximum_fusion
  27.5 69.4 %while.1 = (s32[]{:T(128)}, bf16[13,158,286]{1,2,0:T(8,128)(2,1)}, s32[16,3]{0,1:T(4,128)S(1)}, bf16[16,13,94,94]{3,2,1,0:T(8,128)(2,1)}, s32[]{:T(128)}) while((s32[]{:T(128)}, bf16[13,158,286]{1,2,0:T(8,128)(2,1)}, s32[16,3]{0,1:T(4,128)S(1)}, bf16[16,13,94,94]{3,2,1,0:T(8,128)(2,1)}, s32[]{:T(128)}) %tuple.41), condition=%wide.while_cond, body=%wide.while_body.sunk | while | flops 2 | bytes 1468793 | solution.py:102
  28.2 2.7 constant_dynamic-slice_fusion.5
  32.5 2.7 constant_dynamic-slice_fusion.5
  36.8 2.7 constant_dynamic-slice_fusion.5
  41.2 2.7 constant_dynamic-slice_fusion.5
  45.5 2.7 constant_dynamic-slice_fusion.5
  49.8 2.7 constant_dynamic-slice_fusion.5
  54.2 2.7 constant_dynamic-slice_fusion.5
  58.5 2.7 constant_dynamic-slice_fusion.5
  62.8 2.7 constant_dynamic-slice_fusion.5
  67.2 2.6 constant_dynamic-slice_fusion.5
  71.5 2.7 constant_dynamic-slice_fusion.5
  75.8 2.7 constant_dynamic-slice_fusion.5
  80.2 2.7 constant_dynamic-slice_fusion.5
  84.5 2.7 constant_dynamic-slice_fusion.5
  88.9 2.7 constant_dynamic-slice_fusion.5
  93.2 2.7 constant_dynamic-slice_fusion.5
  96.9 5.1 %bitcast_select_fusion = bf16[16,1,13,94,94]{4,3,2,1,0:T(8,128)(2,1)} fusion(bf16[16,13,94,94]{3,2,1,0:T(8,128)(2,1)} %get-tuple-element.12, pred[16]{0:T(512)(128)(4,1)S(1)} %fusion.27), kind=kLoop, calls=%fused_computation.35 | loop fusion | flops 1837888 | bytes 7351568 | tf_op jit(solution)/shard_map/jit(_where)/select_n | solution.py:115
  102.1 6.7 %all-to-all-start = ((bf16[16,1,13,94,94]{4,3,2,1,0:T(8,128)(2,1)}), bf16[16,1,13,94,94]{4,3,2,1,0:T(8,128)(2,1)}, u32[]{:S(2)}, u32[]{:S(2)}) async-start(bf16[16,1,13,94,94]{4,3,2,1,0:T(8,128)(2,1)} %bitcast_select_fusion), calls=%async_computation | async-start | bytes 10223616 | tf_op jit(solution)/shard_map/all_to_all | solution.py:117
  112.1 72.5 %all-to-all-done = bf16[16,1,13,94,94]{4,3,2,1,0:T(8,128)(2,1)} async-done(((bf16[16,1,13,94,94]{4,3,2,1,0:T(8,128)(2,1)}), bf16[16,1,13,94,94]{4,3,2,1,0:T(8,128)(2,1)}, u32[]{:S(2)}, u32[]{:S(2)}) %all-to-all-start) | async-done | bytes 3675808 | tf_op jit(solution)/shard_map/all_to_all | solution.py:117
  184.6 3.1 gather_fusion.7
  187.7 1.9 copy.109
  191.3 9.5 %copy.94 = bf16[13,94,2,8,14]{0,3,2,4,1:T(8,128)(2,1)} copy(bf16[13,94,2,8,14]{1,2,4,3,0:T(2,128)(2,1)S(1)} %fusion.21) | data formatting | bytes 1094912 | tf_op jit(solution)/shard_map/conv_general_dilated | solution.py:35
  200.8 11.6 %fusion.10 = f32[92,16,12,64]{3,1,2,0:T(8,128)} fusion(bf16[64,13,3,3]{0,1,3,2:T(8,128)(2,1)S(1)} %copy-done.13, bf16[13,94,2,8,14]{0,3,2,4,1:T(8,128)(2,1)} %copy.94), kind=kOutput, calls=%fused_computation.30 | convolution fusion | flops 264536064 | bytes 5084416 | tf_op jit(solution)/shard_map/conv_general_dilated | solution.py:35
  212.4 9.7 %copy.95 = f32[92,16,12,64]{0,3,2,1:T(8,128)} copy(f32[92,16,12,64]{3,1,2,0:T(8,128)} %fusion.10) | data formatting | bytes 9043968 | tf_op jit(solution)/shard_map/conv_general_dilated | solution.py:35
  222.1 5.5 %divide_multiply_fusion.1 = bf16[92,16,12,64]{0,3,2,1:T(8,128)(2,1)S(1)} fusion(f32[92,16,12,64]{0,3,2,1:T(8,128)} %copy.95, f32[64]{0:T(128)S(1)} %copy-done.9, pred[16,12]{1,0:T(8,128)(4,1)S(1)} %copy-done.6), kind=kLoop, calls=%fused_computation.20 | loop fusion | flops 7913472 | bytes 6783424 | tf_op jit(solution)/shard_map/jit(silu)/mul | solution.py:53
  230.0 2.9 fusion.15
  232.9 11.5 %copy.96 = bf16[64,92,2,8,16]{0,3,2,4,1:T(8,128)(2,1)} copy(bf16[64,92,2,8,16]{1,0,4,3,2:T(8,128)(2,1)} %fusion.15) | data formatting | bytes 6029312 | tf_op jit(solution)/shard_map/conv_general_dilated | solution.py:35
  244.4 14.3 %fusion.6 = f32[88,16,12,64]{3,1,2,0:T(8,128)} fusion(bf16[64,64,3,3]{1,0,3,2:T(8,128)(2,1)S(1)} %copy-done, bf16[64,92,2,8,16]{0,3,2,4,1:T(8,128)(2,1)} %copy.96), kind=kOutput, calls=%fused_computation.24 | convolution fusion | flops 1245708288 | bytes 7413760 | tf_op jit(solution)/shard_map/conv_general_dilated | solution.py:35
  258.7 9.3 %copy.97 = f32[88,16,12,64]{0,3,2,1:T(8,128)} copy(f32[88,16,12,64]{3,1,2,0:T(8,128)} %fusion.6) | data formatting | bytes 8650752 | tf_op jit(solution)/shard_map/conv_general_dilated | solution.py:35
  268.0 5.7 %divide_multiply_fusion = bf16[88,16,12,64]{0,3,2,1:T(8,128)(2,1)S(1)} fusion(f32[88,16,12,64]{0,3,2,1:T(8,128)} %copy.97, f32[64]{0:T(128)S(1)} %copy-done.10, pred[16,12]{1,0:T(8,128)(4,1)S(1)} %copy-done.5), kind=kLoop, calls=%fused_computation.19 | loop fusion | flops 7569408 | bytes 6488512 | tf_op jit(solution)/shard_map/jit(silu)/mul | solution.py:53
  275.0 3.7 fusion.14
  278.7 8.8 %copy.98 = bf16[64,88,2,8,19]{0,3,2,4,1:T(8,128)(2,1)} copy(bf16[64,88,2,8,19]{1,0,4,3,2:T(8,128)(2,1)} %fusion.14) | data formatting | bytes 6848512 | tf_op jit(solution)/shard_map/conv_general_dilated | solution.py:35
  287.5 12.5 %fusion.2 = f32[80,16,11,64]{3,1,2,0:T(8,128)} fusion(bf16[64,64,3,3]{1,0,3,2:T(8,128)(2,1)S(1)} %copy-done.11, bf16[64,88,2,8,19]{0,3,2,4,1:T(8,128)(2,1)} %copy.98), kind=kOutput, calls=%fused_computation.17 | convolution fusion | flops 1038090240 | bytes 7102464 | tf_op jit(solution)/shard_map/conv_general_dilated | solution.py:35
  300.0 8.6 %copy.99 = f32[80,16,11,64]{0,3,2,1:T(8,128)} copy(f32[80,16,11,64]{3,1,2,0:T(8,128)} %fusion.2) | data formatting | bytes 7208960 | tf_op jit(solution)/shard_map/conv_general_dilated | solution.py:35
  308.6 4.9 %divide_multiply_fusion.2 = bf16[80,16,11,64]{0,3,2,1:T(8,128)(2,1)S(1)} fusion(f32[80,16,11,64]{0,3,2,1:T(8,128)} %copy.99, f32[64]{0:T(128)S(1)} %copy-done.7, pred[16,11]{1,0:T(8,128)(4,1)S(1)} %copy-done.3), kind=kLoop, calls=%fused_computation.29 | loop fusion | flops 6307840 | bytes 5407152 | tf_op jit(solution)/shard_map/jit(silu)/mul | solution.py:53
  314.6 5.7 %copy.100 = bf16[2,64,80,80]{1,0,3,2:T(2,128)(2,1)} copy(bf16[2,64,80,80]{2,1,3,0:T(8,128)(2,1)S(1)} %fusion.13) | data formatting | bytes 3276800 | tf_op jit(solution)/shard_map/convert_element_type | solution.py:53
  320.4 17.9 %fusion.45 = f32[2,26,64,64]{1,0,3,2:T(2,128)} fusion(bf16[2,64,80,80]{1,0,3,2:T(2,128)(2,1)} %copy.100, bf16[26,64,3,3]{1,0,3,2:T(8,128)(2,1)S(1)} %copy-done.12), kind=kOutput, calls=%fused_computation.144 | convolution fusion | flops 245366784 | bytes 2520320 | tf_op jit(solution)/shard_map/conv_general_dilated | solution.py:35
  338.2 5.5 %copy.101 = f32[2,26,64,64]{3,2,1,0:T(8,128)S(1)} copy(f32[2,26,64,64]{1,0,3,2:T(2,128)} %fusion.45) | data formatting | bytes 1703936 | tf_op jit(solution)/shard_map/conv_general_dilated | solution.py:35
  344.0 4.6 broadcast.712
  348.6 2.6 scatter_fusion
  351.2 13.1 %reshape.561 = bf16[16,2,53248]{2,1,0:T(2,128)(2,1)} reshape(bf16[16,1,26,64,64]{4,3,2,1,0:T(8,128)(2,1)} %bitcast.119) | data formatting | bytes 6815744
  364.3 7.9 %all-to-all-start.1 = ((bf16[16,2,53248]{2,1,0:T(2,128)(2,1)}), bf16[16,2,53248]{2,1,0:T(2,128)(2,1)}, u32[]{:S(2)}, u32[]{:S(2)}) async-start(bf16[16,2,53248]{2,1,0:T(2,128)(2,1)} %reshape.561), calls=%async_computation.1 | async-start | bytes 6815744 | tf_op jit(solution)/shard_map/all_to_all | solution.py:130
  373.2 48.9 %all-to-all-done.1 = bf16[16,2,53248]{2,1,0:T(2,128)(2,1)} async-done(((bf16[16,2,53248]{2,1,0:T(2,128)(2,1)}), bf16[16,2,53248]{2,1,0:T(2,128)(2,1)}, u32[]{:S(2)}, u32[]{:S(2)}) %all-to-all-start.1) | async-done | bytes 3407904 | tf_op jit(solution)/shard_map/all_to_all | solution.py:130
  422.1 12.7 %reshape.562 = bf16[16,1,26,64,64]{4,3,2,1,0:T(8,128)(2,1)} reshape(bf16[16,2,53248]{2,1,0:T(2,128)(2,1)} %all-to-all-done.1) | data formatting | bytes 6815744
  434.8 5.7 %gather_fusion.8 = bf16[8,26,64,64]{3,2,1,0:T(8,128)(2,1)} fusion(bf16[16,26,64,64]{3,2,1,0:T(8,128)(2,1)} %bitcast.124, s32[1024]{0:T(1024)S(1)} %pad_clamp_fusion), kind=kCustom, calls=%fused_computation.8 | custom fusion | bytes 3407904 | tf_op jit(solution)/shard_map/gather | solution.py:138
  440.5 2.3 select_bitcast_fusion
  442.8 5.3 %copy.103 = bf16[26,2,64,4,64]{4,3,2,1,0:T(4,128)(2,1)} copy(bf16[26,2,64,4,64]{4,2,0,3,1:T(8,128)(2,1)S(1)} %select_bitcast_fusion) | data formatting | bytes 3407872 | tf_op jit(solution)/shard_map/transpose | solution.py:141
  448.1 5.1 %reshape.427 = bf16[26,128,256]{2,1,0:T(8,128)(2,1)S(1)} reshape(bf16[26,2,64,4,64]{4,3,2,1,0:T(4,128)(2,1)} %copy.103) | data formatting | bytes 3407872 | tf_op jit(solution)/shard_map/reshape | solution.py:142
  453.3 1.9 collective-permute-start.4
  455.2 2.5 collective-permute-start.5
  457.8 2.6 collective-permute-done.5
  464.2 1.9 copy.104
  466.1 4.1 collective-permute-start.6
  470.8 1.9 collective-permute-start.7
  472.8 2.5 slice_convert_fusion
  478.8 1.9 fusion.20
  480.7 3.8 fusion.19
  (156 shorter events, 54.7 us)
Async XLA Ops:
  0.0 244.4 %copy-start = (bf16[64,64,3,3]{1,0,3,2:T(8,128)(2,1)S(1)}, bf16[64,64,3,3]{1,0,3,2:T(8,128)(2,1)}, u32[]{:S(2)}) copy-start(bf16[64,64,3,3]{1,0,3,2:T(8,128)(2,1)} %param.14) | copy-start | bytes 221188
  1.0 11.7 %collective-permute-start = (bf16[13,15,256]{2,1,0:T(8,128)(2,1)S(1)}, bf16[13,15,256]{2,1,0:T(8,128)(2,1)S(1)}, u32[]{:S(2)}, u32[]{:S(2)}) collective-permute-start(bf16[13,15,256]{2,1,0:T(8,128)(2,1)S(1)} %get-tuple-element.53), channel_id=1, source_target_pairs={{0,16},{16,32},{32,48},{48,64},{64,80},{80,96},{96,112},{1,17},{17... | collective-permute-start | bytes 299528 | tf_op jit(solution)/shard_map/ppermute | solution.py:20
  5.1 8.1 %collective-permute-start.1 = (bf16[13,15,256]{2,1,0:T(8,128)(2,1)S(1)}, bf16[13,15,256]{2,1,0:T(8,128)(2,1)S(1)}, u32[]{:S(2)}, u32[]{:S(2)}) collective-permute-start(bf16[13,15,256]{2,1,0:T(8,128)(2,1)S(1)} %get-tuple-element.54), channel_id=1, source_target_pairs={{16,0},{32,16},{48,32},{64,48},{80,64},{96,80},{112,96},{17,1},{33... | collective-permute-start | bytes 299528 | tf_op jit(solution)/shard_map/ppermute | solution.py:22
  13.9 6.6 %collective-permute-start.2 = (bf16[13,158,15]{1,2,0:T(8,128)(2,1)S(1)}, bf16[13,158,15]{1,2,0:T(8,128)(2,1)S(1)}, u32[]{:S(2)}, u32[]{:S(2)}) collective-permute-start(bf16[13,158,15]{1,2,0:T(8,128)(2,1)S(1)} %get-tuple-element.47), channel_id=1, source_target_pairs={{0,1},{1,2},{2,3},{3,4},{4,5},{5,6},{6,7},{7,8},{8,9},{9,10},{10,1... | collective-permute-start | bytes 184868 | tf_op jit(solution)/shard_map/ppermute | solution.py:20
  17.1 7.6 %collective-permute-start.3 = (bf16[13,158,15]{1,2,0:T(8,128)(2,1)S(1)}, bf16[13,158,15]{1,2,0:T(8,128)(2,1)S(1)}, u32[]{:S(2)}, u32[]{:S(2)}) collective-permute-start(bf16[13,158,15]{1,2,0:T(8,128)(2,1)S(1)} %get-tuple-element.48), channel_id=1, source_target_pairs={{1,0},{2,1},{3,2},{4,3},{5,4},{6,5},{7,6},{8,7},{9,8},{10,9},{11,1... | collective-permute-start | bytes 184868 | tf_op jit(solution)/shard_map/ppermute | solution.py:22
  102.1 8.7 %copy-start.4 = (s32[1,32]{1,0:T(1,128)S(1)}, s32[1,32]{1,0:T(1,128)}, u32[]{:S(2)}) copy-start(s32[1,32]{1,0:T(1,128)} %param.11) | copy-start | bytes 388
  102.1 82.5 %all-to-all-start = ((bf16[16,1,13,94,94]{4,3,2,1,0:T(8,128)(2,1)}), bf16[16,1,13,94,94]{4,3,2,1,0:T(8,128)(2,1)}, u32[]{:S(2)}, u32[]{:S(2)}) async-start(bf16[16,1,13,94,94]{4,3,2,1,0:T(8,128)(2,1)} %bitcast_select_fusion), calls=%async_computation | async-start | bytes 10223616 | tf_op jit(solution)/shard_map/all_to_all | solution.py:117
  190.5 10.3 %copy-start.13 = (bf16[64,13,3,3]{0,1,3,2:T(8,128)(2,1)S(1)}, bf16[64,13,3,3]{0,1,3,2:T(8,128)(2,1)}, u32[]{:S(2)}) copy-start(bf16[64,13,3,3]{0,1,3,2:T(8,128)(2,1)} %param.12) | copy-start | bytes 44932
  212.4 9.7 %copy-start.6 = (pred[16,12]{1,0:T(8,128)(4,1)S(1)}, pred[16,12]{1,0:T(8,128)(4,1)}, u32[]{:S(2)}) copy-start(pred[16,12]{1,0:T(8,128)(4,1)} %constant.185) | copy-start | bytes 580
  212.4 9.7 %copy-start.9 = (f32[64]{0:T(128)S(1)}, f32[64]{0:T(128)}, u32[]{:S(2)}) copy-start(f32[64]{0:T(128)} %param.13) | copy-start | bytes 772
  258.7 9.3 %copy-start.5 = (pred[16,12]{1,0:T(8,128)(4,1)S(1)}, pred[16,12]{1,0:T(8,128)(4,1)}, u32[]{:S(2)}) copy-start(pred[16,12]{1,0:T(8,128)(4,1)} %constant.184) | copy-start | bytes 580
  258.7 9.3 %copy-start.10 = (f32[64]{0:T(128)S(1)}, f32[64]{0:T(128)}, u32[]{:S(2)}) copy-start(f32[64]{0:T(128)} %param.15) | copy-start | bytes 772
  278.7 8.8 %copy-start.11 = (bf16[64,64,3,3]{1,0,3,2:T(8,128)(2,1)S(1)}, bf16[64,64,3,3]{1,0,3,2:T(8,128)(2,1)}, u32[]{:S(2)}) copy-start(bf16[64,64,3,3]{1,0,3,2:T(8,128)(2,1)} %param.16) | copy-start | bytes 221188
  300.0 8.6 %copy-start.3 = (pred[16,11]{1,0:T(8,128)(4,1)S(1)}, pred[16,11]{1,0:T(8,128)(4,1)}, u32[]{:S(2)}) copy-start(pred[16,11]{1,0:T(8,128)(4,1)} %constant.183) | copy-start | bytes 532
  300.0 8.6 %copy-start.7 = (f32[64]{0:T(128)S(1)}, f32[64]{0:T(128)}, u32[]{:S(2)}) copy-start(f32[64]{0:T(128)} %param.17) | copy-start | bytes 772
  314.6 5.7 %copy-start.12 = (bf16[26,64,3,3]{1,0,3,2:T(8,128)(2,1)S(1)}, bf16[26,64,3,3]{1,0,3,2:T(8,128)(2,1)}, u32[]{:S(2)}) copy-start(bf16[26,64,3,3]{1,0,3,2:T(8,128)(2,1)} %param.18) | copy-start | bytes 89860
  338.2 5.5 %copy-start.8 = (f32[26]{0:T(128)S(1)}, f32[26]{0:T(128)}, u32[]{:S(2)}) copy-start(f32[26]{0:T(128)} %param.19) | copy-start | bytes 316
  364.3 57.9 %all-to-all-start.1 = ((bf16[16,2,53248]{2,1,0:T(2,128)(2,1)}), bf16[16,2,53248]{2,1,0:T(2,128)(2,1)}, u32[]{:S(2)}, u32[]{:S(2)}) async-start(bf16[16,2,53248]{2,1,0:T(2,128)(2,1)} %reshape.561), calls=%async_computation.1 | async-start | bytes 6815744 | tf_op jit(solution)/shard_map/all_to_all | solution.py:130
  453.3 4.5 collective-permute-start.4
  455.2 5.2 %collective-permute-start.5 = (bf16[26,1,256]{2,1,0:T(2,128)(2,1)S(1)}, bf16[26,1,256]{2,1,0:T(2,128)(2,1)S(1)}, u32[]{:S(2)}, u32[]{:S(2)}) collective-permute-start(bf16[26,1,256]{2,1,0:T(2,128)(2,1)S(1)} %get-tuple-element.52), channel_id=1, source_target_pairs={{16,0},{32,16},{48,32},{64,48},{80,64},{96,80},{112,96},{17,1},{33... | collective-permute-start | bytes 39944 | tf_op jit(solution)/shard_map/ppermute | solution.py:22
  461.6 1.3 copy-start.2
  466.1 9.3 %collective-permute-start.6 = (bf16[26,130,1]{1,0,2:T(8,128)(2,1)S(1)}, bf16[26,130,1]{1,0,2:T(8,128)(2,1)S(1)}, u32[]{:S(2)}, u32[]{:S(2)}) collective-permute-start(bf16[26,130,1]{1,0,2:T(8,128)(2,1)S(1)} %copy.104), channel_id=1, source_target_pairs={{0,1},{1,2},{2,3},{3,4},{4,5},{5,6},{6,7},{7,8},{8,9},{9,10},{10,1... | collective-permute-start | bytes 20288 | tf_op jit(solution)/shard_map/ppermute | solution.py:20
  470.8 6.6 %collective-permute-start.7 = (bf16[26,130,1]{1,0,2:T(8,128)(2,1)S(1)}, bf16[26,130,1]{1,0,2:T(8,128)(2,1)S(1)}, u32[]{:S(2)}, u32[]{:S(2)}) collective-permute-start(bf16[26,130,1]{1,0,2:T(8,128)(2,1)S(1)} %copy.105), channel_id=1, source_target_pairs={{1,0},{2,1},{3,2},{4,3},{5,4},{6,5},{7,6},{8,7},{9,8},{10,9},{11,1... | collective-permute-start | bytes 20288 | tf_op jit(solution)/shard_map/ppermute | solution.py:22
  478.8 5.7 %copy-start.1 = (bf16[64,64,3,3]{1,0,3,2:T(8,128)(2,1)S(1)}, bf16[64,64,3,3]{1,0,3,2:T(8,128)(2,1)}, u32[]{:S(2)}) copy-start(bf16[64,64,3,3]{1,0,3,2:T(8,128)(2,1)} %param.14) | copy-start | bytes 221188
where the time goes:
time: 493 us; the launch traced here: 485 us
  local copies, waits for them, and re-layouts  210 us (43%)
  waiting for transfers between devices  130 us (26%)
  matrix products  56.2 us (11%)
  other arithmetic  51.9 us (11%)
  starting transfers between devices  36.4 us (7%)
    all_to_all x1, waiting for transfers between devices, body(): lax.all_to_all(windows_out, 'col', split_axis=0, concat_axis=0, tiled=True)  72.5 us
    gather x80, local copies, waits for them, and re-layouts  69.4 us
    conv_general_dilated x10, local copies, waits for them, and re-layouts, evaluate(): lax.conv_general_dilated(values, kernel, (1, 1), 'VALID', rhs_dilation=(s...  63.2 us
    conv_general_dilated x4, matrix products, evaluate(): lax.conv_general_dilated(values, kernel, (1, 1), 'VALID', rhs_dilation=(s...  56.2 us
    all_to_all x1, waiting for transfers between devices, body(): lax.all_to_all(outgoing, 'col', split_axis=0, concat_axis=0, tiled=True)  48.9 us
    unnamed x32, local copies, waits for them, and re-layouts  30.6 us
    mul x3, other arithmetic, evaluate(): values = jnp.where(inside, jax.nn.silu(summed), 0.0).astype(jnp.bfloat16)  16.2 us
    ppermute x4, starting transfers between devices, with_halo(): lax.ppermute(tail, axis, [(i, (i + 1) % count) for i in range(ends)])  13.2 us
  transfers between devices with their start and end apart: 10, of which 5 were waited for; matrix products, arithmetic and copies ran while one was open for 3% of the time, Pallas kernels for 0%

commit v1 on v0

v1 whole, which is shorter than its diff:
```python
import jax
import jax.numpy as jnp
from jax import lax
from jax.sharding import PartitionSpec as P

TILE = 64


dilations = (1, 2, 4, 8)


def with_halo(cells, sides, width):
    for axis, dim in sides:
        count = lax.axis_size(axis)
        ends = count - 1
        head = lax.slice_in_dim(cells, 0, width, axis=dim)
        tail = lax.slice_in_dim(cells, cells.shape[dim] - width, cells.shape[dim], axis=dim)
        cells = jnp.concatenate(
            [
                lax.ppermute(tail, axis, [(i, (i + 1) % count) for i in range(ends)]),
                cells,
                lax.ppermute(head, axis, [((i + 1) % count, i) for i in range(ends)]),
            ],
            axis=dim,
        )
    return cells


def body(
    state,
    tile_ids,
    kernel_one,
    bias_one,
    kernel_two,
    bias_two,
    kernel_three,
    bias_three,
    kernel_flux,
    bias_flux,
):
    moments, block_h, block_w = state.shape
    col_count = lax.axis_size("col")
    row_count = lax.axis_size("row")
    my_row = lax.axis_index("row")
    my_col = lax.axis_index("col")
    margin = sum(dilations)
    per_row = block_h // TILE
    per_col = block_w // TILE
    per_block = per_row * per_col
    grid_h = block_h * row_count
    grid_w = block_w * col_count
    layers = (
        (kernel_one, bias_one),
        (kernel_two, bias_two),
        (kernel_three, bias_three),
        (kernel_flux, bias_flux),
    )
    values = with_halo(state, (("row", 1), ("col", 2)), margin)[None]
    offset = margin
    for layer_index in range(4):
        spread = dilations[layer_index]
        kernel, bias_term = layers[layer_index]
        summed = lax.conv_general_dilated(
            values,
            kernel,
            (1, 1),
            "VALID",
            rhs_dilation=(spread, spread),
            dimension_numbers=("NCHW", "OIHW", "NCHW"),
            preferred_element_type=jnp.float32,
        )
        summed = summed + bias_term[None, :, None, None]
        offset = offset - spread
        if layer_index < 3:
            row_ids = my_row * block_h - offset + jnp.arange(summed.shape[2], dtype=jnp.int32)
            col_ids = my_col * block_w - offset + jnp.arange(summed.shape[3], dtype=jnp.int32)
            inside = ((row_ids >= 0) & (row_ids < grid_h))[:, None] & (
                (col_ids >= 0) & (col_ids < grid_w)
            )[None, :]
            values = jnp.where(inside[None, None], jax.nn.silu(summed), 0.0).astype(jnp.bfloat16)
        else:
            flux = summed[0]
    listed = tile_ids[0]
    mine = (listed // per_block) == my_col
    local_ids = listed % per_block
    chosen = jnp.any(
        mine[None, :] & (local_ids[None, :] == jnp.arange(per_block, dtype=jnp.int32)[:, None]), axis=1
    )
    cell_mask = jnp.broadcast_to(
        chosen.reshape(per_row, 1, per_col, 1), (per_row, TILE, per_col, TILE)
    ).reshape(block_h, block_w)
    flux_field = jnp.where(cell_mask[None], flux, 0.0).astype(jnp.bfloat16)
    rimmed = with_halo(flux_field, (("row", 1), ("col", 2)), 1)
    across = rimmed[:moments, 1:-1, :].astype(jnp.float32)
    downward = rimmed[moments:, :, 1:-1].astype(jnp.float32)
    difference = across[:, :, 2:] - across[:, :, :-2] + (downward[:, 2:, :] - downward[:, :-2, :])
    return (-0.5 * difference).astype(jnp.bfloat16)


def solution(mesh):
    return jax.shard_map(
        body,
        mesh=mesh,
        in_specs=(P(None, "row", "col"), P("row", None), P(), P(), P(), P(), P(), P(), P(), P()),
        out_specs=P(None, "row", "col"),
        check_vma=False,
    )
```

time: 493 us -> 451 us (0.915)
  waiting for transfers between devices: 130 us -> 7.28 us
  matrix products: 56.2 us -> 107 us
  other arithmetic: 51.9 us -> 92.8 us
  starting transfers between devices: 36.4 us -> 24 us
    conv_general_dilated x10 -> x13, local copies, waits for them, and re-layouts: 63.2 us -> 185 us  [body(): lax.conv_general_dilated(values, kernel, (1, 1), 'VALID', rhs_dilation=(s...]
    all_to_all x2 -> x0, waiting for transfers between devices: 121 us -> none  [the longest x1 72.5 us: body(): lax.all_to_all(windows_out, 'col', split_axis=0, concat_axis=0, tiled=True)]
    gather x90 -> x0, local copies, waits for them, and re-layouts: 83.4 us -> none
    conv_general_dilated x4, matrix products: 56.2 us -> 107 us  [body(): lax.conv_general_dilated(values, kernel, (1, 1), 'VALID', rhs_dilation=(s...]
    convert_element_type x4, other arithmetic: 3.65 us -> 37.6 us  [the longest x3 35.7 us: body(): jnp.where(inside[None, None], jax.nn.silu(summed), 0.0).astype(jnp.bfloat16)]
    unnamed x32 -> x33, local copies, waits for them, and re-layouts: 30.6 us -> 1.62 us
    mul x3, other arithmetic: 16.2 us -> 43.9 us  [body(): jax.nn.silu(summed)]
    all_to_all x2 -> x0, starting transfers between devices: 14.6 us -> none  [the longest x1 7.92 us: body(): lax.all_to_all(outgoing, 'col', split_axis=0, concat_axis=0, tiled=True)]
  transfers between devices with their start and end apart: 10 -> 8, of which waited for: 5 -> 3; matrix products, arithmetic and copies ran while one was open for 3% -> 2% of each run, Pallas kernels for 0% -> 0%
where the time goes in v1:
time: 451 us; the launch traced here: 444 us
  local copies, waits for them, and re-layouts  212 us (47%)
  matrix products  107 us (24%)
  other arithmetic  92.8 us (21%)
  starting transfers between devices  24 us (5%)
  waiting for transfers between devices  7.28 us (2%)
    conv_general_dilated x13, local copies, waits for them, and re-layouts, body(): lax.conv_general_dilated(values, kernel, (1, 1), 'VALID', rhs_dilation=(s...  185 us
    conv_general_dilated x4, matrix products, body(): lax.conv_general_dilated(values, kernel, (1, 1), 'VALID', rhs_dilation=(s...  107 us
    mul x3, other arithmetic, body(): jax.nn.silu(summed)  43.9 us
    convert_element_type x3, other arithmetic, body(): jnp.where(inside[None, None], jax.nn.silu(summed), 0.0).astype(jnp.bfloat16)  35.7 us
    ppermute x4, starting transfers between devices, with_halo(): lax.ppermute(tail, axis, [(i, (i + 1) % count) for i in range(ends)])  14.4 us
    convert_element_type x1, local copies, waits for them, and re-layouts, body(): jnp.where(inside[None, None], jax.nn.silu(summed), 0.0).astype(jnp.bfloat16)  10.5 us
    ppermute x4, starting transfers between devices, with_halo(): lax.ppermute(head, axis, [((i + 1) % count, i) for i in range(ends)])  9.66 us
  transfers between devices with their start and end apart: 8, of which 3 were waited for; matrix products, arithmetic and copies ran while one was open for 2% of the time, Pallas kernels for 0%

profile of v1, /device:TPU:7, one launch (start us, length us, event | category | flops | bytes accessed | tf_op | source)
XLA Modules:
  0.0 444.1 jit_solution(11540299029573320295)
XLA Ops:
  0.0 1.0 fusion.72
  1.0 4.1 collective-permute-start
  5.1 1.9 collective-permute-start.1
  7.2 0.7 compare_bitcast_fusion
  8.0 0.1 broadcast_and_fusion.1
  8.1 0.7 broadcast_and_fusion.2
  8.8 0.7 fusion.58
  9.5 1.6 copy.108
  11.0 0.4 copy.107
  11.5 0.4 copy.109
  11.9 0.2 pad_maximum_fusion.8
  12.1 3.1 collective-permute-start.2
  15.2 2.2 collective-permute-start.3
  17.4 0.1 fusion.48
  17.6 0.1 broadcast_in_dim.77
  17.7 0.2 broadcast_in_dim.78
  17.9 0.7 copy.106
  18.6 4.2 collective-permute-done.3
  22.8 1.6 maximum_bitcast_fusion
  24.4 1.6 pad
  26.0 3.0 reshape.146
  29.0 32.1 %copy.111 = bf16[13,158,1,8,36]{0,3,4,1,2:T(8,128)(2,1)} copy(bf16[13,158,1,8,36]{1,4,3,0,2:T(8,128)(2,1)S(1)} %reshape.146) | data formatting | bytes 2366208 | tf_op jit(solution)/shard_map/conv_general_dilated | solution.py:63
  61.0 1.3 slice.64
  62.3 20.6 %fusion.30 = f32[156,8,36,64]{3,1,2,0:T(8,128)} fusion(bf16[64,13,3,3]{0,1,3,2:T(8,128)(2,1)S(1)} %copy-done.15, bf16[13,158,1,7,2]{0,3,4,1,2:T(8,128)(2,1)S(1)} %slice.64, bf16[13,158,1,8,36]{0,3,4,1,2:T(8,128)(2,1)} %copy.111), kind=kOutput, calls=%fused_computation.37 | convolution fusion | flops 676588224 | bytes 12757160 | tf_op jit(solution)/shard_map/conv_general_dilated | solution.py:63
  82.9 25.0 %copy.112 = f32[156,8,36,64]{0,3,2,1:T(8,128)} copy(f32[156,8,36,64]{3,1,2,0:T(8,128)} %fusion.30) | data formatting | bytes 23003136 | tf_op jit(solution)/shard_map/conv_general_dilated | solution.py:63
  107.9 14.8 %divide_multiply_fusion.1 = bf16[156,8,36,64]{0,3,2,1:T(8,128)(2,1)} fusion(f32[156,8,36,64]{0,3,2,1:T(8,128)} %copy.112, f32[64]{0:T(128)S(1)} %copy-done.10, pred[8,36]{1,0:T(8,128)(4,1)S(1)} %copy-done.7), kind=kLoop, calls=%fused_computation.9 | loop fusion | flops 20127744 | bytes 17252896 | tf_op jit(solution)/shard_map/jit(silu)/mul | solution.py:80
  122.7 12.3 %fusion.35 = bf16[64,156,1,284]{1,0,3,2:T(8,128)(2,1)} fusion(bf16[156,1,288,64]{0,3,2,1:T(8,128)(2,1)} %bitcast.51, pred[156,284]{0,1:T(8,128)(4,1)S(1)} %broadcast_and_fusion), kind=kLoop, calls=%fused_computation.41 | loop fusion | flops 2835456 | bytes 11386128 | tf_op jit(solution)/shard_map/convert_element_type | solution.py:80
  135.0 10.5 %pad.2 = bf16[64,156,1,288]{1,0,3,2:T(8,128)(2,1)} pad(bf16[64,156,1,284]{1,0,3,2:T(8,128)(2,1)} %fusion.35, bf16[]{:T(256)} %constant.80), padding=0_0x0_0x0_0x0_4 | pad | bytes 11421698 | tf_op jit(solution)/shard_map/convert_element_type | solution.py:80
  145.5 18.1 %copy.114 = bf16[64,156,1,8,36]{0,3,4,1,2:T(8,128)(2,1)} copy(bf16[64,156,1,8,36]{1,0,4,3,2:T(8,128)(2,1)} %bitcast.50) | data formatting | bytes 11501568 | tf_op jit(solution)/shard_map/conv_general_dilated | solution.py:63
  163.6 1.7 slice.66
  165.3 31.6 %fusion.23 = f32[152,8,36,64]{3,1,2,0:T(8,128)} fusion(bf16[64,64,3,3]{1,0,3,2:T(8,128)(2,1)S(1)} %copy-done, bf16[64,156,1,7,4]{0,3,4,1,2:T(8,128)(2,1)S(1)} %slice.66, bf16[64,156,1,8,36]{0,3,4,1,2:T(8,128)(2,1)} %copy.114), kind=kOutput, calls=%fused_computation.31 | convolution fusion | flops 3246686208 | bytes 17590272 | tf_op jit(solution)/shard_map/conv_general_dilated | solution.py:63
  196.8 24.7 %copy.115 = f32[152,8,36,64]{0,3,2,1:T(8,128)} copy(f32[152,8,36,64]{3,1,2,0:T(8,128)} %fusion.23) | data formatting | bytes 22413312 | tf_op jit(solution)/shard_map/conv_general_dilated | solution.py:63
  221.6 14.7 %divide_multiply_fusion = bf16[152,8,36,64]{0,3,2,1:T(8,128)(2,1)} fusion(f32[152,8,36,64]{0,3,2,1:T(8,128)} %copy.115, f32[64]{0:T(128)S(1)} %copy-done.11, pred[8,36]{1,0:T(8,128)(4,1)S(1)} %copy-done.6), kind=kLoop, calls=%fused_computation.8 | loop fusion | flops 19611648 | bytes 16810528 | tf_op jit(solution)/shard_map/jit(silu)/mul | solution.py:80
  236.2 11.9 %fusion.5 = bf16[152,1,280,64]{0,3,2,1:T(8,128)(2,1)} fusion(bf16[152,1,288,64]{0,3,2,1:T(8,128)(2,1)} %bitcast.52, pred[152,280]{0,1:T(8,128)(4,1)S(1)} %broadcast_and_fusion.1), kind=kLoop, calls=%fused_computation.13 | loop fusion | flops 2723840 | bytes 10937920 | tf_op jit(solution)/shard_map/convert_element_type | solution.py:80
  248.1 17.4 %copy.117 = bf16[64,152,1,8,35]{0,3,4,1,2:T(8,128)(2,1)} copy(bf16[64,152,1,8,35]{1,0,4,3,2:T(8,128)(2,1)} %bitcast.53) | data formatting | bytes 10895360 | tf_op jit(solution)/shard_map/conv_general_dilated | solution.py:63
  265.6 2.4 slice.68
  268.0 28.8 %fusion.16 = f32[144,8,35,64]{3,1,2,0:T(8,128)} fusion(bf16[64,64,3,3]{1,0,3,2:T(8,128)(2,1)S(1)} %copy-done.13, bf16[64,152,1,7,8]{0,3,4,1,2:T(8,128)(2,1)S(1)} %slice.68, bf16[64,152,1,8,35]{0,3,4,1,2:T(8,128)(2,1)} %copy.117), kind=kOutput, calls=%fused_computation.25 | convolution fusion | flops 2992791552 | bytes 16932864 | tf_op jit(solution)/shard_map/conv_general_dilated | solution.py:63
  296.9 24.1 %copy.118 = f32[144,8,35,64]{0,3,2,1:T(8,128)} copy(f32[144,8,35,64]{3,1,2,0:T(8,128)} %fusion.16) | data formatting | bytes 20643840 | tf_op jit(solution)/shard_map/conv_general_dilated | solution.py:63
  321.0 14.5 %divide_multiply_fusion.2 = bf16[144,8,35,64]{0,3,2,1:T(8,128)(2,1)} fusion(f32[144,8,35,64]{0,3,2,1:T(8,128)} %copy.118, f32[64]{0:T(128)S(1)} %copy-done.9, pred[8,35]{1,0:T(8,128)(4,1)S(1)} %copy-done.8), kind=kLoop, calls=%fused_computation.14 | loop fusion | flops 18063360 | bytes 15483416 | tf_op jit(solution)/shard_map/jit(silu)/mul | solution.py:80
  335.5 11.5 %fusion.6 = bf16[144,1,272,64]{0,3,2,1:T(8,128)(2,1)} fusion(bf16[144,1,280,64]{0,3,2,1:T(8,128)(2,1)} %bitcast.54, pred[144,272]{0,1:T(8,128)(4,1)S(1)} %copy-done.3), kind=kLoop, calls=%fused_computation.16 | loop fusion | flops 2506752 | bytes 10066176 | tf_op jit(solution)/shard_map/convert_element_type | solution.py:80
  347.0 16.6 %copy.120 = bf16[64,144,1,8,34]{0,3,4,1,2:T(8,128)(2,1)} copy(bf16[64,144,1,8,34]{1,0,4,3,2:T(8,128)(2,1)} %bitcast.55) | data formatting | bytes 10027008 | tf_op jit(solution)/shard_map/conv_general_dilated | solution.py:63
  363.6 3.7 slice.70
  367.4 25.7 %fusion.9 = f32[128,8,34,26]{3,1,2,0:T(8,128)} fusion(bf16[26,64,3,3]{1,0,3,2:T(8,128)(2,1)S(1)} %copy-done.14, bf16[64,144,1,7,16]{0,3,4,1,2:T(8,128)(2,1)S(1)} %slice.70, bf16[64,144,1,8,34]{0,3,4,1,2:T(8,128)(2,1)} %copy.120), kind=kOutput, calls=%fused_computation.19 | convolution fusion | flops 1064927232 | bytes 10728704 | tf_op jit(solution)/shard_map/conv_general_dilated | solution.py:63
  393.1 14.9 %copy.121 = f32[128,8,34,26]{0,1,3,2:T(8,128)} copy(f32[128,8,34,26]{3,1,2,0:T(8,128)} %fusion.9) | data formatting | bytes 7241728 | tf_op jit(solution)/shard_map/conv_general_dilated | solution.py:63
  408.0 2.5 select_add_fusion
  410.6 0.5 copy.122
  411.1 1.5 reshape.171
  412.6 1.9 fusion.41
  414.6 2.0 fusion.71
  416.5 1.9 copy.123
  418.4 5.2 %collective-permute-start.4 = (bf16[26,1,256]{2,0,1:T(8,128)(2,1)S(1)}, bf16[26,1,256]{2,0,1:T(8,128)(2,1)S(1)}, u32[]{:S(2)}, u32[]{:S(2)}) collective-permute-start(bf16[26,1,256]{2,0,1:T(8,128)(2,1)S(1)} %copy.123), channel_id=1, source_target_pairs={{0,16},{16,32},{32,48},{48,64},{64,80},{80,96},{96,112},{1,17},{17... | collective-permute-start | bytes 39944 | tf_op jit(solution)/shard_map/ppermute | solution.py:20
  423.7 0.9 copy.124
  424.6 1.9 collective-permute-start.5
  426.5 0.9 copy.125
  427.5 2.2 collective-permute-done.5
  429.6 1.6 copy.126
  431.3 1.1 pad_maximum_fusion.10
  432.4 1.9 collective-permute-start.6
  434.3 3.7 collective-permute-start.7
  438.0 2.1 fusion.45
  440.1 0.9 collective-permute-done.7
  441.0 0.7 fusion.46
  441.7 0.6 fusion.44
  442.3 1.3 copy.127
  (45 shorter events, 0.3 us)
Async XLA Ops:
  0.0 165.3 %copy-start = (bf16[64,64,3,3]{1,0,3,2:T(8,128)(2,1)S(1)}, bf16[64,64,3,3]{1,0,3,2:T(8,128)(2,1)}, u32[]{:S(2)}) copy-start(bf16[64,64,3,3]{1,0,3,2:T(8,128)(2,1)} %param.14) | copy-start | bytes 221188
  1.0 10.0 %collective-permute-start = (bf16[13,15,256]{2,1,0:T(8,128)(2,1)S(1)}, bf16[13,15,256]{2,1,0:T(8,128)(2,1)S(1)}, u32[]{:S(2)}, u32[]{:S(2)}) collective-permute-start(bf16[13,15,256]{2,1,0:T(8,128)(2,1)S(1)} %get-tuple-element.11), channel_id=1, source_target_pairs={{0,16},{16,32},{32,48},{48,64},{64,80},{80,96},{96,112},{1,17},{17... | collective-permute-start | bytes 299528 | tf_op jit(solution)/shard_map/ppermute | solution.py:20
  5.1 6.3 %collective-permute-start.1 = (bf16[13,15,256]{2,1,0:T(8,128)(2,1)S(1)}, bf16[13,15,256]{2,1,0:T(8,128)(2,1)S(1)}, u32[]{:S(2)}, u32[]{:S(2)}) collective-permute-start(bf16[13,15,256]{2,1,0:T(8,128)(2,1)S(1)} %get-tuple-element.12), channel_id=1, source_target_pairs={{16,0},{32,16},{48,32},{64,48},{80,64},{96,80},{112,96},{17,1},{33... | collective-permute-start | bytes 299528 | tf_op jit(solution)/shard_map/ppermute | solution.py:22
  12.1 6.5 %collective-permute-start.2 = (bf16[13,158,15]{1,2,0:T(8,128)(2,1)S(1)}, bf16[13,158,15]{1,2,0:T(8,128)(2,1)S(1)}, u32[]{:S(2)}, u32[]{:S(2)}) collective-permute-start(bf16[13,158,15]{1,2,0:T(8,128)(2,1)S(1)} %get-tuple-element.7), channel_id=1, source_target_pairs={{0,1},{1,2},{2,3},{3,4},{4,5},{5,6},{6,7},{7,8},{8,9},{9,10},{10,1... | collective-permute-start | bytes 184868 | tf_op jit(solution)/shard_map/ppermute | solution.py:20
  15.2 7.6 %collective-permute-start.3 = (bf16[13,158,15]{1,2,0:T(8,128)(2,1)S(1)}, bf16[13,158,15]{1,2,0:T(8,128)(2,1)S(1)}, u32[]{:S(2)}, u32[]{:S(2)}) collective-permute-start(bf16[13,158,15]{1,2,0:T(8,128)(2,1)S(1)} %get-tuple-element.8), channel_id=1, source_target_pairs={{1,0},{2,1},{3,2},{4,3},{5,4},{6,5},{7,6},{8,7},{9,8},{10,9},{11,1... | collective-permute-start | bytes 184868 | tf_op jit(solution)/shard_map/ppermute | solution.py:22
  26.0 36.3 %copy-start.15 = (bf16[64,13,3,3]{0,1,3,2:T(8,128)(2,1)S(1)}, bf16[64,13,3,3]{0,1,3,2:T(8,128)(2,1)}, u32[]{:S(2)}) copy-start(bf16[64,13,3,3]{0,1,3,2:T(8,128)(2,1)} %param.12) | copy-start | bytes 44932
  82.9 25.0 %copy-start.7 = (pred[8,36]{1,0:T(8,128)(4,1)S(1)}, pred[8,36]{1,0:T(8,128)(4,1)}, u32[]{:S(2)}) copy-start(pred[8,36]{1,0:T(8,128)(4,1)} %constant.97) | copy-start | bytes 868
  82.9 25.0 %copy-start.10 = (f32[64]{0:T(128)S(1)}, f32[64]{0:T(128)}, u32[]{:S(2)}) copy-start(f32[64]{0:T(128)} %param.13) | copy-start | bytes 772
  196.8 24.7 %copy-start.6 = (pred[8,36]{1,0:T(8,128)(4,1)S(1)}, pred[8,36]{1,0:T(8,128)(4,1)}, u32[]{:S(2)}) copy-start(pred[8,36]{1,0:T(8,128)(4,1)} %constant.96) | copy-start | bytes 868
  196.8 24.7 %copy-start.11 = (f32[64]{0:T(128)S(1)}, f32[64]{0:T(128)}, u32[]{:S(2)}) copy-start(f32[64]{0:T(128)} %param.15) | copy-start | bytes 772
  248.1 19.9 %copy-start.13 = (bf16[64,64,3,3]{1,0,3,2:T(8,128)(2,1)S(1)}, bf16[64,64,3,3]{1,0,3,2:T(8,128)(2,1)}, u32[]{:S(2)}) copy-start(bf16[64,64,3,3]{1,0,3,2:T(8,128)(2,1)} %param.16) | copy-start | bytes 221188
  296.9 24.1 %copy-start.8 = (pred[8,35]{1,0:T(8,128)(4,1)S(1)}, pred[8,35]{1,0:T(8,128)(4,1)}, u32[]{:S(2)}) copy-start(pred[8,35]{1,0:T(8,128)(4,1)} %constant.95) | copy-start | bytes 844
  296.9 24.1 %copy-start.9 = (f32[64]{0:T(128)S(1)}, f32[64]{0:T(128)}, u32[]{:S(2)}) copy-start(f32[64]{0:T(128)} %param.17) | copy-start | bytes 772
  321.0 14.5 %copy-start.3 = (pred[144,272]{0,1:T(8,128)(4,1)S(1)}, pred[144,272]{0,1:T(8,128)(4,1)}, u32[]{:S(2)}) copy-start(pred[144,272]{0,1:T(8,128)(4,1)} %broadcast_and_fusion.2) | copy-start | bytes 117508
  363.6 3.8 copy-start.14
  393.1 14.9 %copy-start.5 = (pred[8,34]{0,1:T(8,128)(4,1)S(1)}, pred[8,34]{0,1:T(8,128)(4,1)}, u32[]{:S(2)}) copy-start(pred[8,34]{0,1:T(8,128)(4,1)} %constant.94) | copy-start | bytes 820
  393.1 14.9 %copy-start.12 = (f32[26]{0:T(128)S(1)}, f32[26]{0:T(128)}, u32[]{:S(2)}) copy-start(f32[26]{0:T(128)} %param.19) | copy-start | bytes 316
  408.0 4.6 %copy-start.4 = (pred[128,256]{0,1:T(8,128)(4,1)S(1)}, pred[128,256]{0,1:T(8,128)(4,1)}, u32[]{:S(2)}) copy-start(pred[128,256]{0,1:T(8,128)(4,1)} %copy.106) | copy-start | bytes 98308
  418.4 8.1 %collective-permute-start.4 = (bf16[26,1,256]{2,0,1:T(8,128)(2,1)S(1)}, bf16[26,1,256]{2,0,1:T(8,128)(2,1)S(1)}, u32[]{:S(2)}, u32[]{:S(2)}) collective-permute-start(bf16[26,1,256]{2,0,1:T(8,128)(2,1)S(1)} %copy.123), channel_id=1, source_target_pairs={{0,16},{16,32},{32,48},{48,64},{64,80},{80,96},{96,112},{1,17},{17... | collective-permute-start | bytes 39944 | tf_op jit(solution)/shard_map/ppermute | solution.py:20
  424.6 5.1 %collective-permute-start.5 = (bf16[26,1,256]{2,0,1:T(8,128)(2,1)S(1)}, bf16[26,1,256]{2,0,1:T(8,128)(2,1)S(1)}, u32[]{:S(2)}, u32[]{:S(2)}) collective-permute-start(bf16[26,1,256]{2,0,1:T(8,128)(2,1)S(1)} %copy.124), channel_id=1, source_target_pairs={{16,0},{32,16},{48,32},{64,48},{80,64},{96,80},{112,96},{17,1},{33... | collective-permute-start | bytes 39944 | tf_op jit(solution)/shard_map/ppermute | solution.py:22
  431.3 9.8 %copy-start.2 = (bf16[26,1,256]{1,2,0:T(8,128)(2,1)S(1)}, bf16[26,1,256]{1,2,0:T(8,128)(2,1)}, u32[]{:S(2)}) copy-start(bf16[26,1,256]{1,2,0:T(8,128)(2,1)} %copy.126) | copy-start | bytes 39940
  432.4 7.7 %collective-permute-start.6 = (bf16[26,130,1]{1,2,0:T(2,128)(2,1)S(1)}, bf16[26,130,1]{1,2,0:T(2,128)(2,1)S(1)}, u32[]{:S(2)}, u32[]{:S(2)}) collective-permute-start(bf16[26,130,1]{1,2,0:T(2,128)(2,1)S(1)} %get-tuple-element.5), channel_id=1, source_target_pairs={{0,1},{1,2},{2,3},{3,4},{4,5},{5,6},{6,7},{7,8},{8,9},{9,10},{10,1... | collective-permute-start | bytes 20288 | tf_op jit(solution)/shard_map/ppermute | solution.py:20
  434.3 6.7 %collective-permute-start.7 = (bf16[26,130,1]{1,2,0:T(2,128)(2,1)S(1)}, bf16[26,130,1]{1,2,0:T(2,128)(2,1)S(1)}, u32[]{:S(2)}, u32[]{:S(2)}) collective-permute-start(bf16[26,130,1]{1,2,0:T(2,128)(2,1)S(1)} %get-tuple-element.6), channel_id=1, source_target_pairs={{1,0},{2,1},{3,2},{4,3},{5,4},{6,5},{7,6},{8,7},{9,8},{10,9},{11,1... | collective-permute-start | bytes 20288 | tf_op jit(solution)/shard_map/ppermute | solution.py:22
  438.0 5.6 %copy-start.1 = (bf16[64,64,3,3]{1,0,3,2:T(8,128)(2,1)S(1)}, bf16[64,64,3,3]{1,0,3,2:T(8,128)(2,1)}, u32[]{:S(2)}) copy-start(bf16[64,64,3,3]{1,0,3,2:T(8,128)(2,1)} %param.14) | copy-start | bytes 221188

commit v2 on v1

--- a/solution.py
+++ b/solution.py
@@ -1,12 +1,88 @@
 import jax
 import jax.numpy as jnp
 from jax import lax
+from jax.experimental import pallas as pl
+from jax.experimental.pallas import tpu as pltpu
 from jax.sharding import PartitionSpec as P
 
 TILE = 64
 
 
 dilations = (1, 2, 4, 8)
+LANES = 384
+
+
+def _net_kernel(lim_ref, x_ref, k1, b1, k2, b2, k3, b3, kf, bfl, out_ref, buf_a, buf_b):
+    lanes = lax.broadcasted_iota(jnp.int32, (1, LANES), 1)
+
+    def layer(src, dst, n_rows, spread, kmat, bias, index, last):
+        kv = kmat[...]
+        bv = bias[...]
+        if not last:
+            row_lo = lim_ref[4 * index]
+            row_hi = lim_ref[4 * index + 1]
+            col_ok = (lanes >= lim_ref[4 * index + 2]) & (lanes < lim_ref[4 * index + 3])
+
+        def row(y, carry):
+            pieces = []
+            for a in range(3):
+                line = src[y + spread * a]
+                for e in range(3):
+                    pieces.append(line if e == 0 else pltpu.roll(line, LANES - spread * e, 1))
+            col = jnp.concatenate(pieces, axis=0)
+            acc = jnp.dot(kv, col, preferred_element_type=jnp.float32) + bv
+            if last:
+                dst[y] = acc[:, : dst.shape[2]].astype(dst.dtype)
+            else:
+                act = acc / (1.0 + jnp.exp(-acc))
+                keep = col_ok & (y >= row_lo) & (y < row_hi)
+                dst[y] = jnp.where(keep, act, 0.0).astype(dst.dtype)
+            return carry
+
+        lax.fori_loop(0, n_rows, row, 0)
+
+    h0 = x_ref.shape[0]
+    h1 = h0 - 2
+    h2 = h1 - 4
+    h3 = h2 - 8
+    h4 = h3 - 16
+    layer(x_ref, buf_a, h1, 1, k1, b1, 0, False)
+    layer(buf_a, buf_b, h2, 2, k2, b2, 1, False)
+    layer(buf_b, buf_a, h3, 4, k3, b3, 2, False)
+    layer(buf_a, out_ref, h4, 8, kf, bfl, 3, True)
+
+
+def _kmat(kernel, cin):
+    o, c = kernel.shape[:2]
+    k = jnp.pad(kernel, ((0, 0), (0, cin - c), (0, 0), (0, 0)))
+    return k.transpose(0, 2, 3, 1).reshape(o, 9 * cin)
+
+
+def run_net(x, lims, layers, out_w, out_ch):
+    (k1, b1), (k2, b2), (k3, b3), (kf, bf) = layers
+    hid = k1.shape[0]
+    h0 = x.shape[0]
+    kf_p = jnp.pad(kf, ((0, out_ch - kf.shape[0]), (0, 0), (0, 0), (0, 0)))
+    bf_p = jnp.pad(bf, (0, out_ch - bf.shape[0]))
+    args = (
+        lims, x,
+        _kmat(k1, x.shape[1]), b1.reshape(-1, 1),
+        _kmat(k2, hid), b2.reshape(-1, 1),
+        _kmat(k3, hid), b3.reshape(-1, 1),
+        _kmat(kf_p, hid), bf_p.reshape(-1, 1),
+    )
+    vspec = pl.BlockSpec(memory_space=pltpu.VMEM)
+    return pl.pallas_call(
+        _net_kernel,
+        out_shape=jax.ShapeDtypeStruct((h0 - 30, out_ch, out_w), jnp.bfloat16),
+        in_specs=[pl.BlockSpec(memory_space=pltpu.SMEM)] + [vspec] * 9,
+        out_specs=vspec,
+        scratch_shapes=[
+            pltpu.VMEM((h0 - 2, hid, LANES), jnp.bfloat16),
+            pltpu.VMEM((h0 - 6, hid, LANES), jnp.bfloat16),
+        ],
+        compiler_params=pltpu.CompilerParams(vmem_limit_bytes=56 * 1024 * 1024),
+    )(*args)
 
 
 def with_halo(cells, sides, width):
@@ -55,31 +131,25 @@
         (kernel_three, bias_three),
         (kernel_flux, bias_flux),
     )
-    values = with_halo(state, (("row", 1), ("col", 2)), margin)[None]
+    extended = with_halo(state, (("row", 1), ("col", 2)), margin)
+    ext_h, ext_w = extended.shape[1:]
+    x = jnp.pad(extended.transpose(1, 0, 2), ((0, 0), (0, 16 - moments), (0, LANES - ext_w)))
+    lims = []
     offset = margin
-    for layer_index in range(4):
-        spread = dilations[layer_index]
-        kernel, bias_term = layers[layer_index]
-        summed = lax.conv_general_dilated(
-            values,
-            kernel,
-            (1, 1),
-            "VALID",
-            rhs_dilation=(spread, spread),
-            dimension_numbers=("NCHW", "OIHW", "NCHW"),
-            preferred_element_type=jnp.float32,
-        )
-        summed = summed + bias_term[None, :, None, None]
+    out_h, out_w = ext_h, ext_w
+    for spread in dilations:
         offset = offset - spread
-        if layer_index < 3:
-            row_ids = my_row * block_h - offset + jnp.arange(summed.shape[2], dtype=jnp.int32)
-            col_ids = my_col * block_w - offset + jnp.arange(summed.shape[3], dtype=jnp.int32)
-            inside = ((row_ids >= 0) & (row_ids < grid_h))[:, None] & (
-                (col_ids >= 0) & (col_ids < grid_w)
-            )[None, :]
-            values = jnp.where(inside[None, None], jax.nn.silu(summed), 0.0).astype(jnp.bfloat16)
-        else:
-            flux = summed[0]
+        out_h, out_w = out_h - 2 * spread, out_w - 2 * spread
+        top = offset - my_row * block_h
+        left = offset - my_col * block_w
+        lims += [
+            jnp.maximum(top, 0),
+            jnp.minimum(out_h, grid_h + top),
+            jnp.maximum(left, 0),
+            jnp.minimum(out_w, grid_w + left),
+        ]
+    lims = jnp.stack(lims).astype(jnp.int32)
+    flux = run_net(x, lims, layers, block_w, 32)[:, : 2 * moments].transpose(1, 0, 2)
     listed = tile_ids[0]
     mine = (listed // per_block) == my_col
     local_ids = listed % per_block
@@ -89,7 +159,7 @@
     cell_mask = jnp.broadcast_to(
         chosen.reshape(per_row, 1, per_col, 1), (per_row, TILE, per_col, TILE)
     ).reshape(block_h, block_w)
-    flux_field = jnp.where(cell_mask[None], flux, 0.0).astype(jnp.bfloat16)
+    flux_field = jnp.where(cell_mask[None], flux, jnp.zeros((), jnp.bfloat16))
     rimmed = with_halo(flux_field, (("row", 1), ("col", 2)), 1)
     across = rimmed[:moments, 1:-1, :].astype(jnp.float32)
     downward = rimmed[moments:, :, 1:-1].astype(jnp.float32)

time: 451 us -> 241 us (0.53); the launches traced: 444 us -> 240 us
  local copies, waits for them, and re-layouts: 212 us -> 27.7 us
  Pallas kernels: 0 us -> 171 us
  matrix products: 107 us -> 0 us
  other arithmetic: 92.8 us -> 10.7 us
    conv_general_dilated x13 -> x0, local copies, waits for them, and re-layouts: 185 us -> none  [body(): lax.conv_general_dilated(values, kernel, (1, 1), 'VALID', rhs_dilation=(s...]
    pallas_call x0 -> x1, Pallas kernels: none -> 171 us  [run_net(): pl.pallas_call(_net_kernel, out_shape=jax.ShapeDtypeStruct((h0 - 30, out_...]
    conv_general_dilated x4 -> x0, matrix products: 107 us -> none  [body(): lax.conv_general_dilated(values, kernel, (1, 1), 'VALID', rhs_dilation=(s...]
    mul x3 -> x0, other arithmetic: 43.9 us -> none  [body(): jax.nn.silu(summed)]
    convert_element_type x4 -> x0, other arithmetic: 37.6 us -> none  [the longest x3 35.7 us: body(): jnp.where(inside[None, None], jax.nn.silu(summed), 0.0).astype(jnp.bfloat16)]
    convert_element_type x1 -> x0, local copies, waits for them, and re-layouts: 10.5 us -> none  [body(): jnp.where(inside[None, None], jax.nn.silu(summed), 0.0).astype(jnp.bfloat16)]
    reshape x0 -> x9, local copies, waits for them, and re-layouts: none -> 8.37 us  [the longest x4 2.96 us: _kmat(): return k.transpose(0, 2, 3, 1).reshape(o, 9 * cin)]
    ppermute x4, starting transfers between devices: 14.4 us -> 18.9 us  [with_halo(): lax.ppermute(tail, axis, [(i, (i + 1) % count) for i in range(ends)])]
  transfers between devices with their start and end apart: 8 -> 8, of which waited for: 3 -> 1; matrix products, arithmetic and copies ran while one was open for 2% -> 8% of each run, Pallas kernels for 0% -> 0%
where the time goes in v2:
time: 241 us; the launch traced here: 240 us
  Pallas kernels  171 us (71%)
  local copies, waits for them, and re-layouts  27.7 us (11%)
  starting transfers between devices  27.1 us (11%)
  other arithmetic  10.7 us (4%)
  waiting for transfers between devices  3.14 us (1%)
    pallas_call x1, Pallas kernels, run_net(): pl.pallas_call(_net_kernel, out_shape=jax.ShapeDtypeStruct((h0 - 30, out_...  171 us
    ppermute x4, starting transfers between devices, with_halo(): lax.ppermute(tail, axis, [(i, (i + 1) % count) for i in range(ends)])  18.9 us
    ppermute x4, starting transfers between devices, with_halo(): lax.ppermute(head, axis, [((i + 1) % count, i) for i in range(ends)])  8.2 us
    slice x5, local copies, waits for them, and re-layouts, with_halo(): lax.slice_in_dim(cells, cells.shape[dim] - width, cells.shape[dim], axis=...  4.99 us
  transfers between devices with their start and end apart: 8, of which 1 were waited for; matrix products, arithmetic and copies ran while one was open for 8% of the time, Pallas kernels for 0%

profile of v2, /device:TPU:7, one launch (start us, length us, event | category | flops | bytes accessed | tf_op | source)
XLA Modules:
  0.0 239.7 jit_solution(10419846482610797142)
XLA Ops:
  0.0 1.1 fusion.11
  1.1 4.1 %collective-permute-start = (bf16[13,15,256]{2,0,1:T(8,128)(2,1)S(1)}, bf16[13,15,256]{2,0,1:T(8,128)(2,1)S(1)}, u32[]{:S(2)}, u32[]{:S(2)}) collective-permute-start(bf16[13,15,256]{2,0,1:T(8,128)(2,1)S(1)} %copy.82), channel_id=1, source_target_pairs={{0,16},{16,32},{32,48},{48,64},{64,80},{80,96},{96,112},{1,17},{17... | collective-permute-start | bytes 299528 | tf_op jit(solution)/shard_map/ppermute | solution.py:96
  5.3 1.9 collective-permute-start.1
  7.2 0.7 compare_bitcast_fusion
  7.9 0.7 fusion.7
  8.5 0.1 fusion.6
  8.7 0.1 broadcast_in_dim.24
  8.7 0.7 pad_bitcast_fusion.1
  9.4 0.7 copy.75.bfl
  10.1 1.3 copy.70.b1
  11.4 1.4 copy.72.b2
  12.8 1.4 copy.74.b3
  14.2 0.8 pad.17
  14.9 0.7 copy.69.k1
  15.6 0.1 broadcast_in_dim.25
  15.7 0.2 broadcast_in_dim.26
  15.9 0.0 collective-permute-done
  15.9 0.0 copy-done.2
  15.9 0.5 constant_dynamic-update-slice_fusion.1
  16.4 0.0 collective-permute-done.1
  16.5 0.0 copy-start.5
  16.5 0.0 copy-start.3
  16.5 0.0 copy-start.4
  16.5 0.3 fusion.10
  16.8 0.6 copy.62
  17.4 0.6 copy.63
  17.9 2.5 %collective-permute-start.3 = (bf16[13,158,15]{1,2,0:T(8,128)(2,1)S(1)}, bf16[13,158,15]{1,2,0:T(8,128)(2,1)S(1)}, u32[]{:S(2)}, u32[]{:S(2)}) collective-permute-start(bf16[13,158,15]{1,2,0:T(8,128)(2,1)S(1)} %copy.63), channel_id=1, source_target_pairs={{1,0},{2,1},{3,2},{4,3},{5,4},{6,5},{7,6},{8,7},{9,8},{10,9},{11,1... | collective-permute-start | bytes 184868 | tf_op jit(solution)/shard_map/ppermute | solution.py:98
  20.4 4.9 %collective-permute-start.2 = (bf16[13,158,15]{1,2,0:T(8,128)(2,1)S(1)}, bf16[13,158,15]{1,2,0:T(8,128)(2,1)S(1)}, u32[]{:S(2)}, u32[]{:S(2)}) collective-permute-start(bf16[13,158,15]{1,2,0:T(8,128)(2,1)S(1)} %copy.62), channel_id=1, source_target_pairs={{0,1},{1,2},{2,3},{3,4},{4,5},{5,6},{6,7},{7,8},{8,9},{9,10},{10,1... | collective-permute-start | bytes 184868 | tf_op jit(solution)/shard_map/ppermute | solution.py:96
  25.3 0.0 copy-done.5
  25.4 0.1 copy.68
  25.4 0.7 reshape.33.kf
  26.2 0.0 copy-done.3
  26.2 0.1 copy.66
  26.3 0.8 copy.71.k2
  27.1 0.0 copy-done.4
  27.1 0.1 copy.67
  27.2 0.8 copy.73.k3
  28.0 0.6 stack.67.lim_ref
  28.6 0.0 collective-permute-done.2
  28.6 0.7 copy.64
  29.3 0.0 collective-permute-done.3
  29.3 0.7 copy.65
  30.0 1.2 maximum_bitcast_fusion
  31.2 1.5 pad.16.x_ref
  32.7 170.8 %shard_map.100 = bf16[128,32,256]{2,1,0:T(8,128)(2,1)} custom-call(s32[16]{0:T(128)} %stack.67.lim_ref, bf16[158,16,384]{2,1,0:T(8,128)(2,1)} %pad.16.x_ref, bf16[64,144]{1,0:T(8,128)(2,1)} %copy.69.k1, f32[64,1]{1,0:T(8,128)} %copy.70.b1, bf16[64,576]{1,0:T(8,128)(2,1)} %copy.71.k2, f32[64,1]{1,0:T(8,128)} %copy.72.b2, bf16[64,576]{1,0:T(8,128)(2,1)} %copy.73.k3, ...), custom_call_target="tpu_custom_call" | custom-call | tf_op jit(solution)/shard_map/pallas_call | solution.py:75
  203.5 1.8 fusion.3
  205.3 4.2 %collective-permute-start.4 = (bf16[26,1,256]{2,0,1:T(8,128)(2,1)S(1)}, bf16[26,1,256]{2,0,1:T(8,128)(2,1)S(1)}, u32[]{:S(2)}, u32[]{:S(2)}) collective-permute-start(bf16[26,1,256]{2,0,1:T(8,128)(2,1)S(1)} %get-tuple-element.7), channel_id=1, source_target_pairs={{0,16},{16,32},{32,48},{48,64},{64,80},{80,96},{96,112},{1,17},{17... | collective-permute-start | bytes 39944 | tf_op jit(solution)/shard_map/ppermute | solution.py:96
  209.6 1.9 collective-permute-start.5
  211.5 0.0 collective-permute-done.4
  211.5 3.1 %collective-permute-done.5 = bf16[26,1,256]{2,0,1:T(8,128)(2,1)S(1)} collective-permute-done((bf16[26,1,256]{2,0,1:T(8,128)(2,1)S(1)}, bf16[26,1,256]{2,0,1:T(8,128)(2,1)S(1)}, u32[]{:S(2)}, u32[]{:S(2)}) %collective-permute-start.5) | collective-permute-done | bytes 13344 | tf_op jit(solution)/shard_map/ppermute | solution.py:98
  214.6 0.3 pad_maximum_fusion
  214.9 1.7 fusion.8
  216.6 2.5 %copy.76 = bf16[26,130,1]{1,0,2:T(8,128)(2,1)S(1)} copy(bf16[26,130,1]{2,0,1:T(8,128)(2,1)} %get-tuple-element.5) | data formatting | bytes 13520 | tf_op jit(solution)/shard_map/slice | solution.py:93
  219.0 1.3 copy.77
  220.4 1.9 collective-permute-start.7
  222.3 5.7 %collective-permute-start.6 = (bf16[26,130,1]{1,0,2:T(8,128)(2,1)S(1)}, bf16[26,130,1]{1,0,2:T(8,128)(2,1)S(1)}, u32[]{:S(2)}, u32[]{:S(2)}) collective-permute-start(bf16[26,130,1]{1,0,2:T(8,128)(2,1)S(1)} %copy.76), channel_id=1, source_target_pairs={{0,1},{1,2},{2,3},{3,4},{4,5},{5,6},{6,7},{7,8},{8,9},{9,10},{10,1... | collective-permute-start | bytes 20288 | tf_op jit(solution)/shard_map/ppermute | solution.py:96
  228.0 3.1 %slice_convert_fusion = f32[13,130,256]{2,0,1:T(8,128)} fusion(bf16[26,130,256]{2,0,1:T(8,128)(2,1)} %copy-done.1), kind=kLoop, calls=%fused_computation.14 | loop fusion | flops 432640 | bytes 2595840 | tf_op jit(solution)/shard_map/convert_element_type | solution.py:165
  231.1 0.0 collective-permute-done.6
  231.1 1.8 copy.78
  233.0 0.0 collective-permute-done.7
  233.0 2.7 %copy.79 = bf16[26,130,1]{2,0,1:T(8,128)(2,1)} copy(bf16[26,130,1]{1,0,2:T(8,128)(2,1)S(1)} %collective-permute-done.7) | data formatting | bytes 13520 | tf_op jit(solution)/shard_map/ppermute | solution.py:98
  235.7 2.1 fusion.4
  237.9 0.7 fusion.2
  238.5 1.2 copy.80
  (11 shorter events, 0.1 us)
Async XLA Ops:
  0.0 15.9 %copy-start.2 = (bf16[13,128,256]{2,1,0:T(8,128)(2,1)S(1)}, bf16[13,128,256]{2,1,0:T(8,128)(2,1)}, u32[]{:S(2)}) copy-start(bf16[13,128,256]{2,1,0:T(8,128)(2,1)} %param.10) | copy-start | bytes 2555908
  1.1 14.8 %collective-permute-start = (bf16[13,15,256]{2,0,1:T(8,128)(2,1)S(1)}, bf16[13,15,256]{2,0,1:T(8,128)(2,1)S(1)}, u32[]{:S(2)}, u32[]{:S(2)}) collective-permute-start(bf16[13,15,256]{2,0,1:T(8,128)(2,1)S(1)} %copy.82), channel_id=1, source_target_pairs={{0,16},{16,32},{32,48},{48,64},{64,80},{80,96},{96,112},{1,17},{17... | collective-permute-start | bytes 299528 | tf_op jit(solution)/shard_map/ppermute | solution.py:96
  5.3 11.2 %collective-permute-start.1 = (bf16[13,15,256]{2,0,1:T(8,128)(2,1)S(1)}, bf16[13,15,256]{2,0,1:T(8,128)(2,1)S(1)}, u32[]{:S(2)}, u32[]{:S(2)}) collective-permute-start(bf16[13,15,256]{2,0,1:T(8,128)(2,1)S(1)} %copy.83), channel_id=1, source_target_pairs={{16,0},{32,16},{48,32},{64,48},{80,64},{96,80},{112,96},{17,1},{33... | collective-permute-start | bytes 299528 | tf_op jit(solution)/shard_map/ppermute | solution.py:98
  16.5 8.9 %copy-start.5 = (bf16[26,64,3,3]{1,0,3,2:T(8,128)(2,1)S(1)}, bf16[26,64,3,3]{1,0,3,2:T(8,128)(2,1)}, u32[]{:S(2)}) copy-start(bf16[26,64,3,3]{1,0,3,2:T(8,128)(2,1)} %param.18) | copy-start | bytes 89860
  16.5 9.7 %copy-start.3 = (bf16[64,64,3,3]{1,0,3,2:T(8,128)(2,1)S(1)}, bf16[64,64,3,3]{1,0,3,2:T(8,128)(2,1)}, u32[]{:S(2)}) copy-start(bf16[64,64,3,3]{1,0,3,2:T(8,128)(2,1)} %param.14) | copy-start | bytes 221188
  16.5 10.6 %copy-start.4 = (bf16[64,64,3,3]{1,0,3,2:T(8,128)(2,1)S(1)}, bf16[64,64,3,3]{1,0,3,2:T(8,128)(2,1)}, u32[]{:S(2)}) copy-start(bf16[64,64,3,3]{1,0,3,2:T(8,128)(2,1)} %param.16) | copy-start | bytes 221188
  17.9 11.3 %collective-permute-start.3 = (bf16[13,158,15]{1,2,0:T(8,128)(2,1)S(1)}, bf16[13,158,15]{1,2,0:T(8,128)(2,1)S(1)}, u32[]{:S(2)}, u32[]{:S(2)}) collective-permute-start(bf16[13,158,15]{1,2,0:T(8,128)(2,1)S(1)} %copy.63), channel_id=1, source_target_pairs={{1,0},{2,1},{3,2},{4,3},{5,4},{6,5},{7,6},{8,7},{9,8},{10,9},{11,1... | collective-permute-start | bytes 184868 | tf_op jit(solution)/shard_map/ppermute | solution.py:98
  20.4 8.2 %collective-permute-start.2 = (bf16[13,158,15]{1,2,0:T(8,128)(2,1)S(1)}, bf16[13,158,15]{1,2,0:T(8,128)(2,1)S(1)}, u32[]{:S(2)}, u32[]{:S(2)}) collective-permute-start(bf16[13,158,15]{1,2,0:T(8,128)(2,1)S(1)} %copy.62), channel_id=1, source_target_pairs={{0,1},{1,2},{2,3},{3,4},{4,5},{5,6},{6,7},{7,8},{8,9},{9,10},{10,1... | collective-permute-start | bytes 184868 | tf_op jit(solution)/shard_map/ppermute | solution.py:96
  205.3 6.1 %collective-permute-start.4 = (bf16[26,1,256]{2,0,1:T(8,128)(2,1)S(1)}, bf16[26,1,256]{2,0,1:T(8,128)(2,1)S(1)}, u32[]{:S(2)}, u32[]{:S(2)}) collective-permute-start(bf16[26,1,256]{2,0,1:T(8,128)(2,1)S(1)} %get-tuple-element.7), channel_id=1, source_target_pairs={{0,16},{16,32},{32,48},{48,64},{64,80},{80,96},{96,112},{1,17},{17... | collective-permute-start | bytes 39944 | tf_op jit(solution)/shard_map/ppermute | solution.py:96
  209.6 5.1 %collective-permute-start.5 = (bf16[26,1,256]{2,0,1:T(8,128)(2,1)S(1)}, bf16[26,1,256]{2,0,1:T(8,128)(2,1)S(1)}, u32[]{:S(2)}, u32[]{:S(2)}) collective-permute-start(bf16[26,1,256]{2,0,1:T(8,128)(2,1)S(1)} %get-tuple-element.8), channel_id=1, source_target_pairs={{16,0},{32,16},{48,32},{64,48},{80,64},{96,80},{112,96},{17,1},{33... | collective-permute-start | bytes 39944 | tf_op jit(solution)/shard_map/ppermute | solution.py:98
  214.9 1.7 copy-start.1
  220.4 12.6 %collective-permute-start.7 = (bf16[26,130,1]{1,0,2:T(8,128)(2,1)S(1)}, bf16[26,130,1]{1,0,2:T(8,128)(2,1)S(1)}, u32[]{:S(2)}, u32[]{:S(2)}) collective-permute-start(bf16[26,130,1]{1,0,2:T(8,128)(2,1)S(1)} %copy.77), channel_id=1, source_target_pairs={{1,0},{2,1},{3,2},{4,3},{5,4},{6,5},{7,6},{8,7},{9,8},{10,9},{11,1... | collective-permute-start | bytes 20288 | tf_op jit(solution)/shard_map/ppermute | solution.py:98
  222.3 8.8 %collective-permute-start.6 = (bf16[26,130,1]{1,0,2:T(8,128)(2,1)S(1)}, bf16[26,130,1]{1,0,2:T(8,128)(2,1)S(1)}, u32[]{:S(2)}, u32[]{:S(2)}) collective-permute-start(bf16[26,130,1]{1,0,2:T(8,128)(2,1)S(1)} %copy.76), channel_id=1, source_target_pairs={{0,1},{1,2},{2,3},{3,4},{4,5},{5,6},{6,7},{7,8},{8,9},{9,10},{10,1... | collective-permute-start | bytes 20288 | tf_op jit(solution)/shard_map/ppermute | solution.py:96
  235.7 2.1 copy-start

commit v3 on v2

--- a/solution.py
+++ b/solution.py
@@ -19,6 +19,7 @@
         kv = kmat[...]
         bv = bias[...]
         if not last:
+            after = dilations[index + 1]
             row_lo = lim_ref[4 * index]
             row_hi = lim_ref[4 * index + 1]
             col_ok = (lanes >= lim_ref[4 * index + 2]) & (lanes < lim_ref[4 * index + 3])
@@ -27,19 +28,26 @@
             pieces = []
             for a in range(3):
                 line = src[y + spread * a]
-                for e in range(3):
-                    pieces.append(line if e == 0 else pltpu.roll(line, LANES - spread * e, 1))
+                if index == 0:
+                    for e in range(3):
+                        pieces.append(line if e == 0 else pltpu.roll(line, LANES - spread * e, 1))
+                else:
+                    pieces.append(line)
             col = jnp.concatenate(pieces, axis=0)
             acc = jnp.dot(kv, col, preferred_element_type=jnp.float32) + bv
             if last:
                 dst[y] = acc[:, : dst.shape[2]].astype(dst.dtype)
             else:
-                act = acc / (1.0 + jnp.exp(-acc))
+                half = 0.5 * acc
+                act = half + half * jnp.tanh(half)
                 keep = col_ok & (y >= row_lo) & (y < row_hi)
-                dst[y] = jnp.where(keep, act, 0.0).astype(dst.dtype)
+                kept = jnp.where(keep, act, 0.0).astype(dst.dtype)
+                dst[y] = jnp.concatenate(
+                    [kept] + [pltpu.roll(kept, LANES - after * e, 1) for e in (1, 2)], axis=0
+                )
             return carry
 
-        lax.fori_loop(0, n_rows, row, 0)
+        lax.fori_loop(0, n_rows, row, 0, unroll=2)
 
     h0 = x_ref.shape[0]
     h1 = h0 - 2
@@ -78,10 +86,10 @@
         in_specs=[pl.BlockSpec(memory_space=pltpu.SMEM)] + [vspec] * 9,
         out_specs=vspec,
         scratch_shapes=[
-            pltpu.VMEM((h0 - 2, hid, LANES), jnp.bfloat16),
-            pltpu.VMEM((h0 - 6, hid, LANES), jnp.bfloat16),
+            pltpu.VMEM((h0 - 2, 3 * hid, LANES), jnp.bfloat16),
+            pltpu.VMEM((h0 - 6, 3 * hid, LANES), jnp.bfloat16),
         ],
-        compiler_params=pltpu.CompilerParams(vmem_limit_bytes=56 * 1024 * 1024),
+        compiler_params=pltpu.CompilerParams(vmem_limit_bytes=60 * 1024 * 1024),
     )(*args)
 
 

time: 241 us -> 172 us (0.71)
  Pallas kernels: 171 us -> 102 us
    pallas_call x1, Pallas kernels: 171 us -> 102 us  [run_net(): pl.pallas_call(_net_kernel, out_shape=jax.ShapeDtypeStruct((h0 - 30, out_...]
  transfers between devices with their start and end apart: 8 -> 8, of which waited for: 1 -> 1; matrix products, arithmetic and copies ran while one was open for 8% -> 11% of each run, Pallas kernels for 0% -> 0%
where the time goes in v3:
time: 172 us; the launch traced here: 171 us
  Pallas kernels  102 us (59%)
  local copies, waits for them, and re-layouts  27.7 us (16%)
  starting transfers between devices  27.1 us (16%)
  other arithmetic  10.7 us (6%)
  waiting for transfers between devices  3.14 us (2%)
    pallas_call x1, Pallas kernels, run_net(): pl.pallas_call(_net_kernel, out_shape=jax.ShapeDtypeStruct((h0 - 30, out_...  102 us
    ppermute x4, starting transfers between devices, with_halo(): lax.ppermute(tail, axis, [(i, (i + 1) % count) for i in range(ends)])  18.9 us
    ppermute x4, starting transfers between devices, with_halo(): lax.ppermute(head, axis, [((i + 1) % count, i) for i in range(ends)])  8.2 us
    slice x5, local copies, waits for them, and re-layouts, with_halo(): lax.slice_in_dim(cells, cells.shape[dim] - width, cells.shape[dim], axis=...  4.99 us
  transfers between devices with their start and end apart: 8, of which 1 were waited for; matrix products, arithmetic and copies ran while one was open for 11% of the time, Pallas kernels for 0%

profile of v3, /device:TPU:7, one launch (start us, length us, event | category | flops | bytes accessed | tf_op | source)
XLA Modules:
  0.0 171.2 jit_solution(9556397771272794326)
XLA Ops:
  0.0 1.1 fusion.11
  1.1 4.1 %collective-permute-start = (bf16[13,15,256]{2,0,1:T(8,128)(2,1)S(1)}, bf16[13,15,256]{2,0,1:T(8,128)(2,1)S(1)}, u32[]{:S(2)}, u32[]{:S(2)}) collective-permute-start(bf16[13,15,256]{2,0,1:T(8,128)(2,1)S(1)} %copy.82), channel_id=1, source_target_pairs={{0,16},{16,32},{32,48},{48,64},{64,80},{80,96},{96,112},{1,17},{17... | collective-permute-start | bytes 299528 | tf_op jit(solution)/shard_map/ppermute | solution.py:104
  5.3 1.9 %collective-permute-start.1 = (bf16[13,15,256]{2,0,1:T(8,128)(2,1)S(1)}, bf16[13,15,256]{2,0,1:T(8,128)(2,1)S(1)}, u32[]{:S(2)}, u32[]{:S(2)}) collective-permute-start(bf16[13,15,256]{2,0,1:T(8,128)(2,1)S(1)} %copy.83), channel_id=1, source_target_pairs={{16,0},{32,16},{48,32},{64,48},{80,64},{96,80},{112,96},{17,1},{33... | collective-permute-start | bytes 299528 | tf_op jit(solution)/shard_map/ppermute | solution.py:106
  7.2 0.7 compare_bitcast_fusion
  7.9 0.7 fusion.7
  8.5 0.1 fusion.6
  8.7 0.1 broadcast_in_dim.24
  8.7 0.7 pad_bitcast_fusion.1
  9.4 0.7 copy.75.bfl
  10.1 1.3 copy.70.b1
  11.4 1.4 copy.72.b2
  12.8 1.4 copy.74.b3
  14.2 0.8 pad.17
  14.9 0.7 copy.69.k1
  15.6 0.1 broadcast_in_dim.25
  15.7 0.2 broadcast_in_dim.26
  15.9 0.0 collective-permute-done
  15.9 0.0 copy-done.2
  15.9 0.5 constant_dynamic-update-slice_fusion.1
  16.4 0.0 collective-permute-done.1
  16.5 0.0 copy-start.5
  16.5 0.0 copy-start.3
  16.5 0.0 copy-start.4
  16.5 0.3 fusion.10
  16.8 0.6 copy.62
  17.4 0.6 copy.63
  17.9 2.5 %collective-permute-start.3 = (bf16[13,158,15]{1,2,0:T(8,128)(2,1)S(1)}, bf16[13,158,15]{1,2,0:T(8,128)(2,1)S(1)}, u32[]{:S(2)}, u32[]{:S(2)}) collective-permute-start(bf16[13,158,15]{1,2,0:T(8,128)(2,1)S(1)} %copy.63), channel_id=1, source_target_pairs={{1,0},{2,1},{3,2},{4,3},{5,4},{6,5},{7,6},{8,7},{9,8},{10,9},{11,1... | collective-permute-start | bytes 184868 | tf_op jit(solution)/shard_map/ppermute | solution.py:106
  20.4 4.9 %collective-permute-start.2 = (bf16[13,158,15]{1,2,0:T(8,128)(2,1)S(1)}, bf16[13,158,15]{1,2,0:T(8,128)(2,1)S(1)}, u32[]{:S(2)}, u32[]{:S(2)}) collective-permute-start(bf16[13,158,15]{1,2,0:T(8,128)(2,1)S(1)} %copy.62), channel_id=1, source_target_pairs={{0,1},{1,2},{2,3},{3,4},{4,5},{5,6},{6,7},{7,8},{8,9},{9,10},{10,1... | collective-permute-start | bytes 184868 | tf_op jit(solution)/shard_map/ppermute | solution.py:104
  25.3 0.0 copy-done.5
  25.4 0.1 copy.68
  25.4 0.7 reshape.33.kf
  26.2 0.0 copy-done.3
  26.2 0.1 copy.66
  26.3 0.8 copy.71.k2
  27.1 0.1 copy.67
  27.2 0.8 copy.73.k3
  28.0 0.6 stack.67.lim_ref
  28.6 0.0 collective-permute-done.2
  28.6 0.7 copy.64
  29.3 0.0 collective-permute-done.3
  29.3 0.7 copy.65
  30.0 1.2 maximum_bitcast_fusion
  31.2 1.5 pad.16.x_ref
  32.7 102.2 %shard_map.100 = bf16[128,32,256]{2,1,0:T(8,128)(2,1)} custom-call(s32[16]{0:T(128)} %stack.67.lim_ref, bf16[158,16,384]{2,1,0:T(8,128)(2,1)} %pad.16.x_ref, bf16[64,144]{1,0:T(8,128)(2,1)} %copy.69.k1, f32[64,1]{1,0:T(8,128)} %copy.70.b1, bf16[64,576]{1,0:T(8,128)(2,1)} %copy.71.k2, f32[64,1]{1,0:T(8,128)} %copy.72.b2, bf16[64,576]{1,0:T(8,128)(2,1)} %copy.73.k3, ...), custom_call_target="tpu_custom_call" | custom-call | tf_op jit(solution)/shard_map/pallas_call | solution.py:83
  135.0 1.8 %fusion.3 = bf16[26,128,256]{2,0,1:T(8,128)(2,1)S(1)} fusion(bf16[128,32,256]{2,1,0:T(8,128)(2,1)} %shard_map.100, pred[128,256]{1,0:T(8,128)(4,1)S(1)} %broadcast_in_dim.26), kind=kLoop, calls=%fused_computation.7 | loop fusion | flops 851968 | bytes 3440640 | tf_op jit(solution)/shard_map/jit(_where)/select_n | solution.py:170
  136.8 4.2 %collective-permute-start.4 = (bf16[26,1,256]{2,0,1:T(8,128)(2,1)S(1)}, bf16[26,1,256]{2,0,1:T(8,128)(2,1)S(1)}, u32[]{:S(2)}, u32[]{:S(2)}) collective-permute-start(bf16[26,1,256]{2,0,1:T(8,128)(2,1)S(1)} %get-tuple-element.7), channel_id=1, source_target_pairs={{0,16},{16,32},{32,48},{48,64},{64,80},{80,96},{96,112},{1,17},{17... | collective-permute-start | bytes 39944 | tf_op jit(solution)/shard_map/ppermute | solution.py:104
  141.0 1.9 %collective-permute-start.5 = (bf16[26,1,256]{2,0,1:T(8,128)(2,1)S(1)}, bf16[26,1,256]{2,0,1:T(8,128)(2,1)S(1)}, u32[]{:S(2)}, u32[]{:S(2)}) collective-permute-start(bf16[26,1,256]{2,0,1:T(8,128)(2,1)S(1)} %get-tuple-element.8), channel_id=1, source_target_pairs={{16,0},{32,16},{48,32},{64,48},{80,64},{96,80},{112,96},{17,1},{33... | collective-permute-start | bytes 39944 | tf_op jit(solution)/shard_map/ppermute | solution.py:106
  142.9 0.0 collective-permute-done.4
  142.9 3.1 %collective-permute-done.5 = bf16[26,1,256]{2,0,1:T(8,128)(2,1)S(1)} collective-permute-done((bf16[26,1,256]{2,0,1:T(8,128)(2,1)S(1)}, bf16[26,1,256]{2,0,1:T(8,128)(2,1)S(1)}, u32[]{:S(2)}, u32[]{:S(2)}) %collective-permute-start.5) | collective-permute-done | bytes 13344 | tf_op jit(solution)/shard_map/ppermute | solution.py:106
  146.0 0.3 pad_maximum_fusion
  146.3 1.7 fusion.8
  148.0 0.0 copy-done.1
  148.0 2.5 %copy.76 = bf16[26,130,1]{1,0,2:T(8,128)(2,1)S(1)} copy(bf16[26,130,1]{2,0,1:T(8,128)(2,1)} %get-tuple-element.5) | data formatting | bytes 13520 | tf_op jit(solution)/shard_map/slice | solution.py:101
  150.5 1.3 copy.77
  151.8 1.9 %collective-permute-start.7 = (bf16[26,130,1]{1,0,2:T(8,128)(2,1)S(1)}, bf16[26,130,1]{1,0,2:T(8,128)(2,1)S(1)}, u32[]{:S(2)}, u32[]{:S(2)}) collective-permute-start(bf16[26,130,1]{1,0,2:T(8,128)(2,1)S(1)} %copy.77), channel_id=1, source_target_pairs={{1,0},{2,1},{3,2},{4,3},{5,4},{6,5},{7,6},{8,7},{9,8},{10,9},{11,1... | collective-permute-start | bytes 20288 | tf_op jit(solution)/shard_map/ppermute | solution.py:106
  153.7 5.7 %collective-permute-start.6 = (bf16[26,130,1]{1,0,2:T(8,128)(2,1)S(1)}, bf16[26,130,1]{1,0,2:T(8,128)(2,1)S(1)}, u32[]{:S(2)}, u32[]{:S(2)}) collective-permute-start(bf16[26,130,1]{1,0,2:T(8,128)(2,1)S(1)} %copy.76), channel_id=1, source_target_pairs={{0,1},{1,2},{2,3},{3,4},{4,5},{5,6},{6,7},{7,8},{8,9},{9,10},{10,1... | collective-permute-start | bytes 20288 | tf_op jit(solution)/shard_map/ppermute | solution.py:104
  159.4 3.1 %slice_convert_fusion = f32[13,130,256]{2,0,1:T(8,128)} fusion(bf16[26,130,256]{2,0,1:T(8,128)(2,1)} %copy-done.1), kind=kLoop, calls=%fused_computation.14 | loop fusion | flops 432640 | bytes 2595840 | tf_op jit(solution)/shard_map/convert_element_type | solution.py:173
  162.5 0.0 collective-permute-done.6
  162.5 1.8 %copy.78 = bf16[26,130,1]{2,0,1:T(8,128)(2,1)S(1)} copy(bf16[26,130,1]{1,0,2:T(8,128)(2,1)S(1)} %collective-permute-done.6) | data formatting | bytes 13520 | tf_op jit(solution)/shard_map/ppermute | solution.py:104
  164.4 0.0 collective-permute-done.7
  164.4 2.7 %copy.79 = bf16[26,130,1]{2,0,1:T(8,128)(2,1)} copy(bf16[26,130,1]{1,0,2:T(8,128)(2,1)S(1)} %collective-permute-done.7) | data formatting | bytes 13520 | tf_op jit(solution)/shard_map/ppermute | solution.py:106
  167.2 2.1 %fusion.4 = f32[13,128,258]{2,0,1:T(8,128)S(1)} fusion(bf16[26,130,1]{2,0,1:T(8,128)(2,1)} %copy.79, bf16[26,130,1]{2,0,1:T(8,128)(2,1)S(1)} %copy.78, bf16[26,1,256]{2,0,1:T(8,128)(2,1)S(1)} %collective-permute-done.5, bf16[26,128,256]{2,0,1:T(8,128)(2,1)S(1)} %fusion.3, bf16[26,1,256]{2,0,1:T(8,128)(2,1)S(1)} %collective-permute-done.4), kind=kLoop, calls=%fused_computation.10 | loop fusion | flops 4293120 | bytes 3461328 | tf_op jit(solution)/shard_map/convert_element_type | solution.py:172
  169.3 0.7 fusion.2
  170.0 1.2 copy.80
  (11 shorter events, 0.1 us)
Async XLA Ops:
  0.0 15.9 %copy-start.2 = (bf16[13,128,256]{2,1,0:T(8,128)(2,1)S(1)}, bf16[13,128,256]{2,1,0:T(8,128)(2,1)}, u32[]{:S(2)}) copy-start(bf16[13,128,256]{2,1,0:T(8,128)(2,1)} %param.10) | copy-start | bytes 2555908
  1.1 14.8 %collective-permute-start = (bf16[13,15,256]{2,0,1:T(8,128)(2,1)S(1)}, bf16[13,15,256]{2,0,1:T(8,128)(2,1)S(1)}, u32[]{:S(2)}, u32[]{:S(2)}) collective-permute-start(bf16[13,15,256]{2,0,1:T(8,128)(2,1)S(1)} %copy.82), channel_id=1, source_target_pairs={{0,16},{16,32},{32,48},{48,64},{64,80},{80,96},{96,112},{1,17},{17... | collective-permute-start | bytes 299528 | tf_op jit(solution)/shard_map/ppermute | solution.py:104
  5.3 11.2 %collective-permute-start.1 = (bf16[13,15,256]{2,0,1:T(8,128)(2,1)S(1)}, bf16[13,15,256]{2,0,1:T(8,128)(2,1)S(1)}, u32[]{:S(2)}, u32[]{:S(2)}) collective-permute-start(bf16[13,15,256]{2,0,1:T(8,128)(2,1)S(1)} %copy.83), channel_id=1, source_target_pairs={{16,0},{32,16},{48,32},{64,48},{80,64},{96,80},{112,96},{17,1},{33... | collective-permute-start | bytes 299528 | tf_op jit(solution)/shard_map/ppermute | solution.py:106
  16.5 8.9 %copy-start.5 = (bf16[26,64,3,3]{1,0,3,2:T(8,128)(2,1)S(1)}, bf16[26,64,3,3]{1,0,3,2:T(8,128)(2,1)}, u32[]{:S(2)}) copy-start(bf16[26,64,3,3]{1,0,3,2:T(8,128)(2,1)} %param.18) | copy-start | bytes 89860
  16.5 9.7 %copy-start.3 = (bf16[64,64,3,3]{1,0,3,2:T(8,128)(2,1)S(1)}, bf16[64,64,3,3]{1,0,3,2:T(8,128)(2,1)}, u32[]{:S(2)}) copy-start(bf16[64,64,3,3]{1,0,3,2:T(8,128)(2,1)} %param.14) | copy-start | bytes 221188
  16.5 10.6 %copy-start.4 = (bf16[64,64,3,3]{1,0,3,2:T(8,128)(2,1)S(1)}, bf16[64,64,3,3]{1,0,3,2:T(8,128)(2,1)}, u32[]{:S(2)}) copy-start(bf16[64,64,3,3]{1,0,3,2:T(8,128)(2,1)} %param.16) | copy-start | bytes 221188
  17.9 11.3 %collective-permute-start.3 = (bf16[13,158,15]{1,2,0:T(8,128)(2,1)S(1)}, bf16[13,158,15]{1,2,0:T(8,128)(2,1)S(1)}, u32[]{:S(2)}, u32[]{:S(2)}) collective-permute-start(bf16[13,158,15]{1,2,0:T(8,128)(2,1)S(1)} %copy.63), channel_id=1, source_target_pairs={{1,0},{2,1},{3,2},{4,3},{5,4},{6,5},{7,6},{8,7},{9,8},{10,9},{11,1... | collective-permute-start | bytes 184868 | tf_op jit(solution)/shard_map/ppermute | solution.py:106
  20.4 8.2 %collective-permute-start.2 = (bf16[13,158,15]{1,2,0:T(8,128)(2,1)S(1)}, bf16[13,158,15]{1,2,0:T(8,128)(2,1)S(1)}, u32[]{:S(2)}, u32[]{:S(2)}) collective-permute-start(bf16[13,158,15]{1,2,0:T(8,128)(2,1)S(1)} %copy.62), channel_id=1, source_target_pairs={{0,1},{1,2},{2,3},{3,4},{4,5},{5,6},{6,7},{7,8},{8,9},{9,10},{10,1... | collective-permute-start | bytes 184868 | tf_op jit(solution)/shard_map/ppermute | solution.py:104
  136.8 6.1 %collective-permute-start.4 = (bf16[26,1,256]{2,0,1:T(8,128)(2,1)S(1)}, bf16[26,1,256]{2,0,1:T(8,128)(2,1)S(1)}, u32[]{:S(2)}, u32[]{:S(2)}) collective-permute-start(bf16[26,1,256]{2,0,1:T(8,128)(2,1)S(1)} %get-tuple-element.7), channel_id=1, source_target_pairs={{0,16},{16,32},{32,48},{48,64},{64,80},{80,96},{96,112},{1,17},{17... | collective-permute-start | bytes 39944 | tf_op jit(solution)/shard_map/ppermute | solution.py:104
  141.0 5.1 %collective-permute-start.5 = (bf16[26,1,256]{2,0,1:T(8,128)(2,1)S(1)}, bf16[26,1,256]{2,0,1:T(8,128)(2,1)S(1)}, u32[]{:S(2)}, u32[]{:S(2)}) collective-permute-start(bf16[26,1,256]{2,0,1:T(8,128)(2,1)S(1)} %get-tuple-element.8), channel_id=1, source_target_pairs={{16,0},{32,16},{48,32},{64,48},{80,64},{96,80},{112,96},{17,1},{33... | collective-permute-start | bytes 39944 | tf_op jit(solution)/shard_map/ppermute | solution.py:106
  146.3 1.7 copy-start.1
  151.8 12.6 %collective-permute-start.7 = (bf16[26,130,1]{1,0,2:T(8,128)(2,1)S(1)}, bf16[26,130,1]{1,0,2:T(8,128)(2,1)S(1)}, u32[]{:S(2)}, u32[]{:S(2)}) collective-permute-start(bf16[26,130,1]{1,0,2:T(8,128)(2,1)S(1)} %copy.77), channel_id=1, source_target_pairs={{1,0},{2,1},{3,2},{4,3},{5,4},{6,5},{7,6},{8,7},{9,8},{10,9},{11,1... | collective-permute-start | bytes 20288 | tf_op jit(solution)/shard_map/ppermute | solution.py:106
  153.7 8.8 %collective-permute-start.6 = (bf16[26,130,1]{1,0,2:T(8,128)(2,1)S(1)}, bf16[26,130,1]{1,0,2:T(8,128)(2,1)S(1)}, u32[]{:S(2)}, u32[]{:S(2)}) collective-permute-start(bf16[26,130,1]{1,0,2:T(8,128)(2,1)S(1)} %copy.76), channel_id=1, source_target_pairs={{0,1},{1,2},{2,3},{3,4},{4,5},{5,6},{6,7},{7,8},{8,9},{9,10},{10,1... | collective-permute-start | bytes 20288 | tf_op jit(solution)/shard_map/ppermute | solution.py:104
  167.2 2.1 %copy-start = (f32[13,130,256]{2,0,1:T(8,128)S(1)}, f32[13,130,256]{2,0,1:T(8,128)}, u32[]{:S(2)}) copy-start(f32[13,130,256]{2,0,1:T(8,128)} %slice_convert_fusion) | copy-start | bytes 5191684

commit v4 on v3

--- a/solution.py
+++ b/solution.py
@@ -93,21 +93,48 @@
     )(*args)
 
 
-def with_halo(cells, sides, width):
-    for axis, dim in sides:
-        count = lax.axis_size(axis)
-        ends = count - 1
-        head = lax.slice_in_dim(cells, 0, width, axis=dim)
-        tail = lax.slice_in_dim(cells, cells.shape[dim] - width, cells.shape[dim], axis=dim)
-        cells = jnp.concatenate(
-            [
-                lax.ppermute(tail, axis, [(i, (i + 1) % count) for i in range(ends)]),
-                cells,
-                lax.ppermute(head, axis, [((i + 1) % count, i) for i in range(ends)]),
-            ],
-            axis=dim,
-        )
-    return cells
+def with_halo(cells, width):
+    rows = lax.axis_size("row")
+    cols = lax.axis_size("col")
+    both = ("row", "col")
+
+    def shift(piece, axis, step_r, step_c):
+        if axis == "row":
+            pairs = [(i, i + step_r) for i in range(rows) if 0 <= i + step_r < rows]
+        elif axis == "col":
+            pairs = [(j, j + step_c) for j in range(cols) if 0 <= j + step_c < cols]
+        else:
+            pairs = [
+                (i * cols + j, (i + step_r) * cols + j + step_c)
+                for i in range(rows)
+                for j in range(cols)
+                if 0 <= i + step_r < rows and 0 <= j + step_c < cols
+            ]
+        return lax.ppermute(piece, axis, pairs)
+
+    top = cells[:, :width]
+    bottom = cells[:, -width:]
+    upper = jnp.concatenate(
+        [
+            shift(bottom[:, :, -width:], both, 1, 1),
+            shift(bottom, "row", 1, 0),
+            shift(bottom[:, :, :width], both, 1, -1),
+        ],
+        axis=2,
+    )
+    middle = jnp.concatenate(
+        [shift(cells[:, :, -width:], "col", 0, 1), cells, shift(cells[:, :, :width], "col", 0, -1)],
+        axis=2,
+    )
+    lower = jnp.concatenate(
+        [
+            shift(top[:, :, -width:], both, -1, 1),
+            shift(top, "row", -1, 0),
+            shift(top[:, :, :width], both, -1, -1),
+        ],
+        axis=2,
+    )
+    return jnp.concatenate([upper, middle, lower], axis=1)
 
 
 def body(
@@ -127,7 +154,7 @@
     row_count = lax.axis_size("row")
     my_row = lax.axis_index("row")
     my_col = lax.axis_index("col")
-    margin = sum(dilations)
+    margin = sum(dilations) + 1
     per_row = block_h // TILE
     per_col = block_w // TILE
     per_block = per_row * per_col
@@ -139,7 +166,7 @@
         (kernel_three, bias_three),
         (kernel_flux, bias_flux),
     )
-    extended = with_halo(state, (("row", 1), ("col", 2)), margin)
+    extended = with_halo(state, margin)
     ext_h, ext_w = extended.shape[1:]
     x = jnp.pad(extended.transpose(1, 0, 2), ((0, 0), (0, 16 - moments), (0, LANES - ext_w)))
     lims = []
@@ -157,18 +184,32 @@
             jnp.minimum(out_w, grid_w + left),
         ]
     lims = jnp.stack(lims).astype(jnp.int32)
-    flux = run_net(x, lims, layers, block_w, 32)[:, : 2 * moments].transpose(1, 0, 2)
-    listed = tile_ids[0]
-    mine = (listed // per_block) == my_col
-    local_ids = listed % per_block
-    chosen = jnp.any(
-        mine[None, :] & (local_ids[None, :] == jnp.arange(per_block, dtype=jnp.int32)[:, None]), axis=1
-    )
-    cell_mask = jnp.broadcast_to(
-        chosen.reshape(per_row, 1, per_col, 1), (per_row, TILE, per_col, TILE)
-    ).reshape(block_h, block_w)
-    flux_field = jnp.where(cell_mask[None], flux, jnp.zeros((), jnp.bfloat16))
-    rimmed = with_halo(flux_field, (("row", 1), ("col", 2)), 1)
+    flux = run_net(x, lims, layers, LANES, 32)[:, : 2 * moments, : block_w + 2].transpose(1, 0, 2)
+
+    every_id = lax.all_gather(tile_ids[0], "row")
+    listed = jnp.any(
+        every_id[:, :, None] == jnp.arange(col_count * per_block, dtype=jnp.int32)[None, None, :], axis=1
+    )
+    strip = jnp.array([-1] + [0] * per_row + [1], jnp.int32) + my_row
+    tile_row = jnp.array([per_row - 1] + list(range(per_row)) + [0], jnp.int32)
+    block = jnp.array([-1] + [0] * per_col + [1], jnp.int32) + my_col
+    tile_col = jnp.array([per_col - 1] + list(range(per_col)) + [0], jnp.int32)
+    ids = (
+        jnp.clip(block, 0, col_count - 1)[None, :] * per_block
+        + tile_row[:, None] * per_col
+        + tile_col[None, :]
+    )
+    piece = listed[jnp.clip(strip, 0, row_count - 1)[:, None], ids]
+    piece = piece & ((strip >= 0) & (strip < row_count))[:, None] & ((block >= 0) & (block < col_count))[None, :]
+    row_sizes = [1] + [TILE] * per_row + [1]
+    col_sizes = [1] + [TILE] * per_col + [1]
+    cell_mask = jnp.repeat(
+        jnp.repeat(piece, jnp.array(row_sizes), axis=0, total_repeat_length=block_h + 2),
+        jnp.array(col_sizes),
+        axis=1,
+        total_repeat_length=block_w + 2,
+    )
+    rimmed = jnp.where(cell_mask[None], flux, jnp.zeros((), jnp.bfloat16))
     across = rimmed[:moments, 1:-1, :].astype(jnp.float32)
     downward = rimmed[moments:, :, 1:-1].astype(jnp.float32)
     difference = across[:, :, 2:] - across[:, :, :-2] + (downward[:, 2:, :] - downward[:, :-2, :])

time: 172 us -> 179 us (1.041)
  blocking collectives: 0 us -> 11.5 us
  local copies, waits for them, and re-layouts: 27.7 us -> 19.8 us
  Pallas kernels: 102 us -> 106 us
    all_gather x0 -> x1, blocking collectives: none -> 11.5 us  [body(): every_id = lax.all_gather(tile_ids[0], 'row')]
    slice x8 -> x3, local copies, waits for them, and re-layouts: 7.95 us -> 1.62 us  [the longest x1 0.71 us: with_halo(): bottom = cells[:, -width:]]
    ppermute x4 -> x0, local copies, waits for them, and re-layouts: 5.93 us -> none  [the longest x2 3.41 us: with_halo(): lax.ppermute(head, axis, [((i + 1) % count, i) for i in range(ends)])]
    pallas_call x1, Pallas kernels: 102 us -> 106 us  [run_net(): pl.pallas_call(_net_kernel, out_shape=jax.ShapeDtypeStruct((h0 - 30, out_...]
    gather x0 -> x6, local copies, waits for them, and re-layouts: none -> 3.63 us  [the longest x2 1.9 us: body(): jnp.repeat(jnp.repeat(piece, jnp.array(row_sizes), axis=0, total_repeat_l...]
    unnamed x16 -> x29, local copies, waits for them, and re-layouts: 0.6 us -> 2.96 us
    convert_element_type x1, other arithmetic: 3.14 us -> 0.96 us  [body(): downward = rimmed[moments:, :, 1:-1].astype(jnp.float32)]
    transpose x1, other arithmetic: 1.2 us -> 3.28 us  [body(): extended.transpose(1, 0, 2)]
  transfers between devices with their start and end apart: 8 -> 8, of which waited for: 1 -> 1; matrix products, arithmetic and copies ran while one was open for 11% -> 9% of each run, Pallas kernels for 0% -> 0%
where the time goes in v4:
time: 179 us
  Pallas kernels  106 us (59%)
  starting transfers between devices  26.1 us (15%)
  local copies, waits for them, and re-layouts  19.8 us (11%)
  blocking collectives  11.5 us (6%)
  other arithmetic  10.5 us (6%)
  waiting for transfers between devices  4.46 us (2%)
    pallas_call x1, Pallas kernels, run_net(): pl.pallas_call(_net_kernel, out_shape=jax.ShapeDtypeStruct((h0 - 30, out_...  106 us
    ppermute x8, starting transfers between devices, shift(): return lax.ppermute(piece, axis, pairs)  26.1 us
    all_gather x1, blocking collectives, body(): every_id = lax.all_gather(tile_ids[0], 'row')  11.5 us
    ppermute x8, waiting for transfers between devices, shift(): return lax.ppermute(piece, axis, pairs)  4.46 us
  transfers between devices with their start and end apart: 8, of which 1 were waited for; matrix products, arithmetic and copies ran while one was open for 9% of the time, Pallas kernels for 0%

profile of v4, /device:TPU:7, one launch (start us, length us, event | category | flops | bytes accessed | tf_op | source)
XLA Modules:
  0.0 178.7 jit_solution(17218050023666125782)
XLA Ops:
  0.0 0.0 copy-start.5
  0.0 0.0 copy-start.10
  0.0 0.0 copy-start
  0.0 0.0 copy-start.13
  0.1 0.0 copy-start.7
  0.1 0.0 copy-start.8
  0.1 0.0 copy-start.9
  0.1 1.7 copy.83
  1.8 0.7 fusion.11
  2.4 5.0 %collective-permute-start = (bf16[13,16,16]{2,0,1:T(8,128)(2,1)S(1)}, bf16[13,16,16]{2,0,1:T(8,128)(2,1)S(1)}, u32[]{:S(2)}, u32[]{:S(2)}) collective-permute-start(bf16[13,16,16]{2,0,1:T(8,128)(2,1)S(1)} %get-tuple-element.29), channel_id=1, source_target_pairs={{0,17},{1,18},{2,19},{3,20},{4,21},{5,22},{6,23},{7,24},{8,25},{9,... | collective-permute-start | bytes 19976 | tf_op jit(solution)/shard_map/ppermute | solution.py:113
  7.5 1.9 %collective-permute-start.7 = (bf16[13,16,16]{2,0,1:T(8,128)(2,1)S(1)}, bf16[13,16,16]{2,0,1:T(8,128)(2,1)S(1)}, u32[]{:S(2)}, u32[]{:S(2)}) collective-permute-start(bf16[13,16,16]{2,0,1:T(8,128)(2,1)S(1)} %get-tuple-element.30), channel_id=1, source_target_pairs={{17,0},{18,1},{19,2},{20,3},{21,4},{22,5},{23,6},{24,7},{25,8},{26... | collective-permute-start | bytes 19976 | tf_op jit(solution)/shard_map/ppermute | solution.py:113
  9.4 1.9 %collective-permute-start.5 = (bf16[13,16,16]{2,0,1:T(8,128)(2,1)S(1)}, bf16[13,16,16]{2,0,1:T(8,128)(2,1)S(1)}, u32[]{:S(2)}, u32[]{:S(2)}) collective-permute-start(bf16[13,16,16]{2,0,1:T(8,128)(2,1)S(1)} %get-tuple-element.31), channel_id=1, source_target_pairs={{16,1},{17,2},{18,3},{19,4},{20,5},{21,6},{22,7},{23,8},{24,9},{25... | collective-permute-start | bytes 19976 | tf_op jit(solution)/shard_map/ppermute | solution.py:113
  11.3 4.5 %collective-permute-start.2 = (bf16[13,16,16]{2,0,1:T(8,128)(2,1)}, bf16[13,16,16]{2,0,1:T(8,128)(2,1)}, u32[]{:S(2)}, u32[]{:S(2)}) collective-permute-start(bf16[13,16,16]{2,0,1:T(8,128)(2,1)} %get-tuple-element.32), channel_id=1, source_target_pairs={{1,16},{2,17},{3,18},{4,19},{5,20},{6,21},{7,22},{8,23},{9,24},{10... | collective-permute-start | bytes 19976 | tf_op jit(solution)/shard_map/ppermute | solution.py:113
  15.9 0.7 fusion.12
  16.6 2.7 %collective-permute-start.1 = (bf16[13,16,256]{2,0,1:T(8,128)(2,1)}, bf16[13,16,256]{2,0,1:T(8,128)(2,1)S(1)}, u32[]{:S(2)}, u32[]{:S(2)}) collective-permute-start(bf16[13,16,256]{2,0,1:T(8,128)(2,1)} %get-tuple-element.33), channel_id=1, source_target_pairs={{0,16},{16,32},{32,48},{48,64},{64,80},{80,96},{96,112},{1,17},{17... | collective-permute-start | bytes 319496 | tf_op jit(solution)/shard_map/ppermute | solution.py:113
  19.3 0.7 compare_and_fusion.1
  20.0 0.7 fusion.10
  20.6 0.7 compare_and_fusion
  21.3 0.7 fusion.8
  21.9 0.2 fusion.13
  22.2 0.1 fusion.7
  22.3 0.1 reshape.264
  22.4 11.5 %all-gather = s32[8,1,32]{2,1,0:T(1,128)S(1)} all-gather(s32[1,1,32]{2,1,0:T(1,128)S(1)} %bitcast.49), channel_id=1, replica_groups=mesh['row'=8,'col'=16] {'row'}, dimensions={0}, use_global_device_ids=true | all-gather | bytes 1152 | tf_op jit(solution)/shard_map/all_gather | solution.py:189
  33.9 0.1 fusion.4
  34.0 0.9 gather_fusion
  34.8 0.1 reshape.267
  35.0 0.1 and_and_fusion
  35.1 0.0 collective-permute-done
  35.1 2.1 %collective-permute-start.6 = (bf16[13,16,256]{2,0,1:T(8,128)(2,1)}, bf16[13,16,256]{2,0,1:T(8,128)(2,1)}, u32[]{:S(2)}, u32[]{:S(2)}) collective-permute-start(bf16[13,16,256]{2,0,1:T(8,128)(2,1)} %get-tuple-element.34), channel_id=1, source_target_pairs={{16,0},{32,16},{48,32},{64,48},{80,64},{96,80},{112,96},{17,1},{33... | collective-permute-start | bytes 319496 | tf_op jit(solution)/shard_map/ppermute | solution.py:113
  37.2 0.0 collective-permute-done.7
  37.2 0.6 copy-done.2
  37.8 6.0 %collective-permute-start.3 = (bf16[13,128,16]{2,0,1:T(8,128)(2,1)S(1)}, bf16[13,128,16]{2,0,1:T(8,128)(2,1)S(1)}, u32[]{:S(2)}, u32[]{:S(2)}) collective-permute-start(bf16[13,128,16]{2,0,1:T(8,128)(2,1)S(1)} %get-tuple-element.35), channel_id=1, source_target_pairs={{0,1},{1,2},{2,3},{3,4},{4,5},{5,6},{6,7},{7,8},{8,9},{9,10},{10,1... | collective-permute-start | bytes 159752 | tf_op jit(solution)/shard_map/ppermute | solution.py:113
  43.8 0.0 collective-permute-done.5
  43.8 0.6 copy-done.3
  44.4 1.9 %collective-permute-start.4 = (bf16[13,128,16]{2,0,1:T(8,128)(2,1)S(1)}, bf16[13,128,16]{2,0,1:T(8,128)(2,1)S(1)}, u32[]{:S(2)}, u32[]{:S(2)}) collective-permute-start(bf16[13,128,16]{2,0,1:T(8,128)(2,1)S(1)} %get-tuple-element.36), channel_id=1, source_target_pairs={{1,0},{2,1},{3,2},{4,3},{5,4},{6,5},{7,6},{8,7},{9,8},{10,9},{11,1... | collective-permute-start | bytes 159752 | tf_op jit(solution)/shard_map/ppermute | solution.py:113
  46.4 0.7 gather_fusion.1
  47.1 0.1 copy.81
  47.2 0.7 copy.101.bfl
  47.9 0.7 copy.96.b1
  48.6 0.7 copy.98.b2
  49.3 0.7 copy.100.b3
  50.1 0.7 copy.95.k1
  50.8 1.7 gather_fusion.2
  52.5 0.2 copy.82
  52.7 0.1 copy.94
  52.7 0.7 reshape.262.kf
  53.5 1.0 copy.92
  54.5 0.8 copy.97.k2
  55.3 1.0 copy.93
  56.3 0.8 copy.99.k3
  57.1 0.7 stack.67.lim_ref
  57.8 0.0 collective-permute-done.2
  57.8 0.0 collective-permute-done.3
  57.8 4.4 %collective-permute-done.4 = bf16[13,128,16]{2,0,1:T(8,128)(2,1)S(1)} collective-permute-done((bf16[13,128,16]{2,0,1:T(8,128)(2,1)S(1)}, bf16[13,128,16]{2,0,1:T(8,128)(2,1)S(1)}, u32[]{:S(2)}, u32[]{:S(2)}) %collective-permute-start.4) | collective-permute-done | bytes 53280 | tf_op jit(solution)/shard_map/ppermute | solution.py:113
  62.3 0.0 collective-permute-done.1
  62.3 0.0 collective-permute-done.6
  62.3 3.3 %maximum_bitcast_fusion = bf16[160,13,288]{2,1,0:T(8,128)(2,1)S(1)} fusion(bf16[13,16,16]{2,0,1:T(8,128)(2,1)} %copy-done.2, bf16[13,16,256]{2,0,1:T(8,128)(2,1)} %collective-permute-done.6, bf16[13,16,16]{2,0,1:T(8,128)(2,1)} %copy-done.3, bf16[13,128,16]{2,0,1:T(8,128)(2,1)S(1)} %collective-permute-done.4, bf16[13,128,256]{2,0,1:T(8,128)(2,1)S(1)} %copy.83, ...), kind=kLoop, calls=%fused_computation.10 | loop fusion | flops 10782720 | bytes 2396160 | tf_op jit(solution)/shard_map/transpose | solution.py:171
  65.5 1.6 pad.28.x_ref
  67.1 106.0 %shard_map.154 = bf16[130,32,384]{2,1,0:T(8,128)(2,1)} custom-call(s32[16]{0:T(128)} %stack.67.lim_ref, bf16[160,16,384]{2,1,0:T(8,128)(2,1)} %pad.28.x_ref, bf16[64,144]{1,0:T(8,128)(2,1)} %copy.95.k1, f32[64,1]{1,0:T(8,128)} %copy.96.b1, bf16[64,576]{1,0:T(8,128)(2,1)} %copy.97.k2, f32[64,1]{1,0:T(8,128)} %copy.98.b2, bf16[64,576]{1,0:T(8,128)(2,1)} %copy.99.k3, ...), custom_call_target="tpu_custom_call" | custom-call | tf_op jit(solution)/shard_map/pallas_call | solution.py:83
  173.2 2.4 %fusion = bf16[26,130,258]{2,0,1:T(8,128)(2,1)S(1)} fusion(bf16[130,32,384]{2,1,0:T(8,128)(2,1)} %shard_map.154, pred[130,258]{1,0:T(8,128)(4,1)S(1)} %copy.82), kind=kLoop, calls=%fused_computation.4 | loop fusion | flops 872040 | bytes 3521700 | tf_op jit(solution)/shard_map/jit(_where)/select_n | solution.py:212
  175.6 1.0 slice_convert_fusion.1
  176.6 0.2 slice_convert_fusion
  176.8 0.7 fusion.3
  177.5 1.2 copy.102
  (24 shorter events, 0.1 us)
Async XLA Ops:
  0.0 22.2 %copy-start.11 = (s32[4]{0:T(128)S(1)}, s32[4]{0:T(128)}, u32[]{:S(2)}) copy-start(s32[4]{0:T(128)} %constant.264) | copy-start | bytes 52
  0.0 22.2 %copy-start.12 = (s32[6]{0:T(128)S(1)}, s32[6]{0:T(128)}, u32[]{:S(2)}) copy-start(s32[6]{0:T(128)} %constant.194.clone) | copy-start | bytes 76
  0.0 34.9 %copy-start.6 = (s32[130]{0:T(256)S(1)}, s32[130]{0:T(256)}, u32[]{:S(2)}) copy-start(s32[130]{0:T(256)} %constant.282) | copy-start | bytes 1564
  0.0 35.0 %copy-start.5 = (s32[258]{0:T(512)S(1)}, s32[258]{0:T(512)}, u32[]{:S(2)}) copy-start(s32[258]{0:T(512)} %constant.283) | copy-start | bytes 3100
  0.0 22.4 %copy-start.10 = (s32[1,32]{1,0:T(1,128)S(1)}, s32[1,32]{1,0:T(1,128)}, u32[]{:S(2)}) copy-start(s32[1,32]{1,0:T(1,128)} %param.21) | copy-start | bytes 388
  0.0 34.9 %copy-start = (bf16[26,64,3,3]{1,0,3,2:T(8,128)(2,1)S(1)}, bf16[26,64,3,3]{1,0,3,2:T(8,128)(2,1)}, u32[]{:S(2)}) copy-start(bf16[26,64,3,3]{1,0,3,2:T(8,128)(2,1)} %param.28) | copy-start | bytes 89860
  0.0 46.3 %copy-start.13 = (f32[26]{0:T(128)S(1)}, f32[26]{0:T(128)}, u32[]{:S(2)}) copy-start(f32[26]{0:T(128)} %param.29) | copy-start | bytes 316
  0.1 47.9 %copy-start.7 = (f32[64]{0:T(128)S(1)}, f32[64]{0:T(128)}, u32[]{:S(2)}) copy-start(f32[64]{0:T(128)} %param.23) | copy-start | bytes 772
  0.1 48.6 %copy-start.8 = (f32[64]{0:T(128)S(1)}, f32[64]{0:T(128)}, u32[]{:S(2)}) copy-start(f32[64]{0:T(128)} %param.25) | copy-start | bytes 772
  0.1 49.3 %copy-start.9 = (f32[64]{0:T(128)S(1)}, f32[64]{0:T(128)}, u32[]{:S(2)}) copy-start(f32[64]{0:T(128)} %param.27) | copy-start | bytes 772
  0.1 50.0 %copy-start.4 = (bf16[64,13,3,3]{0,1,3,2:T(8,128)(2,1)S(1)}, bf16[64,13,3,3]{0,1,3,2:T(8,128)(2,1)}, u32[]{:S(2)}) copy-start(bf16[64,13,3,3]{0,1,3,2:T(8,128)(2,1)} %param.22) | copy-start | bytes 44932
  2.4 32.6 %collective-permute-start = (bf16[13,16,16]{2,0,1:T(8,128)(2,1)S(1)}, bf16[13,16,16]{2,0,1:T(8,128)(2,1)S(1)}, u32[]{:S(2)}, u32[]{:S(2)}) collective-permute-start(bf16[13,16,16]{2,0,1:T(8,128)(2,1)S(1)} %get-tuple-element.29), channel_id=1, source_target_pairs={{0,17},{1,18},{2,19},{3,20},{4,21},{5,22},{6,23},{7,24},{8,25},{9,... | collective-permute-start | bytes 19976 | tf_op jit(solution)/shard_map/ppermute | solution.py:113
  7.5 29.7 %collective-permute-start.7 = (bf16[13,16,16]{2,0,1:T(8,128)(2,1)S(1)}, bf16[13,16,16]{2,0,1:T(8,128)(2,1)S(1)}, u32[]{:S(2)}, u32[]{:S(2)}) collective-permute-start(bf16[13,16,16]{2,0,1:T(8,128)(2,1)S(1)} %get-tuple-element.30), channel_id=1, source_target_pairs={{17,0},{18,1},{19,2},{20,3},{21,4},{22,5},{23,6},{24,7},{25,8},{26... | collective-permute-start | bytes 19976 | tf_op jit(solution)/shard_map/ppermute | solution.py:113
  9.4 34.4 %collective-permute-start.5 = (bf16[13,16,16]{2,0,1:T(8,128)(2,1)S(1)}, bf16[13,16,16]{2,0,1:T(8,128)(2,1)S(1)}, u32[]{:S(2)}, u32[]{:S(2)}) collective-permute-start(bf16[13,16,16]{2,0,1:T(8,128)(2,1)S(1)} %get-tuple-element.31), channel_id=1, source_target_pairs={{16,1},{17,2},{18,3},{19,4},{20,5},{21,6},{22,7},{23,8},{24,9},{25... | collective-permute-start | bytes 19976 | tf_op jit(solution)/shard_map/ppermute | solution.py:113
  11.3 46.5 %collective-permute-start.2 = (bf16[13,16,16]{2,0,1:T(8,128)(2,1)}, bf16[13,16,16]{2,0,1:T(8,128)(2,1)}, u32[]{:S(2)}, u32[]{:S(2)}) collective-permute-start(bf16[13,16,16]{2,0,1:T(8,128)(2,1)} %get-tuple-element.32), channel_id=1, source_target_pairs={{1,16},{2,17},{3,18},{4,19},{5,20},{6,21},{7,22},{8,23},{9,24},{10... | collective-permute-start | bytes 19976 | tf_op jit(solution)/shard_map/ppermute | solution.py:113
  16.6 45.7 %collective-permute-start.1 = (bf16[13,16,256]{2,0,1:T(8,128)(2,1)}, bf16[13,16,256]{2,0,1:T(8,128)(2,1)S(1)}, u32[]{:S(2)}, u32[]{:S(2)}) collective-permute-start(bf16[13,16,256]{2,0,1:T(8,128)(2,1)} %get-tuple-element.33), channel_id=1, source_target_pairs={{0,16},{16,32},{32,48},{48,64},{64,80},{80,96},{96,112},{1,17},{17... | collective-permute-start | bytes 319496 | tf_op jit(solution)/shard_map/ppermute | solution.py:113
  35.1 2.1 %copy-start.1 = (bf16[13,16,16]{2,0,1:T(8,128)(2,1)}, bf16[13,16,16]{2,0,1:T(8,128)(2,1)S(1)}, u32[]{:S(2)}) copy-start(bf16[13,16,16]{2,0,1:T(8,128)(2,1)S(1)} %collective-permute-done) | copy-start | bytes 19972
  35.1 27.2 %collective-permute-start.6 = (bf16[13,16,256]{2,0,1:T(8,128)(2,1)}, bf16[13,16,256]{2,0,1:T(8,128)(2,1)}, u32[]{:S(2)}, u32[]{:S(2)}) collective-permute-start(bf16[13,16,256]{2,0,1:T(8,128)(2,1)} %get-tuple-element.34), channel_id=1, source_target_pairs={{16,0},{32,16},{48,32},{64,48},{80,64},{96,80},{112,96},{17,1},{33... | collective-permute-start | bytes 319496 | tf_op jit(solution)/shard_map/ppermute | solution.py:113
  37.2 0.6 copy-start.2
  37.8 20.0 %collective-permute-start.3 = (bf16[13,128,16]{2,0,1:T(8,128)(2,1)S(1)}, bf16[13,128,16]{2,0,1:T(8,128)(2,1)S(1)}, u32[]{:S(2)}, u32[]{:S(2)}) collective-permute-start(bf16[13,128,16]{2,0,1:T(8,128)(2,1)S(1)} %get-tuple-element.35), channel_id=1, source_target_pairs={{0,1},{1,2},{2,3},{3,4},{4,5},{5,6},{6,7},{7,8},{8,9},{9,10},{10,1... | collective-permute-start | bytes 159752 | tf_op jit(solution)/shard_map/ppermute | solution.py:113
  43.8 0.6 copy-start.3
  44.4 17.8 %collective-permute-start.4 = (bf16[13,128,16]{2,0,1:T(8,128)(2,1)S(1)}, bf16[13,128,16]{2,0,1:T(8,128)(2,1)S(1)}, u32[]{:S(2)}, u32[]{:S(2)}) collective-permute-start(bf16[13,128,16]{2,0,1:T(8,128)(2,1)S(1)} %get-tuple-element.36), channel_id=1, source_target_pairs={{1,0},{2,1},{3,2},{4,3},{5,4},{6,5},{7,6},{8,7},{9,8},{10,9},{11,1... | collective-permute-start | bytes 159752 | tf_op jit(solution)/shard_map/ppermute | solution.py:113

commit v5 on v4

--- a/solution.py
+++ b/solution.py
@@ -186,11 +186,18 @@
     lims = jnp.stack(lims).astype(jnp.int32)
     flux = run_net(x, lims, layers, LANES, 32)[:, : 2 * moments, : block_w + 2].transpose(1, 0, 2)
 
-    every_id = lax.all_gather(tile_ids[0], "row")
+    near_ids = jnp.concatenate(
+        [
+            lax.ppermute(tile_ids, "row", [(i, i + 1) for i in range(row_count - 1)]),
+            tile_ids,
+            lax.ppermute(tile_ids, "row", [(i + 1, i) for i in range(row_count - 1)]),
+        ],
+        axis=0,
+    )
     listed = jnp.any(
-        every_id[:, :, None] == jnp.arange(col_count * per_block, dtype=jnp.int32)[None, None, :], axis=1
-    )
-    strip = jnp.array([-1] + [0] * per_row + [1], jnp.int32) + my_row
+        near_ids[:, :, None] == jnp.arange(col_count * per_block, dtype=jnp.int32)[None, None, :], axis=1
+    )
+    strip = jnp.array([-1] + [0] * per_row + [1], jnp.int32)
     tile_row = jnp.array([per_row - 1] + list(range(per_row)) + [0], jnp.int32)
     block = jnp.array([-1] + [0] * per_col + [1], jnp.int32) + my_col
     tile_col = jnp.array([per_col - 1] + list(range(per_col)) + [0], jnp.int32)
@@ -199,7 +206,8 @@
         + tile_row[:, None] * per_col
         + tile_col[None, :]
     )
-    piece = listed[jnp.clip(strip, 0, row_count - 1)[:, None], ids]
+    piece = listed[(strip + 1)[:, None], ids]
+    strip = strip + my_row
     piece = piece & ((strip >= 0) & (strip < row_count))[:, None] & ((block >= 0) & (block < col_count))[None, :]
     row_sizes = [1] + [TILE] * per_row + [1]
     col_sizes = [1] + [TILE] * per_col + [1]

time: 179 us -> 181 us (1.011); the launches traced: 179 us -> 179 us
  blocking collectives: 11.5 us -> 0 us
  starting transfers between devices: 26.1 us -> 32.9 us
  waiting for transfers between devices: 4.46 us -> 11.2 us
    all_gather x1 -> x0, blocking collectives: 11.5 us -> none  [body(): every_id = lax.all_gather(tile_ids[0], 'row')]
    ppermute x8, waiting for transfers between devices: 4.46 us -> 11.2 us  [shift(): return lax.ppermute(piece, axis, pairs)]
    ppermute x0 -> x2, starting transfers between devices: none -> 6.16 us  [the longest x1 4.24 us: body(): lax.ppermute(tile_ids, 'row', [(i, i + 1) for i in range(row_count - 1)])]
  transfers between devices with their start and end apart: 8 -> 10, of which waited for: 1 -> 2; matrix products, arithmetic and copies ran while one was open for 9% -> 9% of each run, Pallas kernels for 0% -> 0%
where the time goes in v5:
time: 181 us; the launch traced here: 179 us
  Pallas kernels  106 us (59%)
  starting transfers between devices  32.9 us (18%)
  local copies, waits for them, and re-layouts  18.5 us (10%)
  waiting for transfers between devices  11.2 us (6%)
  other arithmetic  9.81 us (5%)
    pallas_call x1, Pallas kernels, run_net(): pl.pallas_call(_net_kernel, out_shape=jax.ShapeDtypeStruct((h0 - 30, out_...  106 us
    ppermute x8, starting transfers between devices, shift(): return lax.ppermute(piece, axis, pairs)  26.8 us
    ppermute x8, waiting for transfers between devices, shift(): return lax.ppermute(piece, axis, pairs)  11.2 us
    ppermute x1, starting transfers between devices, body(): lax.ppermute(tile_ids, 'row', [(i, i + 1) for i in range(row_count - 1)])  4.24 us
  transfers between devices with their start and end apart: 10, of which 2 were waited for; matrix products, arithmetic and copies ran while one was open for 9% of the time, Pallas kernels for 0%

profile of v5, /device:TPU:7, one launch (start us, length us, event | category | flops | bytes accessed | tf_op | source)
XLA Modules:
  0.0 178.9 jit_solution(12254259227949687002)
XLA Ops:
  0.0 0.0 copy-start.15
  0.0 0.0 copy-start.8
  0.0 0.0 copy-start.7
  0.1 4.2 %collective-permute-start = (s32[1,32]{1,0:T(1,128)}, s32[1,32]{1,0:T(1,128)S(1)}, u32[]{:S(2)}, u32[]{:S(2)}) collective-permute-start(s32[1,32]{1,0:T(1,128)} %param.21), channel_id=1, source_target_pairs={{0,16},{16,32},{32,48},{48,64},{64,80},{80,96},{96,112},{1,17},{17... | collective-permute-start | bytes 392 | tf_op jit(solution)/shard_map/ppermute | solution.py:191
  4.4 1.9 %collective-permute-start.1 = (s32[1,32]{1,0:T(1,128)}, s32[1,32]{1,0:T(1,128)S(1)}, u32[]{:S(2)}, u32[]{:S(2)}) collective-permute-start(s32[1,32]{1,0:T(1,128)} %param.21), channel_id=1, source_target_pairs={{16,0},{32,16},{48,32},{64,48},{80,64},{96,80},{112,96},{17,1},{33... | collective-permute-start | bytes 392 | tf_op jit(solution)/shard_map/ppermute | solution.py:193
  6.3 1.6 copy.61
  8.0 0.7 fusion.9
  8.6 4.6 %collective-permute-start.2 = (bf16[13,16,16]{2,0,1:T(8,128)(2,1)S(1)}, bf16[13,16,16]{2,0,1:T(8,128)(2,1)S(1)}, u32[]{:S(2)}, u32[]{:S(2)}) collective-permute-start(bf16[13,16,16]{2,0,1:T(8,128)(2,1)S(1)} %get-tuple-element.29), channel_id=1, source_target_pairs={{0,17},{1,18},{2,19},{3,20},{4,21},{5,22},{6,23},{7,24},{8,25},{9,... | collective-permute-start | bytes 19976 | tf_op jit(solution)/shard_map/ppermute | solution.py:113
  13.2 1.9 %collective-permute-start.9 = (bf16[13,16,16]{2,0,1:T(8,128)(2,1)S(1)}, bf16[13,16,16]{2,0,1:T(8,128)(2,1)S(1)}, u32[]{:S(2)}, u32[]{:S(2)}) collective-permute-start(bf16[13,16,16]{2,0,1:T(8,128)(2,1)S(1)} %get-tuple-element.30), channel_id=1, source_target_pairs={{17,0},{18,1},{19,2},{20,3},{21,4},{22,5},{23,6},{24,7},{25,8},{26... | collective-permute-start | bytes 19976 | tf_op jit(solution)/shard_map/ppermute | solution.py:113
  15.1 1.9 %collective-permute-start.7 = (bf16[13,16,16]{2,0,1:T(8,128)(2,1)S(1)}, bf16[13,16,16]{2,0,1:T(8,128)(2,1)S(1)}, u32[]{:S(2)}, u32[]{:S(2)}) collective-permute-start(bf16[13,16,16]{2,0,1:T(8,128)(2,1)S(1)} %get-tuple-element.31), channel_id=1, source_target_pairs={{16,1},{17,2},{18,3},{19,4},{20,5},{21,6},{22,7},{23,8},{24,9},{25... | collective-permute-start | bytes 19976 | tf_op jit(solution)/shard_map/ppermute | solution.py:113
  17.1 0.7 compare_and_fusion
  17.7 0.7 fusion.8
  18.4 0.7 fusion.10
  19.1 0.2 fusion.11
  19.5 0.1 fusion.7
  19.6 0.1 reshape.264
  19.7 0.7 copy.79.bfl
  20.4 0.7 copy.74.b1
  21.1 0.0 copy-done.10
  21.1 0.7 copy.76.b2
  21.8 0.7 copy.78.b3
  22.5 0.7 copy.73.k1
  23.2 0.1 copy.72
  23.3 0.7 reshape.262.kf
  24.0 0.0 copy-done
  24.0 0.1 copy.70
  24.2 0.8 copy.75.k2
  25.0 0.1 copy.71
  25.1 0.8 copy.77.k3
  25.9 0.6 stack.67.lim_ref
  26.5 0.0 collective-permute-done
  26.5 4.5 %collective-permute-start.4 = (bf16[13,16,16]{2,0,1:T(8,128)(2,1)}, bf16[13,16,16]{2,0,1:T(8,128)(2,1)}, u32[]{:S(2)}, u32[]{:S(2)}) collective-permute-start(bf16[13,16,16]{2,0,1:T(8,128)(2,1)} %get-tuple-element.32), channel_id=1, source_target_pairs={{1,16},{2,17},{3,18},{4,19},{5,20},{6,21},{7,22},{8,23},{9,24},{10... | collective-permute-start | bytes 19976 | tf_op jit(solution)/shard_map/ppermute | solution.py:113
  31.0 0.0 collective-permute-done.1
  31.0 3.1 %collective-permute-start.3 = (bf16[13,16,256]{2,0,1:T(8,128)(2,1)}, bf16[13,16,256]{2,0,1:T(8,128)(2,1)S(1)}, u32[]{:S(2)}, u32[]{:S(2)}) collective-permute-start(bf16[13,16,256]{2,0,1:T(8,128)(2,1)} %get-tuple-element.33), channel_id=1, source_target_pairs={{0,16},{16,32},{32,48},{48,64},{64,80},{80,96},{96,112},{1,17},{17... | collective-permute-start | bytes 319496 | tf_op jit(solution)/shard_map/ppermute | solution.py:113
  34.2 0.0 copy-done.12
  34.2 0.1 fusion.4
  34.3 0.8 gather_fusion
  35.1 0.7 reshape.267
  35.8 0.0 collective-permute-done.2
  35.8 1.9 %collective-permute-start.8 = (bf16[13,16,256]{2,0,1:T(8,128)(2,1)}, bf16[13,16,256]{2,0,1:T(8,128)(2,1)S(1)}, u32[]{:S(2)}, u32[]{:S(2)}) collective-permute-start(bf16[13,16,256]{2,0,1:T(8,128)(2,1)} %get-tuple-element.34), channel_id=1, source_target_pairs={{16,0},{32,16},{48,32},{64,48},{80,64},{96,80},{112,96},{17,1},{33... | collective-permute-start | bytes 319496 | tf_op jit(solution)/shard_map/ppermute | solution.py:113
  37.7 0.0 collective-permute-done.9
  37.8 0.6 copy-done.4
  38.4 6.9 %collective-permute-start.5 = (bf16[13,128,16]{2,0,1:T(8,128)(2,1)S(1)}, bf16[13,128,16]{2,0,1:T(8,128)(2,1)S(1)}, u32[]{:S(2)}, u32[]{:S(2)}) collective-permute-start(bf16[13,128,16]{2,0,1:T(8,128)(2,1)S(1)} %get-tuple-element.35), channel_id=1, source_target_pairs={{0,1},{1,2},{2,3},{3,4},{4,5},{5,6},{6,7},{7,8},{8,9},{9,10},{10,1... | collective-permute-start | bytes 159752 | tf_op jit(solution)/shard_map/ppermute | solution.py:113
  45.3 0.0 collective-permute-done.7
  45.3 0.6 copy-done.5
  45.9 1.9 %collective-permute-start.6 = (bf16[13,128,16]{2,0,1:T(8,128)(2,1)S(1)}, bf16[13,128,16]{2,0,1:T(8,128)(2,1)S(1)}, u32[]{:S(2)}, u32[]{:S(2)}) collective-permute-start(bf16[13,128,16]{2,0,1:T(8,128)(2,1)S(1)} %get-tuple-element.36), channel_id=1, source_target_pairs={{1,0},{2,1},{3,2},{4,3},{5,4},{6,5},{7,6},{8,7},{9,8},{10,9},{11,1... | collective-permute-start | bytes 159752 | tf_op jit(solution)/shard_map/ppermute | solution.py:113
  47.8 0.7 and_and_fusion
  48.6 0.7 gather_fusion.1
  49.3 0.1 copy.59
  49.4 1.7 gather_fusion.2
  51.1 0.2 copy.60
  51.3 0.0 collective-permute-done.4
  51.3 4.3 %collective-permute-done.5 = bf16[13,128,16]{2,0,1:T(8,128)(2,1)S(1)} collective-permute-done((bf16[13,128,16]{2,0,1:T(8,128)(2,1)S(1)}, bf16[13,128,16]{2,0,1:T(8,128)(2,1)S(1)}, u32[]{:S(2)}, u32[]{:S(2)}) %collective-permute-start.5) | collective-permute-done | bytes 53280 | tf_op jit(solution)/shard_map/ppermute | solution.py:113
  55.6 6.8 %collective-permute-done.6 = bf16[13,128,16]{2,0,1:T(8,128)(2,1)S(1)} collective-permute-done((bf16[13,128,16]{2,0,1:T(8,128)(2,1)S(1)}, bf16[13,128,16]{2,0,1:T(8,128)(2,1)S(1)}, u32[]{:S(2)}, u32[]{:S(2)}) %collective-permute-start.6) | collective-permute-done | bytes 53280 | tf_op jit(solution)/shard_map/ppermute | solution.py:113
  62.5 0.0 collective-permute-done.3
  62.5 0.0 collective-permute-done.8
  62.5 3.2 %maximum_bitcast_fusion = bf16[160,13,288]{2,1,0:T(8,128)(2,1)S(1)} fusion(bf16[13,16,16]{2,0,1:T(8,128)(2,1)} %copy-done.4, bf16[13,16,256]{2,0,1:T(8,128)(2,1)S(1)} %collective-permute-done.8, bf16[13,16,16]{2,0,1:T(8,128)(2,1)} %copy-done.5, bf16[13,128,16]{2,0,1:T(8,128)(2,1)S(1)} %collective-permute-done.6, bf16[13,128,256]{2,0,1:T(8,128)(2,1)S(1)} %copy.61, ...), kind=kLoop, calls=%fused_computation.10 | loop fusion | flops 10782720 | bytes 2396160 | tf_op jit(solution)/shard_map/transpose | solution.py:171
  65.7 1.6 pad.28.x_ref
  67.3 106.1 %shard_map.154 = bf16[130,32,384]{2,1,0:T(8,128)(2,1)} custom-call(s32[16]{0:T(128)} %stack.67.lim_ref, bf16[160,16,384]{2,1,0:T(8,128)(2,1)} %pad.28.x_ref, bf16[64,144]{1,0:T(8,128)(2,1)} %copy.73.k1, f32[64,1]{1,0:T(8,128)} %copy.74.b1, bf16[64,576]{1,0:T(8,128)(2,1)} %copy.75.k2, f32[64,1]{1,0:T(8,128)} %copy.76.b2, bf16[64,576]{1,0:T(8,128)(2,1)} %copy.77.k3, ...), custom_call_target="tpu_custom_call" | custom-call | tf_op jit(solution)/shard_map/pallas_call | solution.py:83
  173.4 2.4 %fusion = bf16[26,130,258]{2,0,1:T(8,128)(2,1)S(1)} fusion(bf16[130,32,384]{2,1,0:T(8,128)(2,1)} %shard_map.154, pred[130,258]{1,0:T(8,128)(4,1)S(1)} %copy.60), kind=kLoop, calls=%fused_computation.4 | loop fusion | flops 872040 | bytes 3521700 | tf_op jit(solution)/shard_map/jit(_where)/select_n | solution.py:220
  175.8 1.0 slice_convert_fusion.1
  176.7 0.2 slice_convert_fusion
  177.0 0.7 fusion.3
  177.7 1.2 copy.80
  (35 shorter events, 0.1 us)
Async XLA Ops:
  0.0 19.4 %copy-start.17 = (s32[4]{0:T(128)S(1)}, s32[4]{0:T(128)}, u32[]{:S(2)}) copy-start(s32[4]{0:T(128)} %constant.190.clone) | copy-start | bytes 52
  0.0 19.4 %copy-start.13 = (s32[4]{0:T(128)S(1)}, s32[4]{0:T(128)}, u32[]{:S(2)}) copy-start(s32[4]{0:T(128)} %constant.286) | copy-start | bytes 52
  0.0 19.5 %copy-start.14 = (s32[4]{0:T(128)S(1)}, s32[4]{0:T(128)}, u32[]{:S(2)}) copy-start(s32[4]{0:T(128)} %constant.267) | copy-start | bytes 52
  0.0 19.5 %copy-start.15 = (s32[6]{0:T(128)S(1)}, s32[6]{0:T(128)}, u32[]{:S(2)}) copy-start(s32[6]{0:T(128)} %constant.193.clone) | copy-start | bytes 76
  0.0 19.6 %copy-start.8 = (s32[130]{0:T(256)S(1)}, s32[130]{0:T(256)}, u32[]{:S(2)}) copy-start(s32[130]{0:T(256)} %constant.287) | copy-start | bytes 1564
  0.0 19.6 %copy-start.7 = (s32[258]{0:T(512)S(1)}, s32[258]{0:T(512)}, u32[]{:S(2)}) copy-start(s32[258]{0:T(512)} %constant.288) | copy-start | bytes 3100
  0.0 34.1 %copy-start.12 = (s32[1,32]{1,0:T(1,128)S(1)}, s32[1,32]{1,0:T(1,128)}, u32[]{:S(2)}) copy-start(s32[1,32]{1,0:T(1,128)} %param.21) | copy-start | bytes 388
  0.1 19.4 %copy-start.16 = (f32[26]{0:T(128)S(1)}, f32[26]{0:T(128)}, u32[]{:S(2)}) copy-start(f32[26]{0:T(128)} %param.29) | copy-start | bytes 316
  0.1 20.3 %copy-start.9 = (f32[64]{0:T(128)S(1)}, f32[64]{0:T(128)}, u32[]{:S(2)}) copy-start(f32[64]{0:T(128)} %param.23) | copy-start | bytes 772
  0.1 21.0 %copy-start.10 = (f32[64]{0:T(128)S(1)}, f32[64]{0:T(128)}, u32[]{:S(2)}) copy-start(f32[64]{0:T(128)} %param.25) | copy-start | bytes 772
  0.1 21.7 %copy-start.11 = (f32[64]{0:T(128)S(1)}, f32[64]{0:T(128)}, u32[]{:S(2)}) copy-start(f32[64]{0:T(128)} %param.27) | copy-start | bytes 772
  0.1 22.4 %copy-start.6 = (bf16[64,13,3,3]{0,1,3,2:T(8,128)(2,1)S(1)}, bf16[64,13,3,3]{0,1,3,2:T(8,128)(2,1)}, u32[]{:S(2)}) copy-start(bf16[64,13,3,3]{0,1,3,2:T(8,128)(2,1)} %param.22) | copy-start | bytes 44932
  0.1 23.1 %copy-start.2 = (bf16[26,64,3,3]{1,0,3,2:T(8,128)(2,1)S(1)}, bf16[26,64,3,3]{1,0,3,2:T(8,128)(2,1)}, u32[]{:S(2)}) copy-start(bf16[26,64,3,3]{1,0,3,2:T(8,128)(2,1)} %param.28) | copy-start | bytes 89860
  0.1 23.9 %copy-start = (bf16[64,64,3,3]{1,0,3,2:T(8,128)(2,1)S(1)}, bf16[64,64,3,3]{1,0,3,2:T(8,128)(2,1)}, u32[]{:S(2)}) copy-start(bf16[64,64,3,3]{1,0,3,2:T(8,128)(2,1)} %param.24) | copy-start | bytes 221188
  0.1 24.8 %copy-start.1 = (bf16[64,64,3,3]{1,0,3,2:T(8,128)(2,1)S(1)}, bf16[64,64,3,3]{1,0,3,2:T(8,128)(2,1)}, u32[]{:S(2)}) copy-start(bf16[64,64,3,3]{1,0,3,2:T(8,128)(2,1)} %param.26) | copy-start | bytes 221188
  0.1 26.3 %collective-permute-start = (s32[1,32]{1,0:T(1,128)}, s32[1,32]{1,0:T(1,128)S(1)}, u32[]{:S(2)}, u32[]{:S(2)}) collective-permute-start(s32[1,32]{1,0:T(1,128)} %param.21), channel_id=1, source_target_pairs={{0,16},{16,32},{32,48},{48,64},{64,80},{80,96},{96,112},{1,17},{17... | collective-permute-start | bytes 392 | tf_op jit(solution)/shard_map/ppermute | solution.py:191
  4.4 26.6 %collective-permute-start.1 = (s32[1,32]{1,0:T(1,128)}, s32[1,32]{1,0:T(1,128)S(1)}, u32[]{:S(2)}, u32[]{:S(2)}) collective-permute-start(s32[1,32]{1,0:T(1,128)} %param.21), channel_id=1, source_target_pairs={{16,0},{32,16},{48,32},{64,48},{80,64},{96,80},{112,96},{17,1},{33... | collective-permute-start | bytes 392 | tf_op jit(solution)/shard_map/ppermute | solution.py:193
  8.6 27.2 %collective-permute-start.2 = (bf16[13,16,16]{2,0,1:T(8,128)(2,1)S(1)}, bf16[13,16,16]{2,0,1:T(8,128)(2,1)S(1)}, u32[]{:S(2)}, u32[]{:S(2)}) collective-permute-start(bf16[13,16,16]{2,0,1:T(8,128)(2,1)S(1)} %get-tuple-element.29), channel_id=1, source_target_pairs={{0,17},{1,18},{2,19},{3,20},{4,21},{5,22},{6,23},{7,24},{8,25},{9,... | collective-permute-start | bytes 19976 | tf_op jit(solution)/shard_map/ppermute | solution.py:113
  13.2 24.5 %collective-permute-start.9 = (bf16[13,16,16]{2,0,1:T(8,128)(2,1)S(1)}, bf16[13,16,16]{2,0,1:T(8,128)(2,1)S(1)}, u32[]{:S(2)}, u32[]{:S(2)}) collective-permute-start(bf16[13,16,16]{2,0,1:T(8,128)(2,1)S(1)} %get-tuple-element.30), channel_id=1, source_target_pairs={{17,0},{18,1},{19,2},{20,3},{21,4},{22,5},{23,6},{24,7},{25,8},{26... | collective-permute-start | bytes 19976 | tf_op jit(solution)/shard_map/ppermute | solution.py:113
  15.1 30.2 %collective-permute-start.7 = (bf16[13,16,16]{2,0,1:T(8,128)(2,1)S(1)}, bf16[13,16,16]{2,0,1:T(8,128)(2,1)S(1)}, u32[]{:S(2)}, u32[]{:S(2)}) collective-permute-start(bf16[13,16,16]{2,0,1:T(8,128)(2,1)S(1)} %get-tuple-element.31), channel_id=1, source_target_pairs={{16,1},{17,2},{18,3},{19,4},{20,5},{21,6},{22,7},{23,8},{24,9},{25... | collective-permute-start | bytes 19976 | tf_op jit(solution)/shard_map/ppermute | solution.py:113
  26.5 24.8 %collective-permute-start.4 = (bf16[13,16,16]{2,0,1:T(8,128)(2,1)}, bf16[13,16,16]{2,0,1:T(8,128)(2,1)}, u32[]{:S(2)}, u32[]{:S(2)}) collective-permute-start(bf16[13,16,16]{2,0,1:T(8,128)(2,1)} %get-tuple-element.32), channel_id=1, source_target_pairs={{1,16},{2,17},{3,18},{4,19},{5,20},{6,21},{7,22},{8,23},{9,24},{10... | collective-permute-start | bytes 19976 | tf_op jit(solution)/shard_map/ppermute | solution.py:113
  31.0 31.4 %collective-permute-start.3 = (bf16[13,16,256]{2,0,1:T(8,128)(2,1)}, bf16[13,16,256]{2,0,1:T(8,128)(2,1)S(1)}, u32[]{:S(2)}, u32[]{:S(2)}) collective-permute-start(bf16[13,16,256]{2,0,1:T(8,128)(2,1)} %get-tuple-element.33), channel_id=1, source_target_pairs={{0,16},{16,32},{32,48},{48,64},{64,80},{80,96},{96,112},{1,17},{17... | collective-permute-start | bytes 319496 | tf_op jit(solution)/shard_map/ppermute | solution.py:113
  35.8 1.9 %copy-start.3 = (bf16[13,16,16]{2,0,1:T(8,128)(2,1)}, bf16[13,16,16]{2,0,1:T(8,128)(2,1)S(1)}, u32[]{:S(2)}) copy-start(bf16[13,16,16]{2,0,1:T(8,128)(2,1)S(1)} %collective-permute-done.2) | copy-start | bytes 19972
  35.8 26.7 %collective-permute-start.8 = (bf16[13,16,256]{2,0,1:T(8,128)(2,1)}, bf16[13,16,256]{2,0,1:T(8,128)(2,1)S(1)}, u32[]{:S(2)}, u32[]{:S(2)}) collective-permute-start(bf16[13,16,256]{2,0,1:T(8,128)(2,1)} %get-tuple-element.34), channel_id=1, source_target_pairs={{16,0},{32,16},{48,32},{64,48},{80,64},{96,80},{112,96},{17,1},{33... | collective-permute-start | bytes 319496 | tf_op jit(solution)/shard_map/ppermute | solution.py:113
  37.7 0.6 copy-start.4
  38.4 17.3 %collective-permute-start.5 = (bf16[13,128,16]{2,0,1:T(8,128)(2,1)S(1)}, bf16[13,128,16]{2,0,1:T(8,128)(2,1)S(1)}, u32[]{:S(2)}, u32[]{:S(2)}) collective-permute-start(bf16[13,128,16]{2,0,1:T(8,128)(2,1)S(1)} %get-tuple-element.35), channel_id=1, source_target_pairs={{0,1},{1,2},{2,3},{3,4},{4,5},{5,6},{6,7},{7,8},{8,9},{9,10},{10,1... | collective-permute-start | bytes 159752 | tf_op jit(solution)/shard_map/ppermute | solution.py:113
  45.3 0.6 copy-start.5
  45.9 16.5 %collective-permute-start.6 = (bf16[13,128,16]{2,0,1:T(8,128)(2,1)S(1)}, bf16[13,128,16]{2,0,1:T(8,128)(2,1)S(1)}, u32[]{:S(2)}, u32[]{:S(2)}) collective-permute-start(bf16[13,128,16]{2,0,1:T(8,128)(2,1)S(1)} %get-tuple-element.36), channel_id=1, source_target_pairs={{1,0},{2,1},{3,2},{4,3},{5,4},{6,5},{7,6},{8,7},{9,8},{10,9},{11,1... | collective-permute-start | bytes 159752 | tf_op jit(solution)/shard_map/ppermute | solution.py:113

commit v6 on v3

--- a/solution.py
+++ b/solution.py
@@ -127,7 +127,7 @@
     row_count = lax.axis_size("row")
     my_row = lax.axis_index("row")
     my_col = lax.axis_index("col")
-    margin = sum(dilations)
+    margin = sum(dilations) + 1
     per_row = block_h // TILE
     per_col = block_w // TILE
     per_block = per_row * per_col
@@ -157,18 +157,40 @@
             jnp.minimum(out_w, grid_w + left),
         ]
     lims = jnp.stack(lims).astype(jnp.int32)
-    flux = run_net(x, lims, layers, block_w, 32)[:, : 2 * moments].transpose(1, 0, 2)
-    listed = tile_ids[0]
-    mine = (listed // per_block) == my_col
-    local_ids = listed % per_block
-    chosen = jnp.any(
-        mine[None, :] & (local_ids[None, :] == jnp.arange(per_block, dtype=jnp.int32)[:, None]), axis=1
-    )
-    cell_mask = jnp.broadcast_to(
-        chosen.reshape(per_row, 1, per_col, 1), (per_row, TILE, per_col, TILE)
-    ).reshape(block_h, block_w)
-    flux_field = jnp.where(cell_mask[None], flux, jnp.zeros((), jnp.bfloat16))
-    rimmed = with_halo(flux_field, (("row", 1), ("col", 2)), 1)
+    flux = run_net(x, lims, layers, LANES, 32)[:, : 2 * moments, : block_w + 2].transpose(1, 0, 2)
+
+    near_ids = jnp.concatenate(
+        [
+            lax.ppermute(tile_ids, "row", [(i, i + 1) for i in range(row_count - 1)]),
+            tile_ids,
+            lax.ppermute(tile_ids, "row", [(i + 1, i) for i in range(row_count - 1)]),
+        ],
+        axis=0,
+    )
+    listed = jnp.any(
+        near_ids[:, :, None] == jnp.arange(col_count * per_block, dtype=jnp.int32)[None, None, :], axis=1
+    )
+    strip = jnp.array([-1] + [0] * per_row + [1], jnp.int32)
+    tile_row = jnp.array([per_row - 1] + list(range(per_row)) + [0], jnp.int32)
+    block = jnp.array([-1] + [0] * per_col + [1], jnp.int32) + my_col
+    tile_col = jnp.array([per_col - 1] + list(range(per_col)) + [0], jnp.int32)
+    ids = (
+        jnp.clip(block, 0, col_count - 1)[None, :] * per_block
+        + tile_row[:, None] * per_col
+        + tile_col[None, :]
+    )
+    piece = listed[(strip + 1)[:, None], ids]
+    strip = strip + my_row
+    piece = piece & ((strip >= 0) & (strip < row_count))[:, None] & ((block >= 0) & (block < col_count))[None, :]
+    row_sizes = [1] + [TILE] * per_row + [1]
+    col_sizes = [1] + [TILE] * per_col + [1]
+    cell_mask = jnp.repeat(
+        jnp.repeat(piece, jnp.array(row_sizes), axis=0, total_repeat_length=block_h + 2),
+        jnp.array(col_sizes),
+        axis=1,
+        total_repeat_length=block_w + 2,
+    )
+    rimmed = jnp.where(cell_mask[None], flux, jnp.zeros((), jnp.bfloat16))
     across = rimmed[:moments, 1:-1, :].astype(jnp.float32)
     downward = rimmed[moments:, :, 1:-1].astype(jnp.float32)
     difference = across[:, :, 2:] - across[:, :, :-2] + (downward[:, 2:, :] - downward[:, :-2, :])

time: 172 us -> 160 us (0.930)
  the two profiles are of different devices: /device:TPU:7 before, /device:TPU:56 now
where the time goes in v6:
time: 160 us; the launch traced here: 159 us
  Pallas kernels  106 us (66%)
  local copies, waits for them, and re-layouts  22.4 us (14%)
  starting transfers between devices  18 us (11%)
  other arithmetic  8.42 us (5%)
  waiting for transfers between devices  4.2 us (3%)
    pallas_call x1, Pallas kernels, run_net(): pl.pallas_call(_net_kernel, out_shape=jax.ShapeDtypeStruct((h0 - 30, out_...  106 us
    ppermute x2, starting transfers between devices, with_halo(): lax.ppermute(head, axis, [((i + 1) % count, i) for i in range(ends)])  8.19 us
    ppermute x2, waiting for transfers between devices, with_halo(): lax.ppermute(tail, axis, [(i, (i + 1) % count) for i in range(ends)])  4.19 us
    ppermute x2, starting transfers between devices, with_halo(): lax.ppermute(tail, axis, [(i, (i + 1) % count) for i in range(ends)])  4.13 us
    ppermute x1, starting transfers between devices, body(): lax.ppermute(tile_ids, 'row', [(i + 1, i) for i in range(row_count - 1)])  3.64 us
  transfers between devices with their start and end apart: 6, of which 1 were waited for; matrix products, arithmetic and copies ran while one was open for 13% of the time, Pallas kernels for 0%

profile of v6, /device:TPU:56, one launch (start us, length us, event | category | flops | bytes accessed | tf_op | source)
XLA Modules:
  0.0 159.3 jit_solution(14220331842692040044)
XLA Ops:
  0.0 0.0 copy-start.2
  0.0 0.0 copy-start.3
  0.0 0.0 copy-start
  0.0 0.0 copy-start.1
  0.0 2.1 %collective-permute-start = (s32[1,32]{1,0:T(1,128)}, s32[1,32]{1,0:T(1,128)S(1)}, u32[]{:S(2)}, u32[]{:S(2)}) collective-permute-start(s32[1,32]{1,0:T(1,128)} %param.21), channel_id=1, source_target_pairs={{0,16},{16,32},{32,48},{48,64},{64,80},{80,96},{96,112},{1,17},{17... | collective-permute-start | bytes 392 | tf_op jit(solution)/shard_map/ppermute | solution.py:164
  2.1 3.6 %collective-permute-start.1 = (s32[1,32]{1,0:T(1,128)}, s32[1,32]{1,0:T(1,128)S(1)}, u32[]{:S(2)}, u32[]{:S(2)}) collective-permute-start(s32[1,32]{1,0:T(1,128)} %param.21), channel_id=1, source_target_pairs={{16,0},{32,16},{48,32},{64,48},{80,64},{96,80},{112,96},{17,1},{33... | collective-permute-start | bytes 392 | tf_op jit(solution)/shard_map/ppermute | solution.py:166
  5.7 1.0 fusion.10
  6.8 2.2 %collective-permute-start.2 = (bf16[13,16,256]{2,0,1:T(8,128)(2,1)S(1)}, bf16[13,16,256]{2,0,1:T(8,128)(2,1)S(1)}, u32[]{:S(2)}, u32[]{:S(2)}) collective-permute-start(bf16[13,16,256]{2,0,1:T(8,128)(2,1)S(1)} %copy.88), channel_id=1, source_target_pairs={{0,16},{16,32},{32,48},{48,64},{64,80},{80,96},{96,112},{1,17},{17... | collective-permute-start | bytes 319496 | tf_op jit(solution)/shard_map/ppermute | solution.py:104
  9.0 3.4 %collective-permute-start.3 = (bf16[13,16,256]{2,0,1:T(8,128)(2,1)S(1)}, bf16[13,16,256]{2,0,1:T(8,128)(2,1)S(1)}, u32[]{:S(2)}, u32[]{:S(2)}) collective-permute-start(bf16[13,16,256]{2,0,1:T(8,128)(2,1)S(1)} %copy.89), channel_id=1, source_target_pairs={{16,0},{32,16},{48,32},{64,48},{80,64},{96,80},{112,96},{17,1},{33... | collective-permute-start | bytes 319496 | tf_op jit(solution)/shard_map/ppermute | solution.py:106
  12.4 0.7 compare_and_fusion
  13.1 0.7 fusion.8
  13.7 0.7 compare_and_fusion.1
  14.4 0.7 pad_bitcast_fusion.1
  15.0 0.8 fusion.7
  15.8 0.1 reshape.264
  15.9 0.7 copy.85.bfl
  16.6 1.4 copy.80.b1
  17.9 1.4 copy.82.b2
  19.3 1.4 copy.84.b3
  20.7 0.8 pad.29
  21.4 0.7 copy.79.k1
  22.1 0.9 pad_bitcast_fusion
  23.0 0.1 copy.78
  23.1 0.7 reshape.262.kf
  23.8 1.0 copy.76
  24.9 0.8 copy.81.k2
  25.7 0.0 copy-done.1
  25.7 0.1 copy.77
  25.8 0.8 copy.83.k3
  26.6 0.0 copy-done.2
  26.6 0.0 copy-done.3
  26.6 0.7 stack.67.lim_ref
  27.3 0.0 collective-permute-done
  27.3 0.0 collective-permute-done.1
  27.3 0.0 copy-done.4
  27.3 0.1 fusion.4
  27.4 0.8 gather_fusion
  28.3 0.1 reshape.267
  28.3 0.0 collective-permute-done.2
  28.4 0.0 copy-done
  28.4 0.5 constant_dynamic-update-slice_fusion.1
  28.9 0.0 collective-permute-done.3
  28.9 0.3 fusion.9
  29.2 0.5 copy.72
  29.7 0.5 copy.73
  30.2 4.8 %collective-permute-start.5 = (bf16[13,160,16]{1,2,0:T(8,128)(2,1)S(1)}, bf16[13,160,16]{1,2,0:T(8,128)(2,1)S(1)}, u32[]{:S(2)}, u32[]{:S(2)}) collective-permute-start(bf16[13,160,16]{1,2,0:T(8,128)(2,1)S(1)} %copy.73), channel_id=1, source_target_pairs={{1,0},{2,1},{3,2},{4,3},{5,4},{6,5},{7,6},{8,7},{9,8},{10,9},{11,1... | collective-permute-start | bytes 199688 | tf_op jit(solution)/shard_map/ppermute | solution.py:106
  35.1 1.9 %collective-permute-start.4 = (bf16[13,160,16]{1,2,0:T(8,128)(2,1)S(1)}, bf16[13,160,16]{1,2,0:T(8,128)(2,1)S(1)}, u32[]{:S(2)}, u32[]{:S(2)}) collective-permute-start(bf16[13,160,16]{1,2,0:T(8,128)(2,1)S(1)} %copy.72), channel_id=1, source_target_pairs={{0,1},{1,2},{2,3},{3,4},{4,5},{5,6},{6,7},{7,8},{8,9},{9,10},{10,1... | collective-permute-start | bytes 199688 | tf_op jit(solution)/shard_map/ppermute | solution.py:104
  37.0 0.1 and_and_fusion
  37.1 0.7 gather_fusion.1
  37.8 0.1 copy.67
  37.8 1.7 %gather_fusion.2 = pred[258,130]{1,0:T(8,128)(4,1)S(1)} fusion(pred[130,6]{0,1:T(8,128)(4,1)S(1)} %copy.67, s32[1024]{0:T(1024)S(1)} %get-tuple-element.33), kind=kCustom, calls=%fused_computation.2 | custom fusion | bytes 68112 | tf_op jit(solution)/shard_map/jit(_take)/gather | solution.py:187
  39.6 0.2 copy.68
  39.8 4.2 %collective-permute-done.4 = bf16[13,160,16]{1,2,0:T(8,128)(2,1)S(1)} collective-permute-done((bf16[13,160,16]{1,2,0:T(8,128)(2,1)S(1)}, bf16[13,160,16]{1,2,0:T(8,128)(2,1)S(1)}, u32[]{:S(2)}, u32[]{:S(2)}) %collective-permute-start.4) | collective-permute-done | bytes 66592 | tf_op jit(solution)/shard_map/ppermute | solution.py:104
  44.0 0.5 copy.74
  44.5 0.0 collective-permute-done.5
  44.5 0.5 copy.75
  45.0 1.2 maximum_bitcast_fusion
  46.3 1.6 pad.28.x_ref
  47.8 106.0 %shard_map.154 = bf16[130,32,384]{2,1,0:T(8,128)(2,1)} custom-call(s32[16]{0:T(128)} %stack.67.lim_ref, bf16[160,16,384]{2,1,0:T(8,128)(2,1)} %pad.28.x_ref, bf16[64,144]{1,0:T(8,128)(2,1)} %copy.79.k1, f32[64,1]{1,0:T(8,128)} %copy.80.b1, bf16[64,576]{1,0:T(8,128)(2,1)} %copy.81.k2, f32[64,1]{1,0:T(8,128)} %copy.82.b2, bf16[64,576]{1,0:T(8,128)(2,1)} %copy.83.k3, ...), custom_call_target="tpu_custom_call" | custom-call | tf_op jit(solution)/shard_map/pallas_call | solution.py:83
  153.9 2.4 %fusion = bf16[26,130,258]{2,0,1:T(8,128)(2,1)S(1)} fusion(bf16[130,32,384]{2,1,0:T(8,128)(2,1)} %shard_map.154, pred[130,258]{1,0:T(8,128)(4,1)S(1)} %copy.68), kind=kLoop, calls=%fused_computation.4 | loop fusion | flops 872040 | bytes 3521700 | tf_op jit(solution)/shard_map/jit(_where)/select_n | solution.py:193
  156.3 0.9 slice_convert_fusion.1
  157.3 0.2 slice_convert_fusion
  157.5 0.7 fusion.3
  158.2 1.2 copy.86
  (7 shorter events, 0.1 us)
Async XLA Ops:
  0.0 26.6 %copy-start.2 = (s32[258]{0:T(512)S(1)}, s32[258]{0:T(512)}, u32[]{:S(2)}) copy-start(s32[258]{0:T(512)} %constant.288) | copy-start | bytes 3100
  0.0 26.6 %copy-start.3 = (s32[130]{0:T(256)S(1)}, s32[130]{0:T(256)}, u32[]{:S(2)}) copy-start(s32[130]{0:T(256)} %constant.287) | copy-start | bytes 1564
  0.0 27.3 %copy-start.4 = (s32[1,32]{1,0:T(1,128)S(1)}, s32[1,32]{1,0:T(1,128)}, u32[]{:S(2)}) copy-start(s32[1,32]{1,0:T(1,128)} %param.21) | copy-start | bytes 388
  0.0 28.4 %copy-start = (bf16[13,128,256]{2,1,0:T(8,128)(2,1)S(1)}, bf16[13,128,256]{2,1,0:T(8,128)(2,1)}, u32[]{:S(2)}) copy-start(bf16[13,128,256]{2,1,0:T(8,128)(2,1)} %param.20) | copy-start | bytes 2555908
  0.0 25.6 %copy-start.1 = (bf16[64,64,3,3]{1,0,3,2:T(8,128)(2,1)S(1)}, bf16[64,64,3,3]{1,0,3,2:T(8,128)(2,1)}, u32[]{:S(2)}) copy-start(bf16[64,64,3,3]{1,0,3,2:T(8,128)(2,1)} %param.26) | copy-start | bytes 221188
  0.0 27.3 %collective-permute-start = (s32[1,32]{1,0:T(1,128)}, s32[1,32]{1,0:T(1,128)S(1)}, u32[]{:S(2)}, u32[]{:S(2)}) collective-permute-start(s32[1,32]{1,0:T(1,128)} %param.21), channel_id=1, source_target_pairs={{0,16},{16,32},{32,48},{48,64},{64,80},{80,96},{96,112},{1,17},{17... | collective-permute-start | bytes 392 | tf_op jit(solution)/shard_map/ppermute | solution.py:164
  2.1 25.2 %collective-permute-start.1 = (s32[1,32]{1,0:T(1,128)}, s32[1,32]{1,0:T(1,128)S(1)}, u32[]{:S(2)}, u32[]{:S(2)}) collective-permute-start(s32[1,32]{1,0:T(1,128)} %param.21), channel_id=1, source_target_pairs={{16,0},{32,16},{48,32},{64,48},{80,64},{96,80},{112,96},{17,1},{33... | collective-permute-start | bytes 392 | tf_op jit(solution)/shard_map/ppermute | solution.py:166
  6.8 21.6 %collective-permute-start.2 = (bf16[13,16,256]{2,0,1:T(8,128)(2,1)S(1)}, bf16[13,16,256]{2,0,1:T(8,128)(2,1)S(1)}, u32[]{:S(2)}, u32[]{:S(2)}) collective-permute-start(bf16[13,16,256]{2,0,1:T(8,128)(2,1)S(1)} %copy.88), channel_id=1, source_target_pairs={{0,16},{16,32},{32,48},{48,64},{64,80},{80,96},{96,112},{1,17},{17... | collective-permute-start | bytes 319496 | tf_op jit(solution)/shard_map/ppermute | solution.py:104
  9.0 19.8 %collective-permute-start.3 = (bf16[13,16,256]{2,0,1:T(8,128)(2,1)S(1)}, bf16[13,16,256]{2,0,1:T(8,128)(2,1)S(1)}, u32[]{:S(2)}, u32[]{:S(2)}) collective-permute-start(bf16[13,16,256]{2,0,1:T(8,128)(2,1)S(1)} %copy.89), channel_id=1, source_target_pairs={{16,0},{32,16},{48,32},{64,48},{80,64},{96,80},{112,96},{17,1},{33... | collective-permute-start | bytes 319496 | tf_op jit(solution)/shard_map/ppermute | solution.py:106
  30.2 14.3 %collective-permute-start.5 = (bf16[13,160,16]{1,2,0:T(8,128)(2,1)S(1)}, bf16[13,160,16]{1,2,0:T(8,128)(2,1)S(1)}, u32[]{:S(2)}, u32[]{:S(2)}) collective-permute-start(bf16[13,160,16]{1,2,0:T(8,128)(2,1)S(1)} %copy.73), channel_id=1, source_target_pairs={{1,0},{2,1},{3,2},{4,3},{5,4},{6,5},{7,6},{8,7},{9,8},{10,9},{11,1... | collective-permute-start | bytes 199688 | tf_op jit(solution)/shard_map/ppermute | solution.py:106
  35.1 8.9 %collective-permute-start.4 = (bf16[13,160,16]{1,2,0:T(8,128)(2,1)S(1)}, bf16[13,160,16]{1,2,0:T(8,128)(2,1)S(1)}, u32[]{:S(2)}, u32[]{:S(2)}) collective-permute-start(bf16[13,160,16]{1,2,0:T(8,128)(2,1)S(1)} %copy.72), channel_id=1, source_target_pairs={{0,1},{1,2},{2,3},{3,4},{4,5},{5,6},{6,7},{7,8},{8,9},{9,10},{10,1... | collective-permute-start | bytes 199688 | tf_op jit(solution)/shard_map/ppermute | solution.py:104

commit v7 on v6

--- a/solution.py
+++ b/solution.py
@@ -47,7 +47,7 @@
                 )
             return carry
 
-        lax.fori_loop(0, n_rows, row, 0, unroll=2)
+        lax.fori_loop(0, n_rows, row, 0, unroll=8)
 
     h0 = x_ref.shape[0]
     h1 = h0 - 2
@@ -157,16 +157,17 @@
             jnp.minimum(out_w, grid_w + left),
         ]
     lims = jnp.stack(lims).astype(jnp.int32)
-    flux = run_net(x, lims, layers, LANES, 32)[:, : 2 * moments, : block_w + 2].transpose(1, 0, 2)
-
+
+    x, late_ids = lax.optimization_barrier((x, tile_ids))
     near_ids = jnp.concatenate(
         [
-            lax.ppermute(tile_ids, "row", [(i, i + 1) for i in range(row_count - 1)]),
+            lax.ppermute(late_ids, "row", [(i, i + 1) for i in range(row_count - 1)]),
             tile_ids,
-            lax.ppermute(tile_ids, "row", [(i + 1, i) for i in range(row_count - 1)]),
+            lax.ppermute(late_ids, "row", [(i + 1, i) for i in range(row_count - 1)]),
         ],
         axis=0,
     )
+    flux = run_net(x, lims, layers, LANES, 32)[:, : 2 * moments, : block_w + 2].transpose(1, 0, 2)
     listed = jnp.any(
         near_ids[:, :, None] == jnp.arange(col_count * per_block, dtype=jnp.int32)[None, None, :], axis=1
     )

time: 160 us -> 122 us (0.76)
  the two profiles are of different devices: /device:TPU:56 before, /device:TPU:25 now
where the time goes in v7:
time: 122 us; the launch traced here: 121 us
  Pallas kernels  64.9 us (53%)
  local copies, waits for them, and re-layouts  22.5 us (18%)
  starting transfers between devices  19.9 us (16%)
  other arithmetic  8.41 us (7%)
  waiting for transfers between devices  5.61 us (5%)
    pallas_call x1, Pallas kernels, run_net(): pl.pallas_call(_net_kernel, out_shape=jax.ShapeDtypeStruct((h0 - 30, out_...  64.9 us
    ppermute x2, starting transfers between devices, with_halo(): lax.ppermute(head, axis, [((i + 1) % count, i) for i in range(ends)])  6.48 us
    ppermute x2, starting transfers between devices, with_halo(): lax.ppermute(tail, axis, [(i, (i + 1) % count) for i in range(ends)])  6.03 us
    ppermute x2, waiting for transfers between devices, with_halo(): lax.ppermute(tail, axis, [(i, (i + 1) % count) for i in range(ends)])  5.6 us
    ppermute x1, starting transfers between devices, body(): lax.ppermute(late_ids, 'row', [(i, i + 1) for i in range(row_count - 1)])  5.44 us
    reshape x4, local copies, waits for them, and re-layouts, _kmat(): return k.transpose(0, 2, 3, 1).reshape(o, 9 * cin)  2.97 us
  transfers between devices with their start and end apart: 6, of which 1 were waited for; matrix products, arithmetic and copies ran while one was open for 13% of the time, Pallas kernels for 53%

profile of v7, /device:TPU:25, one launch (start us, length us, event | category | flops | bytes accessed | tf_op | source)
XLA Modules:
  0.0 121.5 jit_solution(8703243872226280806)
XLA Ops:
  0.0 0.0 copy-start.1
  0.0 1.0 fusion.10
  1.1 4.1 %collective-permute-start = (bf16[13,16,256]{2,0,1:T(8,128)(2,1)S(1)}, bf16[13,16,256]{2,0,1:T(8,128)(2,1)S(1)}, u32[]{:S(2)}, u32[]{:S(2)}) collective-permute-start(bf16[13,16,256]{2,0,1:T(8,128)(2,1)S(1)} %copy.88), channel_id=1, source_target_pairs={{0,16},{16,32},{32,48},{48,64},{64,80},{80,96},{96,112},{1,17},{17... | collective-permute-start | bytes 319496 | tf_op jit(solution)/shard_map/ppermute | solution.py:104
  5.3 1.9 %collective-permute-start.1 = (bf16[13,16,256]{2,0,1:T(8,128)(2,1)S(1)}, bf16[13,16,256]{2,0,1:T(8,128)(2,1)S(1)}, u32[]{:S(2)}, u32[]{:S(2)}) collective-permute-start(bf16[13,16,256]{2,0,1:T(8,128)(2,1)S(1)} %copy.89), channel_id=1, source_target_pairs={{16,0},{32,16},{48,32},{64,48},{80,64},{96,80},{112,96},{17,1},{33... | collective-permute-start | bytes 319496 | tf_op jit(solution)/shard_map/ppermute | solution.py:106
  7.2 0.7 compare_and_fusion
  7.9 0.7 fusion.8
  8.5 0.7 compare_and_fusion.1
  9.2 0.7 pad_bitcast_fusion.1
  9.8 0.8 fusion.7
  10.6 0.1 reshape.264
  10.7 0.7 copy.85.bfl
  11.4 1.4 %copy.80.b1 = f32[64,1]{1,0:T(8,128)} copy(f32[64,1]{0,1:T(1,128)} %bitcast.43) | data formatting | bytes 512 | tf_op jit(solution)/shard_map/reshape | solution.py:77
  12.7 1.4 %copy.82.b2 = f32[64,1]{1,0:T(8,128)} copy(f32[64,1]{0,1:T(1,128)} %bitcast.44) | data formatting | bytes 512 | tf_op jit(solution)/shard_map/reshape | solution.py:78
  14.1 1.4 %copy.84.b3 = f32[64,1]{1,0:T(8,128)} copy(f32[64,1]{0,1:T(1,128)} %bitcast.45) | data formatting | bytes 512 | tf_op jit(solution)/shard_map/reshape | solution.py:79
  15.5 0.8 pad.29
  16.2 0.7 copy.79.k1
  17.0 0.9 pad_bitcast_fusion
  17.9 0.1 copy.78
  17.9 0.7 reshape.262.kf
  18.6 1.0 copy.76
  19.7 0.8 copy.81.k2
  20.5 0.0 copy-done.1
  20.5 0.1 copy.77
  20.6 0.8 copy.83.k3
  21.4 0.7 stack.67.lim_ref
  22.1 0.0 collective-permute-done
  22.1 0.0 copy-done
  22.1 0.5 constant_dynamic-update-slice_fusion.1
  22.6 0.0 collective-permute-done.1
  22.6 0.0 copy-start.2
  22.6 0.0 copy-start.3
  22.6 0.3 fusion.9
  23.0 0.5 copy.70
  23.4 0.5 copy.71
  23.9 4.6 %collective-permute-start.3 = (bf16[13,160,16]{1,2,0:T(8,128)(2,1)S(1)}, bf16[13,160,16]{1,2,0:T(8,128)(2,1)S(1)}, u32[]{:S(2)}, u32[]{:S(2)}) collective-permute-start(bf16[13,160,16]{1,2,0:T(8,128)(2,1)S(1)} %copy.71), channel_id=1, source_target_pairs={{1,0},{2,1},{3,2},{4,3},{5,4},{6,5},{7,6},{8,7},{9,8},{10,9},{11,1... | collective-permute-start | bytes 199688 | tf_op jit(solution)/shard_map/ppermute | solution.py:106
  28.5 1.9 %collective-permute-start.2 = (bf16[13,160,16]{1,2,0:T(8,128)(2,1)S(1)}, bf16[13,160,16]{1,2,0:T(8,128)(2,1)S(1)}, u32[]{:S(2)}, u32[]{:S(2)}) collective-permute-start(bf16[13,160,16]{1,2,0:T(8,128)(2,1)S(1)} %copy.70), channel_id=1, source_target_pairs={{0,1},{1,2},{2,3},{3,4},{4,5},{5,6},{6,7},{7,8},{8,9},{9,10},{10,1... | collective-permute-start | bytes 199688 | tf_op jit(solution)/shard_map/ppermute | solution.py:104
  30.4 0.0 copy-done.2
  30.5 0.0 copy-done.3
  30.5 5.6 %collective-permute-done.2 = bf16[13,160,16]{1,2,0:T(8,128)(2,1)S(1)} collective-permute-done((bf16[13,160,16]{1,2,0:T(8,128)(2,1)S(1)}, bf16[13,160,16]{1,2,0:T(8,128)(2,1)S(1)}, u32[]{:S(2)}, u32[]{:S(2)}) %collective-permute-start.2) | collective-permute-done | bytes 66592 | tf_op jit(solution)/shard_map/ppermute | solution.py:104
  36.1 0.5 copy.72
  36.6 0.0 collective-permute-done.3
  36.6 0.5 copy.73
  37.1 1.2 maximum_bitcast_fusion
  38.4 0.0 copy-start.4
  38.4 1.6 %pad.28.x_ref = bf16[160,16,384]{2,1,0:T(8,128)(2,1)} pad(bf16[160,13,288]{2,1,0:T(8,128)(2,1)S(1)} %maximum_bitcast_fusion, bf16[]{:T(256)} %constant.160.clone.1), padding=0_0x0_3x0_96 | pad | bytes 3164162 | tf_op jit(solution)/shard_map/jit(_pad)/pad | solution.py:144
  40.0 0.0 copy-done.4
  40.0 1.9 %collective-permute-start.5 = (s32[1,32]{1,0:T(1,128)S(1)}, s32[1,32]{1,0:T(1,128)S(1)}, u32[]{:S(2)}, u32[]{:S(2)}) collective-permute-start(s32[1,32]{1,0:T(1,128)S(1)} %copy-done.4), channel_id=1, source_target_pairs={{16,0},{32,16},{48,32},{64,48},{80,64},{96,80},{112,96},{17,1},{33... | collective-permute-start | bytes 392 | tf_op jit(solution)/shard_map/ppermute | solution.py:166
  41.9 5.4 %collective-permute-start.4 = (s32[1,32]{1,0:T(1,128)S(1)}, s32[1,32]{1,0:T(1,128)S(1)}, u32[]{:S(2)}, u32[]{:S(2)}) collective-permute-start(s32[1,32]{1,0:T(1,128)S(1)} %copy-done.4), channel_id=1, source_target_pairs={{0,16},{16,32},{32,48},{48,64},{64,80},{80,96},{96,112},{1,17},{17... | collective-permute-start | bytes 392 | tf_op jit(solution)/shard_map/ppermute | solution.py:164
  47.3 64.9 %shard_map.154 = bf16[130,32,384]{2,1,0:T(8,128)(2,1)} custom-call(s32[16]{0:T(128)} %stack.67.lim_ref, bf16[160,16,384]{2,1,0:T(8,128)(2,1)} %pad.28.x_ref, bf16[64,144]{1,0:T(8,128)(2,1)} %copy.79.k1, f32[64,1]{1,0:T(8,128)} %copy.80.b1, bf16[64,576]{1,0:T(8,128)(2,1)} %copy.81.k2, f32[64,1]{1,0:T(8,128)} %copy.82.b2, bf16[64,576]{1,0:T(8,128)(2,1)} %copy.83.k3, ...), custom_call_target="tpu_custom_call" | custom-call | tf_op jit(solution)/shard_map/pallas_call | solution.py:83
  112.2 0.0 collective-permute-done.5
  112.2 0.0 collective-permute-done.4
  112.2 0.1 fusion.4
  112.3 0.8 gather_fusion
  113.1 0.1 reshape.267
  113.2 0.1 and_and_fusion
  113.3 0.7 gather_fusion.1
  114.0 0.1 copy.74
  114.1 1.7 %gather_fusion.2 = pred[258,130]{1,0:T(8,128)(4,1)S(1)} fusion(pred[130,6]{0,1:T(8,128)(4,1)S(1)} %copy.74, s32[1024]{0:T(1024)S(1)} %get-tuple-element.37), kind=kCustom, calls=%fused_computation.2 | custom fusion | bytes 68112 | tf_op jit(solution)/shard_map/jit(_take)/gather | solution.py:188
  115.9 0.2 copy.75
  116.0 2.4 %fusion = bf16[26,130,258]{2,0,1:T(8,128)(2,1)S(1)} fusion(bf16[130,32,384]{2,1,0:T(8,128)(2,1)} %shard_map.154, pred[130,258]{1,0:T(8,128)(4,1)S(1)} %copy.75), kind=kLoop, calls=%fused_computation.4 | loop fusion | flops 872040 | bytes 3521700 | tf_op jit(solution)/shard_map/jit(_where)/select_n | solution.py:194
  118.5 0.9 slice_convert_fusion.1
  119.4 0.2 slice_convert_fusion
  119.6 0.7 fusion.3
  120.3 1.2 copy.86
  (7 shorter events, 0.1 us)
Async XLA Ops:
  0.0 22.1 %copy-start = (bf16[13,128,256]{2,1,0:T(8,128)(2,1)S(1)}, bf16[13,128,256]{2,1,0:T(8,128)(2,1)}, u32[]{:S(2)}) copy-start(bf16[13,128,256]{2,1,0:T(8,128)(2,1)} %param.20) | copy-start | bytes 2555908
  0.0 20.5 %copy-start.1 = (bf16[64,64,3,3]{1,0,3,2:T(8,128)(2,1)S(1)}, bf16[64,64,3,3]{1,0,3,2:T(8,128)(2,1)}, u32[]{:S(2)}) copy-start(bf16[64,64,3,3]{1,0,3,2:T(8,128)(2,1)} %param.26) | copy-start | bytes 221188
  1.1 21.0 %collective-permute-start = (bf16[13,16,256]{2,0,1:T(8,128)(2,1)S(1)}, bf16[13,16,256]{2,0,1:T(8,128)(2,1)S(1)}, u32[]{:S(2)}, u32[]{:S(2)}) collective-permute-start(bf16[13,16,256]{2,0,1:T(8,128)(2,1)S(1)} %copy.88), channel_id=1, source_target_pairs={{0,16},{16,32},{32,48},{48,64},{64,80},{80,96},{96,112},{1,17},{17... | collective-permute-start | bytes 319496 | tf_op jit(solution)/shard_map/ppermute | solution.py:104
  5.3 17.3 %collective-permute-start.1 = (bf16[13,16,256]{2,0,1:T(8,128)(2,1)S(1)}, bf16[13,16,256]{2,0,1:T(8,128)(2,1)S(1)}, u32[]{:S(2)}, u32[]{:S(2)}) collective-permute-start(bf16[13,16,256]{2,0,1:T(8,128)(2,1)S(1)} %copy.89), channel_id=1, source_target_pairs={{16,0},{32,16},{48,32},{64,48},{80,64},{96,80},{112,96},{17,1},{33... | collective-permute-start | bytes 319496 | tf_op jit(solution)/shard_map/ppermute | solution.py:106
  22.6 7.8 %copy-start.2 = (s32[258]{0:T(512)S(1)}, s32[258]{0:T(512)}, u32[]{:S(2)}) copy-start(s32[258]{0:T(512)} %constant.288) | copy-start | bytes 3100
  22.6 7.8 %copy-start.3 = (s32[130]{0:T(256)S(1)}, s32[130]{0:T(256)}, u32[]{:S(2)}) copy-start(s32[130]{0:T(256)} %constant.287) | copy-start | bytes 1564
  23.9 12.7 %collective-permute-start.3 = (bf16[13,160,16]{1,2,0:T(8,128)(2,1)S(1)}, bf16[13,160,16]{1,2,0:T(8,128)(2,1)S(1)}, u32[]{:S(2)}, u32[]{:S(2)}) collective-permute-start(bf16[13,160,16]{1,2,0:T(8,128)(2,1)S(1)} %copy.71), channel_id=1, source_target_pairs={{1,0},{2,1},{3,2},{4,3},{5,4},{6,5},{7,6},{8,7},{9,8},{10,9},{11,1... | collective-permute-start | bytes 199688 | tf_op jit(solution)/shard_map/ppermute | solution.py:106
  28.5 7.6 %collective-permute-start.2 = (bf16[13,160,16]{1,2,0:T(8,128)(2,1)S(1)}, bf16[13,160,16]{1,2,0:T(8,128)(2,1)S(1)}, u32[]{:S(2)}, u32[]{:S(2)}) collective-permute-start(bf16[13,160,16]{1,2,0:T(8,128)(2,1)S(1)} %copy.70), channel_id=1, source_target_pairs={{0,1},{1,2},{2,3},{3,4},{4,5},{5,6},{6,7},{7,8},{8,9},{9,10},{10,1... | collective-permute-start | bytes 199688 | tf_op jit(solution)/shard_map/ppermute | solution.py:104
  38.4 1.6 %copy-start.4 = (s32[1,32]{1,0:T(1,128)S(1)}, s32[1,32]{1,0:T(1,128)}, u32[]{:S(2)}) copy-start(s32[1,32]{1,0:T(1,128)} %param.21) | copy-start | bytes 388
  40.0 72.2 %collective-permute-start.5 = (s32[1,32]{1,0:T(1,128)S(1)}, s32[1,32]{1,0:T(1,128)S(1)}, u32[]{:S(2)}, u32[]{:S(2)}) collective-permute-start(s32[1,32]{1,0:T(1,128)S(1)} %copy-done.4), channel_id=1, source_target_pairs={{16,0},{32,16},{48,32},{64,48},{80,64},{96,80},{112,96},{17,1},{33... | collective-permute-start | bytes 392 | tf_op jit(solution)/shard_map/ppermute | solution.py:166
  41.9 70.3 %collective-permute-start.4 = (s32[1,32]{1,0:T(1,128)S(1)}, s32[1,32]{1,0:T(1,128)S(1)}, u32[]{:S(2)}, u32[]{:S(2)}) collective-permute-start(s32[1,32]{1,0:T(1,128)S(1)} %copy-done.4), channel_id=1, source_target_pairs={{0,16},{16,32},{32,48},{48,64},{64,80},{80,96},{96,112},{1,17},{17... | collective-permute-start | bytes 392 | tf_op jit(solution)/shard_map/ppermute | solution.py:164

commit v8 on v3

--- a/solution.py
+++ b/solution.py
@@ -47,7 +47,7 @@
                 )
             return carry
 
-        lax.fori_loop(0, n_rows, row, 0, unroll=2)
+        lax.fori_loop(0, n_rows, row, 0, unroll=8)
 
     h0 = x_ref.shape[0]
     h1 = h0 - 2
@@ -127,7 +127,7 @@
     row_count = lax.axis_size("row")
     my_row = lax.axis_index("row")
     my_col = lax.axis_index("col")
-    margin = sum(dilations)
+    margin = sum(dilations) + 1
     per_row = block_h // TILE
     per_col = block_w // TILE
     per_block = per_row * per_col
@@ -139,9 +139,19 @@
         (kernel_three, bias_three),
         (kernel_flux, bias_flux),
     )
-    extended = with_halo(state, (("row", 1), ("col", 2)), margin)
+    listed = tile_ids[0]
+    mine = (listed // per_block) == my_col
+    local_ids = listed % per_block
+    chosen = jnp.any(
+        mine[None, :] & (local_ids[None, :] == jnp.arange(per_block, dtype=jnp.int32)[:, None]), axis=1
+    )
+    own_mask = jnp.broadcast_to(
+        chosen.reshape(per_row, 1, per_col, 1), (per_row, TILE, per_col, TILE)
+    ).reshape(1, block_h, block_w)
+    marked = jnp.concatenate([state, own_mask.astype(state.dtype)], axis=0)
+    extended = with_halo(marked, (("row", 1), ("col", 2)), margin)
     ext_h, ext_w = extended.shape[1:]
-    x = jnp.pad(extended.transpose(1, 0, 2), ((0, 0), (0, 16 - moments), (0, LANES - ext_w)))
+    x = jnp.pad(extended.transpose(1, 0, 2), ((0, 0), (0, 15 - moments), (0, LANES - ext_w)))
     lims = []
     offset = margin
     out_h, out_w = ext_h, ext_w
@@ -157,18 +167,10 @@
             jnp.minimum(out_w, grid_w + left),
         ]
     lims = jnp.stack(lims).astype(jnp.int32)
-    flux = run_net(x, lims, layers, block_w, 32)[:, : 2 * moments].transpose(1, 0, 2)
-    listed = tile_ids[0]
-    mine = (listed // per_block) == my_col
-    local_ids = listed % per_block
-    chosen = jnp.any(
-        mine[None, :] & (local_ids[None, :] == jnp.arange(per_block, dtype=jnp.int32)[:, None]), axis=1
-    )
-    cell_mask = jnp.broadcast_to(
-        chosen.reshape(per_row, 1, per_col, 1), (per_row, TILE, per_col, TILE)
-    ).reshape(block_h, block_w)
-    flux_field = jnp.where(cell_mask[None], flux, jnp.zeros((), jnp.bfloat16))
-    rimmed = with_halo(flux_field, (("row", 1), ("col", 2)), 1)
+
+    flux = run_net(x, lims, layers, LANES, 32)[:, : 2 * moments, : block_w + 2].transpose(1, 0, 2)
+    cell_mask = extended[moments, margin - 1 : margin + block_h + 1, margin - 1 : margin + block_w + 1] > 0
+    rimmed = jnp.where(cell_mask[None], flux, jnp.zeros((), jnp.bfloat16))
     across = rimmed[:moments, 1:-1, :].astype(jnp.float32)
     downward = rimmed[moments:, :, 1:-1].astype(jnp.float32)
     difference = across[:, :, 2:] - across[:, :, :-2] + (downward[:, 2:, :] - downward[:, :-2, :])

time: 172 us -> 112 us (0.65)
  the two profiles are of different devices: /device:TPU:7 before, /device:TPU:57 now
where the time goes in v8:
time: 112 us; the launch traced here: 111 us
  Pallas kernels  64.8 us (58%)
  other arithmetic  15.3 us (14%)
  local copies, waits for them, and re-layouts  14 us (12%)
  starting transfers between devices  12.5 us (11%)
  waiting for transfers between devices  4.43 us (4%)
    pallas_call x1, Pallas kernels, run_net(): pl.pallas_call(_net_kernel, out_shape=jax.ShapeDtypeStruct((h0 - 30, out_...  64.8 us
    ppermute x2, starting transfers between devices, with_halo(): lax.ppermute(head, axis, [((i + 1) % count, i) for i in range(ends)])  6.48 us
    ppermute x2, starting transfers between devices, with_halo(): lax.ppermute(tail, axis, [(i, (i + 1) % count) for i in range(ends)])  6.03 us
    concatenate x2, other arithmetic, with_halo(): jnp.concatenate([lax.ppermute(tail, axis, [(i, (i + 1) % count) for i in...  4.76 us
    transpose x1, other arithmetic, body(): extended.transpose(1, 0, 2)  4.2 us
    ppermute x2, waiting for transfers between devices, with_halo(): lax.ppermute(tail, axis, [(i, (i + 1) % count) for i in range(ends)])  3.68 us
    reshape x4, local copies, waits for them, and re-layouts, _kmat(): return k.transpose(0, 2, 3, 1).reshape(o, 9 * cin)  2.98 us
    select_n x1, other arithmetic, body(): rimmed = jnp.where(cell_mask[None], flux, jnp.zeros((), jnp.bfloat16))  2.42 us
  transfers between devices with their start and end apart: 4, of which 2 were waited for; matrix products, arithmetic and copies ran while one was open for 7% of the time, Pallas kernels for 0%

profile of v8, /device:TPU:57, one launch (start us, length us, event | category | flops | bytes accessed | tf_op | source)
XLA Modules:
  0.0 111.3 jit_solution(11139512562970447205)
XLA Ops:
  0.0 0.0 copy-start.7
  0.0 0.0 copy-start.4
  0.0 0.0 copy-start.5
  0.0 0.0 copy-start.6
  0.0 0.0 copy-start.3
  0.0 0.7 fusion.6
  0.7 0.7 compare_bitcast_fusion
  1.4 0.1 fusion.5
  1.5 0.1 reshape.50
  1.6 0.1 broadcast_in_dim.23
  1.7 0.1 convert_element_type.42
  1.9 1.6 %copy.51 = bf16[13,128,256]{2,0,1:T(8,128)(2,1)S(1)} copy(bf16[13,128,256]{2,1,0:T(8,128)(2,1)} %param.10) | data formatting | bytes 1703936 | tf_op args[0]
  3.5 0.1 pad_maximum_fusion.3
  3.6 4.1 %collective-permute-start = (bf16[14,16,256]{2,0,1:T(8,128)(2,1)S(1)}, bf16[14,16,256]{2,0,1:T(8,128)(2,1)S(1)}, u32[]{:S(2)}, u32[]{:S(2)}) collective-permute-start(bf16[14,16,256]{2,0,1:T(8,128)(2,1)S(1)} %get-tuple-element.7), channel_id=1, source_target_pairs={{0,16},{16,32},{32,48},{48,64},{64,80},{80,96},{96,112},{1,17},{17... | collective-permute-start | bytes 344072 | tf_op jit(solution)/shard_map/ppermute | solution.py:104
  7.7 1.9 %collective-permute-start.1 = (bf16[14,16,256]{2,0,1:T(8,128)(2,1)S(1)}, bf16[14,16,256]{2,0,1:T(8,128)(2,1)S(1)}, u32[]{:S(2)}, u32[]{:S(2)}) collective-permute-start(bf16[14,16,256]{2,0,1:T(8,128)(2,1)S(1)} %get-tuple-element.8), channel_id=1, source_target_pairs={{16,0},{32,16},{48,32},{64,48},{80,64},{96,80},{112,96},{17,1},{33... | collective-permute-start | bytes 344072 | tf_op jit(solution)/shard_map/ppermute | solution.py:106
  9.7 0.0 copy-done.7
  9.7 0.7 copy.66.bfl
  10.4 0.0 copy-done.4
  10.4 0.7 copy.61.b1
  11.1 0.0 copy-done.5
  11.1 0.7 copy.63.b2
  11.8 0.0 copy-done.6
  11.8 0.7 copy.65.b3
  12.5 0.0 copy-done.3
  12.5 0.7 copy.60.k1
  13.2 0.0 collective-permute-done
  13.2 0.7 collective-permute-done.1
  14.0 0.4 pad_maximum_fusion.1
  14.4 0.0 copy-start.2
  14.4 0.0 copy-start
  14.4 0.0 copy-start.1
  14.4 0.3 fusion.7
  14.7 0.5 copy.53
  15.2 0.5 copy.54
  15.7 4.6 %collective-permute-start.3 = (bf16[14,160,16]{1,2,0:T(8,128)(2,1)S(1)}, bf16[14,160,16]{1,2,0:T(8,128)(2,1)S(1)}, u32[]{:S(2)}, u32[]{:S(2)}) collective-permute-start(bf16[14,160,16]{1,2,0:T(8,128)(2,1)S(1)} %copy.54), channel_id=1, source_target_pairs={{1,0},{2,1},{3,2},{4,3},{5,4},{6,5},{7,6},{8,7},{9,8},{10,9},{11,1... | collective-permute-start | bytes 215048 | tf_op jit(solution)/shard_map/ppermute | solution.py:106
  20.3 1.9 %collective-permute-start.2 = (bf16[14,160,16]{1,2,0:T(8,128)(2,1)S(1)}, bf16[14,160,16]{1,2,0:T(8,128)(2,1)S(1)}, u32[]{:S(2)}, u32[]{:S(2)}) collective-permute-start(bf16[14,160,16]{1,2,0:T(8,128)(2,1)S(1)} %copy.53), channel_id=1, source_target_pairs={{0,1},{1,2},{2,3},{3,4},{4,5},{5,6},{6,7},{7,8},{8,9},{9,10},{10,1... | collective-permute-start | bytes 215048 | tf_op jit(solution)/shard_map/ppermute | solution.py:104
  22.2 0.0 copy-done.2
  22.2 0.1 copy.59
  22.3 0.7 reshape.48.kf
  23.0 0.0 copy-done
  23.0 0.1 copy.57
  23.2 0.8 copy.62.k2
  24.0 0.0 copy-done.1
  24.0 0.1 copy.58
  24.1 0.8 copy.64.k3
  24.9 0.7 stack.67.lim_ref
  25.6 3.7 %collective-permute-done.2 = bf16[14,160,16]{1,2,0:T(8,128)(2,1)S(1)} collective-permute-done((bf16[14,160,16]{1,2,0:T(8,128)(2,1)S(1)}, bf16[14,160,16]{1,2,0:T(8,128)(2,1)S(1)}, u32[]{:S(2)}, u32[]{:S(2)}) %collective-permute-start.2) | collective-permute-done | bytes 71712 | tf_op jit(solution)/shard_map/ppermute | solution.py:104
  29.2 0.5 copy.55
  29.8 0.0 collective-permute-done.3
  29.8 0.5 copy.56
  30.3 4.4 %pad_maximum_fusion = bf16[14,160,288]{2,0,1:T(8,128)(2,1)S(1)} fusion(bf16[14,160,16]{2,0,1:T(8,128)(2,1)S(1)} %copy.56, bf16[14,16,256]{2,0,1:T(8,128)(2,1)S(1)} %collective-permute-done.1, bf16[1,128,256]{2,0,1:T(2,128)(2,1)S(1)} %convert_element_type.42, bf16[13,128,256]{2,0,1:T(8,128)(2,1)S(1)} %copy.51, ...), kind=kLoop, calls=%fused_computation.7 | loop fusion | flops 7741440 | bytes 2580480 | tf_op jit(solution)/shard_map/concatenate | solution.py:102
  34.7 0.5 slice_compare_fusion
  35.2 4.2 %fusion.8 = bf16[160,14,288]{2,1,0:T(8,128)(2,1)S(1)} fusion(bf16[14,160,16]{2,0,1:T(8,128)(2,1)S(1)} %copy.56, bf16[14,16,256]{2,0,1:T(8,128)(2,1)S(1)} %collective-permute-done.1, bf16[1,128,256]{2,0,1:T(2,128)(2,1)S(1)} %convert_element_type.42, bf16[13,128,256]{2,0,1:T(8,128)(2,1)S(1)} %copy.51, bf16[14,16,256]{2,0,1:T(8,128)(2,1)S(1)} %collective-permute-done, ...), kind=kLoop, calls=%fused_computation.28 | loop fusion | flops 7741440 | bytes 2580480 | tf_op jit(solution)/shard_map/transpose | solution.py:154
  39.5 1.6 %pad.16.x_ref = bf16[160,16,384]{2,1,0:T(8,128)(2,1)} pad(bf16[160,14,288]{2,1,0:T(8,128)(2,1)S(1)} %fusion.8, bf16[]{:T(256)} %constant.67.clone.1), padding=0_0x0_2x0_96 | pad | bytes 3256322 | tf_op jit(solution)/shard_map/jit(_pad)/pad | solution.py:154
  41.0 64.8 %shard_map.100 = bf16[130,32,384]{2,1,0:T(8,128)(2,1)} custom-call(s32[16]{0:T(128)} %stack.67.lim_ref, bf16[160,16,384]{2,1,0:T(8,128)(2,1)} %pad.16.x_ref, bf16[64,144]{1,0:T(8,128)(2,1)} %copy.60.k1, f32[64,1]{1,0:T(8,128)} %copy.61.b1, bf16[64,576]{1,0:T(8,128)(2,1)} %copy.62.k2, f32[64,1]{1,0:T(8,128)} %copy.63.b2, bf16[64,576]{1,0:T(8,128)(2,1)} %copy.64.k3, ...), custom_call_target="tpu_custom_call" | custom-call | tf_op jit(solution)/shard_map/pallas_call | solution.py:83
  105.9 2.4 %fusion = bf16[26,130,258]{2,0,1:T(8,128)(2,1)S(1)} fusion(bf16[130,32,384]{2,1,0:T(8,128)(2,1)} %shard_map.100, pred[130,258]{1,0:T(8,128)(4,1)S(1)} %bitcast.43), kind=kLoop, calls=%fused_computation.1 | loop fusion | flops 872040 | bytes 3521700 | tf_op jit(solution)/shard_map/jit(_where)/select_n | solution.py:173
  108.3 0.9 slice_convert_fusion.1
  109.3 0.2 slice_convert_fusion
  109.5 0.7 fusion.3
  110.2 1.2 %copy.67 = bf16[13,128,256]{2,1,0:T(8,128)(2,1)} copy(bf16[13,128,256]{2,0,1:T(8,128)(2,1)S(1)} %fusion.3) | data formatting | bytes 1703936 | tf_op jit(solution)/shard_map/convert_element_type | solution.py:177
  (5 shorter events, 0.1 us)
Async XLA Ops:
  0.0 9.7 %copy-start.7 = (f32[26]{0:T(128)S(1)}, f32[26]{0:T(128)}, u32[]{:S(2)}) copy-start(f32[26]{0:T(128)} %param.19) | copy-start | bytes 316
  0.0 10.4 %copy-start.4 = (f32[64]{0:T(128)S(1)}, f32[64]{0:T(128)}, u32[]{:S(2)}) copy-start(f32[64]{0:T(128)} %param.13) | copy-start | bytes 772
  0.0 11.1 %copy-start.5 = (f32[64]{0:T(128)S(1)}, f32[64]{0:T(128)}, u32[]{:S(2)}) copy-start(f32[64]{0:T(128)} %param.15) | copy-start | bytes 772
  0.0 11.8 %copy-start.6 = (f32[64]{0:T(128)S(1)}, f32[64]{0:T(128)}, u32[]{:S(2)}) copy-start(f32[64]{0:T(128)} %param.17) | copy-start | bytes 772
  0.0 12.5 %copy-start.3 = (bf16[64,13,3,3]{0,1,3,2:T(8,128)(2,1)S(1)}, bf16[64,13,3,3]{0,1,3,2:T(8,128)(2,1)}, u32[]{:S(2)}) copy-start(bf16[64,13,3,3]{0,1,3,2:T(8,128)(2,1)} %param.12) | copy-start | bytes 44932
  3.6 9.7 %collective-permute-start = (bf16[14,16,256]{2,0,1:T(8,128)(2,1)S(1)}, bf16[14,16,256]{2,0,1:T(8,128)(2,1)S(1)}, u32[]{:S(2)}, u32[]{:S(2)}) collective-permute-start(bf16[14,16,256]{2,0,1:T(8,128)(2,1)S(1)} %get-tuple-element.7), channel_id=1, source_target_pairs={{0,16},{16,32},{32,48},{48,64},{64,80},{80,96},{96,112},{1,17},{17... | collective-permute-start | bytes 344072 | tf_op jit(solution)/shard_map/ppermute | solution.py:104
  7.7 6.3 %collective-permute-start.1 = (bf16[14,16,256]{2,0,1:T(8,128)(2,1)S(1)}, bf16[14,16,256]{2,0,1:T(8,128)(2,1)S(1)}, u32[]{:S(2)}, u32[]{:S(2)}) collective-permute-start(bf16[14,16,256]{2,0,1:T(8,128)(2,1)S(1)} %get-tuple-element.8), channel_id=1, source_target_pairs={{16,0},{32,16},{48,32},{64,48},{80,64},{96,80},{112,96},{17,1},{33... | collective-permute-start | bytes 344072 | tf_op jit(solution)/shard_map/ppermute | solution.py:106
  14.4 7.8 %copy-start.2 = (bf16[26,64,3,3]{1,0,3,2:T(8,128)(2,1)S(1)}, bf16[26,64,3,3]{1,0,3,2:T(8,128)(2,1)}, u32[]{:S(2)}) copy-start(bf16[26,64,3,3]{1,0,3,2:T(8,128)(2,1)} %param.18) | copy-start | bytes 89860
  14.4 8.7 %copy-start = (bf16[64,64,3,3]{1,0,3,2:T(8,128)(2,1)S(1)}, bf16[64,64,3,3]{1,0,3,2:T(8,128)(2,1)}, u32[]{:S(2)}) copy-start(bf16[64,64,3,3]{1,0,3,2:T(8,128)(2,1)} %param.14) | copy-start | bytes 221188
  14.4 9.6 %copy-start.1 = (bf16[64,64,3,3]{1,0,3,2:T(8,128)(2,1)S(1)}, bf16[64,64,3,3]{1,0,3,2:T(8,128)(2,1)}, u32[]{:S(2)}) copy-start(bf16[64,64,3,3]{1,0,3,2:T(8,128)(2,1)} %param.16) | copy-start | bytes 221188
  15.7 14.1 %collective-permute-start.3 = (bf16[14,160,16]{1,2,0:T(8,128)(2,1)S(1)}, bf16[14,160,16]{1,2,0:T(8,128)(2,1)S(1)}, u32[]{:S(2)}, u32[]{:S(2)}) collective-permute-start(bf16[14,160,16]{1,2,0:T(8,128)(2,1)S(1)} %copy.54), channel_id=1, source_target_pairs={{1,0},{2,1},{3,2},{4,3},{5,4},{6,5},{7,6},{8,7},{9,8},{10,9},{11,1... | collective-permute-start | bytes 215048 | tf_op jit(solution)/shard_map/ppermute | solution.py:106
  20.3 9.0 %collective-permute-start.2 = (bf16[14,160,16]{1,2,0:T(8,128)(2,1)S(1)}, bf16[14,160,16]{1,2,0:T(8,128)(2,1)S(1)}, u32[]{:S(2)}, u32[]{:S(2)}) collective-permute-start(bf16[14,160,16]{1,2,0:T(8,128)(2,1)S(1)} %copy.53), channel_id=1, source_target_pairs={{0,1},{1,2},{2,3},{3,4},{4,5},{5,6},{6,7},{7,8},{8,9},{9,10},{10,1... | collective-permute-start | bytes 215048 | tf_op jit(solution)/shard_map/ppermute | solution.py:104

commit v9 on v8

--- a/solution.py
+++ b/solution.py
@@ -148,10 +148,21 @@
     own_mask = jnp.broadcast_to(
         chosen.reshape(per_row, 1, per_col, 1), (per_row, TILE, per_col, TILE)
     ).reshape(1, block_h, block_w)
-    marked = jnp.concatenate([state, own_mask.astype(state.dtype)], axis=0)
-    extended = with_halo(marked, (("row", 1), ("col", 2)), margin)
-    ext_h, ext_w = extended.shape[1:]
-    x = jnp.pad(extended.transpose(1, 0, 2), ((0, 0), (0, 15 - moments), (0, LANES - ext_w)))
+    spare = jnp.zeros((16 - moments - 1, block_h, block_w), state.dtype)
+    marked = jnp.concatenate([state, own_mask.astype(state.dtype), spare], axis=0).transpose(1, 0, 2)
+    rows_done = with_halo(marked, (("row", 0),), margin)
+    ext_h = rows_done.shape[0]
+    ext_w = block_w + 2 * margin
+    ends = col_count - 1
+    x = jnp.concatenate(
+        [
+            lax.ppermute(rows_done[:, :, -margin:], "col", [(i, i + 1) for i in range(ends)]),
+            rows_done,
+            lax.ppermute(rows_done[:, :, :margin], "col", [(i + 1, i) for i in range(ends)]),
+            jnp.zeros((ext_h, 16, LANES - ext_w), state.dtype),
+        ],
+        axis=2,
+    )
     lims = []
     offset = margin
     out_h, out_w = ext_h, ext_w
@@ -169,7 +180,7 @@
     lims = jnp.stack(lims).astype(jnp.int32)
 
     flux = run_net(x, lims, layers, LANES, 32)[:, : 2 * moments, : block_w + 2].transpose(1, 0, 2)
-    cell_mask = extended[moments, margin - 1 : margin + block_h + 1, margin - 1 : margin + block_w + 1] > 0
+    cell_mask = x[margin - 1 : margin + block_h + 1, moments, margin - 1 : margin + block_w + 1] > 0
     rimmed = jnp.where(cell_mask[None], flux, jnp.zeros((), jnp.bfloat16))
     across = rimmed[:moments, 1:-1, :].astype(jnp.float32)
     downward = rimmed[moments:, :, 1:-1].astype(jnp.float32)

time: 112 us -> 106 us (0.946)
  the two profiles are of different devices: /device:TPU:57 before, /device:TPU:56 now
where the time goes in v9:
time: 106 us; the launch traced here: 105 us
  Pallas kernels  64.9 us (61%)
  local copies, waits for them, and re-layouts  12.7 us (12%)
  starting transfers between devices  12.5 us (12%)
  other arithmetic  10.4 us (10%)
  waiting for transfers between devices  4.64 us (4%)
    pallas_call x1, Pallas kernels, run_net(): pl.pallas_call(_net_kernel, out_shape=jax.ShapeDtypeStruct((h0 - 30, out_...  64.9 us
    ppermute x1, starting transfers between devices, body(): lax.ppermute(rows_done[:, :, :margin], 'col', [(i + 1, i) for i in range(...  4.84 us
    ppermute x1, waiting for transfers between devices, body(): lax.ppermute(rows_done[:, :, -margin:], 'col', [(i, i + 1) for i in range...  4.63 us
    ppermute x1, starting transfers between devices, with_halo(): lax.ppermute(head, axis, [((i + 1) % count, i) for i in range(ends)])  3.64 us
    concatenate x1, other arithmetic, body(): jnp.concatenate([lax.ppermute(rows_done[:, :, -margin:], 'col', [(i, i +...  2.98 us
    reshape x4, local copies, waits for them, and re-layouts, _kmat(): return k.transpose(0, 2, 3, 1).reshape(o, 9 * cin)  2.98 us
    select_n x1, other arithmetic, body(): rimmed = jnp.where(cell_mask[None], flux, jnp.zeros((), jnp.bfloat16))  2.42 us
  transfers between devices with their start and end apart: 4, of which 1 were waited for; matrix products, arithmetic and copies ran while one was open for 7% of the time, Pallas kernels for 0%

profile of v9, /device:TPU:56, one launch (start us, length us, event | category | flops | bytes accessed | tf_op | source)
XLA Modules:
  0.0 105.3 jit_solution(9763061027935560088)
XLA Ops:
  0.0 0.7 fusion.7
  0.7 0.7 compare_bitcast_fusion
  1.3 0.1 fusion.6
  1.5 0.1 reshape.57
  1.5 0.1 broadcast_in_dim.27
  1.7 0.1 convert_element_type.40
  1.8 0.0 copy-start.7
  1.8 0.0 copy-start.4
  1.8 0.0 copy-start.5
  1.8 0.0 copy-start.6
  1.8 0.0 copy-start.3
  1.8 1.7 %copy.53 = bf16[13,128,256]{2,0,1:T(8,128)(2,1)S(1)} copy(bf16[13,128,256]{2,1,0:T(8,128)(2,1)} %param.10) | data formatting | bytes 1703936 | tf_op args[0]
  3.5 0.1 pad.31.clone
  3.6 0.7 maximum_bitcast_fusion
  4.3 1.9 %collective-permute-start = (bf16[16,16,256]{2,1,0:T(8,128)(2,1)S(1)}, bf16[16,16,256]{2,1,0:T(8,128)(2,1)S(1)}, u32[]{:S(2)}, u32[]{:S(2)}) collective-permute-start(bf16[16,16,256]{2,1,0:T(8,128)(2,1)S(1)} %get-tuple-element.7), channel_id=1, source_target_pairs={{0,16},{16,32},{32,48},{48,64},{64,80},{80,96},{96,112},{1,17},{17... | collective-permute-start | bytes 393224 | tf_op jit(solution)/shard_map/ppermute | solution.py:104
  6.2 3.6 %collective-permute-start.1 = (bf16[16,16,256]{2,1,0:T(8,128)(2,1)S(1)}, bf16[16,16,256]{2,1,0:T(8,128)(2,1)S(1)}, u32[]{:S(2)}, u32[]{:S(2)}) collective-permute-start(bf16[16,16,256]{2,1,0:T(8,128)(2,1)S(1)} %get-tuple-element.8), channel_id=1, source_target_pairs={{16,0},{32,16},{48,32},{64,48},{80,64},{96,80},{112,96},{17,1},{33... | collective-permute-start | bytes 393224 | tf_op jit(solution)/shard_map/ppermute | solution.py:106
  9.9 0.1 pad.20.clone
  10.0 0.0 copy-done.7
  10.0 0.7 copy.70.bfl
  10.7 0.0 copy-done.4
  10.7 0.7 copy.65.b1
  11.4 0.0 copy-done.5
  11.4 0.7 copy.67.b2
  12.1 0.0 copy-done.6
  12.1 0.7 copy.69.b3
  12.8 0.0 copy-done.3
  12.9 0.7 copy.64.k1
  13.6 0.0 collective-permute-done
  13.6 0.0 collective-permute-done.1
  13.6 0.2 pad_maximum_fusion
  13.7 0.0 copy-start.2
  13.8 0.0 copy-start
  13.8 0.0 copy-start.1
  13.8 0.3 fusion.8
  14.1 0.5 copy.55
  14.6 0.5 copy.56
  15.2 4.8 %collective-permute-start.3 = (bf16[160,16,16]{0,2,1:T(8,128)(2,1)S(1)}, bf16[160,16,16]{0,2,1:T(8,128)(2,1)S(1)}, u32[]{:S(2)}, u32[]{:S(2)}) collective-permute-start(bf16[160,16,16]{0,2,1:T(8,128)(2,1)S(1)} %copy.56), channel_id=1, source_target_pairs={{1,0},{2,1},{3,2},{4,3},{5,4},{6,5},{7,6},{8,7},{9,8},{10,9},{11,1... | collective-permute-start | bytes 245768 | tf_op jit(solution)/shard_map/ppermute | solution.py:161
  20.0 2.1 %collective-permute-start.2 = (bf16[160,16,16]{0,2,1:T(8,128)(2,1)S(1)}, bf16[160,16,16]{0,2,1:T(8,128)(2,1)S(1)}, u32[]{:S(2)}, u32[]{:S(2)}) collective-permute-start(bf16[160,16,16]{0,2,1:T(8,128)(2,1)S(1)} %copy.55), channel_id=1, source_target_pairs={{0,1},{1,2},{2,3},{3,4},{4,5},{5,6},{6,7},{7,8},{8,9},{9,10},{10,1... | collective-permute-start | bytes 245768 | tf_op jit(solution)/shard_map/ppermute | solution.py:159
  22.1 0.0 copy-done.2
  22.2 0.1 copy.63
  22.2 0.7 reshape.55.kf
  23.0 0.0 copy-done
  23.0 0.1 copy.61
  23.1 0.8 copy.66.k2
  23.9 0.0 copy-done.1
  23.9 0.1 copy.62
  24.0 0.8 copy.68.k3
  24.8 0.7 stack.67.lim_ref
  25.5 4.6 %collective-permute-done.2 = bf16[160,16,16]{0,2,1:T(8,128)(2,1)S(1)} collective-permute-done((bf16[160,16,16]{0,2,1:T(8,128)(2,1)S(1)}, bf16[160,16,16]{0,2,1:T(8,128)(2,1)S(1)}, u32[]{:S(2)}, u32[]{:S(2)}) %collective-permute-start.2) | collective-permute-done | bytes 81952 | tf_op jit(solution)/shard_map/ppermute | solution.py:159
  30.1 0.5 copy.57
  30.7 0.0 collective-permute-done.3
  30.7 0.5 copy.58
  31.2 0.8 fusion.4
  32.0 3.0 %maximum_maximum_fusion.x_ref = bf16[160,16,384]{2,1,0:T(8,128)(2,1)} fusion(bf16[160,16,16]{2,1,0:T(8,128)(2,1)S(1)} %copy.58, bf16[16,16,256]{2,1,0:T(8,128)(2,1)S(1)} %collective-permute-done.1, bf16[128,16,256]{2,1,0:T(8,128)(2,1)S(1)} %maximum_bitcast_fusion, bf16[16,16,256]{2,1,0:T(8,128)(2,1)S(1)} %collective-permute-done, ...), kind=kLoop, calls=%fused_computation.7 | loop fusion | flops 11796480 | bytes 3441408 | tf_op jit(solution)/shard_map/concatenate | solution.py:157
  35.0 64.9 %shard_map.100 = bf16[130,32,384]{2,1,0:T(8,128)(2,1)} custom-call(s32[16]{0:T(128)} %stack.67.lim_ref, bf16[160,16,384]{2,1,0:T(8,128)(2,1)} %maximum_maximum_fusion.x_ref, bf16[64,144]{1,0:T(8,128)(2,1)} %copy.64.k1, f32[64,1]{1,0:T(8,128)} %copy.65.b1, bf16[64,576]{1,0:T(8,128)(2,1)} %copy.66.k2, f32[64,1]{1,0:T(8,128)} %copy.67.b2, ...), custom_call_target="tpu_custom_call" | custom-call | tf_op jit(solution)/shard_map/pallas_call | solution.py:83
  99.9 2.4 %fusion = bf16[26,130,258]{2,0,1:T(8,128)(2,1)S(1)} fusion(bf16[130,32,384]{2,1,0:T(8,128)(2,1)} %shard_map.100, pred[130,258]{1,0:T(8,128)(4,1)S(1)} %bitcast.43), kind=kLoop, calls=%fused_computation.1 | loop fusion | flops 872040 | bytes 3521700 | tf_op jit(solution)/shard_map/jit(_where)/select_n | solution.py:184
  102.3 0.9 slice_convert_fusion.1
  103.3 0.2 slice_convert_fusion
  103.5 0.7 fusion.3
  104.1 1.2 %copy.71 = bf16[13,128,256]{2,1,0:T(8,128)(2,1)} copy(bf16[13,128,256]{2,0,1:T(8,128)(2,1)S(1)} %fusion.3) | data formatting | bytes 1703936 | tf_op jit(solution)/shard_map/convert_element_type | solution.py:188
  (8 shorter events, 0.1 us)
Async XLA Ops:
  1.8 8.2 %copy-start.7 = (f32[26]{0:T(128)S(1)}, f32[26]{0:T(128)}, u32[]{:S(2)}) copy-start(f32[26]{0:T(128)} %param.19) | copy-start | bytes 316
  1.8 8.9 %copy-start.4 = (f32[64]{0:T(128)S(1)}, f32[64]{0:T(128)}, u32[]{:S(2)}) copy-start(f32[64]{0:T(128)} %param.13) | copy-start | bytes 772
  1.8 9.6 %copy-start.5 = (f32[64]{0:T(128)S(1)}, f32[64]{0:T(128)}, u32[]{:S(2)}) copy-start(f32[64]{0:T(128)} %param.15) | copy-start | bytes 772
  1.8 10.3 %copy-start.6 = (f32[64]{0:T(128)S(1)}, f32[64]{0:T(128)}, u32[]{:S(2)}) copy-start(f32[64]{0:T(128)} %param.17) | copy-start | bytes 772
  1.8 11.0 %copy-start.3 = (bf16[64,13,3,3]{0,1,3,2:T(8,128)(2,1)S(1)}, bf16[64,13,3,3]{0,1,3,2:T(8,128)(2,1)}, u32[]{:S(2)}) copy-start(bf16[64,13,3,3]{0,1,3,2:T(8,128)(2,1)} %param.12) | copy-start | bytes 44932
  4.3 9.3 %collective-permute-start = (bf16[16,16,256]{2,1,0:T(8,128)(2,1)S(1)}, bf16[16,16,256]{2,1,0:T(8,128)(2,1)S(1)}, u32[]{:S(2)}, u32[]{:S(2)}) collective-permute-start(bf16[16,16,256]{2,1,0:T(8,128)(2,1)S(1)} %get-tuple-element.7), channel_id=1, source_target_pairs={{0,16},{16,32},{32,48},{48,64},{64,80},{80,96},{96,112},{1,17},{17... | collective-permute-start | bytes 393224 | tf_op jit(solution)/shard_map/ppermute | solution.py:104
  6.2 7.3 %collective-permute-start.1 = (bf16[16,16,256]{2,1,0:T(8,128)(2,1)S(1)}, bf16[16,16,256]{2,1,0:T(8,128)(2,1)S(1)}, u32[]{:S(2)}, u32[]{:S(2)}) collective-permute-start(bf16[16,16,256]{2,1,0:T(8,128)(2,1)S(1)} %get-tuple-element.8), channel_id=1, source_target_pairs={{16,0},{32,16},{48,32},{64,48},{80,64},{96,80},{112,96},{17,1},{33... | collective-permute-start | bytes 393224 | tf_op jit(solution)/shard_map/ppermute | solution.py:106
  13.7 8.4 %copy-start.2 = (bf16[26,64,3,3]{1,0,3,2:T(8,128)(2,1)S(1)}, bf16[26,64,3,3]{1,0,3,2:T(8,128)(2,1)}, u32[]{:S(2)}) copy-start(bf16[26,64,3,3]{1,0,3,2:T(8,128)(2,1)} %param.18) | copy-start | bytes 89860
  13.8 9.2 %copy-start = (bf16[64,64,3,3]{1,0,3,2:T(8,128)(2,1)S(1)}, bf16[64,64,3,3]{1,0,3,2:T(8,128)(2,1)}, u32[]{:S(2)}) copy-start(bf16[64,64,3,3]{1,0,3,2:T(8,128)(2,1)} %param.14) | copy-start | bytes 221188
  13.8 10.1 %copy-start.1 = (bf16[64,64,3,3]{1,0,3,2:T(8,128)(2,1)S(1)}, bf16[64,64,3,3]{1,0,3,2:T(8,128)(2,1)}, u32[]{:S(2)}) copy-start(bf16[64,64,3,3]{1,0,3,2:T(8,128)(2,1)} %param.16) | copy-start | bytes 221188
  15.2 15.5 %collective-permute-start.3 = (bf16[160,16,16]{0,2,1:T(8,128)(2,1)S(1)}, bf16[160,16,16]{0,2,1:T(8,128)(2,1)S(1)}, u32[]{:S(2)}, u32[]{:S(2)}) collective-permute-start(bf16[160,16,16]{0,2,1:T(8,128)(2,1)S(1)} %copy.56), channel_id=1, source_target_pairs={{1,0},{2,1},{3,2},{4,3},{5,4},{6,5},{7,6},{8,7},{9,8},{10,9},{11,1... | collective-permute-start | bytes 245768 | tf_op jit(solution)/shard_map/ppermute | solution.py:161
  20.0 10.1 %collective-permute-start.2 = (bf16[160,16,16]{0,2,1:T(8,128)(2,1)S(1)}, bf16[160,16,16]{0,2,1:T(8,128)(2,1)S(1)}, u32[]{:S(2)}, u32[]{:S(2)}) collective-permute-start(bf16[160,16,16]{0,2,1:T(8,128)(2,1)S(1)} %copy.55), channel_id=1, source_target_pairs={{0,1},{1,2},{2,3},{3,4},{4,5},{5,6},{6,7},{7,8},{8,9},{9,10},{10,1... | collective-permute-start | bytes 245768 | tf_op jit(solution)/shard_map/ppermute | solution.py:159

commit v10 on v9

--- a/solution.py
+++ b/solution.py
@@ -47,7 +47,7 @@
                 )
             return carry
 
-        lax.fori_loop(0, n_rows, row, 0, unroll=8)
+        lax.fori_loop(0, n_rows, row, 0, unroll=(8, 14, 16, 16)[index])
 
     h0 = x_ref.shape[0]
     h1 = h0 - 2

time: 106 us -> 100 us (0.943)
  Pallas kernels: 64.9 us -> 59.6 us
    pallas_call x1, Pallas kernels: 64.9 us -> 59.6 us  [run_net(): pl.pallas_call(_net_kernel, out_shape=jax.ShapeDtypeStruct((h0 - 30, out_...]
where the time goes in v10:
time: 100 us
  Pallas kernels  59.6 us (60%)
  local copies, waits for them, and re-layouts  12.7 us (13%)
  starting transfers between devices  12.5 us (12%)
  other arithmetic  10.4 us (10%)
  waiting for transfers between devices  4.64 us (5%)
    pallas_call x1, Pallas kernels, run_net(): pl.pallas_call(_net_kernel, out_shape=jax.ShapeDtypeStruct((h0 - 30, out_...  59.6 us
    ppermute x1, starting transfers between devices, body(): lax.ppermute(rows_done[:, :, :margin], 'col', [(i + 1, i) for i in range(...  4.84 us
    ppermute x1, waiting for transfers between devices, body(): lax.ppermute(rows_done[:, :, -margin:], 'col', [(i, i + 1) for i in range...  4.63 us
    ppermute x1, starting transfers between devices, with_halo(): lax.ppermute(head, axis, [((i + 1) % count, i) for i in range(ends)])  3.64 us
    concatenate x1, other arithmetic, body(): jnp.concatenate([lax.ppermute(rows_done[:, :, -margin:], 'col', [(i, i +...  2.98 us
    reshape x4, local copies, waits for them, and re-layouts, _kmat(): return k.transpose(0, 2, 3, 1).reshape(o, 9 * cin)  2.98 us
    select_n x1, other arithmetic, body(): rimmed = jnp.where(cell_mask[None], flux, jnp.zeros((), jnp.bfloat16))  2.42 us
    ppermute x1, starting transfers between devices, body(): lax.ppermute(rows_done[:, :, -margin:], 'col', [(i, i + 1) for i in range...  2.1 us
  transfers between devices with their start and end apart: 4, of which 1 were waited for; matrix products, arithmetic and copies ran while one was open for 7% of the time, Pallas kernels for 0%

profile of v10, /device:TPU:56, one launch (start us, length us, event | category | flops | bytes accessed | tf_op | source)
XLA Modules:
  0.0 100.1 jit_solution(9180523737448197054)
XLA Ops:
  0.0 0.7 fusion.7
  0.7 0.7 compare_bitcast_fusion
  1.3 0.1 fusion.6
  1.5 0.1 reshape.57
  1.5 0.1 broadcast_in_dim.27
  1.7 0.1 convert_element_type.40
  1.8 0.0 copy-start.7
  1.8 0.0 copy-start.4
  1.8 0.0 copy-start.5
  1.8 0.0 copy-start.6
  1.8 0.0 copy-start.3
  1.8 1.7 %copy.53 = bf16[13,128,256]{2,0,1:T(8,128)(2,1)S(1)} copy(bf16[13,128,256]{2,1,0:T(8,128)(2,1)} %param.10) | data formatting | bytes 1703936 | tf_op args[0]
  3.5 0.1 pad.31.clone
  3.6 0.7 maximum_bitcast_fusion
  4.3 1.9 %collective-permute-start = (bf16[16,16,256]{2,1,0:T(8,128)(2,1)S(1)}, bf16[16,16,256]{2,1,0:T(8,128)(2,1)S(1)}, u32[]{:S(2)}, u32[]{:S(2)}) collective-permute-start(bf16[16,16,256]{2,1,0:T(8,128)(2,1)S(1)} %get-tuple-element.7), channel_id=1, source_target_pairs={{0,16},{16,32},{32,48},{48,64},{64,80},{80,96},{96,112},{1,17},{17... | collective-permute-start | bytes 393224 | tf_op jit(solution)/shard_map/ppermute | solution.py:104
  6.2 3.6 %collective-permute-start.1 = (bf16[16,16,256]{2,1,0:T(8,128)(2,1)S(1)}, bf16[16,16,256]{2,1,0:T(8,128)(2,1)S(1)}, u32[]{:S(2)}, u32[]{:S(2)}) collective-permute-start(bf16[16,16,256]{2,1,0:T(8,128)(2,1)S(1)} %get-tuple-element.8), channel_id=1, source_target_pairs={{16,0},{32,16},{48,32},{64,48},{80,64},{96,80},{112,96},{17,1},{33... | collective-permute-start | bytes 393224 | tf_op jit(solution)/shard_map/ppermute | solution.py:106
  9.9 0.1 pad.20.clone
  10.0 0.0 copy-done.7
  10.0 0.7 copy.70.bfl
  10.7 0.0 copy-done.4
  10.7 0.7 copy.65.b1
  11.4 0.0 copy-done.5
  11.4 0.7 copy.67.b2
  12.1 0.0 copy-done.6
  12.1 0.7 copy.69.b3
  12.8 0.0 copy-done.3
  12.9 0.7 copy.64.k1
  13.6 0.0 collective-permute-done
  13.6 0.0 collective-permute-done.1
  13.6 0.2 pad_maximum_fusion
  13.7 0.0 copy-start.2
  13.8 0.0 copy-start
  13.8 0.0 copy-start.1
  13.8 0.3 fusion.8
  14.1 0.5 copy.55
  14.6 0.5 copy.56
  15.2 4.8 %collective-permute-start.3 = (bf16[160,16,16]{0,2,1:T(8,128)(2,1)S(1)}, bf16[160,16,16]{0,2,1:T(8,128)(2,1)S(1)}, u32[]{:S(2)}, u32[]{:S(2)}) collective-permute-start(bf16[160,16,16]{0,2,1:T(8,128)(2,1)S(1)} %copy.56), channel_id=1, source_target_pairs={{1,0},{2,1},{3,2},{4,3},{5,4},{6,5},{7,6},{8,7},{9,8},{10,9},{11,1... | collective-permute-start | bytes 245768 | tf_op jit(solution)/shard_map/ppermute | solution.py:161
  20.0 2.1 %collective-permute-start.2 = (bf16[160,16,16]{0,2,1:T(8,128)(2,1)S(1)}, bf16[160,16,16]{0,2,1:T(8,128)(2,1)S(1)}, u32[]{:S(2)}, u32[]{:S(2)}) collective-permute-start(bf16[160,16,16]{0,2,1:T(8,128)(2,1)S(1)} %copy.55), channel_id=1, source_target_pairs={{0,1},{1,2},{2,3},{3,4},{4,5},{5,6},{6,7},{7,8},{8,9},{9,10},{10,1... | collective-permute-start | bytes 245768 | tf_op jit(solution)/shard_map/ppermute | solution.py:159
  22.1 0.0 copy-done.2
  22.2 0.1 copy.63
  22.2 0.7 reshape.55.kf
  23.0 0.0 copy-done
  23.0 0.1 copy.61
  23.1 0.8 copy.66.k2
  23.9 0.0 copy-done.1
  23.9 0.1 copy.62
  24.0 0.8 copy.68.k3
  24.8 0.7 stack.67.lim_ref
  25.5 4.6 %collective-permute-done.2 = bf16[160,16,16]{0,2,1:T(8,128)(2,1)S(1)} collective-permute-done((bf16[160,16,16]{0,2,1:T(8,128)(2,1)S(1)}, bf16[160,16,16]{0,2,1:T(8,128)(2,1)S(1)}, u32[]{:S(2)}, u32[]{:S(2)}) %collective-permute-start.2) | collective-permute-done | bytes 81952 | tf_op jit(solution)/shard_map/ppermute | solution.py:159
  30.1 0.5 copy.57
  30.7 0.0 collective-permute-done.3
  30.7 0.5 copy.58
  31.2 0.8 fusion.4
  32.0 3.0 %maximum_maximum_fusion.x_ref = bf16[160,16,384]{2,1,0:T(8,128)(2,1)} fusion(bf16[160,16,16]{2,1,0:T(8,128)(2,1)S(1)} %copy.58, bf16[16,16,256]{2,1,0:T(8,128)(2,1)S(1)} %collective-permute-done.1, bf16[128,16,256]{2,1,0:T(8,128)(2,1)S(1)} %maximum_bitcast_fusion, bf16[16,16,256]{2,1,0:T(8,128)(2,1)S(1)} %collective-permute-done, ...), kind=kLoop, calls=%fused_computation.7 | loop fusion | flops 11796480 | bytes 3441408 | tf_op jit(solution)/shard_map/concatenate | solution.py:157
  35.0 59.6 %shard_map.100 = bf16[130,32,384]{2,1,0:T(8,128)(2,1)} custom-call(s32[16]{0:T(128)} %stack.67.lim_ref, bf16[160,16,384]{2,1,0:T(8,128)(2,1)} %maximum_maximum_fusion.x_ref, bf16[64,144]{1,0:T(8,128)(2,1)} %copy.64.k1, f32[64,1]{1,0:T(8,128)} %copy.65.b1, bf16[64,576]{1,0:T(8,128)(2,1)} %copy.66.k2, f32[64,1]{1,0:T(8,128)} %copy.67.b2, ...), custom_call_target="tpu_custom_call" | custom-call | tf_op jit(solution)/shard_map/pallas_call | solution.py:83
  94.6 2.4 %fusion = bf16[26,130,258]{2,0,1:T(8,128)(2,1)S(1)} fusion(bf16[130,32,384]{2,1,0:T(8,128)(2,1)} %shard_map.100, pred[130,258]{1,0:T(8,128)(4,1)S(1)} %bitcast.43), kind=kLoop, calls=%fused_computation.1 | loop fusion | flops 872040 | bytes 3521700 | tf_op jit(solution)/shard_map/jit(_where)/select_n | solution.py:184
  97.0 0.9 slice_convert_fusion.1
  98.0 0.2 slice_convert_fusion
  98.2 0.7 fusion.3
  98.9 1.2 %copy.71 = bf16[13,128,256]{2,1,0:T(8,128)(2,1)} copy(bf16[13,128,256]{2,0,1:T(8,128)(2,1)S(1)} %fusion.3) | data formatting | bytes 1703936 | tf_op jit(solution)/shard_map/convert_element_type | solution.py:188
  (8 shorter events, 0.1 us)
Async XLA Ops:
  1.8 8.2 %copy-start.7 = (f32[26]{0:T(128)S(1)}, f32[26]{0:T(128)}, u32[]{:S(2)}) copy-start(f32[26]{0:T(128)} %param.19) | copy-start | bytes 316
  1.8 8.9 %copy-start.4 = (f32[64]{0:T(128)S(1)}, f32[64]{0:T(128)}, u32[]{:S(2)}) copy-start(f32[64]{0:T(128)} %param.13) | copy-start | bytes 772
  1.8 9.6 %copy-start.5 = (f32[64]{0:T(128)S(1)}, f32[64]{0:T(128)}, u32[]{:S(2)}) copy-start(f32[64]{0:T(128)} %param.15) | copy-start | bytes 772
  1.8 10.3 %copy-start.6 = (f32[64]{0:T(128)S(1)}, f32[64]{0:T(128)}, u32[]{:S(2)}) copy-start(f32[64]{0:T(128)} %param.17) | copy-start | bytes 772
  1.8 11.0 %copy-start.3 = (bf16[64,13,3,3]{0,1,3,2:T(8,128)(2,1)S(1)}, bf16[64,13,3,3]{0,1,3,2:T(8,128)(2,1)}, u32[]{:S(2)}) copy-start(bf16[64,13,3,3]{0,1,3,2:T(8,128)(2,1)} %param.12) | copy-start | bytes 44932
  4.3 9.3 %collective-permute-start = (bf16[16,16,256]{2,1,0:T(8,128)(2,1)S(1)}, bf16[16,16,256]{2,1,0:T(8,128)(2,1)S(1)}, u32[]{:S(2)}, u32[]{:S(2)}) collective-permute-start(bf16[16,16,256]{2,1,0:T(8,128)(2,1)S(1)} %get-tuple-element.7), channel_id=1, source_target_pairs={{0,16},{16,32},{32,48},{48,64},{64,80},{80,96},{96,112},{1,17},{17... | collective-permute-start | bytes 393224 | tf_op jit(solution)/shard_map/ppermute | solution.py:104
  6.2 7.3 %collective-permute-start.1 = (bf16[16,16,256]{2,1,0:T(8,128)(2,1)S(1)}, bf16[16,16,256]{2,1,0:T(8,128)(2,1)S(1)}, u32[]{:S(2)}, u32[]{:S(2)}) collective-permute-start(bf16[16,16,256]{2,1,0:T(8,128)(2,1)S(1)} %get-tuple-element.8), channel_id=1, source_target_pairs={{16,0},{32,16},{48,32},{64,48},{80,64},{96,80},{112,96},{17,1},{33... | collective-permute-start | bytes 393224 | tf_op jit(solution)/shard_map/ppermute | solution.py:106
  13.7 8.4 %copy-start.2 = (bf16[26,64,3,3]{1,0,3,2:T(8,128)(2,1)S(1)}, bf16[26,64,3,3]{1,0,3,2:T(8,128)(2,1)}, u32[]{:S(2)}) copy-start(bf16[26,64,3,3]{1,0,3,2:T(8,128)(2,1)} %param.18) | copy-start | bytes 89860
  13.8 9.2 %copy-start = (bf16[64,64,3,3]{1,0,3,2:T(8,128)(2,1)S(1)}, bf16[64,64,3,3]{1,0,3,2:T(8,128)(2,1)}, u32[]{:S(2)}) copy-start(bf16[64,64,3,3]{1,0,3,2:T(8,128)(2,1)} %param.14) | copy-start | bytes 221188
  13.8 10.1 %copy-start.1 = (bf16[64,64,3,3]{1,0,3,2:T(8,128)(2,1)S(1)}, bf16[64,64,3,3]{1,0,3,2:T(8,128)(2,1)}, u32[]{:S(2)}) copy-start(bf16[64,64,3,3]{1,0,3,2:T(8,128)(2,1)} %param.16) | copy-start | bytes 221188
  15.2 15.5 %collective-permute-start.3 = (bf16[160,16,16]{0,2,1:T(8,128)(2,1)S(1)}, bf16[160,16,16]{0,2,1:T(8,128)(2,1)S(1)}, u32[]{:S(2)}, u32[]{:S(2)}) collective-permute-start(bf16[160,16,16]{0,2,1:T(8,128)(2,1)S(1)} %copy.56), channel_id=1, source_target_pairs={{1,0},{2,1},{3,2},{4,3},{5,4},{6,5},{7,6},{8,7},{9,8},{10,9},{11,1... | collective-permute-start | bytes 245768 | tf_op jit(solution)/shard_map/ppermute | solution.py:161
  20.0 10.1 %collective-permute-start.2 = (bf16[160,16,16]{0,2,1:T(8,128)(2,1)S(1)}, bf16[160,16,16]{0,2,1:T(8,128)(2,1)S(1)}, u32[]{:S(2)}, u32[]{:S(2)}) collective-permute-start(bf16[160,16,16]{0,2,1:T(8,128)(2,1)S(1)} %copy.55), channel_id=1, source_target_pairs={{0,1},{1,2},{2,3},{3,4},{4,5},{5,6},{6,7},{7,8},{8,9},{9,10},{10,1... | collective-permute-start | bytes 245768 | tf_op jit(solution)/shard_map/ppermute | solution.py:159

commit v11 on v10

--- a/solution.py
+++ b/solution.py
@@ -149,8 +149,15 @@
         chosen.reshape(per_row, 1, per_col, 1), (per_row, TILE, per_col, TILE)
     ).reshape(1, block_h, block_w)
     spare = jnp.zeros((16 - moments - 1, block_h, block_w), state.dtype)
-    marked = jnp.concatenate([state, own_mask.astype(state.dtype), spare], axis=0).transpose(1, 0, 2)
-    rows_done = with_halo(marked, (("row", 0),), margin)
+    marked = jnp.concatenate([state, own_mask.astype(state.dtype), spare], axis=0)
+    rows_done = jnp.concatenate(
+        [
+            lax.ppermute(marked[:, -margin:], "row", [(i, i + 1) for i in range(row_count - 1)]),
+            marked,
+            lax.ppermute(marked[:, :margin], "row", [(i + 1, i) for i in range(row_count - 1)]),
+        ],
+        axis=1,
+    ).transpose(1, 0, 2)
     ext_h = rows_done.shape[0]
     ext_w = block_w + 2 * margin
     ends = col_count - 1

time: 100 us -> 100 us (level)
  the two profiles are of different devices: /device:TPU:56 before, /device:TPU:57 now
where the time goes in v11:
time: 100 us; the launch traced here: 99.7 us
  Pallas kernels  59.6 us (60%)
  starting transfers between devices  12.7 us (13%)
  local copies, waits for them, and re-layouts  12.6 us (13%)
  other arithmetic  10 us (10%)
  waiting for transfers between devices  4.52 us (5%)
    pallas_call x1, Pallas kernels, run_net(): pl.pallas_call(_net_kernel, out_shape=jax.ShapeDtypeStruct((h0 - 30, out_...  59.6 us
    ppermute x1, starting transfers between devices, body(): lax.ppermute(rows_done[:, :, :margin], 'col', [(i + 1, i) for i in range(...  4.56 us
    ppermute x1, starting transfers between devices, body(): lax.ppermute(marked[:, -margin:], 'row', [(i, i + 1) for i in range(row_c...  4.11 us
    ppermute x1, waiting for transfers between devices, body(): lax.ppermute(rows_done[:, :, -margin:], 'col', [(i, i + 1) for i in range...  3.76 us
    reshape x4, local copies, waits for them, and re-layouts, _kmat(): return k.transpose(0, 2, 3, 1).reshape(o, 9 * cin)  2.98 us
    concatenate x1, other arithmetic, body(): jnp.concatenate([lax.ppermute(rows_done[:, :, -margin:], 'col', [(i, i +...  2.69 us
    select_n x1, other arithmetic, body(): rimmed = jnp.where(cell_mask[None], flux, jnp.zeros((), jnp.bfloat16))  2.42 us
    ppermute x1, starting transfers between devices, body(): lax.ppermute(rows_done[:, :, -margin:], 'col', [(i, i + 1) for i in range...  2.1 us
  transfers between devices with their start and end apart: 4, of which 2 were waited for; matrix products, arithmetic and copies ran while one was open for 7% of the time, Pallas kernels for 0%

profile of v11, /device:TPU:57, one launch (start us, length us, event | category | flops | bytes accessed | tf_op | source)
XLA Modules:
  0.0 99.7 jit_solution(5726776531564460502)
XLA Ops:
  0.0 0.0 copy-start.7
  0.0 0.0 copy-start.4
  0.0 0.0 copy-start.5
  0.0 0.0 copy-start.6
  0.0 0.0 copy-start.3
  0.0 0.7 fusion.7
  0.7 0.7 compare_bitcast_fusion
  1.4 0.1 fusion.6
  1.5 0.1 reshape.57
  1.6 0.1 broadcast_in_dim.27
  1.7 0.1 convert_element_type.40
  1.9 1.6 %copy.53 = bf16[13,128,256]{2,0,1:T(8,128)(2,1)S(1)} copy(bf16[13,128,256]{2,1,0:T(8,128)(2,1)} %param.10) | data formatting | bytes 1703936 | tf_op args[0]
  3.5 0.1 broadcast_in_dim.28
  3.6 0.1 pad_maximum_fusion.4
  3.7 4.1 %collective-permute-start = (bf16[16,16,256]{2,0,1:T(8,128)(2,1)S(1)}, bf16[16,16,256]{2,0,1:T(8,128)(2,1)S(1)}, u32[]{:S(2)}, u32[]{:S(2)}) collective-permute-start(bf16[16,16,256]{2,0,1:T(8,128)(2,1)S(1)} %get-tuple-element.7), channel_id=1, source_target_pairs={{0,16},{16,32},{32,48},{48,64},{64,80},{80,96},{96,112},{1,17},{17... | collective-permute-start | bytes 393224 | tf_op jit(solution)/shard_map/ppermute | solution.py:155
  7.8 1.9 %collective-permute-start.1 = (bf16[16,16,256]{2,0,1:T(8,128)(2,1)S(1)}, bf16[16,16,256]{2,0,1:T(8,128)(2,1)S(1)}, u32[]{:S(2)}, u32[]{:S(2)}) collective-permute-start(bf16[16,16,256]{2,0,1:T(8,128)(2,1)S(1)} %get-tuple-element.8), channel_id=1, source_target_pairs={{16,0},{32,16},{48,32},{64,48},{80,64},{96,80},{112,96},{17,1},{33... | collective-permute-start | bytes 393224 | tf_op jit(solution)/shard_map/ppermute | solution.py:157
  9.8 0.0 copy-done.7
  9.8 0.7 copy.70.bfl
  10.5 0.0 copy-done.4
  10.5 0.7 copy.65.b1
  11.2 0.0 copy-done.5
  11.2 0.7 copy.67.b2
  11.9 0.0 copy-done.6
  11.9 0.7 copy.69.b3
  12.6 0.0 copy-done.3
  12.7 0.7 copy.64.k1
  13.4 0.0 collective-permute-done
  13.4 0.7 collective-permute-done.1
  14.1 0.6 maximum_bitcast_fusion
  14.7 0.0 copy-start.2
  14.7 0.0 copy-start
  14.8 0.0 copy-start.1
  14.8 0.3 fusion.8
  15.1 0.5 copy.55
  15.6 0.5 copy.56
  16.2 4.6 %collective-permute-start.3 = (bf16[160,16,16]{0,2,1:T(8,128)(2,1)S(1)}, bf16[160,16,16]{0,2,1:T(8,128)(2,1)S(1)}, u32[]{:S(2)}, u32[]{:S(2)}) collective-permute-start(bf16[160,16,16]{0,2,1:T(8,128)(2,1)S(1)} %copy.56), channel_id=1, source_target_pairs={{1,0},{2,1},{3,2},{4,3},{5,4},{6,5},{7,6},{8,7},{9,8},{10,9},{11,1... | collective-permute-start | bytes 245768 | tf_op jit(solution)/shard_map/ppermute | solution.py:168
  20.7 2.1 %collective-permute-start.2 = (bf16[160,16,16]{0,2,1:T(8,128)(2,1)S(1)}, bf16[160,16,16]{0,2,1:T(8,128)(2,1)S(1)}, u32[]{:S(2)}, u32[]{:S(2)}) collective-permute-start(bf16[160,16,16]{0,2,1:T(8,128)(2,1)S(1)} %copy.55), channel_id=1, source_target_pairs={{0,1},{1,2},{2,3},{3,4},{4,5},{5,6},{6,7},{7,8},{8,9},{9,10},{10,1... | collective-permute-start | bytes 245768 | tf_op jit(solution)/shard_map/ppermute | solution.py:166
  22.8 0.0 copy-done.2
  22.9 0.1 copy.63
  22.9 0.7 reshape.55.kf
  23.7 0.0 copy-done
  23.7 0.1 copy.61
  23.8 0.8 copy.66.k2
  24.6 0.0 copy-done.1
  24.6 0.1 copy.62
  24.7 0.8 copy.68.k3
  25.5 0.1 pad.18.clone
  25.6 0.7 stack.67.lim_ref
  26.3 3.8 %collective-permute-done.2 = bf16[160,16,16]{0,2,1:T(8,128)(2,1)S(1)} collective-permute-done((bf16[160,16,16]{0,2,1:T(8,128)(2,1)S(1)}, bf16[160,16,16]{0,2,1:T(8,128)(2,1)S(1)}, u32[]{:S(2)}, u32[]{:S(2)}) %collective-permute-start.2) | collective-permute-done | bytes 81952 | tf_op jit(solution)/shard_map/ppermute | solution.py:166
  30.1 0.5 copy.57
  30.6 0.0 collective-permute-done.3
  30.6 0.5 copy.58
  31.1 0.8 fusion.4
  31.9 2.7 %maximum_maximum_fusion.x_ref = bf16[160,16,384]{2,1,0:T(8,128)(2,1)} fusion(bf16[160,16,16]{2,1,0:T(8,128)(2,1)S(1)} %copy.58, bf16[160,16,256]{2,1,0:T(8,128)(2,1)S(1)} %maximum_bitcast_fusion, bf16[160,16,16]{2,1,0:T(8,128)(2,1)S(1)} %copy.57, bf16[384]{0:T(512)(128)(2,1)S(1)} %pad.18.clone), kind=kLoop, calls=%fused_computation.7 | loop fusion | flops 7864320 | bytes 3441408 | tf_op jit(solution)/shard_map/concatenate | solution.py:164
  34.7 59.6 %shard_map.100 = bf16[130,32,384]{2,1,0:T(8,128)(2,1)} custom-call(s32[16]{0:T(128)} %stack.67.lim_ref, bf16[160,16,384]{2,1,0:T(8,128)(2,1)} %maximum_maximum_fusion.x_ref, bf16[64,144]{1,0:T(8,128)(2,1)} %copy.64.k1, f32[64,1]{1,0:T(8,128)} %copy.65.b1, bf16[64,576]{1,0:T(8,128)(2,1)} %copy.66.k2, f32[64,1]{1,0:T(8,128)} %copy.67.b2, ...), custom_call_target="tpu_custom_call" | custom-call | tf_op jit(solution)/shard_map/pallas_call | solution.py:83
  94.3 2.4 %fusion = bf16[26,130,258]{2,0,1:T(8,128)(2,1)S(1)} fusion(bf16[130,32,384]{2,1,0:T(8,128)(2,1)} %shard_map.100, pred[130,258]{1,0:T(8,128)(4,1)S(1)} %bitcast.43), kind=kLoop, calls=%fused_computation.1 | loop fusion | flops 872040 | bytes 3521700 | tf_op jit(solution)/shard_map/jit(_where)/select_n | solution.py:191
  96.7 0.9 slice_convert_fusion.1
  97.6 0.2 slice_convert_fusion
  97.9 0.7 fusion.3
  98.5 1.2 %copy.71 = bf16[13,128,256]{2,1,0:T(8,128)(2,1)} copy(bf16[13,128,256]{2,0,1:T(8,128)(2,1)S(1)} %fusion.3) | data formatting | bytes 1703936 | tf_op jit(solution)/shard_map/convert_element_type | solution.py:195
  (6 shorter events, 0.1 us)
Async XLA Ops:
  0.0 9.8 %copy-start.7 = (f32[26]{0:T(128)S(1)}, f32[26]{0:T(128)}, u32[]{:S(2)}) copy-start(f32[26]{0:T(128)} %param.19) | copy-start | bytes 316
  0.0 10.5 %copy-start.4 = (f32[64]{0:T(128)S(1)}, f32[64]{0:T(128)}, u32[]{:S(2)}) copy-start(f32[64]{0:T(128)} %param.13) | copy-start | bytes 772
  0.0 11.2 %copy-start.5 = (f32[64]{0:T(128)S(1)}, f32[64]{0:T(128)}, u32[]{:S(2)}) copy-start(f32[64]{0:T(128)} %param.15) | copy-start | bytes 772
  0.0 11.9 %copy-start.6 = (f32[64]{0:T(128)S(1)}, f32[64]{0:T(128)}, u32[]{:S(2)}) copy-start(f32[64]{0:T(128)} %param.17) | copy-start | bytes 772
  0.0 12.6 %copy-start.3 = (bf16[64,13,3,3]{0,1,3,2:T(8,128)(2,1)S(1)}, bf16[64,13,3,3]{0,1,3,2:T(8,128)(2,1)}, u32[]{:S(2)}) copy-start(bf16[64,13,3,3]{0,1,3,2:T(8,128)(2,1)} %param.12) | copy-start | bytes 44932
  3.7 9.7 %collective-permute-start = (bf16[16,16,256]{2,0,1:T(8,128)(2,1)S(1)}, bf16[16,16,256]{2,0,1:T(8,128)(2,1)S(1)}, u32[]{:S(2)}, u32[]{:S(2)}) collective-permute-start(bf16[16,16,256]{2,0,1:T(8,128)(2,1)S(1)} %get-tuple-element.7), channel_id=1, source_target_pairs={{0,16},{16,32},{32,48},{48,64},{64,80},{80,96},{96,112},{1,17},{17... | collective-permute-start | bytes 393224 | tf_op jit(solution)/shard_map/ppermute | solution.py:155
  7.8 6.3 %collective-permute-start.1 = (bf16[16,16,256]{2,0,1:T(8,128)(2,1)S(1)}, bf16[16,16,256]{2,0,1:T(8,128)(2,1)S(1)}, u32[]{:S(2)}, u32[]{:S(2)}) collective-permute-start(bf16[16,16,256]{2,0,1:T(8,128)(2,1)S(1)} %get-tuple-element.8), channel_id=1, source_target_pairs={{16,0},{32,16},{48,32},{64,48},{80,64},{96,80},{112,96},{17,1},{33... | collective-permute-start | bytes 393224 | tf_op jit(solution)/shard_map/ppermute | solution.py:157
  14.7 8.1 %copy-start.2 = (bf16[26,64,3,3]{1,0,3,2:T(8,128)(2,1)S(1)}, bf16[26,64,3,3]{1,0,3,2:T(8,128)(2,1)}, u32[]{:S(2)}) copy-start(bf16[26,64,3,3]{1,0,3,2:T(8,128)(2,1)} %param.18) | copy-start | bytes 89860
  14.7 8.9 %copy-start = (bf16[64,64,3,3]{1,0,3,2:T(8,128)(2,1)S(1)}, bf16[64,64,3,3]{1,0,3,2:T(8,128)(2,1)}, u32[]{:S(2)}) copy-start(bf16[64,64,3,3]{1,0,3,2:T(8,128)(2,1)} %param.14) | copy-start | bytes 221188
  14.8 9.8 %copy-start.1 = (bf16[64,64,3,3]{1,0,3,2:T(8,128)(2,1)S(1)}, bf16[64,64,3,3]{1,0,3,2:T(8,128)(2,1)}, u32[]{:S(2)}) copy-start(bf16[64,64,3,3]{1,0,3,2:T(8,128)(2,1)} %param.16) | copy-start | bytes 221188
  16.2 14.4 %collective-permute-start.3 = (bf16[160,16,16]{0,2,1:T(8,128)(2,1)S(1)}, bf16[160,16,16]{0,2,1:T(8,128)(2,1)S(1)}, u32[]{:S(2)}, u32[]{:S(2)}) collective-permute-start(bf16[160,16,16]{0,2,1:T(8,128)(2,1)S(1)} %copy.56), channel_id=1, source_target_pairs={{1,0},{2,1},{3,2},{4,3},{5,4},{6,5},{7,6},{8,7},{9,8},{10,9},{11,1... | collective-permute-start | bytes 245768 | tf_op jit(solution)/shard_map/ppermute | solution.py:168
  20.7 9.3 %collective-permute-start.2 = (bf16[160,16,16]{0,2,1:T(8,128)(2,1)S(1)}, bf16[160,16,16]{0,2,1:T(8,128)(2,1)S(1)}, u32[]{:S(2)}, u32[]{:S(2)}) collective-permute-start(bf16[160,16,16]{0,2,1:T(8,128)(2,1)S(1)} %copy.55), channel_id=1, source_target_pairs={{0,1},{1,2},{2,3},{3,4},{4,5},{5,6},{6,7},{7,8},{8,9},{9,10},{10,1... | collective-permute-start | bytes 245768 | tf_op jit(solution)/shard_map/ppermute | solution.py:166

commit v12 on v10

--- a/solution.py
+++ b/solution.py
@@ -149,16 +149,31 @@
         chosen.reshape(per_row, 1, per_col, 1), (per_row, TILE, per_col, TILE)
     ).reshape(1, block_h, block_w)
     spare = jnp.zeros((16 - moments - 1, block_h, block_w), state.dtype)
-    marked = jnp.concatenate([state, own_mask.astype(state.dtype), spare], axis=0).transpose(1, 0, 2)
-    rows_done = with_halo(marked, (("row", 0),), margin)
-    ext_h = rows_done.shape[0]
+    marked = jnp.concatenate([state, own_mask.astype(state.dtype), spare], axis=0)
+    turned = marked.transpose(1, 0, 2)
+    downs = [(i, i + 1) for i in range(row_count - 1)]
+    ups = [(i + 1, i) for i in range(row_count - 1)]
+    ends = col_count - 1
+    from_above = lax.ppermute(marked[:, -margin:], "row", downs).transpose(1, 0, 2)
+    from_below = lax.ppermute(marked[:, :margin], "row", ups).transpose(1, 0, 2)
+    sides = jnp.concatenate(
+        [
+            lax.ppermute(turned[:, :, -margin:], "col", [(i, i + 1) for i in range(ends)]),
+            lax.ppermute(turned[:, :, :margin], "col", [(i + 1, i) for i in range(ends)]),
+        ],
+        axis=2,
+    )
+    side_rows = jnp.concatenate(
+        [lax.ppermute(sides[-margin:], "row", downs), sides, lax.ppermute(sides[:margin], "row", ups)],
+        axis=0,
+    )
+    ext_h = block_h + 2 * margin
     ext_w = block_w + 2 * margin
-    ends = col_count - 1
     x = jnp.concatenate(
         [
-            lax.ppermute(rows_done[:, :, -margin:], "col", [(i, i + 1) for i in range(ends)]),
-            rows_done,
-            lax.ppermute(rows_done[:, :, :margin], "col", [(i + 1, i) for i in range(ends)]),
+            side_rows[:, :, :margin],
+            jnp.concatenate([from_above, turned, from_below], axis=0),
+            side_rows[:, :, margin:],
             jnp.zeros((ext_h, 16, LANES - ext_w), state.dtype),
         ],
         axis=2,

time: 100 us -> 117 us (1.17)
  the two profiles are of different devices: /device:TPU:56 before, /device:TPU:7 now
where the time goes in v12:
time: 117 us
  Pallas kernels  59.6 us (51%)
  starting transfers between devices  19.2 us (16%)
  waiting for transfers between devices  13.5 us (12%)
  local copies, waits for them, and re-layouts  13 us (11%)
  other arithmetic  11.2 us (10%)
    pallas_call x1, Pallas kernels, run_net(): pl.pallas_call(_net_kernel, out_shape=jax.ShapeDtypeStruct((h0 - 30, out_...  59.6 us
    ppermute x1, waiting for transfers between devices, body(): lax.ppermute(turned[:, :, -margin:], 'col', [(i, i + 1) for i in range(en...  8.65 us
    ppermute x1, starting transfers between devices, body(): lax.ppermute(sides[-margin:], 'row', downs)  5.69 us
    ppermute x1, waiting for transfers between devices, body(): lax.ppermute(turned[:, :, :margin], 'col', [(i + 1, i) for i in range(end...  4.79 us
    ppermute x1, starting transfers between devices, body(): lax.ppermute(marked[:, -margin:], 'row', downs).transpose(1, 0, 2)  4.09 us
    ppermute x1, starting transfers between devices, body(): lax.ppermute(turned[:, :, -margin:], 'col', [(i, i + 1) for i in range(en...  3.12 us
    concatenate x1, other arithmetic, body(): jnp.concatenate([side_rows[:, :, :margin], jnp.concatenate([from_above, t...  2.97 us
    reshape x4, local copies, waits for them, and re-layouts, _kmat(): return k.transpose(0, 2, 3, 1).reshape(o, 9 * cin)  2.97 us
  transfers between devices with their start and end apart: 6, of which 2 were waited for; matrix products, arithmetic and copies ran while one was open for 9% of the time, Pallas kernels for 0%

profile of v12, /device:TPU:7, one launch (start us, length us, event | category | flops | bytes accessed | tf_op | source)
XLA Modules:
  0.0 116.8 jit_solution(8097148747364915206)
XLA Ops:
  0.0 0.7 fusion.7
  0.7 0.7 compare_bitcast_fusion
  1.3 0.1 fusion.6
  1.5 0.1 reshape.57
  1.5 0.1 broadcast_in_dim.27
  1.7 0.1 convert_element_type.40
  1.8 1.6 %copy.51 = bf16[13,128,256]{2,0,1:T(8,128)(2,1)S(1)} copy(bf16[13,128,256]{2,1,0:T(8,128)(2,1)} %param.10) | data formatting | bytes 1703936 | tf_op args[0]
  3.4 0.1 pad.34.clone
  3.5 0.7 maximum_maximum_fusion.1
  4.2 0.7 fusion.8
  4.9 4.1 %collective-permute-start.4 = (bf16[16,16,256]{2,0,1:T(8,128)(2,1)}, bf16[16,16,256]{2,0,1:T(8,128)(2,1)S(1)}, u32[]{:S(2)}, u32[]{:S(2)}) collective-permute-start(bf16[16,16,256]{2,0,1:T(8,128)(2,1)} %get-tuple-element.5), channel_id=1, source_target_pairs={{0,16},{16,32},{32,48},{48,64},{64,80},{80,96},{96,112},{1,17},{17... | collective-permute-start | bytes 393224 | tf_op jit(solution)/shard_map/ppermute | solution.py:157
  9.0 0.0 copy-start.2
  9.0 2.1 %collective-permute-start.5 = (bf16[16,16,256]{2,0,1:T(8,128)(2,1)}, bf16[16,16,256]{2,0,1:T(8,128)(2,1)S(1)}, u32[]{:S(2)}, u32[]{:S(2)}) collective-permute-start(bf16[16,16,256]{2,0,1:T(8,128)(2,1)} %get-tuple-element.6), channel_id=1, source_target_pairs={{16,0},{32,16},{48,32},{64,48},{80,64},{96,80},{112,96},{17,1},{33... | collective-permute-start | bytes 393224 | tf_op jit(solution)/shard_map/ppermute | solution.py:158
  11.1 0.7 fusion.11
  11.8 0.0 copy-start.7
  11.8 0.0 copy-start.4
  11.8 0.0 copy-start.5
  11.8 0.0 copy-start.6
  11.8 0.0 copy-start.3
  11.9 0.0 copy-start
  11.9 0.0 copy-start.1
  11.9 0.2 fusion.9
  12.1 3.1 %collective-permute-start = (bf16[128,16,16]{2,1,0:T(8,128)(2,1)S(1)}, bf16[128,16,16]{2,1,0:T(8,128)(2,1)S(1)}, u32[]{:S(2)}, u32[]{:S(2)}) collective-permute-start(bf16[128,16,16]{2,1,0:T(8,128)(2,1)S(1)} %get-tuple-element.7), channel_id=1, source_target_pairs={{0,1},{1,2},{2,3},{3,4},{4,5},{5,6},{6,7},{7,8},{8,9},{9,10},{10,1... | collective-permute-start | bytes 196616 | tf_op jit(solution)/shard_map/ppermute | solution.py:161
  15.3 2.2 %collective-permute-start.1 = (bf16[128,16,16]{2,1,0:T(8,128)(2,1)S(1)}, bf16[128,16,16]{2,1,0:T(8,128)(2,1)S(1)}, u32[]{:S(2)}, u32[]{:S(2)}) collective-permute-start(bf16[128,16,16]{2,1,0:T(8,128)(2,1)S(1)} %get-tuple-element.8), channel_id=1, source_target_pairs={{1,0},{2,1},{3,2},{4,3},{5,4},{6,5},{7,6},{8,7},{9,8},{10,9},{11,1... | collective-permute-start | bytes 196616 | tf_op jit(solution)/shard_map/ppermute | solution.py:162
  17.4 0.0 copy-done.2
  17.5 8.6 %collective-permute-done = bf16[128,16,16]{2,1,0:T(8,128)(2,1)S(1)} collective-permute-done((bf16[128,16,16]{2,1,0:T(8,128)(2,1)S(1)}, bf16[128,16,16]{2,1,0:T(8,128)(2,1)S(1)}, u32[]{:S(2)}, u32[]{:S(2)}) %collective-permute-start) | collective-permute-done | bytes 65568 | tf_op jit(solution)/shard_map/ppermute | solution.py:161
  26.1 0.4 copy.53
  26.5 4.8 %collective-permute-done.1 = bf16[128,16,16]{2,1,0:T(8,128)(2,1)S(1)} collective-permute-done((bf16[128,16,16]{2,1,0:T(8,128)(2,1)S(1)}, bf16[128,16,16]{2,1,0:T(8,128)(2,1)S(1)}, u32[]{:S(2)}, u32[]{:S(2)}) %collective-permute-start.1) | collective-permute-done | bytes 65568 | tf_op jit(solution)/shard_map/ppermute | solution.py:162
  31.3 0.4 copy.54
  31.8 0.1 slice_maximum_fusion
  31.9 5.7 %collective-permute-start.2 = (bf16[16,16,32]{0,2,1:T(8,128)(2,1)S(1)}, bf16[16,16,32]{0,2,1:T(8,128)(2,1)S(1)}, u32[]{:S(2)}, u32[]{:S(2)}) collective-permute-start(bf16[16,16,32]{0,2,1:T(8,128)(2,1)S(1)} %get-tuple-element.11), channel_id=1, source_target_pairs={{0,16},{16,32},{32,48},{48,64},{64,80},{80,96},{96,112},{1,17},{17... | collective-permute-start | bytes 49160 | tf_op jit(solution)/shard_map/ppermute | solution.py:167
  37.6 2.1 %collective-permute-start.3 = (bf16[16,16,32]{0,2,1:T(8,128)(2,1)S(1)}, bf16[16,16,32]{0,2,1:T(8,128)(2,1)S(1)}, u32[]{:S(2)}, u32[]{:S(2)}) collective-permute-start(bf16[16,16,32]{0,2,1:T(8,128)(2,1)S(1)} %get-tuple-element.12), channel_id=1, source_target_pairs={{16,0},{32,16},{48,32},{64,48},{80,64},{96,80},{112,96},{17,1},{33... | collective-permute-start | bytes 49160 | tf_op jit(solution)/shard_map/ppermute | solution.py:167
  39.7 0.0 copy-done.7
  39.8 0.1 pad.20.clone
  39.8 0.7 copy.66.bfl
  40.5 0.0 copy-done.4
  40.5 0.7 copy.61.b1
  41.2 0.0 copy-done.5
  41.2 0.7 copy.63.b2
  41.9 0.0 copy-done.6
  41.9 0.7 copy.65.b3
  42.6 0.7 copy.60.k1
  43.4 0.1 copy.59
  43.4 0.7 reshape.55.kf
  44.1 0.1 copy.57
  44.3 0.8 copy.62.k2
  45.1 0.1 copy.58
  45.2 0.8 copy.64.k3
  46.0 0.6 stack.67.lim_ref
  46.6 0.0 collective-permute-done.2
  46.6 0.0 collective-permute-done.3
  46.6 0.2 pad_maximum_fusion
  46.8 0.5 copy.69
  47.3 0.5 copy.70
  47.9 0.0 collective-permute-done.4
  47.9 0.0 collective-permute-done.5
  47.9 0.8 fusion.4
  48.7 3.0 %maximum_maximum_fusion.x_ref = bf16[160,16,384]{2,1,0:T(8,128)(2,1)} fusion(bf16[160,16,16]{2,1,0:T(8,128)(2,1)S(1)} %copy.70, bf16[16,16,256]{2,1,0:T(8,128)(2,1)S(1)} %bitcast.48, bf16[128,16,256]{2,1,0:T(8,128)(2,1)S(1)} %fusion.11, bf16[16,16,256]{2,1,0:T(8,128)(2,1)S(1)} %bitcast.46, bf16[160,16,16]{2,1,0:T(8,128)(2,1)S(1)} %copy.69, ...), kind=kLoop, calls=%fused_computation.7 | loop fusion | flops 11796480 | bytes 3441408 | tf_op jit(solution)/shard_map/concatenate | solution.py:172
  51.7 59.6 %shard_map.100 = bf16[130,32,384]{2,1,0:T(8,128)(2,1)} custom-call(s32[16]{0:T(128)} %stack.67.lim_ref, bf16[160,16,384]{2,1,0:T(8,128)(2,1)} %maximum_maximum_fusion.x_ref, bf16[64,144]{1,0:T(8,128)(2,1)} %copy.60.k1, f32[64,1]{1,0:T(8,128)} %copy.61.b1, bf16[64,576]{1,0:T(8,128)(2,1)} %copy.62.k2, f32[64,1]{1,0:T(8,128)} %copy.63.b2, ...), custom_call_target="tpu_custom_call" | custom-call | tf_op jit(solution)/shard_map/pallas_call | solution.py:83
  111.3 2.4 %fusion = bf16[26,130,258]{2,0,1:T(8,128)(2,1)S(1)} fusion(bf16[130,32,384]{2,1,0:T(8,128)(2,1)} %shard_map.100, pred[130,258]{1,0:T(8,128)(4,1)S(1)} %bitcast.49), kind=kLoop, calls=%fused_computation.1 | loop fusion | flops 872040 | bytes 3521700 | tf_op jit(solution)/shard_map/jit(_where)/select_n | solution.py:199
  113.7 0.9 slice_convert_fusion.1
  114.7 0.2 slice_convert_fusion
  114.9 0.7 fusion.3
  115.6 1.2 %copy.67 = bf16[13,128,256]{2,1,0:T(8,128)(2,1)} copy(bf16[13,128,256]{2,0,1:T(8,128)(2,1)S(1)} %fusion.3) | data formatting | bytes 1703936 | tf_op jit(solution)/shard_map/convert_element_type | solution.py:203
  (11 shorter events, 0.1 us)
Async XLA Ops:
  4.9 42.9 %collective-permute-start.4 = (bf16[16,16,256]{2,0,1:T(8,128)(2,1)}, bf16[16,16,256]{2,0,1:T(8,128)(2,1)S(1)}, u32[]{:S(2)}, u32[]{:S(2)}) collective-permute-start(bf16[16,16,256]{2,0,1:T(8,128)(2,1)} %get-tuple-element.5), channel_id=1, source_target_pairs={{0,16},{16,32},{32,48},{48,64},{64,80},{80,96},{96,112},{1,17},{17... | collective-permute-start | bytes 393224 | tf_op jit(solution)/shard_map/ppermute | solution.py:157
  9.0 8.4 %copy-start.2 = (bf16[26,64,3,3]{1,0,3,2:T(8,128)(2,1)S(1)}, bf16[26,64,3,3]{1,0,3,2:T(8,128)(2,1)}, u32[]{:S(2)}) copy-start(bf16[26,64,3,3]{1,0,3,2:T(8,128)(2,1)} %param.18) | copy-start | bytes 89860
  9.0 38.8 %collective-permute-start.5 = (bf16[16,16,256]{2,0,1:T(8,128)(2,1)}, bf16[16,16,256]{2,0,1:T(8,128)(2,1)S(1)}, u32[]{:S(2)}, u32[]{:S(2)}) collective-permute-start(bf16[16,16,256]{2,0,1:T(8,128)(2,1)} %get-tuple-element.6), channel_id=1, source_target_pairs={{16,0},{32,16},{48,32},{64,48},{80,64},{96,80},{112,96},{17,1},{33... | collective-permute-start | bytes 393224 | tf_op jit(solution)/shard_map/ppermute | solution.py:158
  11.8 27.9 %copy-start.7 = (f32[26]{0:T(128)S(1)}, f32[26]{0:T(128)}, u32[]{:S(2)}) copy-start(f32[26]{0:T(128)} %param.19) | copy-start | bytes 316
  11.8 28.7 %copy-start.4 = (f32[64]{0:T(128)S(1)}, f32[64]{0:T(128)}, u32[]{:S(2)}) copy-start(f32[64]{0:T(128)} %param.13) | copy-start | bytes 772
  11.8 29.4 %copy-start.5 = (f32[64]{0:T(128)S(1)}, f32[64]{0:T(128)}, u32[]{:S(2)}) copy-start(f32[64]{0:T(128)} %param.15) | copy-start | bytes 772
  11.8 30.1 %copy-start.6 = (f32[64]{0:T(128)S(1)}, f32[64]{0:T(128)}, u32[]{:S(2)}) copy-start(f32[64]{0:T(128)} %param.17) | copy-start | bytes 772
  11.8 30.8 %copy-start.3 = (bf16[64,13,3,3]{0,1,3,2:T(8,128)(2,1)S(1)}, bf16[64,13,3,3]{0,1,3,2:T(8,128)(2,1)}, u32[]{:S(2)}) copy-start(bf16[64,13,3,3]{0,1,3,2:T(8,128)(2,1)} %param.12) | copy-start | bytes 44932
  11.9 32.3 %copy-start = (bf16[64,64,3,3]{1,0,3,2:T(8,128)(2,1)S(1)}, bf16[64,64,3,3]{1,0,3,2:T(8,128)(2,1)}, u32[]{:S(2)}) copy-start(bf16[64,64,3,3]{1,0,3,2:T(8,128)(2,1)} %param.14) | copy-start | bytes 221188
  11.9 33.2 %copy-start.1 = (bf16[64,64,3,3]{1,0,3,2:T(8,128)(2,1)S(1)}, bf16[64,64,3,3]{1,0,3,2:T(8,128)(2,1)}, u32[]{:S(2)}) copy-start(bf16[64,64,3,3]{1,0,3,2:T(8,128)(2,1)} %param.16) | copy-start | bytes 221188
  12.1 14.0 %collective-permute-start = (bf16[128,16,16]{2,1,0:T(8,128)(2,1)S(1)}, bf16[128,16,16]{2,1,0:T(8,128)(2,1)S(1)}, u32[]{:S(2)}, u32[]{:S(2)}) collective-permute-start(bf16[128,16,16]{2,1,0:T(8,128)(2,1)S(1)} %get-tuple-element.7), channel_id=1, source_target_pairs={{0,1},{1,2},{2,3},{3,4},{4,5},{5,6},{6,7},{7,8},{8,9},{9,10},{10,1... | collective-permute-start | bytes 196616 | tf_op jit(solution)/shard_map/ppermute | solution.py:161
  15.3 16.1 %collective-permute-start.1 = (bf16[128,16,16]{2,1,0:T(8,128)(2,1)S(1)}, bf16[128,16,16]{2,1,0:T(8,128)(2,1)S(1)}, u32[]{:S(2)}, u32[]{:S(2)}) collective-permute-start(bf16[128,16,16]{2,1,0:T(8,128)(2,1)S(1)} %get-tuple-element.8), channel_id=1, source_target_pairs={{1,0},{2,1},{3,2},{4,3},{5,4},{6,5},{7,6},{8,7},{9,8},{10,9},{11,1... | collective-permute-start | bytes 196616 | tf_op jit(solution)/shard_map/ppermute | solution.py:162
  31.9 14.7 %collective-permute-start.2 = (bf16[16,16,32]{0,2,1:T(8,128)(2,1)S(1)}, bf16[16,16,32]{0,2,1:T(8,128)(2,1)S(1)}, u32[]{:S(2)}, u32[]{:S(2)}) collective-permute-start(bf16[16,16,32]{0,2,1:T(8,128)(2,1)S(1)} %get-tuple-element.11), channel_id=1, source_target_pairs={{0,16},{16,32},{32,48},{48,64},{64,80},{80,96},{96,112},{1,17},{17... | collective-permute-start | bytes 49160 | tf_op jit(solution)/shard_map/ppermute | solution.py:167
  37.6 9.0 %collective-permute-start.3 = (bf16[16,16,32]{0,2,1:T(8,128)(2,1)S(1)}, bf16[16,16,32]{0,2,1:T(8,128)(2,1)S(1)}, u32[]{:S(2)}, u32[]{:S(2)}) collective-permute-start(bf16[16,16,32]{0,2,1:T(8,128)(2,1)S(1)} %get-tuple-element.12), channel_id=1, source_target_pairs={{16,0},{32,16},{48,32},{64,48},{80,64},{96,80},{112,96},{17,1},{33... | collective-permute-start | bytes 49160 | tf_op jit(solution)/shard_map/ppermute | solution.py:167

commit v13 on v10

--- a/solution.py
+++ b/solution.py
@@ -150,19 +150,26 @@
     ).reshape(1, block_h, block_w)
     spare = jnp.zeros((16 - moments - 1, block_h, block_w), state.dtype)
     marked = jnp.concatenate([state, own_mask.astype(state.dtype), spare], axis=0).transpose(1, 0, 2)
-    rows_done = with_halo(marked, (("row", 0),), margin)
-    ext_h = rows_done.shape[0]
-    ext_w = block_w + 2 * margin
     ends = col_count - 1
+    cols_done = jnp.concatenate(
+        [
+            lax.ppermute(marked[:, :, -margin:], "col", [(i, i + 1) for i in range(ends)]),
+            marked,
+            lax.ppermute(marked[:, :, :margin], "col", [(i + 1, i) for i in range(ends)]),
+            jnp.zeros((block_h, 16, LANES - block_w - 2 * margin), state.dtype),
+        ],
+        axis=2,
+    )
     x = jnp.concatenate(
         [
-            lax.ppermute(rows_done[:, :, -margin:], "col", [(i, i + 1) for i in range(ends)]),
-            rows_done,
-            lax.ppermute(rows_done[:, :, :margin], "col", [(i + 1, i) for i in range(ends)]),
-            jnp.zeros((ext_h, 16, LANES - ext_w), state.dtype),
+            lax.ppermute(cols_done[-margin:], "row", [(i, i + 1) for i in range(row_count - 1)]),
+            cols_done,
+            lax.ppermute(cols_done[:margin], "row", [(i + 1, i) for i in range(row_count - 1)]),
         ],
-        axis=2,
-    )
+        axis=0,
+    )
+    ext_h = block_h + 2 * margin
+    ext_w = block_w + 2 * margin
     lims = []
     offset = margin
     out_h, out_w = ext_h, ext_w

time: 100 us -> 111 us (1.11)
  the two profiles are of different devices: /device:TPU:56 before, /device:TPU:7 now
where the time goes in v13:
time: 111 us
  Pallas kernels  59.6 us (54%)
  waiting for transfers between devices  14.3 us (13%)
  local copies, waits for them, and re-layouts  13.6 us (12%)
  starting transfers between devices  12.8 us (12%)
  other arithmetic  10 us (9%)
    pallas_call x1, Pallas kernels, run_net(): pl.pallas_call(_net_kernel, out_shape=jax.ShapeDtypeStruct((h0 - 30, out_...  59.6 us
    ppermute x1, waiting for transfers between devices, body(): lax.ppermute(marked[:, :, -margin:], 'col', [(i, i + 1) for i in range(en...  9.36 us
    ppermute x1, starting transfers between devices, body(): lax.ppermute(cols_done[-margin:], 'row', [(i, i + 1) for i in range(row_c...  5.24 us
    ppermute x1, waiting for transfers between devices, body(): lax.ppermute(marked[:, :, :margin], 'col', [(i + 1, i) for i in range(end...  4.95 us
    ppermute x1, starting transfers between devices, body(): lax.ppermute(marked[:, :, -margin:], 'col', [(i, i + 1) for i in range(en...  3.25 us
    unnamed x22, local copies, waits for them, and re-layouts  3.13 us
    reshape x4, local copies, waits for them, and re-layouts, _kmat(): return k.transpose(0, 2, 3, 1).reshape(o, 9 * cin)  2.98 us
    concatenate x1, other arithmetic, body(): jnp.concatenate([lax.ppermute(cols_done[-margin:], 'row', [(i, i + 1) for...  2.8 us
  transfers between devices with their start and end apart: 4, of which 2 were waited for; matrix products, arithmetic and copies ran while one was open for 8% of the time, Pallas kernels for 0%

profile of v13, /device:TPU:7, one launch (start us, length us, event | category | flops | bytes accessed | tf_op | source)
XLA Modules:
  0.0 110.6 jit_solution(12020444272887763580)
XLA Ops:
  0.0 0.7 fusion.6
  0.7 0.7 compare_bitcast_fusion
  1.3 0.1 fusion.5
  1.5 0.1 reshape.57
  1.5 0.1 broadcast_in_dim.27
  1.7 0.1 convert_element_type.40
  1.8 1.6 %copy.34 = bf16[13,128,256]{2,0,1:T(8,128)(2,1)S(1)} copy(bf16[13,128,256]{2,1,0:T(8,128)(2,1)} %param.10) | data formatting | bytes 1703936 | tf_op args[0]
  3.4 0.1 pad.27.clone
  3.5 0.7 maximum_bitcast_fusion
  4.2 0.2 fusion.7
  4.5 0.0 copy-start.9
  4.5 0.0 copy-start.6
  4.5 0.0 copy-start.7
  4.5 0.0 copy-start.8
  4.5 0.0 copy-start.5
  4.5 3.3 %collective-permute-start = (bf16[128,16,16]{2,1,0:T(8,128)(2,1)S(1)}, bf16[128,16,16]{2,1,0:T(8,128)(2,1)S(1)}, u32[]{:S(2)}, u32[]{:S(2)}) collective-permute-start(bf16[128,16,16]{2,1,0:T(8,128)(2,1)S(1)} %get-tuple-element.7), channel_id=1, source_target_pairs={{0,1},{1,2},{2,3},{3,4},{4,5},{5,6},{6,7},{7,8},{8,9},{9,10},{10,1... | collective-permute-start | bytes 196616 | tf_op jit(solution)/shard_map/ppermute | solution.py:156
  7.8 2.2 %collective-permute-start.1 = (bf16[128,16,16]{2,1,0:T(8,128)(2,1)S(1)}, bf16[128,16,16]{2,1,0:T(8,128)(2,1)S(1)}, u32[]{:S(2)}, u32[]{:S(2)}) collective-permute-start(bf16[128,16,16]{2,1,0:T(8,128)(2,1)S(1)} %get-tuple-element.8), channel_id=1, source_target_pairs={{1,0},{2,1},{3,2},{4,3},{5,4},{6,5},{7,6},{8,7},{9,8},{10,9},{11,1... | collective-permute-start | bytes 196616 | tf_op jit(solution)/shard_map/ppermute | solution.py:158
  10.0 0.0 copy-start.4
  10.0 9.4 %collective-permute-done = bf16[128,16,16]{2,1,0:T(8,128)(2,1)S(1)} collective-permute-done((bf16[128,16,16]{2,1,0:T(8,128)(2,1)S(1)}, bf16[128,16,16]{2,1,0:T(8,128)(2,1)S(1)}, u32[]{:S(2)}, u32[]{:S(2)}) %collective-permute-start) | collective-permute-done | bytes 65568 | tf_op jit(solution)/shard_map/ppermute | solution.py:156
  19.4 0.0 copy-start.1
  19.4 5.0 %collective-permute-done.1 = bf16[128,16,16]{2,1,0:T(8,128)(2,1)S(1)} collective-permute-done((bf16[128,16,16]{2,1,0:T(8,128)(2,1)S(1)}, bf16[128,16,16]{2,1,0:T(8,128)(2,1)S(1)}, u32[]{:S(2)}, u32[]{:S(2)}) %collective-permute-start.1) | collective-permute-done | bytes 65568 | tf_op jit(solution)/shard_map/ppermute | solution.py:158
  24.3 0.0 copy-start.2
  24.3 0.1 broadcast_in_dim.29
  24.4 0.3 pad_maximum_fusion.4
  24.7 5.2 %collective-permute-start.2 = (bf16[16,16,384]{2,1,0:T(8,128)(2,1)S(1)}, bf16[16,16,384]{2,1,0:T(8,128)(2,1)S(1)}, u32[]{:S(2)}, u32[]{:S(2)}) collective-permute-start(bf16[16,16,384]{2,1,0:T(8,128)(2,1)S(1)} %get-tuple-element.5), channel_id=1, source_target_pairs={{0,16},{16,32},{32,48},{48,64},{64,80},{80,96},{96,112},{1,17},{17... | collective-permute-start | bytes 589832 | tf_op jit(solution)/shard_map/ppermute | solution.py:165
  29.9 2.1 %collective-permute-start.3 = (bf16[16,16,384]{2,1,0:T(8,128)(2,1)S(1)}, bf16[16,16,384]{2,1,0:T(8,128)(2,1)}, u32[]{:S(2)}, u32[]{:S(2)}) collective-permute-start(bf16[16,16,384]{2,1,0:T(8,128)(2,1)S(1)} %get-tuple-element.6), channel_id=1, source_target_pairs={{16,0},{32,16},{48,32},{64,48},{80,64},{96,80},{112,96},{17,1},{33... | collective-permute-start | bytes 589832 | tf_op jit(solution)/shard_map/ppermute | solution.py:167
  32.0 0.0 copy-done.9
  32.1 0.7 copy.45.bfl
  32.8 0.0 copy-done.6
  32.8 0.7 copy.40.b1
  33.5 0.0 copy-done.7
  33.5 0.7 copy.42.b2
  34.2 0.0 copy-done.8
  34.2 0.7 copy.44.b3
  34.9 0.0 copy-done.5
  34.9 0.7 copy.39.k1
  35.6 0.9 pad_bitcast_fusion
  36.5 0.1 copy.38
  36.5 0.7 reshape.55.kf
  37.3 0.0 copy-done.1
  37.3 0.0 copy-done.2
  37.3 0.0 copy-done.4
  37.3 0.1 copy.36
  37.4 0.8 copy.41.k2
  38.2 1.0 copy.37
  39.3 0.8 copy.43.k3
  40.0 0.6 stack.67.lim_ref
  40.7 0.0 collective-permute-done.2
  40.7 0.0 copy-start.3
  40.7 0.7 copy-done.3
  41.4 0.0 collective-permute-done.3
  41.4 2.8 %pad_maximum_fusion.x_ref = bf16[160,16,384]{2,1,0:T(8,128)(2,1)S(1)} fusion(bf16[16,16,384]{2,1,0:T(8,128)(2,1)} %collective-permute-done.3, bf16[128,16,96]{2,1,0:T(8,128)(2,1)S(1)} %broadcast_in_dim.29, bf16[128,16,16]{2,1,0:T(8,128)(2,1)} %copy-done.2, bf16[128,16,256]{2,1,0:T(8,128)(2,1)S(1)} %maximum_bitcast_fusion, bf16[128,16,16]{2,1,0:T(8,128)(2,1)} %copy-done.1, ...), kind=kLoop, calls=%fused_computation.7 | loop fusion | flops 11796480 | bytes 3932160 | tf_op jit(solution)/shard_map/concatenate | solution.py:163
  44.2 0.0 copy-start
  44.2 0.5 slice_compare_fusion
  44.7 0.7 copy-done
  45.5 59.6 %shard_map.100 = bf16[130,32,384]{2,1,0:T(8,128)(2,1)} custom-call(s32[16]{0:T(128)} %stack.67.lim_ref, bf16[160,16,384]{2,1,0:T(8,128)(2,1)} %copy-done, bf16[64,144]{1,0:T(8,128)(2,1)} %copy.39.k1, f32[64,1]{1,0:T(8,128)} %copy.40.b1, bf16[64,576]{1,0:T(8,128)(2,1)} %copy.41.k2, f32[64,1]{1,0:T(8,128)} %copy.42.b2, bf16[64,576]{1,0:T(8,128)(2,1)} %copy.43.k3, ...), custom_call_target="tpu_custom_call" | custom-call | tf_op jit(solution)/shard_map/pallas_call | solution.py:83
  105.1 2.4 %fusion = bf16[26,130,258]{2,0,1:T(8,128)(2,1)S(1)} fusion(bf16[130,32,384]{2,1,0:T(8,128)(2,1)} %shard_map.100, pred[130,258]{1,0:T(8,128)(4,1)S(1)} %bitcast.43), kind=kLoop, calls=%fused_computation.1 | loop fusion | flops 872040 | bytes 3521700 | tf_op jit(solution)/shard_map/jit(_where)/select_n | solution.py:191
  107.5 1.0 slice_convert_fusion.1
  108.5 0.2 slice_convert_fusion
  108.7 0.7 fusion.3
  109.4 1.2 %copy.46 = bf16[13,128,256]{2,1,0:T(8,128)(2,1)} copy(bf16[13,128,256]{2,0,1:T(8,128)(2,1)S(1)} %fusion.3) | data formatting | bytes 1703936 | tf_op jit(solution)/shard_map/convert_element_type | solution.py:195
  (5 shorter events, 0.1 us)
Async XLA Ops:
  4.5 27.6 %copy-start.9 = (f32[26]{0:T(128)S(1)}, f32[26]{0:T(128)}, u32[]{:S(2)}) copy-start(f32[26]{0:T(128)} %param.19) | copy-start | bytes 316
  4.5 28.3 %copy-start.6 = (f32[64]{0:T(128)S(1)}, f32[64]{0:T(128)}, u32[]{:S(2)}) copy-start(f32[64]{0:T(128)} %param.13) | copy-start | bytes 772
  4.5 29.0 %copy-start.7 = (f32[64]{0:T(128)S(1)}, f32[64]{0:T(128)}, u32[]{:S(2)}) copy-start(f32[64]{0:T(128)} %param.15) | copy-start | bytes 772
  4.5 29.7 %copy-start.8 = (f32[64]{0:T(128)S(1)}, f32[64]{0:T(128)}, u32[]{:S(2)}) copy-start(f32[64]{0:T(128)} %param.17) | copy-start | bytes 772
  4.5 30.4 %copy-start.5 = (bf16[64,13,3,3]{0,1,3,2:T(8,128)(2,1)S(1)}, bf16[64,13,3,3]{0,1,3,2:T(8,128)(2,1)}, u32[]{:S(2)}) copy-start(bf16[64,13,3,3]{0,1,3,2:T(8,128)(2,1)} %param.12) | copy-start | bytes 44932
  4.5 14.8 %collective-permute-start = (bf16[128,16,16]{2,1,0:T(8,128)(2,1)S(1)}, bf16[128,16,16]{2,1,0:T(8,128)(2,1)S(1)}, u32[]{:S(2)}, u32[]{:S(2)}) collective-permute-start(bf16[128,16,16]{2,1,0:T(8,128)(2,1)S(1)} %get-tuple-element.7), channel_id=1, source_target_pairs={{0,1},{1,2},{2,3},{3,4},{4,5},{5,6},{6,7},{7,8},{8,9},{9,10},{10,1... | collective-permute-start | bytes 196616 | tf_op jit(solution)/shard_map/ppermute | solution.py:156
  7.8 16.5 %collective-permute-start.1 = (bf16[128,16,16]{2,1,0:T(8,128)(2,1)S(1)}, bf16[128,16,16]{2,1,0:T(8,128)(2,1)S(1)}, u32[]{:S(2)}, u32[]{:S(2)}) collective-permute-start(bf16[128,16,16]{2,1,0:T(8,128)(2,1)S(1)} %get-tuple-element.8), channel_id=1, source_target_pairs={{1,0},{2,1},{3,2},{4,3},{5,4},{6,5},{7,6},{8,7},{9,8},{10,9},{11,1... | collective-permute-start | bytes 196616 | tf_op jit(solution)/shard_map/ppermute | solution.py:158
  10.0 27.3 %copy-start.4 = (bf16[64,64,3,3]{1,0,3,2:T(8,128)(2,1)S(1)}, bf16[64,64,3,3]{1,0,3,2:T(8,128)(2,1)}, u32[]{:S(2)}) copy-start(bf16[64,64,3,3]{1,0,3,2:T(8,128)(2,1)} %param.14) | copy-start | bytes 221188
  19.4 17.9 %copy-start.1 = (bf16[128,16,16]{2,1,0:T(8,128)(2,1)}, bf16[128,16,16]{2,1,0:T(8,128)(2,1)S(1)}, u32[]{:S(2)}) copy-start(bf16[128,16,16]{2,1,0:T(8,128)(2,1)S(1)} %collective-permute-done) | copy-start | bytes 196612
  24.3 13.0 %copy-start.2 = (bf16[128,16,16]{2,1,0:T(8,128)(2,1)}, bf16[128,16,16]{2,1,0:T(8,128)(2,1)S(1)}, u32[]{:S(2)}) copy-start(bf16[128,16,16]{2,1,0:T(8,128)(2,1)S(1)} %collective-permute-done.1) | copy-start | bytes 196612
  24.7 16.0 %collective-permute-start.2 = (bf16[16,16,384]{2,1,0:T(8,128)(2,1)S(1)}, bf16[16,16,384]{2,1,0:T(8,128)(2,1)S(1)}, u32[]{:S(2)}, u32[]{:S(2)}) collective-permute-start(bf16[16,16,384]{2,1,0:T(8,128)(2,1)S(1)} %get-tuple-element.5), channel_id=1, source_target_pairs={{0,16},{16,32},{32,48},{48,64},{64,80},{80,96},{96,112},{1,17},{17... | collective-permute-start | bytes 589832 | tf_op jit(solution)/shard_map/ppermute | solution.py:165
  29.9 11.4 %collective-permute-start.3 = (bf16[16,16,384]{2,1,0:T(8,128)(2,1)S(1)}, bf16[16,16,384]{2,1,0:T(8,128)(2,1)}, u32[]{:S(2)}, u32[]{:S(2)}) collective-permute-start(bf16[16,16,384]{2,1,0:T(8,128)(2,1)S(1)} %get-tuple-element.6), channel_id=1, source_target_pairs={{16,0},{32,16},{48,32},{64,48},{80,64},{96,80},{112,96},{17,1},{33... | collective-permute-start | bytes 589832 | tf_op jit(solution)/shard_map/ppermute | solution.py:167
  40.7 0.7 copy-start.3
  44.2 1.3 %copy-start = (bf16[160,16,384]{2,1,0:T(8,128)(2,1)}, bf16[160,16,384]{2,1,0:T(8,128)(2,1)S(1)}, u32[]{:S(2)}) copy-start(bf16[160,16,384]{2,1,0:T(8,128)(2,1)S(1)} %pad_maximum_fusion.x_ref) | copy-start | bytes 5898244

commit v14 on v11

--- a/solution.py
+++ b/solution.py
@@ -12,7 +12,7 @@
 LANES = 384
 
 
-def _net_kernel(lim_ref, x_ref, k1, b1, k2, b2, k3, b3, kf, bfl, out_ref, buf_a, buf_b):
+def _net_kernel(lim_ref, x_ref, k1, b1, k2, b2, k3, b3, kf, bfl, ring_ref, out_ref, buf_a, buf_b):
     lanes = lax.broadcasted_iota(jnp.int32, (1, LANES), 1)
 
     def layer(src, dst, n_rows, spread, kmat, bias, index, last):
@@ -36,7 +36,7 @@
             col = jnp.concatenate(pieces, axis=0)
             acc = jnp.dot(kv, col, preferred_element_type=jnp.float32) + bv
             if last:
-                dst[y] = acc[:, : dst.shape[2]].astype(dst.dtype)
+                dst[y, : acc.shape[0]] = jnp.where(ring_ref[y] > 0, acc, 0.0).astype(dst.dtype)
             else:
                 half = 0.5 * acc
                 act = half + half * jnp.tanh(half)
@@ -57,7 +57,17 @@
     layer(x_ref, buf_a, h1, 1, k1, b1, 0, False)
     layer(buf_a, buf_b, h2, 2, k2, b2, 1, False)
     layer(buf_b, buf_a, h3, 4, k3, b3, 2, False)
-    layer(buf_a, out_ref, h4, 8, kf, bfl, 3, True)
+    layer(buf_a, buf_b, h4, 8, kf, bfl, 3, True)
+    half_ch = kf.shape[0] // 2
+
+    def close(y, carry):
+        across = buf_b[y + 1, :half_ch].astype(jnp.float32)
+        down = buf_b[y + 2, half_ch : 2 * half_ch].astype(jnp.float32) - buf_b[y, half_ch : 2 * half_ch].astype(jnp.float32)
+        diff = (pltpu.roll(across, LANES - 2, 1) - across) + pltpu.roll(down, LANES - 1, 1)
+        out_ref[y] = (-0.5 * diff)[: out_ref.shape[1], : out_ref.shape[2]].astype(out_ref.dtype)
+        return carry
+
+    lax.fori_loop(0, h4 - 2, close, 0, unroll=8)
 
 
 def _kmat(kernel, cin):
@@ -66,24 +76,29 @@
     return k.transpose(0, 2, 3, 1).reshape(o, 9 * cin)
 
 
-def run_net(x, lims, layers, out_w, out_ch):
+def run_net(x, lims, ring, layers, out_w, out_ch):
     (k1, b1), (k2, b2), (k3, b3), (kf, bf) = layers
     hid = k1.shape[0]
     h0 = x.shape[0]
-    kf_p = jnp.pad(kf, ((0, out_ch - kf.shape[0]), (0, 0), (0, 0), (0, 0)))
-    bf_p = jnp.pad(bf, (0, out_ch - bf.shape[0]))
+    moments = kf.shape[0] // 2
+    gap = out_ch // 2 - moments
+    kf_p = jnp.concatenate(
+        [jnp.pad(part, ((0, gap), (0, 0), (0, 0), (0, 0))) for part in (kf[:moments], kf[moments:])], axis=0
+    )
+    bf_p = jnp.concatenate([jnp.pad(part, (0, gap)) for part in (bf[:moments], bf[moments:])])
     args = (
         lims, x,
         _kmat(k1, x.shape[1]), b1.reshape(-1, 1),
         _kmat(k2, hid), b2.reshape(-1, 1),
         _kmat(k3, hid), b3.reshape(-1, 1),
         _kmat(kf_p, hid), bf_p.reshape(-1, 1),
+        ring,
     )
     vspec = pl.BlockSpec(memory_space=pltpu.VMEM)
     return pl.pallas_call(
         _net_kernel,
-        out_shape=jax.ShapeDtypeStruct((h0 - 30, out_ch, out_w), jnp.bfloat16),
-        in_specs=[pl.BlockSpec(memory_space=pltpu.SMEM)] + [vspec] * 9,
+        out_shape=jax.ShapeDtypeStruct((h0 - 32, moments, out_w), jnp.bfloat16),
+        in_specs=[pl.BlockSpec(memory_space=pltpu.SMEM)] + [vspec] * 10,
         out_specs=vspec,
         scratch_shapes=[
             pltpu.VMEM((h0 - 2, 3 * hid, LANES), jnp.bfloat16),
@@ -186,13 +201,10 @@
         ]
     lims = jnp.stack(lims).astype(jnp.int32)
 
-    flux = run_net(x, lims, layers, LANES, 32)[:, : 2 * moments, : block_w + 2].transpose(1, 0, 2)
-    cell_mask = x[margin - 1 : margin + block_h + 1, moments, margin - 1 : margin + block_w + 1] > 0
-    rimmed = jnp.where(cell_mask[None], flux, jnp.zeros((), jnp.bfloat16))
-    across = rimmed[:moments, 1:-1, :].astype(jnp.float32)
-    downward = rimmed[moments:, :, 1:-1].astype(jnp.float32)
-    difference = across[:, :, 2:] - across[:, :, :-2] + (downward[:, 2:, :] - downward[:, :-2, :])
-    return (-0.5 * difference).astype(jnp.bfloat16)
+    ring = x[margin - 1 : margin + block_h + 1, moments : moments + 1, margin - 1 :].astype(jnp.float32)
+    ring = jnp.pad(ring, ((0, 0), (0, 0), (0, LANES - ring.shape[2])))
+    closure = run_net(x, lims, ring, layers, block_w, 32)
+    return closure.transpose(1, 0, 2)
 
 
 def solution(mesh):

time: 100 us -> 99.5 us (level)
  the two profiles are of different devices: /device:TPU:57 before, /device:TPU:7 now
where the time goes in v14:
time: 99.5 us; the launch traced here: 97.7 us
  Pallas kernels  61.3 us (62%)
  local copies, waits for them, and re-layouts  15.9 us (16%)
  starting transfers between devices  11.5 us (12%)
  other arithmetic  6.05 us (6%)
  waiting for transfers between devices  2.67 us (3%)
    pallas_call x1, Pallas kernels, run_net(): pl.pallas_call(_net_kernel, out_shape=jax.ShapeDtypeStruct((h0 - 32, mome...  61.3 us
    ppermute x1, starting transfers between devices, body(): lax.ppermute(marked[:, -margin:], 'row', [(i, i + 1) for i in range(row_c...  4.11 us
    ppermute x1, starting transfers between devices, body(): lax.ppermute(rows_done[:, :, -margin:], 'col', [(i, i + 1) for i in range...  3.11 us
    reshape x4, local copies, waits for them, and re-layouts, _kmat(): return k.transpose(0, 2, 3, 1).reshape(o, 9 * cin)  2.96 us
    concatenate x1, other arithmetic, body(): jnp.concatenate([lax.ppermute(rows_done[:, :, -margin:], 'col', [(i, i +...  2.75 us
    ppermute x1, waiting for transfers between devices, body(): lax.ppermute(rows_done[:, :, :margin], 'col', [(i + 1, i) for i in range(...  2.66 us
    transpose x1, local copies, waits for them, and re-layouts, body(): return closure.transpose(1, 0, 2)  2.41 us
    ppermute x1, starting transfers between devices, body(): lax.ppermute(rows_done[:, :, :margin], 'col', [(i + 1, i) for i in range(...  2.34 us
  transfers between devices with their start and end apart: 4, of which 1 were waited for; matrix products, arithmetic and copies ran while one was open for 9% of the time, Pallas kernels for 0%

profile of v14, /device:TPU:7, one launch (start us, length us, event | category | flops | bytes accessed | tf_op | source)
XLA Modules:
  0.0 97.7 jit_solution(932991349669726153)
XLA Ops:
  0.0 0.7 fusion.5
  0.7 0.7 compare_bitcast_fusion
  1.3 0.1 fusion.4
  1.5 0.1 reshape.50
  1.5 0.1 broadcast_in_dim.6
  1.7 0.0 copy-start.3
  1.7 0.0 copy-start.8
  1.7 0.1 convert_element_type.33
  1.8 0.0 copy-start.1
  1.8 0.0 copy-start.2
  1.8 1.7 %copy.51 = bf16[13,128,256]{2,0,1:T(8,128)(2,1)S(1)} copy(bf16[13,128,256]{2,1,0:T(8,128)(2,1)} %param.10) | data formatting | bytes 1703936 | tf_op args[0]
  3.5 0.0 copy-start.4
  3.5 0.0 copy-start.5
  3.5 0.0 copy-start.6
  3.5 0.0 copy-start.7
  3.6 0.0 copy-start.9
  3.6 0.1 broadcast_in_dim.7
  3.6 0.1 pad_maximum_fusion.2
  3.8 4.1 %collective-permute-start = (bf16[16,16,256]{2,0,1:T(8,128)(2,1)S(1)}, bf16[16,16,256]{2,0,1:T(8,128)(2,1)S(1)}, u32[]{:S(2)}, u32[]{:S(2)}) collective-permute-start(bf16[16,16,256]{2,0,1:T(8,128)(2,1)S(1)} %get-tuple-element.7), channel_id=1, source_target_pairs={{0,16},{16,32},{32,48},{48,64},{64,80},{80,96},{96,112},{1,17},{17... | collective-permute-start | bytes 393224 | tf_op jit(solution)/shard_map/ppermute | solution.py:170
  7.9 1.9 %collective-permute-start.1 = (bf16[16,16,256]{2,0,1:T(8,128)(2,1)S(1)}, bf16[16,16,256]{2,0,1:T(8,128)(2,1)S(1)}, u32[]{:S(2)}, u32[]{:S(2)}) collective-permute-start(bf16[16,16,256]{2,0,1:T(8,128)(2,1)S(1)} %get-tuple-element.8), channel_id=1, source_target_pairs={{16,0},{32,16},{48,32},{64,48},{80,64},{96,80},{112,96},{17,1},{33... | collective-permute-start | bytes 393224 | tf_op jit(solution)/shard_map/ppermute | solution.py:172
  9.9 0.0 copy-done.3
  9.9 0.0 copy-done.8
  9.9 0.1 slice_select_fusion
  10.0 0.1 copy.59
  10.1 0.7 reshape.48.kf
  10.8 0.0 copy-done.1
  10.8 0.1 copy.57
  10.9 0.8 copy.62.k2
  11.7 0.0 copy-done.2
  11.7 0.1 copy.58
  11.9 0.8 copy.64.k3
  12.6 0.0 copy-done.4
  12.6 0.7 copy.60.k1
  13.3 0.0 copy-done.5
  13.3 0.7 copy.61.b1
  14.1 0.0 copy-done.6
  14.1 0.7 copy.63.b2
  14.8 0.0 copy-done.7
  14.8 0.7 copy.65.b3
  15.5 0.0 copy-done.9
  15.5 0.1 slice.36
  15.6 0.0 collective-permute-done
  15.6 0.0 collective-permute-done.1
  15.6 0.6 maximum_bitcast_fusion
  16.2 0.3 fusion.8
  16.5 0.5 copy.53
  17.0 3.1 %collective-permute-start.2 = (bf16[160,16,16]{0,2,1:T(8,128)(2,1)S(1)}, bf16[160,16,16]{0,2,1:T(8,128)(2,1)S(1)}, u32[]{:S(2)}, u32[]{:S(2)}) collective-permute-start(bf16[160,16,16]{0,2,1:T(8,128)(2,1)S(1)} %copy.53), channel_id=1, source_target_pairs={{0,1},{1,2},{2,3},{3,4},{4,5},{5,6},{6,7},{7,8},{8,9},{9,10},{10,1... | collective-permute-start | bytes 245768 | tf_op jit(solution)/shard_map/ppermute | solution.py:181
  20.2 0.5 copy.54
  20.7 2.3 %collective-permute-start.3 = (bf16[160,16,16]{0,2,1:T(8,128)(2,1)S(1)}, bf16[160,16,16]{0,2,1:T(8,128)(2,1)S(1)}, u32[]{:S(2)}, u32[]{:S(2)}) collective-permute-start(bf16[160,16,16]{0,2,1:T(8,128)(2,1)S(1)} %copy.54), channel_id=1, source_target_pairs={{1,0},{2,1},{3,2},{4,3},{5,4},{6,5},{7,6},{8,7},{9,8},{10,9},{11,1... | collective-permute-start | bytes 245768 | tf_op jit(solution)/shard_map/ppermute | solution.py:183
  23.0 0.1 fusion.7
  23.1 0.7 copy.66.bfl
  23.8 0.1 pad.38.clone
  23.9 0.6 stack.67.lim_ref
  24.5 0.0 collective-permute-done.2
  24.5 1.3 %copy.55 = bf16[160,16,16]{2,1,0:T(8,128)(2,1)} copy(bf16[160,16,16]{0,2,1:T(8,128)(2,1)S(1)} %collective-permute-done.2) | data formatting | bytes 163840 | tf_op jit(solution)/shard_map/ppermute | solution.py:181
  25.9 2.7 %collective-permute-done.3 = bf16[160,16,16]{0,2,1:T(8,128)(2,1)S(1)} collective-permute-done((bf16[160,16,16]{0,2,1:T(8,128)(2,1)S(1)}, bf16[160,16,16]{0,2,1:T(8,128)(2,1)S(1)}, u32[]{:S(2)}, u32[]{:S(2)}) %collective-permute-start.3) | collective-permute-done | bytes 81952 | tf_op jit(solution)/shard_map/ppermute | solution.py:183
  28.5 1.3 %copy.56 = bf16[160,16,16]{2,1,0:T(8,128)(2,1)} copy(bf16[160,16,16]{0,2,1:T(8,128)(2,1)S(1)} %collective-permute-done.3) | data formatting | bytes 163840 | tf_op jit(solution)/shard_map/ppermute | solution.py:183
  29.8 2.8 %maximum_maximum_fusion.x_ref = bf16[160,16,384]{2,1,0:T(8,128)(2,1)S(1)} fusion(bf16[160,16,16]{2,1,0:T(8,128)(2,1)} %copy.56, bf16[160,16,256]{2,1,0:T(8,128)(2,1)S(1)} %maximum_bitcast_fusion, bf16[160,16,16]{2,1,0:T(8,128)(2,1)} %copy.55, bf16[384]{0:T(512)(128)(2,1)S(1)} %pad.38.clone), kind=kLoop, calls=%fused_computation | loop fusion | flops 7864320 | bytes 3441408 | tf_op jit(solution)/shard_map/concatenate | solution.py:179
  32.6 0.0 copy-start
  32.6 0.5 slice.40
  33.1 0.9 pad_convert_fusion.ring_ref
  34.0 0.0 copy-done
  34.0 61.3 %shard_map.100 = bf16[128,13,256]{2,1,0:T(8,128)(2,1)} custom-call(s32[16]{0:T(128)} %stack.67.lim_ref, bf16[160,16,384]{2,1,0:T(8,128)(2,1)} %copy-done, bf16[64,144]{1,0:T(8,128)(2,1)} %copy.60.k1, f32[64,1]{1,0:T(8,128)} %copy.61.b1, bf16[64,576]{1,0:T(8,128)(2,1)} %copy.62.k2, f32[64,1]{1,0:T(8,128)} %copy.63.b2, bf16[64,576]{1,0:T(8,128)(2,1)} %copy.64.k3, ...), custom_call_target="tpu_custom_call" | custom-call | tf_op jit(solution)/shard_map/pallas_call | solution.py:98
  95.3 2.4 %copy.67 = bf16[13,128,256]{2,1,0:T(8,128)(2,1)} copy(bf16[13,128,256]{2,0,1:T(8,128)(2,1)} %bitcast.37) | data formatting | bytes 1703936 | tf_op jit(solution)/shard_map/transpose | solution.py:207
  (6 shorter events, 0.1 us)
Async XLA Ops:
  1.7 8.2 %copy-start.3 = (bf16[26,64,3,3]{1,0,3,2:T(8,128)(2,1)S(1)}, bf16[26,64,3,3]{1,0,3,2:T(8,128)(2,1)}, u32[]{:S(2)}) copy-start(bf16[26,64,3,3]{1,0,3,2:T(8,128)(2,1)} %param.18) | copy-start | bytes 89860
  1.7 8.2 %copy-start.8 = (pred[16]{0:T(512)(128)(4,1)S(1)}, pred[16]{0:T(512)(128)(4,1)}, u32[]{:S(2)}) copy-start(pred[16]{0:T(512)(128)(4,1)} %constant.93.clone.1) | copy-start | bytes 52
  1.8 9.0 %copy-start.1 = (bf16[64,64,3,3]{1,0,3,2:T(8,128)(2,1)S(1)}, bf16[64,64,3,3]{1,0,3,2:T(8,128)(2,1)}, u32[]{:S(2)}) copy-start(bf16[64,64,3,3]{1,0,3,2:T(8,128)(2,1)} %param.14) | copy-start | bytes 221188
  1.8 9.9 %copy-start.2 = (bf16[64,64,3,3]{1,0,3,2:T(8,128)(2,1)S(1)}, bf16[64,64,3,3]{1,0,3,2:T(8,128)(2,1)}, u32[]{:S(2)}) copy-start(bf16[64,64,3,3]{1,0,3,2:T(8,128)(2,1)} %param.16) | copy-start | bytes 221188
  3.5 9.1 %copy-start.4 = (bf16[64,13,3,3]{0,1,3,2:T(8,128)(2,1)S(1)}, bf16[64,13,3,3]{0,1,3,2:T(8,128)(2,1)}, u32[]{:S(2)}) copy-start(bf16[64,13,3,3]{0,1,3,2:T(8,128)(2,1)} %param.12) | copy-start | bytes 44932
  3.5 9.8 %copy-start.5 = (f32[64]{0:T(128)S(1)}, f32[64]{0:T(128)}, u32[]{:S(2)}) copy-start(f32[64]{0:T(128)} %param.13) | copy-start | bytes 772
  3.5 10.5 %copy-start.6 = (f32[64]{0:T(128)S(1)}, f32[64]{0:T(128)}, u32[]{:S(2)}) copy-start(f32[64]{0:T(128)} %param.15) | copy-start | bytes 772
  3.5 11.2 %copy-start.7 = (f32[64]{0:T(128)S(1)}, f32[64]{0:T(128)}, u32[]{:S(2)}) copy-start(f32[64]{0:T(128)} %param.17) | copy-start | bytes 772
  3.6 11.9 %copy-start.9 = (f32[26]{0:T(128)S(1)}, f32[26]{0:T(128)}, u32[]{:S(2)}) copy-start(f32[26]{0:T(128)} %param.19) | copy-start | bytes 316
  3.8 11.8 %collective-permute-start = (bf16[16,16,256]{2,0,1:T(8,128)(2,1)S(1)}, bf16[16,16,256]{2,0,1:T(8,128)(2,1)S(1)}, u32[]{:S(2)}, u32[]{:S(2)}) collective-permute-start(bf16[16,16,256]{2,0,1:T(8,128)(2,1)S(1)} %get-tuple-element.7), channel_id=1, source_target_pairs={{0,16},{16,32},{32,48},{48,64},{64,80},{80,96},{96,112},{1,17},{17... | collective-permute-start | bytes 393224 | tf_op jit(solution)/shard_map/ppermute | solution.py:170
  7.9 7.7 %collective-permute-start.1 = (bf16[16,16,256]{2,0,1:T(8,128)(2,1)S(1)}, bf16[16,16,256]{2,0,1:T(8,128)(2,1)S(1)}, u32[]{:S(2)}, u32[]{:S(2)}) collective-permute-start(bf16[16,16,256]{2,0,1:T(8,128)(2,1)S(1)} %get-tuple-element.8), channel_id=1, source_target_pairs={{16,0},{32,16},{48,32},{64,48},{80,64},{96,80},{112,96},{17,1},{33... | collective-permute-start | bytes 393224 | tf_op jit(solution)/shard_map/ppermute | solution.py:172
  17.0 7.5 %collective-permute-start.2 = (bf16[160,16,16]{0,2,1:T(8,128)(2,1)S(1)}, bf16[160,16,16]{0,2,1:T(8,128)(2,1)S(1)}, u32[]{:S(2)}, u32[]{:S(2)}) collective-permute-start(bf16[160,16,16]{0,2,1:T(8,128)(2,1)S(1)} %copy.53), channel_id=1, source_target_pairs={{0,1},{1,2},{2,3},{3,4},{4,5},{5,6},{6,7},{7,8},{8,9},{9,10},{10,1... | collective-permute-start | bytes 245768 | tf_op jit(solution)/shard_map/ppermute | solution.py:181
  20.7 7.8 %collective-permute-start.3 = (bf16[160,16,16]{0,2,1:T(8,128)(2,1)S(1)}, bf16[160,16,16]{0,2,1:T(8,128)(2,1)S(1)}, u32[]{:S(2)}, u32[]{:S(2)}) collective-permute-start(bf16[160,16,16]{0,2,1:T(8,128)(2,1)S(1)} %copy.54), channel_id=1, source_target_pairs={{1,0},{2,1},{3,2},{4,3},{5,4},{6,5},{7,6},{8,7},{9,8},{10,9},{11,1... | collective-permute-start | bytes 245768 | tf_op jit(solution)/shard_map/ppermute | solution.py:183
  32.6 1.4 %copy-start = (bf16[160,16,384]{2,1,0:T(8,128)(2,1)}, bf16[160,16,384]{2,1,0:T(8,128)(2,1)S(1)}, u32[]{:S(2)}) copy-start(bf16[160,16,384]{2,1,0:T(8,128)(2,1)S(1)} %maximum_maximum_fusion.x_ref) | copy-start | bytes 5898244

commit v15 on v14

--- a/solution.py
+++ b/solution.py
@@ -60,14 +60,19 @@
     layer(buf_a, buf_b, h4, 8, kf, bfl, 3, True)
     half_ch = kf.shape[0] // 2
 
-    def close(y, carry):
+    def close_row(y):
         across = buf_b[y + 1, :half_ch].astype(jnp.float32)
         down = buf_b[y + 2, half_ch : 2 * half_ch].astype(jnp.float32) - buf_b[y, half_ch : 2 * half_ch].astype(jnp.float32)
         diff = (pltpu.roll(across, LANES - 2, 1) - across) + pltpu.roll(down, LANES - 1, 1)
-        out_ref[y] = (-0.5 * diff)[: out_ref.shape[1], : out_ref.shape[2]].astype(out_ref.dtype)
+        return (-0.5 * diff)[: out_ref.shape[0], : out_ref.shape[2]]
+
+    def close(t, carry):
+        y = pl.multiple_of(16 * t, 16)
+        group = jnp.stack([close_row(y + k) for k in range(16)], axis=1)
+        out_ref[:, pl.ds(y, 16), :] = group.astype(out_ref.dtype)
         return carry
 
-    lax.fori_loop(0, h4 - 2, close, 0, unroll=8)
+    lax.fori_loop(0, (h4 - 2) // 16, close, 0)
 
 
 def _kmat(kernel, cin):
@@ -97,7 +102,7 @@
     vspec = pl.BlockSpec(memory_space=pltpu.VMEM)
     return pl.pallas_call(
         _net_kernel,
-        out_shape=jax.ShapeDtypeStruct((h0 - 32, moments, out_w), jnp.bfloat16),
+        out_shape=jax.ShapeDtypeStruct((moments, h0 - 32, out_w), jnp.bfloat16),
         in_specs=[pl.BlockSpec(memory_space=pltpu.SMEM)] + [vspec] * 10,
         out_specs=vspec,
         scratch_shapes=[
@@ -204,7 +209,7 @@
     ring = x[margin - 1 : margin + block_h + 1, moments : moments + 1, margin - 1 :].astype(jnp.float32)
     ring = jnp.pad(ring, ((0, 0), (0, 0), (0, LANES - ring.shape[2])))
     closure = run_net(x, lims, ring, layers, block_w, 32)
-    return closure.transpose(1, 0, 2)
+    return closure
 
 
 def solution(mesh):

time: 99.5 us -> 97 us (0.975)
  local copies, waits for them, and re-layouts: 15.9 us -> 13.5 us
    transpose x1 -> x0, local copies, waits for them, and re-layouts: 2.41 us -> none  [body(): return closure.transpose(1, 0, 2)]
where the time goes in v15:
time: 97 us; the launch traced here: 95.3 us
  Pallas kernels  61.3 us (63%)
  local copies, waits for them, and re-layouts  13.5 us (14%)
  starting transfers between devices  11.5 us (12%)
  other arithmetic  6.06 us (6%)
  waiting for transfers between devices  2.68 us (3%)
    pallas_call x1, Pallas kernels, run_net(): pl.pallas_call(_net_kernel, out_shape=jax.ShapeDtypeStruct((moments, h0 -...  61.3 us
    ppermute x1, starting transfers between devices, body(): lax.ppermute(marked[:, -margin:], 'row', [(i, i + 1) for i in range(row_c...  4.11 us
    ppermute x1, starting transfers between devices, body(): lax.ppermute(rows_done[:, :, -margin:], 'col', [(i, i + 1) for i in range...  3.11 us
    reshape x4, local copies, waits for them, and re-layouts, _kmat(): return k.transpose(0, 2, 3, 1).reshape(o, 9 * cin)  2.95 us
    concatenate x1, other arithmetic, body(): jnp.concatenate([lax.ppermute(rows_done[:, :, -margin:], 'col', [(i, i +...  2.75 us
    ppermute x1, waiting for transfers between devices, body(): lax.ppermute(rows_done[:, :, :margin], 'col', [(i + 1, i) for i in range(...  2.67 us
    ppermute x1, starting transfers between devices, body(): lax.ppermute(rows_done[:, :, :margin], 'col', [(i + 1, i) for i in range(...  2.34 us
  transfers between devices with their start and end apart: 4, of which 1 were waited for; matrix products, arithmetic and copies ran while one was open for 9% of the time, Pallas kernels for 0%

profile of v15, /device:TPU:7, one launch (start us, length us, event | category | flops | bytes accessed | tf_op | source)
XLA Modules:
  0.0 95.3 jit_solution(5236501615725787699)
XLA Ops:
  0.0 0.7 fusion.5
  0.7 0.7 compare_bitcast_fusion
  1.3 0.1 fusion.4
  1.5 0.1 reshape.50
  1.5 0.1 broadcast_in_dim.6
  1.7 0.0 copy-start.3
  1.7 0.0 copy-start.8
  1.7 0.1 convert_element_type.33
  1.8 0.0 copy-start.1
  1.8 0.0 copy-start.2
  1.8 1.7 %copy.48 = bf16[13,128,256]{2,0,1:T(8,128)(2,1)S(1)} copy(bf16[13,128,256]{2,1,0:T(8,128)(2,1)} %param.10) | data formatting | bytes 1703936 | tf_op args[0]
  3.5 0.0 copy-start.4
  3.5 0.0 copy-start.5
  3.5 0.0 copy-start.6
  3.5 0.0 copy-start.7
  3.6 0.0 copy-start.9
  3.6 0.1 broadcast_in_dim.7
  3.6 0.1 pad_maximum_fusion.2
  3.8 4.1 %collective-permute-start = (bf16[16,16,256]{2,0,1:T(8,128)(2,1)S(1)}, bf16[16,16,256]{2,0,1:T(8,128)(2,1)S(1)}, u32[]{:S(2)}, u32[]{:S(2)}) collective-permute-start(bf16[16,16,256]{2,0,1:T(8,128)(2,1)S(1)} %get-tuple-element.7), channel_id=1, source_target_pairs={{0,16},{16,32},{32,48},{48,64},{64,80},{80,96},{96,112},{1,17},{17... | collective-permute-start | bytes 393224 | tf_op jit(solution)/shard_map/ppermute | solution.py:175
  7.9 1.9 %collective-permute-start.1 = (bf16[16,16,256]{2,0,1:T(8,128)(2,1)S(1)}, bf16[16,16,256]{2,0,1:T(8,128)(2,1)S(1)}, u32[]{:S(2)}, u32[]{:S(2)}) collective-permute-start(bf16[16,16,256]{2,0,1:T(8,128)(2,1)S(1)} %get-tuple-element.8), channel_id=1, source_target_pairs={{16,0},{32,16},{48,32},{64,48},{80,64},{96,80},{112,96},{17,1},{33... | collective-permute-start | bytes 393224 | tf_op jit(solution)/shard_map/ppermute | solution.py:177
  9.9 0.0 copy-done.3
  9.9 0.0 copy-done.8
  9.9 0.1 slice_select_fusion
  10.0 0.1 copy.56
  10.1 0.7 reshape.48.kf
  10.8 0.0 copy-done.1
  10.8 0.1 copy.54
  10.9 0.8 copy.59.k2
  11.7 0.0 copy-done.2
  11.7 0.1 copy.55
  11.9 0.8 copy.61.k3
  12.6 0.0 copy-done.4
  12.6 0.7 copy.57.k1
  13.3 0.0 copy-done.5
  13.3 0.7 copy.58.b1
  14.0 0.0 copy-done.6
  14.0 0.7 copy.60.b2
  14.7 0.0 copy-done.7
  14.7 0.7 copy.62.b3
  15.4 0.0 copy-done.9
  15.4 0.1 slice.36
  15.5 0.0 collective-permute-done
  15.5 0.0 collective-permute-done.1
  15.5 0.6 maximum_bitcast_fusion
  16.1 0.3 fusion.8
  16.5 0.5 copy.50
  17.0 3.1 %collective-permute-start.2 = (bf16[160,16,16]{0,2,1:T(8,128)(2,1)S(1)}, bf16[160,16,16]{0,2,1:T(8,128)(2,1)S(1)}, u32[]{:S(2)}, u32[]{:S(2)}) collective-permute-start(bf16[160,16,16]{0,2,1:T(8,128)(2,1)S(1)} %copy.50), channel_id=1, source_target_pairs={{0,1},{1,2},{2,3},{3,4},{4,5},{5,6},{6,7},{7,8},{8,9},{9,10},{10,1... | collective-permute-start | bytes 245768 | tf_op jit(solution)/shard_map/ppermute | solution.py:186
  20.1 0.5 copy.51
  20.7 2.3 %collective-permute-start.3 = (bf16[160,16,16]{0,2,1:T(8,128)(2,1)S(1)}, bf16[160,16,16]{0,2,1:T(8,128)(2,1)S(1)}, u32[]{:S(2)}, u32[]{:S(2)}) collective-permute-start(bf16[160,16,16]{0,2,1:T(8,128)(2,1)S(1)} %copy.51), channel_id=1, source_target_pairs={{1,0},{2,1},{3,2},{4,3},{5,4},{6,5},{7,6},{8,7},{9,8},{10,9},{11,1... | collective-permute-start | bytes 245768 | tf_op jit(solution)/shard_map/ppermute | solution.py:188
  23.0 0.1 fusion.7
  23.1 0.7 copy.63.bfl
  23.8 0.1 pad.38.clone
  23.9 0.6 stack.67.lim_ref
  24.5 0.0 collective-permute-done.2
  24.5 1.3 %copy.52 = bf16[160,16,16]{2,1,0:T(8,128)(2,1)} copy(bf16[160,16,16]{0,2,1:T(8,128)(2,1)S(1)} %collective-permute-done.2) | data formatting | bytes 163840 | tf_op jit(solution)/shard_map/ppermute | solution.py:186
  25.8 2.7 %collective-permute-done.3 = bf16[160,16,16]{0,2,1:T(8,128)(2,1)S(1)} collective-permute-done((bf16[160,16,16]{0,2,1:T(8,128)(2,1)S(1)}, bf16[160,16,16]{0,2,1:T(8,128)(2,1)S(1)}, u32[]{:S(2)}, u32[]{:S(2)}) %collective-permute-start.3) | collective-permute-done | bytes 81952 | tf_op jit(solution)/shard_map/ppermute | solution.py:188
  28.5 1.3 %copy.53 = bf16[160,16,16]{2,1,0:T(8,128)(2,1)} copy(bf16[160,16,16]{0,2,1:T(8,128)(2,1)S(1)} %collective-permute-done.3) | data formatting | bytes 163840 | tf_op jit(solution)/shard_map/ppermute | solution.py:188
  29.8 2.8 %maximum_maximum_fusion.x_ref = bf16[160,16,384]{2,1,0:T(8,128)(2,1)S(1)} fusion(bf16[160,16,16]{2,1,0:T(8,128)(2,1)} %copy.53, bf16[160,16,256]{2,1,0:T(8,128)(2,1)S(1)} %maximum_bitcast_fusion, bf16[160,16,16]{2,1,0:T(8,128)(2,1)} %copy.52, bf16[384]{0:T(512)(128)(2,1)S(1)} %pad.38.clone), kind=kLoop, calls=%fused_computation | loop fusion | flops 7864320 | bytes 3441408 | tf_op jit(solution)/shard_map/concatenate | solution.py:184
  32.6 0.0 copy-start
  32.6 0.5 slice.40
  33.0 0.9 pad_convert_fusion.ring_ref
  33.9 0.0 copy-done
  33.9 61.3 %shard_map.100 = bf16[13,128,256]{2,1,0:T(8,128)(2,1)} custom-call(s32[16]{0:T(128)} %stack.67.lim_ref, bf16[160,16,384]{2,1,0:T(8,128)(2,1)} %copy-done, bf16[64,144]{1,0:T(8,128)(2,1)} %copy.57.k1, f32[64,1]{1,0:T(8,128)} %copy.58.b1, bf16[64,576]{1,0:T(8,128)(2,1)} %copy.59.k2, f32[64,1]{1,0:T(8,128)} %copy.60.b2, bf16[64,576]{1,0:T(8,128)(2,1)} %copy.61.k3, ...), custom_call_target="tpu_custom_call" | custom-call | tf_op jit(solution)/shard_map/pallas_call | solution.py:103
  (6 shorter events, 0.1 us)
Async XLA Ops:
  1.7 8.2 %copy-start.3 = (bf16[26,64,3,3]{1,0,3,2:T(8,128)(2,1)S(1)}, bf16[26,64,3,3]{1,0,3,2:T(8,128)(2,1)}, u32[]{:S(2)}) copy-start(bf16[26,64,3,3]{1,0,3,2:T(8,128)(2,1)} %param.18) | copy-start | bytes 89860
  1.7 8.2 %copy-start.8 = (pred[16]{0:T(512)(128)(4,1)S(1)}, pred[16]{0:T(512)(128)(4,1)}, u32[]{:S(2)}) copy-start(pred[16]{0:T(512)(128)(4,1)} %constant.93.clone.1) | copy-start | bytes 52
  1.8 9.0 %copy-start.1 = (bf16[64,64,3,3]{1,0,3,2:T(8,128)(2,1)S(1)}, bf16[64,64,3,3]{1,0,3,2:T(8,128)(2,1)}, u32[]{:S(2)}) copy-start(bf16[64,64,3,3]{1,0,3,2:T(8,128)(2,1)} %param.14) | copy-start | bytes 221188
  1.8 9.9 %copy-start.2 = (bf16[64,64,3,3]{1,0,3,2:T(8,128)(2,1)S(1)}, bf16[64,64,3,3]{1,0,3,2:T(8,128)(2,1)}, u32[]{:S(2)}) copy-start(bf16[64,64,3,3]{1,0,3,2:T(8,128)(2,1)} %param.16) | copy-start | bytes 221188
  3.5 9.1 %copy-start.4 = (bf16[64,13,3,3]{0,1,3,2:T(8,128)(2,1)S(1)}, bf16[64,13,3,3]{0,1,3,2:T(8,128)(2,1)}, u32[]{:S(2)}) copy-start(bf16[64,13,3,3]{0,1,3,2:T(8,128)(2,1)} %param.12) | copy-start | bytes 44932
  3.5 9.8 %copy-start.5 = (f32[64]{0:T(128)S(1)}, f32[64]{0:T(128)}, u32[]{:S(2)}) copy-start(f32[64]{0:T(128)} %param.13) | copy-start | bytes 772
  3.5 10.5 %copy-start.6 = (f32[64]{0:T(128)S(1)}, f32[64]{0:T(128)}, u32[]{:S(2)}) copy-start(f32[64]{0:T(128)} %param.15) | copy-start | bytes 772
  3.5 11.2 %copy-start.7 = (f32[64]{0:T(128)S(1)}, f32[64]{0:T(128)}, u32[]{:S(2)}) copy-start(f32[64]{0:T(128)} %param.17) | copy-start | bytes 772
  3.6 11.9 %copy-start.9 = (f32[26]{0:T(128)S(1)}, f32[26]{0:T(128)}, u32[]{:S(2)}) copy-start(f32[26]{0:T(128)} %param.19) | copy-start | bytes 316
  3.8 11.7 %collective-permute-start = (bf16[16,16,256]{2,0,1:T(8,128)(2,1)S(1)}, bf16[16,16,256]{2,0,1:T(8,128)(2,1)S(1)}, u32[]{:S(2)}, u32[]{:S(2)}) collective-permute-start(bf16[16,16,256]{2,0,1:T(8,128)(2,1)S(1)} %get-tuple-element.7), channel_id=1, source_target_pairs={{0,16},{16,32},{32,48},{48,64},{64,80},{80,96},{96,112},{1,17},{17... | collective-permute-start | bytes 393224 | tf_op jit(solution)/shard_map/ppermute | solution.py:175
  7.9 7.6 %collective-permute-start.1 = (bf16[16,16,256]{2,0,1:T(8,128)(2,1)S(1)}, bf16[16,16,256]{2,0,1:T(8,128)(2,1)S(1)}, u32[]{:S(2)}, u32[]{:S(2)}) collective-permute-start(bf16[16,16,256]{2,0,1:T(8,128)(2,1)S(1)} %get-tuple-element.8), channel_id=1, source_target_pairs={{16,0},{32,16},{48,32},{64,48},{80,64},{96,80},{112,96},{17,1},{33... | collective-permute-start | bytes 393224 | tf_op jit(solution)/shard_map/ppermute | solution.py:177
  17.0 7.5 %collective-permute-start.2 = (bf16[160,16,16]{0,2,1:T(8,128)(2,1)S(1)}, bf16[160,16,16]{0,2,1:T(8,128)(2,1)S(1)}, u32[]{:S(2)}, u32[]{:S(2)}) collective-permute-start(bf16[160,16,16]{0,2,1:T(8,128)(2,1)S(1)} %copy.50), channel_id=1, source_target_pairs={{0,1},{1,2},{2,3},{3,4},{4,5},{5,6},{6,7},{7,8},{8,9},{9,10},{10,1... | collective-permute-start | bytes 245768 | tf_op jit(solution)/shard_map/ppermute | solution.py:186
  20.7 7.8 %collective-permute-start.3 = (bf16[160,16,16]{0,2,1:T(8,128)(2,1)S(1)}, bf16[160,16,16]{0,2,1:T(8,128)(2,1)S(1)}, u32[]{:S(2)}, u32[]{:S(2)}) collective-permute-start(bf16[160,16,16]{0,2,1:T(8,128)(2,1)S(1)} %copy.51), channel_id=1, source_target_pairs={{1,0},{2,1},{3,2},{4,3},{5,4},{6,5},{7,6},{8,7},{9,8},{10,9},{11,1... | collective-permute-start | bytes 245768 | tf_op jit(solution)/shard_map/ppermute | solution.py:188
  32.6 1.4 %copy-start = (bf16[160,16,384]{2,1,0:T(8,128)(2,1)}, bf16[160,16,384]{2,1,0:T(8,128)(2,1)S(1)}, u32[]{:S(2)}) copy-start(bf16[160,16,384]{2,1,0:T(8,128)(2,1)S(1)} %maximum_maximum_fusion.x_ref) | copy-start | bytes 5898244

commit v16 on v15

--- a/solution.py
+++ b/solution.py
@@ -1,3 +1,4 @@
+import functools
 import jax
 import jax.numpy as jnp
 from jax import lax
@@ -12,7 +13,7 @@
 LANES = 384
 
 
-def _net_kernel(lim_ref, x_ref, k1, b1, k2, b2, k3, b3, kf, bfl, ring_ref, out_ref, buf_a, buf_b):
+def _net_kernel(mark, lim_ref, x_ref, k1, b1, k2, b2, k3, b3, kf, bfl, out_ref, buf_a, buf_b):
     lanes = lax.broadcasted_iota(jnp.int32, (1, LANES), 1)
 
     def layer(src, dst, n_rows, spread, kmat, bias, index, last):
@@ -36,7 +37,10 @@
             col = jnp.concatenate(pieces, axis=0)
             acc = jnp.dot(kv, col, preferred_element_type=jnp.float32) + bv
             if last:
-                dst[y, : acc.shape[0]] = jnp.where(ring_ref[y] > 0, acc, 0.0).astype(dst.dtype)
+                reach = sum(dilations)
+                flag = x_ref[y + reach].astype(jnp.float32)[mark : mark + 1]
+                flag = pltpu.roll(flag, LANES - reach, 1)
+                dst[y, : acc.shape[0]] = jnp.where(flag > 0, acc, 0.0).astype(dst.dtype)
             else:
                 half = 0.5 * acc
                 act = half + half * jnp.tanh(half)
@@ -81,7 +85,7 @@
     return k.transpose(0, 2, 3, 1).reshape(o, 9 * cin)
 
 
-def run_net(x, lims, ring, layers, out_w, out_ch):
+def run_net(x, lims, layers, out_w, out_ch):
     (k1, b1), (k2, b2), (k3, b3), (kf, bf) = layers
     hid = k1.shape[0]
     h0 = x.shape[0]
@@ -97,13 +101,12 @@
         _kmat(k2, hid), b2.reshape(-1, 1),
         _kmat(k3, hid), b3.reshape(-1, 1),
         _kmat(kf_p, hid), bf_p.reshape(-1, 1),
-        ring,
     )
     vspec = pl.BlockSpec(memory_space=pltpu.VMEM)
     return pl.pallas_call(
-        _net_kernel,
+        functools.partial(_net_kernel, moments),
         out_shape=jax.ShapeDtypeStruct((moments, h0 - 32, out_w), jnp.bfloat16),
-        in_specs=[pl.BlockSpec(memory_space=pltpu.SMEM)] + [vspec] * 10,
+        in_specs=[pl.BlockSpec(memory_space=pltpu.SMEM)] + [vspec] * 9,
         out_specs=vspec,
         scratch_shapes=[
             pltpu.VMEM((h0 - 2, 3 * hid, LANES), jnp.bfloat16),
@@ -206,9 +209,7 @@
         ]
     lims = jnp.stack(lims).astype(jnp.int32)
 
-    ring = x[margin - 1 : margin + block_h + 1, moments : moments + 1, margin - 1 :].astype(jnp.float32)
-    ring = jnp.pad(ring, ((0, 0), (0, 0), (0, LANES - ring.shape[2])))
-    closure = run_net(x, lims, ring, layers, block_w, 32)
+    closure = run_net(x, lims, layers, block_w, 32)
     return closure
 
 

time: 97 us -> 94.8 us (0.977)
  local copies, waits for them, and re-layouts: 13.5 us -> 11.4 us
  other arithmetic: 6.06 us -> 5.07 us
where the time goes in v16:
time: 94.8 us; the launch traced here: 93.1 us
  Pallas kernels  61.3 us (65%)
  local copies, waits for them, and re-layouts  11.4 us (12%)
  starting transfers between devices  11.3 us (12%)
  other arithmetic  5.07 us (5%)
  waiting for transfers between devices  3.65 us (4%)
    pallas_call x1, Pallas kernels, run_net(): pl.pallas_call(functools.partial(_net_kernel, moments), out_shape=jax.Sha...  61.3 us
    ppermute x1, starting transfers between devices, body(): lax.ppermute(marked[:, -margin:], 'row', [(i, i + 1) for i in range(row_c...  4.11 us
    ppermute x1, waiting for transfers between devices, body(): lax.ppermute(rows_done[:, :, :margin], 'col', [(i + 1, i) for i in range(...  3.64 us
    ppermute x1, starting transfers between devices, body(): lax.ppermute(rows_done[:, :, -margin:], 'col', [(i, i + 1) for i in range...  3.11 us
    reshape x4, local copies, waits for them, and re-layouts, _kmat(): return k.transpose(0, 2, 3, 1).reshape(o, 9 * cin)  2.97 us
    concatenate x1, other arithmetic, body(): jnp.concatenate([lax.ppermute(rows_done[:, :, -margin:], 'col', [(i, i +...  2.68 us
    ppermute x1, starting transfers between devices, body(): lax.ppermute(rows_done[:, :, :margin], 'col', [(i + 1, i) for i in range(...  2.16 us
    ppermute x1, starting transfers between devices, body(): lax.ppermute(marked[:, :margin], 'row', [(i + 1, i) for i in range(row_co...  1.92 us
  transfers between devices with their start and end apart: 4, of which 1 were waited for; matrix products, arithmetic and copies ran while one was open for 9% of the time, Pallas kernels for 0%

profile of v16, /device:TPU:7, one launch (start us, length us, event | category | flops | bytes accessed | tf_op | source)
XLA Modules:
  0.0 93.1 jit_solution(9399241653956738914)
XLA Ops:
  0.0 0.7 fusion.5
  0.7 0.7 compare_bitcast_fusion
  1.3 0.1 fusion.4
  1.5 0.1 reshape.50
  1.5 0.1 broadcast_in_dim.6
  1.7 0.0 copy-start.2
  1.7 0.0 copy-start.7
  1.7 0.1 convert_element_type.30
  1.8 0.0 copy-start
  1.8 0.0 copy-start.1
  1.8 1.7 %copy.48 = bf16[13,128,256]{2,0,1:T(8,128)(2,1)S(1)} copy(bf16[13,128,256]{2,1,0:T(8,128)(2,1)} %param.10) | data formatting | bytes 1703936 | tf_op args[0]
  3.5 0.0 copy-start.3
  3.5 0.0 copy-start.4
  3.5 0.0 copy-start.5
  3.5 0.0 copy-start.6
  3.6 0.0 copy-start.8
  3.6 0.1 broadcast_in_dim.7
  3.6 0.1 pad_maximum_fusion.2
  3.8 4.1 %collective-permute-start = (bf16[16,16,256]{2,0,1:T(8,128)(2,1)S(1)}, bf16[16,16,256]{2,0,1:T(8,128)(2,1)S(1)}, u32[]{:S(2)}, u32[]{:S(2)}) collective-permute-start(bf16[16,16,256]{2,0,1:T(8,128)(2,1)S(1)} %get-tuple-element.7), channel_id=1, source_target_pairs={{0,16},{16,32},{32,48},{48,64},{64,80},{80,96},{96,112},{1,17},{17... | collective-permute-start | bytes 393224 | tf_op jit(solution)/shard_map/ppermute | solution.py:178
  7.9 1.9 %collective-permute-start.1 = (bf16[16,16,256]{2,0,1:T(8,128)(2,1)S(1)}, bf16[16,16,256]{2,0,1:T(8,128)(2,1)S(1)}, u32[]{:S(2)}, u32[]{:S(2)}) collective-permute-start(bf16[16,16,256]{2,0,1:T(8,128)(2,1)S(1)} %get-tuple-element.8), channel_id=1, source_target_pairs={{16,0},{32,16},{48,32},{64,48},{80,64},{96,80},{112,96},{17,1},{33... | collective-permute-start | bytes 393224 | tf_op jit(solution)/shard_map/ppermute | solution.py:180
  9.9 0.0 copy-done.2
  9.9 0.0 copy-done.7
  9.9 0.1 slice_select_fusion
  10.0 0.1 copy.56
  10.1 0.7 reshape.48.kf
  10.8 0.0 copy-done
  10.8 0.1 copy.54
  10.9 0.8 copy.59.k2
  11.7 0.0 copy-done.1
  11.7 0.1 copy.55
  11.9 0.8 copy.61.k3
  12.6 0.0 copy-done.3
  12.7 0.7 copy.57.k1
  13.4 0.0 copy-done.4
  13.4 0.7 copy.58.b1
  14.1 0.0 copy-done.5
  14.1 0.7 copy.60.b2
  14.8 0.0 copy-done.6
  14.8 0.7 copy.62.b3
  15.4 0.0 copy-done.8
  15.4 0.1 slice.33
  15.5 0.0 collective-permute-done
  15.5 0.0 collective-permute-done.1
  15.5 0.6 maximum_bitcast_fusion
  16.2 0.3 fusion.8
  16.5 0.5 copy.50
  17.0 3.1 %collective-permute-start.2 = (bf16[160,16,16]{0,2,1:T(8,128)(2,1)S(1)}, bf16[160,16,16]{0,2,1:T(8,128)(2,1)S(1)}, u32[]{:S(2)}, u32[]{:S(2)}) collective-permute-start(bf16[160,16,16]{0,2,1:T(8,128)(2,1)S(1)} %copy.50), channel_id=1, source_target_pairs={{0,1},{1,2},{2,3},{3,4},{4,5},{5,6},{6,7},{7,8},{8,9},{9,10},{10,1... | collective-permute-start | bytes 245768 | tf_op jit(solution)/shard_map/ppermute | solution.py:189
  20.1 0.5 copy.51
  20.7 2.2 %collective-permute-start.3 = (bf16[160,16,16]{0,2,1:T(8,128)(2,1)S(1)}, bf16[160,16,16]{0,2,1:T(8,128)(2,1)S(1)}, u32[]{:S(2)}, u32[]{:S(2)}) collective-permute-start(bf16[160,16,16]{0,2,1:T(8,128)(2,1)S(1)} %copy.51), channel_id=1, source_target_pairs={{1,0},{2,1},{3,2},{4,3},{5,4},{6,5},{7,6},{8,7},{9,8},{10,9},{11,1... | collective-permute-start | bytes 245768 | tf_op jit(solution)/shard_map/ppermute | solution.py:191
  22.8 0.1 fusion.7
  22.9 0.7 copy.63.bfl
  23.6 0.1 pad.30.clone
  23.7 0.6 stack.67.lim_ref
  24.3 0.0 collective-permute-done.2
  24.3 0.5 copy.52
  24.9 3.6 %collective-permute-done.3 = bf16[160,16,16]{0,2,1:T(8,128)(2,1)S(1)} collective-permute-done((bf16[160,16,16]{0,2,1:T(8,128)(2,1)S(1)}, bf16[160,16,16]{0,2,1:T(8,128)(2,1)S(1)}, u32[]{:S(2)}, u32[]{:S(2)}) %collective-permute-start.3) | collective-permute-done | bytes 81952 | tf_op jit(solution)/shard_map/ppermute | solution.py:191
  28.5 0.5 copy.53
  29.0 2.7 %maximum_maximum_fusion.x_ref = bf16[160,16,384]{2,1,0:T(8,128)(2,1)} fusion(bf16[160,16,16]{2,1,0:T(8,128)(2,1)S(1)} %copy.53, bf16[160,16,256]{2,1,0:T(8,128)(2,1)S(1)} %maximum_bitcast_fusion, bf16[160,16,16]{2,1,0:T(8,128)(2,1)S(1)} %copy.52, bf16[384]{0:T(512)(128)(2,1)S(1)} %pad.30.clone), kind=kLoop, calls=%fused_computation | loop fusion | flops 7864320 | bytes 3441408 | tf_op jit(solution)/shard_map/concatenate | solution.py:187
  31.7 61.3 %shard_map.100 = bf16[13,128,256]{2,1,0:T(8,128)(2,1)} custom-call(s32[16]{0:T(128)} %stack.67.lim_ref, bf16[160,16,384]{2,1,0:T(8,128)(2,1)} %maximum_maximum_fusion.x_ref, bf16[64,144]{1,0:T(8,128)(2,1)} %copy.57.k1, f32[64,1]{1,0:T(8,128)} %copy.58.b1, bf16[64,576]{1,0:T(8,128)(2,1)} %copy.59.k2, f32[64,1]{1,0:T(8,128)} %copy.60.b2, ...), custom_call_target="tpu_custom_call" | custom-call | tf_op jit(solution)/shard_map/pallas_call | solution.py:106
  (6 shorter events, 0.1 us)
Async XLA Ops:
  1.7 8.2 %copy-start.2 = (bf16[26,64,3,3]{1,0,3,2:T(8,128)(2,1)S(1)}, bf16[26,64,3,3]{1,0,3,2:T(8,128)(2,1)}, u32[]{:S(2)}) copy-start(bf16[26,64,3,3]{1,0,3,2:T(8,128)(2,1)} %param.18) | copy-start | bytes 89860
  1.7 8.2 %copy-start.7 = (pred[16]{0:T(512)(128)(4,1)S(1)}, pred[16]{0:T(512)(128)(4,1)}, u32[]{:S(2)}) copy-start(pred[16]{0:T(512)(128)(4,1)} %constant.92.clone.1) | copy-start | bytes 52
  1.8 9.0 %copy-start = (bf16[64,64,3,3]{1,0,3,2:T(8,128)(2,1)S(1)}, bf16[64,64,3,3]{1,0,3,2:T(8,128)(2,1)}, u32[]{:S(2)}) copy-start(bf16[64,64,3,3]{1,0,3,2:T(8,128)(2,1)} %param.14) | copy-start | bytes 221188
  1.8 9.9 %copy-start.1 = (bf16[64,64,3,3]{1,0,3,2:T(8,128)(2,1)S(1)}, bf16[64,64,3,3]{1,0,3,2:T(8,128)(2,1)}, u32[]{:S(2)}) copy-start(bf16[64,64,3,3]{1,0,3,2:T(8,128)(2,1)} %param.16) | copy-start | bytes 221188
  3.5 9.1 %copy-start.3 = (bf16[64,13,3,3]{0,1,3,2:T(8,128)(2,1)S(1)}, bf16[64,13,3,3]{0,1,3,2:T(8,128)(2,1)}, u32[]{:S(2)}) copy-start(bf16[64,13,3,3]{0,1,3,2:T(8,128)(2,1)} %param.12) | copy-start | bytes 44932
  3.5 9.8 %copy-start.4 = (f32[64]{0:T(128)S(1)}, f32[64]{0:T(128)}, u32[]{:S(2)}) copy-start(f32[64]{0:T(128)} %param.13) | copy-start | bytes 772
  3.5 10.5 %copy-start.5 = (f32[64]{0:T(128)S(1)}, f32[64]{0:T(128)}, u32[]{:S(2)}) copy-start(f32[64]{0:T(128)} %param.15) | copy-start | bytes 772
  3.5 11.2 %copy-start.6 = (f32[64]{0:T(128)S(1)}, f32[64]{0:T(128)}, u32[]{:S(2)}) copy-start(f32[64]{0:T(128)} %param.17) | copy-start | bytes 772
  3.6 11.9 %copy-start.8 = (f32[26]{0:T(128)S(1)}, f32[26]{0:T(128)}, u32[]{:S(2)}) copy-start(f32[26]{0:T(128)} %param.19) | copy-start | bytes 316
  3.8 11.7 %collective-permute-start = (bf16[16,16,256]{2,0,1:T(8,128)(2,1)S(1)}, bf16[16,16,256]{2,0,1:T(8,128)(2,1)S(1)}, u32[]{:S(2)}, u32[]{:S(2)}) collective-permute-start(bf16[16,16,256]{2,0,1:T(8,128)(2,1)S(1)} %get-tuple-element.7), channel_id=1, source_target_pairs={{0,16},{16,32},{32,48},{48,64},{64,80},{80,96},{96,112},{1,17},{17... | collective-permute-start | bytes 393224 | tf_op jit(solution)/shard_map/ppermute | solution.py:178
  7.9 7.6 %collective-permute-start.1 = (bf16[16,16,256]{2,0,1:T(8,128)(2,1)S(1)}, bf16[16,16,256]{2,0,1:T(8,128)(2,1)S(1)}, u32[]{:S(2)}, u32[]{:S(2)}) collective-permute-start(bf16[16,16,256]{2,0,1:T(8,128)(2,1)S(1)} %get-tuple-element.8), channel_id=1, source_target_pairs={{16,0},{32,16},{48,32},{64,48},{80,64},{96,80},{112,96},{17,1},{33... | collective-permute-start | bytes 393224 | tf_op jit(solution)/shard_map/ppermute | solution.py:180
  17.0 7.3 %collective-permute-start.2 = (bf16[160,16,16]{0,2,1:T(8,128)(2,1)S(1)}, bf16[160,16,16]{0,2,1:T(8,128)(2,1)S(1)}, u32[]{:S(2)}, u32[]{:S(2)}) collective-permute-start(bf16[160,16,16]{0,2,1:T(8,128)(2,1)S(1)} %copy.50), channel_id=1, source_target_pairs={{0,1},{1,2},{2,3},{3,4},{4,5},{5,6},{6,7},{7,8},{8,9},{9,10},{10,1... | collective-permute-start | bytes 245768 | tf_op jit(solution)/shard_map/ppermute | solution.py:189
  20.7 7.8 %collective-permute-start.3 = (bf16[160,16,16]{0,2,1:T(8,128)(2,1)S(1)}, bf16[160,16,16]{0,2,1:T(8,128)(2,1)S(1)}, u32[]{:S(2)}, u32[]{:S(2)}) collective-permute-start(bf16[160,16,16]{0,2,1:T(8,128)(2,1)S(1)} %copy.51), channel_id=1, source_target_pairs={{1,0},{2,1},{3,2},{4,3},{5,4},{6,5},{7,6},{8,7},{9,8},{10,9},{11,1... | collective-permute-start | bytes 245768 | tf_op jit(solution)/shard_map/ppermute | solution.py:191

commit v17 on v16

--- a/solution.py
+++ b/solution.py
@@ -51,14 +51,14 @@
                 )
             return carry
 
-        lax.fori_loop(0, n_rows, row, 0, unroll=(8, 14, 16, 16)[index])
-
-    h0 = x_ref.shape[0]
+        lax.fori_loop(0, n_rows, row, 0, unroll=(8, 14, 16, 13)[index])
+
+    h0 = x_ref.shape[0] - 2
     h1 = h0 - 2
     h2 = h1 - 4
     h3 = h2 - 8
     h4 = h3 - 16
-    layer(x_ref, buf_a, h1, 1, k1, b1, 0, False)
+    layer(x_ref, buf_a, h1 + 2, 1, k1, b1, 0, False)
     layer(buf_a, buf_b, h2, 2, k2, b2, 1, False)
     layer(buf_b, buf_a, h3, 4, k3, b3, 2, False)
     layer(buf_a, buf_b, h4, 8, kf, bfl, 3, True)
@@ -88,7 +88,7 @@
 def run_net(x, lims, layers, out_w, out_ch):
     (k1, b1), (k2, b2), (k3, b3), (kf, bf) = layers
     hid = k1.shape[0]
-    h0 = x.shape[0]
+    h0 = x.shape[0] - 2
     moments = kf.shape[0] // 2
     gap = out_ch // 2 - moments
     kf_p = jnp.concatenate(
@@ -109,7 +109,7 @@
         in_specs=[pl.BlockSpec(memory_space=pltpu.SMEM)] + [vspec] * 9,
         out_specs=vspec,
         scratch_shapes=[
-            pltpu.VMEM((h0 - 2, 3 * hid, LANES), jnp.bfloat16),
+            pltpu.VMEM((h0, 3 * hid, LANES), jnp.bfloat16),
             pltpu.VMEM((h0 - 6, 3 * hid, LANES), jnp.bfloat16),
         ],
         compiler_params=pltpu.CompilerParams(vmem_limit_bytes=60 * 1024 * 1024),
@@ -193,6 +193,7 @@
         ],
         axis=2,
     )
+    x = jnp.concatenate([x, jnp.zeros((2,) + x.shape[1:], x.dtype)], axis=0)
     lims = []
     offset = margin
     out_h, out_w = ext_h, ext_w

time: 94.8 us -> 93.9 us (level)
  local copies, waits for them, and re-layouts: 11.4 us -> 12.9 us
  other arithmetic: 5.07 us -> 3.81 us
  Pallas kernels: 61.3 us -> 60.2 us
    concatenate x0 -> x1, local copies, waits for them, and re-layouts: none -> 1.51 us  [body(): x = jnp.concatenate([x, jnp.zeros((2,) + x.shape[1:], x.dtype)], axis=0)]
    concatenate x1, other arithmetic: 2.68 us -> 1.43 us  [body(): jnp.concatenate([lax.ppermute(rows_done[:, :, -margin:], 'col', [(i, i +...]
    pallas_call x1, Pallas kernels: 61.3 us -> 60.2 us  [run_net(): pl.pallas_call(functools.partial(_net_kernel, moments), out_shape=jax.Sha...]
where the time goes in v17:
time: 93.9 us; the launch traced here: 92.1 us
  Pallas kernels  60.2 us (64%)
  local copies, waits for them, and re-layouts  12.9 us (14%)
  starting transfers between devices  11.3 us (12%)
  other arithmetic  3.81 us (4%)
  waiting for transfers between devices  3.66 us (4%)
    pallas_call x1, Pallas kernels, run_net(): pl.pallas_call(functools.partial(_net_kernel, moments), out_shape=jax.Sha...  60.2 us
    ppermute x1, starting transfers between devices, body(): lax.ppermute(marked[:, -margin:], 'row', [(i, i + 1) for i in range(row_c...  4.11 us
    ppermute x1, waiting for transfers between devices, body(): lax.ppermute(rows_done[:, :, :margin], 'col', [(i + 1, i) for i in range(...  3.65 us
    ppermute x1, starting transfers between devices, body(): lax.ppermute(rows_done[:, :, -margin:], 'col', [(i, i + 1) for i in range...  3.11 us
    reshape x4, local copies, waits for them, and re-layouts, _kmat(): return k.transpose(0, 2, 3, 1).reshape(o, 9 * cin)  2.94 us
    ppermute x1, starting transfers between devices, body(): lax.ppermute(rows_done[:, :, :margin], 'col', [(i + 1, i) for i in range(...  2.16 us
    ppermute x1, starting transfers between devices, body(): lax.ppermute(marked[:, :margin], 'row', [(i + 1, i) for i in range(row_co...  1.92 us
  transfers between devices with their start and end apart: 4, of which 1 were waited for; matrix products, arithmetic and copies ran while one was open for 9% of the time, Pallas kernels for 0%

profile of v17, /device:TPU:7, one launch (start us, length us, event | category | flops | bytes accessed | tf_op | source)
XLA Modules:
  0.0 92.1 jit_solution(9770833967619035382)
XLA Ops:
  0.0 0.7 fusion.5
  0.7 0.7 compare_bitcast_fusion
  1.3 0.1 fusion.4
  1.5 0.1 reshape.50
  1.5 0.1 broadcast_in_dim.6
  1.7 0.0 copy-start.2
  1.7 0.0 copy-start.7
  1.7 0.1 convert_element_type.30
  1.8 0.0 copy-start
  1.8 0.0 copy-start.1
  1.8 1.7 %copy.48 = bf16[13,128,256]{2,0,1:T(8,128)(2,1)S(1)} copy(bf16[13,128,256]{2,1,0:T(8,128)(2,1)} %param.10) | data formatting | bytes 1703936 | tf_op args[0]
  3.5 0.0 copy-start.3
  3.5 0.0 copy-start.4
  3.5 0.0 copy-start.5
  3.5 0.0 copy-start.6
  3.6 0.0 copy-start.8
  3.6 0.1 broadcast_in_dim.7
  3.6 0.1 pad_maximum_fusion.2
  3.8 4.1 %collective-permute-start = (bf16[16,16,256]{2,0,1:T(8,128)(2,1)S(1)}, bf16[16,16,256]{2,0,1:T(8,128)(2,1)S(1)}, u32[]{:S(2)}, u32[]{:S(2)}) collective-permute-start(bf16[16,16,256]{2,0,1:T(8,128)(2,1)S(1)} %get-tuple-element.7), channel_id=1, source_target_pairs={{0,16},{16,32},{32,48},{48,64},{64,80},{80,96},{96,112},{1,17},{17... | collective-permute-start | bytes 393224 | tf_op jit(solution)/shard_map/ppermute | solution.py:178
  7.9 1.9 %collective-permute-start.1 = (bf16[16,16,256]{2,0,1:T(8,128)(2,1)S(1)}, bf16[16,16,256]{2,0,1:T(8,128)(2,1)S(1)}, u32[]{:S(2)}, u32[]{:S(2)}) collective-permute-start(bf16[16,16,256]{2,0,1:T(8,128)(2,1)S(1)} %get-tuple-element.8), channel_id=1, source_target_pairs={{16,0},{32,16},{48,32},{64,48},{80,64},{96,80},{112,96},{17,1},{33... | collective-permute-start | bytes 393224 | tf_op jit(solution)/shard_map/ppermute | solution.py:180
  9.9 0.0 copy-done.2
  9.9 0.0 copy-done.7
  9.9 0.1 slice_select_fusion
  10.0 0.1 copy.56
  10.1 0.7 reshape.48.kf
  10.8 0.0 copy-done
  10.8 0.1 copy.54
  10.9 0.8 copy.59.k2
  11.7 0.0 copy-done.1
  11.7 0.1 copy.55
  11.8 0.8 copy.61.k3
  12.6 0.0 copy-done.3
  12.6 0.7 copy.57.k1
  13.3 0.0 copy-done.4
  13.3 0.7 copy.58.b1
  14.0 0.0 copy-done.5
  14.0 0.7 copy.60.b2
  14.7 0.0 copy-done.6
  14.7 0.7 copy.62.b3
  15.4 0.0 copy-done.8
  15.4 0.1 slice.33
  15.5 0.0 collective-permute-done
  15.5 0.0 collective-permute-done.1
  15.5 0.6 maximum_bitcast_fusion
  16.1 0.3 fusion.8
  16.5 0.5 copy.50
  17.0 3.1 %collective-permute-start.2 = (bf16[160,16,16]{0,2,1:T(8,128)(2,1)S(1)}, bf16[160,16,16]{0,2,1:T(8,128)(2,1)S(1)}, u32[]{:S(2)}, u32[]{:S(2)}) collective-permute-start(bf16[160,16,16]{0,2,1:T(8,128)(2,1)S(1)} %copy.50), channel_id=1, source_target_pairs={{0,1},{1,2},{2,3},{3,4},{4,5},{5,6},{6,7},{7,8},{8,9},{9,10},{10,1... | collective-permute-start | bytes 245768 | tf_op jit(solution)/shard_map/ppermute | solution.py:189
  20.1 0.5 copy.51
  20.7 2.2 %collective-permute-start.3 = (bf16[160,16,16]{0,2,1:T(8,128)(2,1)S(1)}, bf16[160,16,16]{0,2,1:T(8,128)(2,1)S(1)}, u32[]{:S(2)}, u32[]{:S(2)}) collective-permute-start(bf16[160,16,16]{0,2,1:T(8,128)(2,1)S(1)} %copy.51), channel_id=1, source_target_pairs={{1,0},{2,1},{3,2},{4,3},{5,4},{6,5},{7,6},{8,7},{9,8},{10,9},{11,1... | collective-permute-start | bytes 245768 | tf_op jit(solution)/shard_map/ppermute | solution.py:191
  22.8 0.1 fusion.7
  22.9 0.7 copy.63.bfl
  23.6 0.1 pad.31.clone
  23.7 0.6 stack.67.lim_ref
  24.3 0.0 collective-permute-done.2
  24.3 0.5 copy.52
  24.8 3.6 %collective-permute-done.3 = bf16[160,16,16]{0,2,1:T(8,128)(2,1)S(1)} collective-permute-done((bf16[160,16,16]{0,2,1:T(8,128)(2,1)S(1)}, bf16[160,16,16]{0,2,1:T(8,128)(2,1)S(1)}, u32[]{:S(2)}, u32[]{:S(2)}) %collective-permute-start.3) | collective-permute-done | bytes 81952 | tf_op jit(solution)/shard_map/ppermute | solution.py:191
  28.5 0.5 copy.53
  29.0 1.4 %maximum_maximum_fusion = bf16[160,16,384]{2,1,0:T(8,128)(2,1)S(1)} fusion(bf16[160,16,16]{2,1,0:T(8,128)(2,1)S(1)} %copy.53, bf16[160,16,256]{2,1,0:T(8,128)(2,1)S(1)} %maximum_bitcast_fusion, bf16[160,16,16]{2,1,0:T(8,128)(2,1)S(1)} %copy.52, bf16[384]{0:T(512)(128)(2,1)S(1)} %pad.31.clone), kind=kLoop, calls=%fused_computation | loop fusion | flops 7864320 | bytes 3441408 | tf_op jit(solution)/shard_map/concatenate | solution.py:187
  30.4 1.5 %concatenate.21.x_ref = bf16[162,16,384]{2,1,0:T(8,128)(2,1)} pad(bf16[160,16,384]{2,1,0:T(8,128)(2,1)S(1)} %maximum_maximum_fusion, bf16[]{:T(256)} %constant.92.clone.1), padding=0_2x0_0x0_0 | pad | bytes 3956738 | tf_op jit(solution)/shard_map/concatenate | solution.py:196
  31.9 60.2 %shard_map.100 = bf16[13,128,256]{2,1,0:T(8,128)(2,1)} custom-call(s32[16]{0:T(128)} %stack.67.lim_ref, bf16[162,16,384]{2,1,0:T(8,128)(2,1)} %concatenate.21.x_ref, bf16[64,144]{1,0:T(8,128)(2,1)} %copy.57.k1, f32[64,1]{1,0:T(8,128)} %copy.58.b1, bf16[64,576]{1,0:T(8,128)(2,1)} %copy.59.k2, f32[64,1]{1,0:T(8,128)} %copy.60.b2, bf16[64,576]{1,0:T(8,128)(2,1)} %copy.61.k3, ...), custom_call_target="tpu_custom_call" | custom-call | tf_op jit(solution)/shard_map/pallas_call | solution.py:106
  (6 shorter events, 0.1 us)
Async XLA Ops:
  1.7 8.2 %copy-start.2 = (bf16[26,64,3,3]{1,0,3,2:T(8,128)(2,1)S(1)}, bf16[26,64,3,3]{1,0,3,2:T(8,128)(2,1)}, u32[]{:S(2)}) copy-start(bf16[26,64,3,3]{1,0,3,2:T(8,128)(2,1)} %param.18) | copy-start | bytes 89860
  1.7 8.2 %copy-start.7 = (pred[16]{0:T(512)(128)(4,1)S(1)}, pred[16]{0:T(512)(128)(4,1)}, u32[]{:S(2)}) copy-start(pred[16]{0:T(512)(128)(4,1)} %constant.93.clone.1) | copy-start | bytes 52
  1.8 9.0 %copy-start = (bf16[64,64,3,3]{1,0,3,2:T(8,128)(2,1)S(1)}, bf16[64,64,3,3]{1,0,3,2:T(8,128)(2,1)}, u32[]{:S(2)}) copy-start(bf16[64,64,3,3]{1,0,3,2:T(8,128)(2,1)} %param.14) | copy-start | bytes 221188
  1.8 9.9 %copy-start.1 = (bf16[64,64,3,3]{1,0,3,2:T(8,128)(2,1)S(1)}, bf16[64,64,3,3]{1,0,3,2:T(8,128)(2,1)}, u32[]{:S(2)}) copy-start(bf16[64,64,3,3]{1,0,3,2:T(8,128)(2,1)} %param.16) | copy-start | bytes 221188
  3.5 9.1 %copy-start.3 = (bf16[64,13,3,3]{0,1,3,2:T(8,128)(2,1)S(1)}, bf16[64,13,3,3]{0,1,3,2:T(8,128)(2,1)}, u32[]{:S(2)}) copy-start(bf16[64,13,3,3]{0,1,3,2:T(8,128)(2,1)} %param.12) | copy-start | bytes 44932
  3.5 9.8 %copy-start.4 = (f32[64]{0:T(128)S(1)}, f32[64]{0:T(128)}, u32[]{:S(2)}) copy-start(f32[64]{0:T(128)} %param.13) | copy-start | bytes 772
  3.5 10.5 %copy-start.5 = (f32[64]{0:T(128)S(1)}, f32[64]{0:T(128)}, u32[]{:S(2)}) copy-start(f32[64]{0:T(128)} %param.15) | copy-start | bytes 772
  3.5 11.2 %copy-start.6 = (f32[64]{0:T(128)S(1)}, f32[64]{0:T(128)}, u32[]{:S(2)}) copy-start(f32[64]{0:T(128)} %param.17) | copy-start | bytes 772
  3.6 11.9 %copy-start.8 = (f32[26]{0:T(128)S(1)}, f32[26]{0:T(128)}, u32[]{:S(2)}) copy-start(f32[26]{0:T(128)} %param.19) | copy-start | bytes 316
  3.8 11.7 %collective-permute-start = (bf16[16,16,256]{2,0,1:T(8,128)(2,1)S(1)}, bf16[16,16,256]{2,0,1:T(8,128)(2,1)S(1)}, u32[]{:S(2)}, u32[]{:S(2)}) collective-permute-start(bf16[16,16,256]{2,0,1:T(8,128)(2,1)S(1)} %get-tuple-element.7), channel_id=1, source_target_pairs={{0,16},{16,32},{32,48},{48,64},{64,80},{80,96},{96,112},{1,17},{17... | collective-permute-start | bytes 393224 | tf_op jit(solution)/shard_map/ppermute | solution.py:178
  7.9 7.6 %collective-permute-start.1 = (bf16[16,16,256]{2,0,1:T(8,128)(2,1)S(1)}, bf16[16,16,256]{2,0,1:T(8,128)(2,1)S(1)}, u32[]{:S(2)}, u32[]{:S(2)}) collective-permute-start(bf16[16,16,256]{2,0,1:T(8,128)(2,1)S(1)} %get-tuple-element.8), channel_id=1, source_target_pairs={{16,0},{32,16},{48,32},{64,48},{80,64},{96,80},{112,96},{17,1},{33... | collective-permute-start | bytes 393224 | tf_op jit(solution)/shard_map/ppermute | solution.py:180
  17.0 7.3 %collective-permute-start.2 = (bf16[160,16,16]{0,2,1:T(8,128)(2,1)S(1)}, bf16[160,16,16]{0,2,1:T(8,128)(2,1)S(1)}, u32[]{:S(2)}, u32[]{:S(2)}) collective-permute-start(bf16[160,16,16]{0,2,1:T(8,128)(2,1)S(1)} %copy.50), channel_id=1, source_target_pairs={{0,1},{1,2},{2,3},{3,4},{4,5},{5,6},{6,7},{7,8},{8,9},{9,10},{10,1... | collective-permute-start | bytes 245768 | tf_op jit(solution)/shard_map/ppermute | solution.py:189
  20.7 7.8 %collective-permute-start.3 = (bf16[160,16,16]{0,2,1:T(8,128)(2,1)S(1)}, bf16[160,16,16]{0,2,1:T(8,128)(2,1)S(1)}, u32[]{:S(2)}, u32[]{:S(2)}) collective-permute-start(bf16[160,16,16]{0,2,1:T(8,128)(2,1)S(1)} %copy.51), channel_id=1, source_target_pairs={{1,0},{2,1},{3,2},{4,3},{5,4},{6,5},{7,6},{8,7},{9,8},{10,9},{11,1... | collective-permute-start | bytes 245768 | tf_op jit(solution)/shard_map/ppermute | solution.py:191

commit v18 on v17

--- a/solution.py
+++ b/solution.py
@@ -51,7 +51,7 @@
                 )
             return carry
 
-        lax.fori_loop(0, n_rows, row, 0, unroll=(8, 14, 16, 13)[index])
+        lax.fori_loop(0, n_rows, row, 0, unroll=(8, 22, 16, 13)[index])
 
     h0 = x_ref.shape[0] - 2
     h1 = h0 - 2

time: 93.9 us -> 92.9 us (0.989)
  no operation moved by 1% of the time
where the time goes in v18:
time: 92.9 us; the launch traced here: 91.2 us
  Pallas kernels  59.3 us (64%)
  local copies, waits for them, and re-layouts  12.9 us (14%)
  starting transfers between devices  11.5 us (12%)
  other arithmetic  3.81 us (4%)
  waiting for transfers between devices  3.48 us (4%)
    pallas_call x1, Pallas kernels, run_net(): pl.pallas_call(functools.partial(_net_kernel, moments), out_shape=jax.Sha...  59.3 us
    ppermute x1, starting transfers between devices, body(): lax.ppermute(marked[:, -margin:], 'row', [(i, i + 1) for i in range(row_c...  4.11 us
    ppermute x1, waiting for transfers between devices, body(): lax.ppermute(rows_done[:, :, :margin], 'col', [(i + 1, i) for i in range(...  3.47 us
    ppermute x1, starting transfers between devices, body(): lax.ppermute(rows_done[:, :, -margin:], 'col', [(i, i + 1) for i in range...  3.11 us
    reshape x4, local copies, waits for them, and re-layouts, _kmat(): return k.transpose(0, 2, 3, 1).reshape(o, 9 * cin)  2.94 us
    ppermute x1, starting transfers between devices, body(): lax.ppermute(rows_done[:, :, :margin], 'col', [(i + 1, i) for i in range(...  2.34 us
    ppermute x1, starting transfers between devices, body(): lax.ppermute(marked[:, :margin], 'row', [(i + 1, i) for i in range(row_co...  1.92 us
  transfers between devices with their start and end apart: 4, of which 1 were waited for; matrix products, arithmetic and copies ran while one was open for 9% of the time, Pallas kernels for 0%

profile of v18, /device:TPU:7, one launch (start us, length us, event | category | flops | bytes accessed | tf_op | source)
XLA Modules:
  0.0 91.2 jit_solution(5826642506251531874)
XLA Ops:
  0.0 0.7 fusion.5
  0.7 0.7 compare_bitcast_fusion
  1.3 0.1 fusion.4
  1.5 0.1 reshape.50
  1.5 0.1 broadcast_in_dim.6
  1.7 0.0 copy-start.2
  1.7 0.0 copy-start.7
  1.7 0.1 convert_element_type.30
  1.8 0.0 copy-start
  1.8 0.0 copy-start.1
  1.8 1.7 %copy.48 = bf16[13,128,256]{2,0,1:T(8,128)(2,1)S(1)} copy(bf16[13,128,256]{2,1,0:T(8,128)(2,1)} %param.10) | data formatting | bytes 1703936 | tf_op args[0]
  3.5 0.0 copy-start.3
  3.5 0.0 copy-start.4
  3.5 0.0 copy-start.5
  3.5 0.0 copy-start.6
  3.6 0.0 copy-start.8
  3.6 0.1 broadcast_in_dim.7
  3.6 0.1 pad_maximum_fusion.2
  3.8 4.1 %collective-permute-start = (bf16[16,16,256]{2,0,1:T(8,128)(2,1)S(1)}, bf16[16,16,256]{2,0,1:T(8,128)(2,1)S(1)}, u32[]{:S(2)}, u32[]{:S(2)}) collective-permute-start(bf16[16,16,256]{2,0,1:T(8,128)(2,1)S(1)} %get-tuple-element.7), channel_id=1, source_target_pairs={{0,16},{16,32},{32,48},{48,64},{64,80},{80,96},{96,112},{1,17},{17... | collective-permute-start | bytes 393224 | tf_op jit(solution)/shard_map/ppermute | solution.py:178
  7.9 1.9 %collective-permute-start.1 = (bf16[16,16,256]{2,0,1:T(8,128)(2,1)S(1)}, bf16[16,16,256]{2,0,1:T(8,128)(2,1)S(1)}, u32[]{:S(2)}, u32[]{:S(2)}) collective-permute-start(bf16[16,16,256]{2,0,1:T(8,128)(2,1)S(1)} %get-tuple-element.8), channel_id=1, source_target_pairs={{16,0},{32,16},{48,32},{64,48},{80,64},{96,80},{112,96},{17,1},{33... | collective-permute-start | bytes 393224 | tf_op jit(solution)/shard_map/ppermute | solution.py:180
  9.9 0.0 copy-done.2
  9.9 0.0 copy-done.7
  9.9 0.1 slice_select_fusion
  10.0 0.1 copy.56
  10.1 0.7 reshape.48.kf
  10.8 0.0 copy-done
  10.8 0.1 copy.54
  10.9 0.8 copy.59.k2
  11.7 0.0 copy-done.1
  11.7 0.1 copy.55
  11.8 0.8 copy.61.k3
  12.6 0.0 copy-done.3
  12.6 0.7 copy.57.k1
  13.3 0.0 copy-done.4
  13.3 0.7 copy.58.b1
  14.0 0.0 copy-done.5
  14.0 0.7 copy.60.b2
  14.7 0.0 copy-done.6
  14.7 0.7 copy.62.b3
  15.4 0.0 copy-done.8
  15.4 0.1 slice.33
  15.5 0.0 collective-permute-done
  15.5 0.0 collective-permute-done.1
  15.5 0.6 maximum_bitcast_fusion
  16.1 0.3 fusion.8
  16.5 0.5 copy.50
  17.0 3.1 %collective-permute-start.2 = (bf16[160,16,16]{0,2,1:T(8,128)(2,1)S(1)}, bf16[160,16,16]{0,2,1:T(8,128)(2,1)S(1)}, u32[]{:S(2)}, u32[]{:S(2)}) collective-permute-start(bf16[160,16,16]{0,2,1:T(8,128)(2,1)S(1)} %copy.50), channel_id=1, source_target_pairs={{0,1},{1,2},{2,3},{3,4},{4,5},{5,6},{6,7},{7,8},{8,9},{9,10},{10,1... | collective-permute-start | bytes 245768 | tf_op jit(solution)/shard_map/ppermute | solution.py:189
  20.1 0.5 copy.51
  20.7 2.3 %collective-permute-start.3 = (bf16[160,16,16]{0,2,1:T(8,128)(2,1)S(1)}, bf16[160,16,16]{0,2,1:T(8,128)(2,1)S(1)}, u32[]{:S(2)}, u32[]{:S(2)}) collective-permute-start(bf16[160,16,16]{0,2,1:T(8,128)(2,1)S(1)} %copy.51), channel_id=1, source_target_pairs={{1,0},{2,1},{3,2},{4,3},{5,4},{6,5},{7,6},{8,7},{9,8},{10,9},{11,1... | collective-permute-start | bytes 245768 | tf_op jit(solution)/shard_map/ppermute | solution.py:191
  23.0 0.1 fusion.7
  23.1 0.7 copy.63.bfl
  23.8 0.1 pad.31.clone
  23.9 0.6 stack.67.lim_ref
  24.5 0.0 collective-permute-done.2
  24.5 0.5 copy.52
  25.0 3.5 %collective-permute-done.3 = bf16[160,16,16]{0,2,1:T(8,128)(2,1)S(1)} collective-permute-done((bf16[160,16,16]{0,2,1:T(8,128)(2,1)S(1)}, bf16[160,16,16]{0,2,1:T(8,128)(2,1)S(1)}, u32[]{:S(2)}, u32[]{:S(2)}) %collective-permute-start.3) | collective-permute-done | bytes 81952 | tf_op jit(solution)/shard_map/ppermute | solution.py:191
  28.5 0.5 copy.53
  29.0 1.4 %maximum_maximum_fusion = bf16[160,16,384]{2,1,0:T(8,128)(2,1)S(1)} fusion(bf16[160,16,16]{2,1,0:T(8,128)(2,1)S(1)} %copy.53, bf16[160,16,256]{2,1,0:T(8,128)(2,1)S(1)} %maximum_bitcast_fusion, bf16[160,16,16]{2,1,0:T(8,128)(2,1)S(1)} %copy.52, bf16[384]{0:T(512)(128)(2,1)S(1)} %pad.31.clone), kind=kLoop, calls=%fused_computation | loop fusion | flops 7864320 | bytes 3441408 | tf_op jit(solution)/shard_map/concatenate | solution.py:187
  30.4 1.5 %concatenate.21.x_ref = bf16[162,16,384]{2,1,0:T(8,128)(2,1)} pad(bf16[160,16,384]{2,1,0:T(8,128)(2,1)S(1)} %maximum_maximum_fusion, bf16[]{:T(256)} %constant.92.clone.1), padding=0_2x0_0x0_0 | pad | bytes 3956738 | tf_op jit(solution)/shard_map/concatenate | solution.py:196
  31.9 59.3 %shard_map.100 = bf16[13,128,256]{2,1,0:T(8,128)(2,1)} custom-call(s32[16]{0:T(128)} %stack.67.lim_ref, bf16[162,16,384]{2,1,0:T(8,128)(2,1)} %concatenate.21.x_ref, bf16[64,144]{1,0:T(8,128)(2,1)} %copy.57.k1, f32[64,1]{1,0:T(8,128)} %copy.58.b1, bf16[64,576]{1,0:T(8,128)(2,1)} %copy.59.k2, f32[64,1]{1,0:T(8,128)} %copy.60.b2, bf16[64,576]{1,0:T(8,128)(2,1)} %copy.61.k3, ...), custom_call_target="tpu_custom_call" | custom-call | tf_op jit(solution)/shard_map/pallas_call | solution.py:106
  (6 shorter events, 0.1 us)
Async XLA Ops:
  1.7 8.2 %copy-start.2 = (bf16[26,64,3,3]{1,0,3,2:T(8,128)(2,1)S(1)}, bf16[26,64,3,3]{1,0,3,2:T(8,128)(2,1)}, u32[]{:S(2)}) copy-start(bf16[26,64,3,3]{1,0,3,2:T(8,128)(2,1)} %param.18) | copy-start | bytes 89860
  1.7 8.2 %copy-start.7 = (pred[16]{0:T(512)(128)(4,1)S(1)}, pred[16]{0:T(512)(128)(4,1)}, u32[]{:S(2)}) copy-start(pred[16]{0:T(512)(128)(4,1)} %constant.93.clone.1) | copy-start | bytes 52
  1.8 9.0 %copy-start = (bf16[64,64,3,3]{1,0,3,2:T(8,128)(2,1)S(1)}, bf16[64,64,3,3]{1,0,3,2:T(8,128)(2,1)}, u32[]{:S(2)}) copy-start(bf16[64,64,3,3]{1,0,3,2:T(8,128)(2,1)} %param.14) | copy-start | bytes 221188
  1.8 9.9 %copy-start.1 = (bf16[64,64,3,3]{1,0,3,2:T(8,128)(2,1)S(1)}, bf16[64,64,3,3]{1,0,3,2:T(8,128)(2,1)}, u32[]{:S(2)}) copy-start(bf16[64,64,3,3]{1,0,3,2:T(8,128)(2,1)} %param.16) | copy-start | bytes 221188
  3.5 9.1 %copy-start.3 = (bf16[64,13,3,3]{0,1,3,2:T(8,128)(2,1)S(1)}, bf16[64,13,3,3]{0,1,3,2:T(8,128)(2,1)}, u32[]{:S(2)}) copy-start(bf16[64,13,3,3]{0,1,3,2:T(8,128)(2,1)} %param.12) | copy-start | bytes 44932
  3.5 9.8 %copy-start.4 = (f32[64]{0:T(128)S(1)}, f32[64]{0:T(128)}, u32[]{:S(2)}) copy-start(f32[64]{0:T(128)} %param.13) | copy-start | bytes 772
  3.5 10.5 %copy-start.5 = (f32[64]{0:T(128)S(1)}, f32[64]{0:T(128)}, u32[]{:S(2)}) copy-start(f32[64]{0:T(128)} %param.15) | copy-start | bytes 772
  3.5 11.2 %copy-start.6 = (f32[64]{0:T(128)S(1)}, f32[64]{0:T(128)}, u32[]{:S(2)}) copy-start(f32[64]{0:T(128)} %param.17) | copy-start | bytes 772
  3.6 11.9 %copy-start.8 = (f32[26]{0:T(128)S(1)}, f32[26]{0:T(128)}, u32[]{:S(2)}) copy-start(f32[26]{0:T(128)} %param.19) | copy-start | bytes 316
  3.8 11.7 %collective-permute-start = (bf16[16,16,256]{2,0,1:T(8,128)(2,1)S(1)}, bf16[16,16,256]{2,0,1:T(8,128)(2,1)S(1)}, u32[]{:S(2)}, u32[]{:S(2)}) collective-permute-start(bf16[16,16,256]{2,0,1:T(8,128)(2,1)S(1)} %get-tuple-element.7), channel_id=1, source_target_pairs={{0,16},{16,32},{32,48},{48,64},{64,80},{80,96},{96,112},{1,17},{17... | collective-permute-start | bytes 393224 | tf_op jit(solution)/shard_map/ppermute | solution.py:178
  7.9 7.6 %collective-permute-start.1 = (bf16[16,16,256]{2,0,1:T(8,128)(2,1)S(1)}, bf16[16,16,256]{2,0,1:T(8,128)(2,1)S(1)}, u32[]{:S(2)}, u32[]{:S(2)}) collective-permute-start(bf16[16,16,256]{2,0,1:T(8,128)(2,1)S(1)} %get-tuple-element.8), channel_id=1, source_target_pairs={{16,0},{32,16},{48,32},{64,48},{80,64},{96,80},{112,96},{17,1},{33... | collective-permute-start | bytes 393224 | tf_op jit(solution)/shard_map/ppermute | solution.py:180
  17.0 7.5 %collective-permute-start.2 = (bf16[160,16,16]{0,2,1:T(8,128)(2,1)S(1)}, bf16[160,16,16]{0,2,1:T(8,128)(2,1)S(1)}, u32[]{:S(2)}, u32[]{:S(2)}) collective-permute-start(bf16[160,16,16]{0,2,1:T(8,128)(2,1)S(1)} %copy.50), channel_id=1, source_target_pairs={{0,1},{1,2},{2,3},{3,4},{4,5},{5,6},{6,7},{7,8},{8,9},{9,10},{10,1... | collective-permute-start | bytes 245768 | tf_op jit(solution)/shard_map/ppermute | solution.py:189
  20.7 7.8 %collective-permute-start.3 = (bf16[160,16,16]{0,2,1:T(8,128)(2,1)S(1)}, bf16[160,16,16]{0,2,1:T(8,128)(2,1)S(1)}, u32[]{:S(2)}, u32[]{:S(2)}) collective-permute-start(bf16[160,16,16]{0,2,1:T(8,128)(2,1)S(1)} %copy.51), channel_id=1, source_target_pairs={{1,0},{2,1},{3,2},{4,3},{5,4},{6,5},{7,6},{8,7},{9,8},{10,9},{11,1... | collective-permute-start | bytes 245768 | tf_op jit(solution)/shard_map/ppermute | solution.py:191

commit v19 on v18

--- a/solution.py
+++ b/solution.py
@@ -51,7 +51,7 @@
                 )
             return carry
 
-        lax.fori_loop(0, n_rows, row, 0, unroll=(8, 22, 16, 13)[index])
+        lax.fori_loop(0, n_rows, row, 0, unroll=(8, 22, 16, 26)[index])
 
     h0 = x_ref.shape[0] - 2
     h1 = h0 - 2

time: 92.9 us -> 92.4 us (level)
  no operation moved by 1% of the time
where the time goes in v19:
time: 92.4 us; the launch traced here: 90.7 us
  Pallas kernels  58.8 us (64%)
  local copies, waits for them, and re-layouts  12.9 us (14%)
  starting transfers between devices  11.5 us (12%)
  other arithmetic  3.81 us (4%)
  waiting for transfers between devices  3.48 us (4%)
    pallas_call x1, Pallas kernels, run_net(): pl.pallas_call(functools.partial(_net_kernel, moments), out_shape=jax.Sha...  58.8 us
    ppermute x1, starting transfers between devices, body(): lax.ppermute(marked[:, -margin:], 'row', [(i, i + 1) for i in range(row_c...  4.11 us
    ppermute x1, waiting for transfers between devices, body(): lax.ppermute(rows_done[:, :, :margin], 'col', [(i + 1, i) for i in range(...  3.47 us
    ppermute x1, starting transfers between devices, body(): lax.ppermute(rows_done[:, :, -margin:], 'col', [(i, i + 1) for i in range...  3.11 us
    reshape x4, local copies, waits for them, and re-layouts, _kmat(): return k.transpose(0, 2, 3, 1).reshape(o, 9 * cin)  2.94 us
    ppermute x1, starting transfers between devices, body(): lax.ppermute(rows_done[:, :, :margin], 'col', [(i + 1, i) for i in range(...  2.34 us
    ppermute x1, starting transfers between devices, body(): lax.ppermute(marked[:, :margin], 'row', [(i + 1, i) for i in range(row_co...  1.92 us
  transfers between devices with their start and end apart: 4, of which 1 were waited for; matrix products, arithmetic and copies ran while one was open for 9% of the time, Pallas kernels for 0%

profile of v19, /device:TPU:7, one launch (start us, length us, event | category | flops | bytes accessed | tf_op | source)
XLA Modules:
  0.0 90.7 jit_solution(7189866520578422505)
XLA Ops:
  0.0 0.7 fusion.5
  0.7 0.7 compare_bitcast_fusion
  1.3 0.1 fusion.4
  1.5 0.1 reshape.50
  1.5 0.1 broadcast_in_dim.6
  1.7 0.0 copy-start.2
  1.7 0.0 copy-start.7
  1.7 0.1 convert_element_type.30
  1.8 0.0 copy-start
  1.8 0.0 copy-start.1
  1.8 1.7 %copy.48 = bf16[13,128,256]{2,0,1:T(8,128)(2,1)S(1)} copy(bf16[13,128,256]{2,1,0:T(8,128)(2,1)} %param.10) | data formatting | bytes 1703936 | tf_op args[0]
  3.5 0.0 copy-start.3
  3.5 0.0 copy-start.4
  3.5 0.0 copy-start.5
  3.5 0.0 copy-start.6
  3.6 0.0 copy-start.8
  3.6 0.1 broadcast_in_dim.7
  3.6 0.1 pad_maximum_fusion.2
  3.8 4.1 %collective-permute-start = (bf16[16,16,256]{2,0,1:T(8,128)(2,1)S(1)}, bf16[16,16,256]{2,0,1:T(8,128)(2,1)S(1)}, u32[]{:S(2)}, u32[]{:S(2)}) collective-permute-start(bf16[16,16,256]{2,0,1:T(8,128)(2,1)S(1)} %get-tuple-element.7), channel_id=1, source_target_pairs={{0,16},{16,32},{32,48},{48,64},{64,80},{80,96},{96,112},{1,17},{17... | collective-permute-start | bytes 393224 | tf_op jit(solution)/shard_map/ppermute | solution.py:178
  7.9 1.9 %collective-permute-start.1 = (bf16[16,16,256]{2,0,1:T(8,128)(2,1)S(1)}, bf16[16,16,256]{2,0,1:T(8,128)(2,1)S(1)}, u32[]{:S(2)}, u32[]{:S(2)}) collective-permute-start(bf16[16,16,256]{2,0,1:T(8,128)(2,1)S(1)} %get-tuple-element.8), channel_id=1, source_target_pairs={{16,0},{32,16},{48,32},{64,48},{80,64},{96,80},{112,96},{17,1},{33... | collective-permute-start | bytes 393224 | tf_op jit(solution)/shard_map/ppermute | solution.py:180
  9.9 0.0 copy-done.2
  9.9 0.0 copy-done.7
  9.9 0.1 slice_select_fusion
  10.0 0.1 copy.56
  10.1 0.7 reshape.48.kf
  10.8 0.0 copy-done
  10.8 0.1 copy.54
  10.9 0.8 copy.59.k2
  11.7 0.0 copy-done.1
  11.7 0.1 copy.55
  11.8 0.8 copy.61.k3
  12.6 0.0 copy-done.3
  12.6 0.7 copy.57.k1
  13.3 0.0 copy-done.4
  13.3 0.7 copy.58.b1
  14.0 0.0 copy-done.5
  14.0 0.7 copy.60.b2
  14.7 0.0 copy-done.6
  14.7 0.7 copy.62.b3
  15.4 0.0 copy-done.8
  15.4 0.1 slice.33
  15.5 0.0 collective-permute-done
  15.5 0.0 collective-permute-done.1
  15.5 0.6 maximum_bitcast_fusion
  16.1 0.3 fusion.8
  16.5 0.5 copy.50
  17.0 3.1 %collective-permute-start.2 = (bf16[160,16,16]{0,2,1:T(8,128)(2,1)S(1)}, bf16[160,16,16]{0,2,1:T(8,128)(2,1)S(1)}, u32[]{:S(2)}, u32[]{:S(2)}) collective-permute-start(bf16[160,16,16]{0,2,1:T(8,128)(2,1)S(1)} %copy.50), channel_id=1, source_target_pairs={{0,1},{1,2},{2,3},{3,4},{4,5},{5,6},{6,7},{7,8},{8,9},{9,10},{10,1... | collective-permute-start | bytes 245768 | tf_op jit(solution)/shard_map/ppermute | solution.py:189
  20.1 0.5 copy.51
  20.7 2.3 %collective-permute-start.3 = (bf16[160,16,16]{0,2,1:T(8,128)(2,1)S(1)}, bf16[160,16,16]{0,2,1:T(8,128)(2,1)S(1)}, u32[]{:S(2)}, u32[]{:S(2)}) collective-permute-start(bf16[160,16,16]{0,2,1:T(8,128)(2,1)S(1)} %copy.51), channel_id=1, source_target_pairs={{1,0},{2,1},{3,2},{4,3},{5,4},{6,5},{7,6},{8,7},{9,8},{10,9},{11,1... | collective-permute-start | bytes 245768 | tf_op jit(solution)/shard_map/ppermute | solution.py:191
  23.0 0.1 fusion.7
  23.1 0.7 copy.63.bfl
  23.8 0.1 pad.31.clone
  23.9 0.6 stack.67.lim_ref
  24.5 0.0 collective-permute-done.2
  24.5 0.5 copy.52
  25.0 3.5 %collective-permute-done.3 = bf16[160,16,16]{0,2,1:T(8,128)(2,1)S(1)} collective-permute-done((bf16[160,16,16]{0,2,1:T(8,128)(2,1)S(1)}, bf16[160,16,16]{0,2,1:T(8,128)(2,1)S(1)}, u32[]{:S(2)}, u32[]{:S(2)}) %collective-permute-start.3) | collective-permute-done | bytes 81952 | tf_op jit(solution)/shard_map/ppermute | solution.py:191
  28.5 0.5 copy.53
  29.0 1.4 %maximum_maximum_fusion = bf16[160,16,384]{2,1,0:T(8,128)(2,1)S(1)} fusion(bf16[160,16,16]{2,1,0:T(8,128)(2,1)S(1)} %copy.53, bf16[160,16,256]{2,1,0:T(8,128)(2,1)S(1)} %maximum_bitcast_fusion, bf16[160,16,16]{2,1,0:T(8,128)(2,1)S(1)} %copy.52, bf16[384]{0:T(512)(128)(2,1)S(1)} %pad.31.clone), kind=kLoop, calls=%fused_computation | loop fusion | flops 7864320 | bytes 3441408 | tf_op jit(solution)/shard_map/concatenate | solution.py:187
  30.4 1.5 %concatenate.21.x_ref = bf16[162,16,384]{2,1,0:T(8,128)(2,1)} pad(bf16[160,16,384]{2,1,0:T(8,128)(2,1)S(1)} %maximum_maximum_fusion, bf16[]{:T(256)} %constant.92.clone.1), padding=0_2x0_0x0_0 | pad | bytes 3956738 | tf_op jit(solution)/shard_map/concatenate | solution.py:196
  31.9 58.8 %shard_map.100 = bf16[13,128,256]{2,1,0:T(8,128)(2,1)} custom-call(s32[16]{0:T(128)} %stack.67.lim_ref, bf16[162,16,384]{2,1,0:T(8,128)(2,1)} %concatenate.21.x_ref, bf16[64,144]{1,0:T(8,128)(2,1)} %copy.57.k1, f32[64,1]{1,0:T(8,128)} %copy.58.b1, bf16[64,576]{1,0:T(8,128)(2,1)} %copy.59.k2, f32[64,1]{1,0:T(8,128)} %copy.60.b2, bf16[64,576]{1,0:T(8,128)(2,1)} %copy.61.k3, ...), custom_call_target="tpu_custom_call" | custom-call | tf_op jit(solution)/shard_map/pallas_call | solution.py:106
  (6 shorter events, 0.1 us)
Async XLA Ops:
  1.7 8.2 %copy-start.2 = (bf16[26,64,3,3]{1,0,3,2:T(8,128)(2,1)S(1)}, bf16[26,64,3,3]{1,0,3,2:T(8,128)(2,1)}, u32[]{:S(2)}) copy-start(bf16[26,64,3,3]{1,0,3,2:T(8,128)(2,1)} %param.18) | copy-start | bytes 89860
  1.7 8.2 %copy-start.7 = (pred[16]{0:T(512)(128)(4,1)S(1)}, pred[16]{0:T(512)(128)(4,1)}, u32[]{:S(2)}) copy-start(pred[16]{0:T(512)(128)(4,1)} %constant.93.clone.1) | copy-start | bytes 52
  1.8 9.0 %copy-start = (bf16[64,64,3,3]{1,0,3,2:T(8,128)(2,1)S(1)}, bf16[64,64,3,3]{1,0,3,2:T(8,128)(2,1)}, u32[]{:S(2)}) copy-start(bf16[64,64,3,3]{1,0,3,2:T(8,128)(2,1)} %param.14) | copy-start | bytes 221188
  1.8 9.9 %copy-start.1 = (bf16[64,64,3,3]{1,0,3,2:T(8,128)(2,1)S(1)}, bf16[64,64,3,3]{1,0,3,2:T(8,128)(2,1)}, u32[]{:S(2)}) copy-start(bf16[64,64,3,3]{1,0,3,2:T(8,128)(2,1)} %param.16) | copy-start | bytes 221188
  3.5 9.1 %copy-start.3 = (bf16[64,13,3,3]{0,1,3,2:T(8,128)(2,1)S(1)}, bf16[64,13,3,3]{0,1,3,2:T(8,128)(2,1)}, u32[]{:S(2)}) copy-start(bf16[64,13,3,3]{0,1,3,2:T(8,128)(2,1)} %param.12) | copy-start | bytes 44932
  3.5 9.8 %copy-start.4 = (f32[64]{0:T(128)S(1)}, f32[64]{0:T(128)}, u32[]{:S(2)}) copy-start(f32[64]{0:T(128)} %param.13) | copy-start | bytes 772
  3.5 10.5 %copy-start.5 = (f32[64]{0:T(128)S(1)}, f32[64]{0:T(128)}, u32[]{:S(2)}) copy-start(f32[64]{0:T(128)} %param.15) | copy-start | bytes 772
  3.5 11.2 %copy-start.6 = (f32[64]{0:T(128)S(1)}, f32[64]{0:T(128)}, u32[]{:S(2)}) copy-start(f32[64]{0:T(128)} %param.17) | copy-start | bytes 772
  3.6 11.9 %copy-start.8 = (f32[26]{0:T(128)S(1)}, f32[26]{0:T(128)}, u32[]{:S(2)}) copy-start(f32[26]{0:T(128)} %param.19) | copy-start | bytes 316
  3.8 11.7 %collective-permute-start = (bf16[16,16,256]{2,0,1:T(8,128)(2,1)S(1)}, bf16[16,16,256]{2,0,1:T(8,128)(2,1)S(1)}, u32[]{:S(2)}, u32[]{:S(2)}) collective-permute-start(bf16[16,16,256]{2,0,1:T(8,128)(2,1)S(1)} %get-tuple-element.7), channel_id=1, source_target_pairs={{0,16},{16,32},{32,48},{48,64},{64,80},{80,96},{96,112},{1,17},{17... | collective-permute-start | bytes 393224 | tf_op jit(solution)/shard_map/ppermute | solution.py:178
  7.9 7.6 %collective-permute-start.1 = (bf16[16,16,256]{2,0,1:T(8,128)(2,1)S(1)}, bf16[16,16,256]{2,0,1:T(8,128)(2,1)S(1)}, u32[]{:S(2)}, u32[]{:S(2)}) collective-permute-start(bf16[16,16,256]{2,0,1:T(8,128)(2,1)S(1)} %get-tuple-element.8), channel_id=1, source_target_pairs={{16,0},{32,16},{48,32},{64,48},{80,64},{96,80},{112,96},{17,1},{33... | collective-permute-start | bytes 393224 | tf_op jit(solution)/shard_map/ppermute | solution.py:180
  17.0 7.5 %collective-permute-start.2 = (bf16[160,16,16]{0,2,1:T(8,128)(2,1)S(1)}, bf16[160,16,16]{0,2,1:T(8,128)(2,1)S(1)}, u32[]{:S(2)}, u32[]{:S(2)}) collective-permute-start(bf16[160,16,16]{0,2,1:T(8,128)(2,1)S(1)} %copy.50), channel_id=1, source_target_pairs={{0,1},{1,2},{2,3},{3,4},{4,5},{5,6},{6,7},{7,8},{8,9},{9,10},{10,1... | collective-permute-start | bytes 245768 | tf_op jit(solution)/shard_map/ppermute | solution.py:189
  20.7 7.8 %collective-permute-start.3 = (bf16[160,16,16]{0,2,1:T(8,128)(2,1)S(1)}, bf16[160,16,16]{0,2,1:T(8,128)(2,1)S(1)}, u32[]{:S(2)}, u32[]{:S(2)}) collective-permute-start(bf16[160,16,16]{0,2,1:T(8,128)(2,1)S(1)} %copy.51), channel_id=1, source_target_pairs={{1,0},{2,1},{3,2},{4,3},{5,4},{6,5},{7,6},{8,7},{9,8},{10,9},{11,1... | collective-permute-start | bytes 245768 | tf_op jit(solution)/shard_map/ppermute | solution.py:191
